TPU v7x, 32 devices: a whole 2x2x4 slice. The times are simulated.
32 devices in a mesh: groups: 2 (over y), ctx: 4 (over z), head: 2 (over x), rep: 2 (over core).
Axes of the slice: x: 2, y: 2, z: 4, core: 2. Of those that a mesh axis runs over, the one named last changes fastest.
Arguments:
- query: bfloat16 [2048, 4096], P(('groups', 'ctx', 'rep'), 'head'), parts along dimension 0, may hold values from -23.069359 to 23.069359
- key: bfloat16 [4096, 1024], P(('groups', 'ctx'), 'head'), parts along dimension 0, may hold values from -6 to 6
- value: bfloat16 [4096, 1024], P(('groups', 'ctx'), 'head'), parts along dimension 0, may hold values from -24 to 24
- out_weight: bfloat16 [4096, 4096], P('head'), may hold values from -0.375 to 0.375
- cotangent: bfloat16 [2048, 4096], P(('groups', 'ctx', 'rep')), parts along dimension 0, may hold values from -6 to 6
- response: int32 [2048], P(('groups', 'ctx', 'rep')), parts along dimension 0, may hold values 0 or 1
- segment_ids: int32 [4096], P(('groups', 'ctx')), parts along dimension 0, may hold values from 0 to 31, never falling along the last dimension, each value on 1 to 128 neighbouring positions
- masked_segments: int32 [8], P('groups'), parts along dimension 0, may hold values from 0 to 31
Outputs:
- patch_effect: bfloat16 [2048, 4096], P(('groups', 'ctx', 'rep'), 'head'), parts along dimension 0
- token_attr: float32 [4096], P(('groups', 'ctx')), parts along dimension 0
- segment_attr: float32 [64], P('groups'), parts along dimension 0
There are 2 independent parts, one for each index of `groups`. A program takes and returns all parts, laid end to end along the dimension named above; an argument that names none is the same for every part. Nothing has to cross between parts.
All inputs are finite; a program needn't handle non-finite values. No bound on the sum of `response` on one device may be relied on, other than what follows from the above.
Results may differ from a plain program's by a relative error of at most 0.0095.
Values may be sent and summed in bfloat16 or wider, within the bound.
No kernel may reach another device: no remote copies, remote signals or barrier semaphores. Data moves between devices by JAX's collectives and lax.ppermute only.
A program may use at most 128 MiB of HBM per device.

v0:
```python
from functools import partial

import jax
import jax.numpy as jnp
from jax import lax
from jax.sharding import PartitionSpec as P

HD = 128
SEG_DEV = 8


NEG_FILL = -1e30


def split_heads(incoming):
    return incoming.reshape(incoming.shape[0], -1, HD)


def block_scores(query_rows, key_block):
    raw_scores = jnp.einsum(
        "gqd,tgd->gqt", query_rows, split_heads(key_block), preferred_element_type=jnp.float32
    )
    return raw_scores * HD ** (-0.5)


def visible_keys(row_pos, first_key, key_rows):
    key_pos = first_key + jnp.arange(key_rows, dtype=jnp.int32)
    return key_pos[None, None, :] <= row_pos[None, :, None]


def online_update(running, scores, allowed, value_heads):
    row_top, row_total, weighted = running
    chosen = jnp.where(allowed, scores, NEG_FILL)
    new_top = jnp.maximum(row_top, jnp.max(chosen, axis=2))
    shrink = jnp.exp(row_top - new_top)
    weights = jnp.where(allowed, jnp.exp(chosen - new_top[:, :, None]), 0.0)
    row_total = row_total * shrink + jnp.sum(weights, axis=2)
    weighted = weighted * shrink[:, :, None] + jnp.einsum(
        "gqt,tgd->gqd",
        weights.astype(jnp.bfloat16),
        value_heads,
        preferred_element_type=jnp.float32,
    )
    return (new_top, row_total, weighted)


def forward_piece(query_rows, row_pos, running, incoming, first_key):
    key_block, value_block, kept_flag = incoming
    scores = block_scores(query_rows, key_block)
    visible = visible_keys(row_pos, first_key, key_block.shape[0])
    kept_visible = jnp.logical_and(visible, kept_flag[None, None, :] > 0)
    value_heads = split_heads(value_block)
    return (
        online_update(running[0], scores, visible, value_heads),
        online_update(running[1], scores, kept_visible, value_heads),
    )


def backward_terms(
    query_rows, row_pos, grad_rows, log_total, row_dot, key_block, value_block, first_key
):
    scores = block_scores(query_rows, key_block)
    visible = visible_keys(row_pos, first_key, key_block.shape[0])
    shifted = jnp.where(visible, scores - log_total[:, :, None], 0.0)
    probability = jnp.where(visible, jnp.exp(shifted), 0.0)
    grad_prob = jnp.einsum(
        "gqd,tgd->gqt", grad_rows, split_heads(value_block), preferred_element_type=jnp.float32
    )
    return jnp.sum(
        probability * (grad_prob + (grad_prob - row_dot[:, :, None]) * shifted), axis=(0, 1)
    )


def blockwise(stepper, state_in, incoming, block_rows):
    length = jax.tree.leaves(incoming)[0].shape[0]

    def advance(counter, state_now):
        offset = counter * block_rows
        portion = jax.tree.map(
            lambda member: lax.dynamic_slice_in_dim(member, offset, block_rows, 0), incoming
        )
        return stepper(state_now, portion, offset)

    return lax.fori_loop(0, length // block_rows, advance, state_in)


def finish_pass(running):
    row_top, row_total, weighted = running
    return (weighted / row_total[:, :, None], row_top + jnp.log(row_total))


def local(query, key, value, out_weight, cotangent, response, segment_ids, masked_segments):
    ctx_count = lax.axis_size("ctx")
    rep_count = lax.axis_size("rep")
    ctx_at = lax.axis_index("ctx")
    rep_at = lax.axis_index("rep")
    query_count = query.shape[0]
    key_count = key.shape[0]
    kv_local = key.shape[1] // HD
    heads_local = query.shape[1] // HD
    group_size = heads_local // kv_local
    context_len = key_count * ctx_count
    query_base = context_len - query_count * ctx_count * rep_count
    row_width = group_size * query_count
    kept_flag = jnp.where(
        jnp.any(segment_ids[:, None] == masked_segments[None, :], axis=1), 0.0, 1.0
    ).astype(jnp.bfloat16)
    grad_masked = jnp.where(response[:, None] > 0, cotangent, jnp.zeros_like(cotangent))
    grad_out = jnp.dot(grad_masked, out_weight.T, preferred_element_type=jnp.float32).astype(
        jnp.bfloat16
    )

    def grouped(rows_in):
        return rows_in.reshape(query_count, kv_local, group_size, HD).transpose(1, 2, 0, 3)

    fresh_state = (
        jnp.full((kv_local, row_width), NEG_FILL, jnp.float32),
        jnp.zeros((kv_local, row_width), jnp.float32),
        jnp.zeros((kv_local, row_width, HD), jnp.float32),
    )
    starting = (fresh_state, fresh_state)
    query_rows = grouped(query).reshape(kv_local, row_width, HD)
    grad_own = grouped(grad_out).reshape(kv_local, row_width, HD)
    base_pos = (
        query_base
        + (ctx_at * rep_count + rep_at) * query_count
        + jnp.arange(query_count, dtype=jnp.int32)
    )
    own_pos = jnp.tile(base_pos, group_size)
    forward_step = partial(forward_piece, query_rows, own_pos)
    running = blockwise(
        forward_step,
        starting,
        (
            lax.all_gather(key, "ctx", axis=0, tiled=True),
            lax.all_gather(value, "ctx", axis=0, tiled=True),
            lax.all_gather(kept_flag, "ctx", axis=0, tiled=True),
        ),
        key_count,
    )
    clean_out, log_total = finish_pass(running[0])
    masked_out, _ = finish_pass(running[1])
    row_dot = jnp.sum(grad_own.astype(jnp.float32) * clean_out, axis=2)

    def backward_step(total_now, incoming, first_key):
        added = backward_terms(
            query_rows, own_pos, grad_own, log_total, row_dot, incoming[0], incoming[1], first_key
        )
        current = lax.dynamic_slice_in_dim(total_now, first_key, incoming[0].shape[0], 0)
        return lax.dynamic_update_slice_in_dim(total_now, current + added, first_key, 0)

    empty_attr = jnp.zeros((context_len,), jnp.float32)
    attr_all = blockwise(
        backward_step,
        empty_attr,
        (
            lax.all_gather(key, "ctx", axis=0, tiled=True),
            lax.all_gather(value, "ctx", axis=0, tiled=True),
        ),
        key_count,
    )
    local_attr = lax.psum_scatter(attr_all, "ctx", scatter_dimension=0, tiled=True)
    change = (
        (masked_out - clean_out)
        .reshape(kv_local, group_size, query_count, HD)
        .transpose(2, 0, 1, 3)
        .reshape(query_count, heads_local * HD)
        .astype(jnp.bfloat16)
    )
    projected = jnp.dot(change, out_weight, preferred_element_type=jnp.float32)
    patch_effect = lax.psum_scatter(projected, "head", scatter_dimension=1, tiled=True).astype(
        jnp.bfloat16
    )
    token_attr = lax.psum(local_attr, ("head", "rep"))
    onehot = (
        segment_ids[:, None] == jnp.arange(SEG_DEV * ctx_count, dtype=jnp.int32)[None, :]
    ).astype(jnp.float32)
    segment_attr = lax.psum(jnp.dot(token_attr, onehot, precision=lax.Precision.HIGHEST), "ctx")
    return (patch_effect, token_attr, segment_attr)


def solution(mesh):
    return jax.shard_map(
        local,
        mesh=mesh,
        in_specs=(
            P(("groups", "ctx", "rep"), "head"),
            P(("groups", "ctx"), "head"),
            P(("groups", "ctx"), "head"),
            P("head", None),
            P(("groups", "ctx", "rep"), None),
            P(("groups", "ctx", "rep")),
            P(("groups", "ctx")),
            P("groups"),
        ),
        out_specs=(P(("groups", "ctx", "rep"), "head"), P(("groups", "ctx")), P("groups")),
        check_vma=False,
    )
```

profile of v0, /device:TPU:0, one launch (start us, length us, event | category | flops | bytes accessed | tf_op | source)
XLA Modules:
  0.0 224.0 jit_solution(5980120812336782876)
XLA Ops:
  7.3 2.1 copy.57
  9.5 2.0 copy.59
  11.6 1.4 reshape.201
  13.3 13.7 %all-gather = bf16[4,1,512]{2,1,0:T(2,128)(2,1)S(1)} all-gather(bf16[1,1,512]{2,1,0:T(2,128)(2,1)S(1)} %reshape.205), channel_id=1, replica_groups=mesh['groups'=2,'ctx'=4,'head'=2,'rep'=2] {'ctx'}, dimensions={0}, use_global_device_ids=true | all-gather | bytes 5120 | tf_op jit(solution)/shard_map/all_gather | solution.py:137
  27.1 11.5 %convolution_convert_fusion = bf16[128,2048]{1,0:T(8,128)(2,1)S(1)} fusion(bf16[2048,4096]{1,0:T(8,128)(2,1)} %param.15, bf16[128,4096]{1,0:T(8,128)(2,1)S(1)} %copy-done.3, pred[128]{0:T(512)(128)(4,1)S(1)} %broadcast_compare_fusion.2), kind=kOutput, calls=%fused_computation.53 | convolution fusion | flops 2148270080 | bytes 18350208 | tf_op jit(solution)/shard_map/dot_general | solution.py:109
  38.6 0.4 reshape.203
  39.2 0.7 dynamic-slice
  40.5 18.3 %all-gather.4.cloned.1.call-done = bf16[2048,512]{0,1:T(8,128)(2,1)} async-done(((bf16[512,512]{0,1:T(8,128)(2,1)}), bf16[2048,512]{0,1:T(8,128)(2,1)}) %all-gather.4.cloned.1.call-update) | async-done | bytes 2097168 | tf_op jit(solution)/shard_map/all_gather | solution.py:135
  58.9 46.4 %all-gather.6.cloned.1.call-done = bf16[2048,512]{0,1:T(8,128)(2,1)} async-done(((bf16[512,512]{0,1:T(8,128)(2,1)}), bf16[2048,512]{0,1:T(8,128)(2,1)}) %all-gather.6.cloned.1.call-update) | async-done | bytes 2097168 | tf_op jit(solution)/shard_map/all_gather | solution.py:136
  105.2 54.5 %while.39 = (s32[]{:T(128)}, f32[4,512]{1,0:T(4,128)S(1)}, f32[4,512]{1,0:T(4,128)S(1)}, f32[4,512,128]{2,1,0:T(8,128)S(1)}, f32[4,512]{1,0:T(4,128)S(1)}, /*ind...) while((s32[]{:T(128)}, f32[4,512]{1,0:T(4,128)S(1)}, ...), condition=%wide.region_6.7_spmd.clone, body=%wide.region_1.6_spmd.clone.sunk | while | flops 832591872 | bytes 52702004 | solution.py:84
  105.3 0.3 broadcast_compare_fusion.6
  105.6 1.1 constant_dynamic-slice_fusion.8
  106.7 3.4 %fusion.81 = (f32[4,512]{1,0:T(4,128)S(1)}, f32[4,512]{1,0:T(4,128)S(1)}, f32[4,512,512]{2,1,0:T(8,128)}) fusion(pred[512,512]{0,1:T(8,128)(4,1)S(1)} %get-tuple-element.631, pred[512,512]{0,1:T(8,128)(4,1)S(1)} %get-tuple-element.632, bf16[512,4,128]{0,2,1:T(8,128)(2,1)S(1)} %bitcast.121, bf16[4,512,128]{2,1,0:T(8,128)(2,1)S(1)} %get-tuple-element.682), kind=kOutput, calls=%fused_computation.19.clone.1 | convolution fusion | flops 273674240 | bytes 5783552 | tf_op jit(solution)/shard_map/while/body/eval_jaxpr/gqd,tgd->gqt/dot_general | solution.py:20
  110.1 3.7 %fusion.82 = (f32[4,512]{1,0:T(4,128)S(1)}, f32[4,512]{1,0:T(4,128)S(1)}) fusion(f32[4,512,512]{2,1,0:T(8,128)} %get-tuple-element.634, f32[4,512]{1,0:T(4,128)S(1)} %select_maximum_fusion.5, pred[512,512]{0,1:T(8,128)(4,1)S(1)} %get-tuple-element.631, f32[4,512]{1,0:T(4,128)S(1)} %select_maximum_fusion.4, pred[512,512]{0,1:T(8,128)(4,1)S(1)} %get-tuple-element.632), kind=kLoop, calls=%fused_computation.23.clone.1 | loop fusion | flops 9433088 | bytes 4751360 | tf_op jit(solution)/shard_map/while/body/eval_jaxpr/reduce_sum | solution.py:37
  113.9 1.1 constant_dynamic-slice_fusion.9
  115.0 1.9 fusion.85
  116.9 1.9 fusion.84
  119.0 0.3 broadcast_compare_fusion.6
  119.3 1.1 constant_dynamic-slice_fusion.8
  120.4 3.4 %fusion.81 = (f32[4,512]{1,0:T(4,128)S(1)}, f32[4,512]{1,0:T(4,128)S(1)}, f32[4,512,512]{2,1,0:T(8,128)}) fusion(pred[512,512]{0,1:T(8,128)(4,1)S(1)} %get-tuple-element.631, pred[512,512]{0,1:T(8,128)(4,1)S(1)} %get-tuple-element.632, bf16[512,4,128]{0,2,1:T(8,128)(2,1)S(1)} %bitcast.121, bf16[4,512,128]{2,1,0:T(8,128)(2,1)S(1)} %get-tuple-element.682), kind=kOutput, calls=%fused_computation.19.clone.1 | convolution fusion | flops 273674240 | bytes 5783552 | tf_op jit(solution)/shard_map/while/body/eval_jaxpr/gqd,tgd->gqt/dot_general | solution.py:20
  123.8 3.7 %fusion.82 = (f32[4,512]{1,0:T(4,128)S(1)}, f32[4,512]{1,0:T(4,128)S(1)}) fusion(f32[4,512,512]{2,1,0:T(8,128)} %get-tuple-element.634, f32[4,512]{1,0:T(4,128)S(1)} %select_maximum_fusion.5, pred[512,512]{0,1:T(8,128)(4,1)S(1)} %get-tuple-element.631, f32[4,512]{1,0:T(4,128)S(1)} %select_maximum_fusion.4, pred[512,512]{0,1:T(8,128)(4,1)S(1)} %get-tuple-element.632), kind=kLoop, calls=%fused_computation.23.clone.1 | loop fusion | flops 9433088 | bytes 4751360 | tf_op jit(solution)/shard_map/while/body/eval_jaxpr/reduce_sum | solution.py:37
  127.5 1.1 constant_dynamic-slice_fusion.9
  128.6 1.9 fusion.85
  130.6 1.9 fusion.84
  132.6 0.3 broadcast_compare_fusion.6
  132.9 1.1 constant_dynamic-slice_fusion.8
  134.0 3.4 %fusion.81 = (f32[4,512]{1,0:T(4,128)S(1)}, f32[4,512]{1,0:T(4,128)S(1)}, f32[4,512,512]{2,1,0:T(8,128)}) fusion(pred[512,512]{0,1:T(8,128)(4,1)S(1)} %get-tuple-element.631, pred[512,512]{0,1:T(8,128)(4,1)S(1)} %get-tuple-element.632, bf16[512,4,128]{0,2,1:T(8,128)(2,1)S(1)} %bitcast.121, bf16[4,512,128]{2,1,0:T(8,128)(2,1)S(1)} %get-tuple-element.682), kind=kOutput, calls=%fused_computation.19.clone.1 | convolution fusion | flops 273674240 | bytes 5783552 | tf_op jit(solution)/shard_map/while/body/eval_jaxpr/gqd,tgd->gqt/dot_general | solution.py:20
  137.4 3.7 %fusion.82 = (f32[4,512]{1,0:T(4,128)S(1)}, f32[4,512]{1,0:T(4,128)S(1)}) fusion(f32[4,512,512]{2,1,0:T(8,128)} %get-tuple-element.634, f32[4,512]{1,0:T(4,128)S(1)} %select_maximum_fusion.5, pred[512,512]{0,1:T(8,128)(4,1)S(1)} %get-tuple-element.631, f32[4,512]{1,0:T(4,128)S(1)} %select_maximum_fusion.4, pred[512,512]{0,1:T(8,128)(4,1)S(1)} %get-tuple-element.632), kind=kLoop, calls=%fused_computation.23.clone.1 | loop fusion | flops 9433088 | bytes 4751360 | tf_op jit(solution)/shard_map/while/body/eval_jaxpr/reduce_sum | solution.py:37
  141.2 1.1 constant_dynamic-slice_fusion.9
  142.3 1.9 fusion.85
  144.2 1.9 fusion.84
  146.2 0.3 broadcast_compare_fusion.6
  146.6 1.1 constant_dynamic-slice_fusion.8
  147.7 3.4 %fusion.81 = (f32[4,512]{1,0:T(4,128)S(1)}, f32[4,512]{1,0:T(4,128)S(1)}, f32[4,512,512]{2,1,0:T(8,128)}) fusion(pred[512,512]{0,1:T(8,128)(4,1)S(1)} %get-tuple-element.631, pred[512,512]{0,1:T(8,128)(4,1)S(1)} %get-tuple-element.632, bf16[512,4,128]{0,2,1:T(8,128)(2,1)S(1)} %bitcast.121, bf16[4,512,128]{2,1,0:T(8,128)(2,1)S(1)} %get-tuple-element.682), kind=kOutput, calls=%fused_computation.19.clone.1 | convolution fusion | flops 273674240 | bytes 5783552 | tf_op jit(solution)/shard_map/while/body/eval_jaxpr/gqd,tgd->gqt/dot_general | solution.py:20
  151.1 3.7 %fusion.82 = (f32[4,512]{1,0:T(4,128)S(1)}, f32[4,512]{1,0:T(4,128)S(1)}) fusion(f32[4,512,512]{2,1,0:T(8,128)} %get-tuple-element.634, f32[4,512]{1,0:T(4,128)S(1)} %select_maximum_fusion.5, pred[512,512]{0,1:T(8,128)(4,1)S(1)} %get-tuple-element.631, f32[4,512]{1,0:T(4,128)S(1)} %select_maximum_fusion.4, pred[512,512]{0,1:T(8,128)(4,1)S(1)} %get-tuple-element.632), kind=kLoop, calls=%fused_computation.23.clone.1 | loop fusion | flops 9433088 | bytes 4751360 | tf_op jit(solution)/shard_map/while/body/eval_jaxpr/reduce_sum | solution.py:37
  154.8 1.1 constant_dynamic-slice_fusion.9
  155.9 1.9 fusion.85
  157.8 1.9 fusion.84
  159.8 2.1 multiply_reduce_fusion
  162.0 0.3 copy.60
  162.2 9.5 %fusion.39 = f32[128,4096]{1,0:T(8,128)} fusion(bf16[128,2048]{0,1:T(8,128)(2,1)S(1)} %bitcast.122, bf16[2048,4096]{1,0:T(8,128)(2,1)} %param.15), kind=kOutput, calls=%fused_computation.70 | convolution fusion | flops 2147483648 | bytes 19398656 | tf_op jit(solution)/shard_map/dot_general | solution.py:170
  171.8 18.3 %while.38 = (s32[]{:T(128)}, f32[2048]{0:T(1024)S(1)}, bf16[2048,512]{0,1:T(8,128)(2,1)}, bf16[4,512,128]{2,1,0:T(8,128)(2,1)S(1)}, f32[4,512]{1,0:T(4,128)S(1)}...) while((s32[]{:T(128)}, f32[2048]{0:T(1024)S(1)}, ...), condition=%wide.region_11.12_spmd.clone, body=%wide.region_9.11_spmd.clone.sunk | while | flops 546570752 | bytes 13140663 | solution.py:84
  171.8 1.3 constant_dynamic-slice_fusion.7
  173.1 0.7 fusion.73
  173.8 0.2 broadcast_compare_fusion.5
  174.0 2.1 fusion.74
  176.1 0.2 add_dynamic-update-slice_fusion.2
  176.3 1.5 constant_dynamic-slice_fusion.7
  177.8 0.7 fusion.73
  178.5 0.2 broadcast_compare_fusion.5
  178.7 2.1 fusion.74
  181.0 1.3 constant_dynamic-slice_fusion.7
  182.3 0.7 fusion.73
  183.0 0.2 broadcast_compare_fusion.5
  183.2 2.1 fusion.74
  185.5 1.3 constant_dynamic-slice_fusion.7
  186.8 0.7 fusion.73
  187.5 0.2 broadcast_compare_fusion.5
  187.7 2.1 fusion.74
  190.0 9.4 %all-reduce = f32[2048]{0:T(1024)S(1)} all-reduce(f32[2048]{0:T(1024)S(1)} %get-tuple-element.365), channel_id=3, replica_groups=mesh['groups'=2,'ctx'=4,'head'=2,'rep'=2] {'ctx'}, use_global_device_ids=true, to_apply=%region_12.13.clone | all-reduce | flops 2048 | bytes 16384
  199.5 5.6 %psum.14 = f32[512]{0:T(512)S(1)} all-reduce(f32[512]{0:T(512)S(1)} %dynamic-slice.1), channel_id=1, replica_groups=mesh['groups'=2,'ctx'=4,'head'=2,'rep'=2] {'head','rep'}, use_global_device_ids=true, to_apply=%region_13.14 | all-reduce | flops 512 | bytes 4096 | tf_op jit(solution)/shard_map/psum | solution.py:174
  205.1 0.3 convolution_bitcast_fusion
  205.4 10.0 %psum.15 = f32[32]{0:T(128)} all-reduce(f32[32]{0:T(128)S(1)} %convolution_bitcast_fusion), channel_id=1, replica_groups=mesh['groups'=2,'ctx'=4,'head'=2,'rep'=2] {'ctx'}, use_global_device_ids=true, to_apply=%region_14.15 | all-reduce | flops 32 | bytes 256 | tf_op jit(solution)/shard_map/psum | solution.py:178
  215.4 2.1 convert_element_type.44
  (104 shorter events, 1.9 us)
Async XLA Ops:
  7.2 6.0 %copy-start.4 = (s32[512]{0:T(512)S(1)}, s32[512]{0:T(512)}, u32[]{:S(2)}) copy-start(s32[512]{0:T(512)} %param.18) | copy-start | bytes 6148
  7.2 6.0 %copy-start.6 = (s32[4]{0:T(128)S(1)}, s32[4]{0:T(128)}, u32[]{:S(2)}) copy-start(s32[4]{0:T(128)} %param.19) | copy-start | bytes 52
  7.2 19.9 %copy-start.7 = (s32[128]{0:T(128)S(1)}, s32[128]{0:T(128)}, u32[]{:S(2)}) copy-start(s32[128]{0:T(128)} %param.17) | copy-start | bytes 1540
  7.2 19.9 %copy-start.3 = (bf16[128,4096]{1,0:T(8,128)(2,1)S(1)}, bf16[128,4096]{1,0:T(8,128)(2,1)}, u32[]{:S(2)}) copy-start(bf16[128,4096]{1,0:T(8,128)(2,1)} %param.16) | copy-start | bytes 3145732
  7.2 51.7 %all-gather.4.cloned.1.call-start = ((), (), s32[]{:S(2)}) async-start(), calls=%async_computation.1 | async-start | bytes 2621440 | tf_op jit(solution)/shard_map/all_gather | solution.py:135
  9.4 95.8 %all-gather.6.cloned.1.call-start = ((), (), s32[]{:S(2)}) async-start(), calls=%async_computation.2 | async-start | bytes 2621440 | tf_op jit(solution)/shard_map/all_gather | solution.py:136
  11.5 203.9 %reduce-scatter.2.cloned.1.call-start = ((), (), s32[]{:S(2)}) async-start(), calls=%async_computation.3 | async-start | bytes 3145728 | tf_op jit(solution)/shard_map/reduce_scatter | solution.py:171
  27.1 12.1 %copy-start.8 = (u32[32]{0:T(128)S(1)}, u32[32]{0:T(128)}, u32[]{:S(2)}) copy-start(u32[32]{0:T(128)} %constant.131) | copy-start | bytes 388
  110.1 4.9 %copy-start = (f32[4,512,512]{2,1,0:T(8,128)S(1)}, f32[4,512,512]{2,1,0:T(8,128)}, u32[]{:S(2)}) copy-start(f32[4,512,512]{2,1,0:T(8,128)} %get-tuple-element.634) | copy-start | bytes 12582916 | tf_op jit(solution)/shard_map/while
  110.1 4.9 %copy-start.1 = (f32[4,512,128]{2,1,0:T(8,128)S(1)}, f32[4,512,128]{2,1,0:T(8,128)}, u32[]{:S(2)}) copy-start(f32[4,512,128]{2,1,0:T(8,128)} %get-tuple-element.664) | copy-start | bytes 3145732 | tf_op jit(solution)/shard_map/while
  116.9 1.9 copy-start.2
  123.8 4.9 %copy-start = (f32[4,512,512]{2,1,0:T(8,128)S(1)}, f32[4,512,512]{2,1,0:T(8,128)}, u32[]{:S(2)}) copy-start(f32[4,512,512]{2,1,0:T(8,128)} %get-tuple-element.634) | copy-start | bytes 12582916 | tf_op jit(solution)/shard_map/while
  123.8 4.9 %copy-start.1 = (f32[4,512,128]{2,1,0:T(8,128)S(1)}, f32[4,512,128]{2,1,0:T(8,128)}, u32[]{:S(2)}) copy-start(f32[4,512,128]{2,1,0:T(8,128)} %get-tuple-element.664) | copy-start | bytes 3145732 | tf_op jit(solution)/shard_map/while
  130.6 1.9 copy-start.2
  137.4 4.9 %copy-start = (f32[4,512,512]{2,1,0:T(8,128)S(1)}, f32[4,512,512]{2,1,0:T(8,128)}, u32[]{:S(2)}) copy-start(f32[4,512,512]{2,1,0:T(8,128)} %get-tuple-element.634) | copy-start | bytes 12582916 | tf_op jit(solution)/shard_map/while
  137.4 4.9 %copy-start.1 = (f32[4,512,128]{2,1,0:T(8,128)S(1)}, f32[4,512,128]{2,1,0:T(8,128)}, u32[]{:S(2)}) copy-start(f32[4,512,128]{2,1,0:T(8,128)} %get-tuple-element.664) | copy-start | bytes 3145732 | tf_op jit(solution)/shard_map/while
  144.2 1.9 copy-start.2
  151.0 4.9 %copy-start = (f32[4,512,512]{2,1,0:T(8,128)S(1)}, f32[4,512,512]{2,1,0:T(8,128)}, u32[]{:S(2)}) copy-start(f32[4,512,512]{2,1,0:T(8,128)} %get-tuple-element.634) | copy-start | bytes 12582916 | tf_op jit(solution)/shard_map/while
  151.0 4.9 %copy-start.1 = (f32[4,512,128]{2,1,0:T(8,128)S(1)}, f32[4,512,128]{2,1,0:T(8,128)}, u32[]{:S(2)}) copy-start(f32[4,512,128]{2,1,0:T(8,128)} %get-tuple-element.664) | copy-start | bytes 3145732 | tf_op jit(solution)/shard_map/while
  157.8 1.9 copy-start.2
  205.1 12.4 %copy-start.5 = (f32[512]{0:T(512)}, f32[512]{0:T(512)S(1)}, u32[]{:S(2)}) copy-start(f32[512]{0:T(512)S(1)} %psum.14) | copy-start | bytes 6148
Sparse Core Ops, SparseCore 0:
  10.2 48.6 all-gather.3
  60.4 44.7 all-gather.5
  171.9 30.5 reduce-scatter.1
where the time goes:
time: 225 us; the launch traced here: 224 us
  waiting for transfers between devices  64.7 us (29%)
  matrix products  61.2 us (27%)
  blocking collectives  38.7 us (17%)
  other arithmetic  22.6 us (10%)
  local copies, waits for them, and re-layouts  21.4 us (10%)
  between operations  14.7 us (7%)
    all_gather x1, waiting for transfers between devices, local(): lax.all_gather(value, 'ctx', axis=0, tiled=True)  46.4 us
    all_gather x1, waiting for transfers between devices, local(): lax.all_gather(key, 'ctx', axis=0, tiled=True)  18.3 us
    dot_general x8, matrix products, block_scores(): jnp.einsum('gqd,tgd->gqt', query_rows, split_heads(key_block), preferred_...  16.3 us
    dot_general x8, matrix products, online_update(): jnp.einsum('gqt,tgd->gqd', weights.astype(jnp.bfloat16), value_heads, pre...  15.3 us
    reduce_sum x4, other arithmetic, online_update(): row_total = row_total * shrink + jnp.sum(weights, axis=2)  14.8 us
    dynamic_slice x12, local copies, waits for them, and re-layouts, advance(): lax.dynamic_slice_in_dim(member, offset, block_rows, 0)  14 us
    all_gather x1, blocking collectives, local(): lax.all_gather(kept_flag, 'ctx', axis=0, tiled=True)  13.7 us
    dot_general x1, matrix products, local(): jnp.dot(grad_masked, out_weight.T, preferred_element_type=jnp.float32)  11.5 us
  transfers between devices with their start and end apart: 3, of which 2 were waited for; matrix products, arithmetic and copies ran while one was open for 16% of the time, Pallas kernels for 0%

commit v1 on v0

v1 whole, which is shorter than its diff:
```python
import functools

import jax
import jax.numpy as jnp
from jax import lax
from jax.experimental import pallas as pl
from jax.experimental.pallas import tpu as pltpu
from jax.sharding import PartitionSpec as P

HD = 128
SEG_DEV = 8
NEG_FILL = -1e30
NT_DIMS = (((1,), (1,)), ((), ()))


def attention_kernel(base_ref, q_ref, k_ref, v_ref, kept_ref, do_ref, delta_ref, attr_ref, *, tq):
    r = pl.program_id(2)
    first = (pl.program_id(0) == 0) & (pl.program_id(1) == 0) & (r == 0)

    @pl.when(first)
    def _():
        attr_ref[...] = jnp.zeros_like(attr_ref)

    q = q_ref[...]
    k = k_ref[...]
    v = v_ref[...]
    keys = k.shape[0]
    s = lax.dot_general(q, k, NT_DIMS, preferred_element_type=jnp.float32) * (HD ** -0.5)
    row_pos = base_ref[0] + r * tq + lax.broadcasted_iota(jnp.int32, (tq, keys), 0)
    key_pos = lax.broadcasted_iota(jnp.int32, (tq, keys), 1)
    vis = key_pos <= row_pos
    kvis = jnp.logical_and(vis, kept_ref[...] > 0.0)
    m_c = jnp.max(jnp.where(vis, s, NEG_FILL), axis=1, keepdims=True)
    m_m = jnp.max(jnp.where(kvis, s, NEG_FILL), axis=1, keepdims=True)
    e_c = jnp.where(vis, jnp.exp(s - m_c), 0.0)
    e_m = jnp.where(kvis, jnp.exp(s - m_m), 0.0)
    l_c = jnp.sum(e_c, axis=1, keepdims=True)
    l_m = jnp.sum(e_m, axis=1, keepdims=True)
    o_c = jnp.dot(e_c.astype(jnp.bfloat16), v, preferred_element_type=jnp.float32) / l_c
    o_m = jnp.dot(e_m.astype(jnp.bfloat16), v, preferred_element_type=jnp.float32) / l_m
    delta_ref[...] = (o_m - o_c).astype(delta_ref.dtype)
    g_rows = do_ref[...]
    row_dot = jnp.sum(g_rows.astype(jnp.float32) * o_c, axis=1, keepdims=True)
    d_p = lax.dot_general(g_rows, v, NT_DIMS, preferred_element_type=jnp.float32)
    log_total = m_c + jnp.log(l_c)
    prob = e_c * (1.0 / l_c)
    contrib = prob * (d_p + (d_p - row_dot) * (s - log_total))
    attr_ref[...] += jnp.sum(contrib, axis=0, keepdims=True)


def fused_attention(base, query, key_all, value_all, kept, grad_out, group_size):
    qc, width = query.shape
    keys, kv_width = key_all.shape
    kv_local = kv_width // HD
    tq = max(8, min(qc, (128 * 2048) // keys))
    n_rows = qc // tq
    grid = (kv_local, group_size, n_rows)

    def head_map(g, j, r, b):
        return (r, g * group_size + j)

    def kv_map(g, j, r, b):
        return (0, g)

    def fixed(g, j, r, b):
        return (0, 0)

    flops = 8 * qc * keys * HD * kv_local * group_size
    cost = pl.CostEstimate(
        flops=flops,
        transcendentals=2 * qc * keys * kv_local * group_size,
        bytes_accessed=2 * (query.size + key_all.size + value_all.size + grad_out.size + query.size)
        + 4 * keys,
    )
    return pl.pallas_call(
        functools.partial(attention_kernel, tq=tq),
        grid_spec=pltpu.PrefetchScalarGridSpec(
            num_scalar_prefetch=1,
            grid=grid,
            in_specs=[
                pl.BlockSpec((tq, HD), head_map),
                pl.BlockSpec((keys, HD), kv_map),
                pl.BlockSpec((keys, HD), kv_map),
                pl.BlockSpec((1, keys), fixed),
                pl.BlockSpec((tq, HD), head_map),
            ],
            out_specs=[
                pl.BlockSpec((tq, HD), head_map),
                pl.BlockSpec((1, keys), fixed),
            ],
        ),
        out_shape=[
            jax.ShapeDtypeStruct((qc, width), jnp.bfloat16),
            jax.ShapeDtypeStruct((1, keys), jnp.float32),
        ],
        compiler_params=pltpu.CompilerParams(
            dimension_semantics=("arbitrary", "arbitrary", "arbitrary")
        ),
        cost_estimate=cost,
    )(base, query, key_all, value_all, kept, grad_out)


def gather_kv(key, value, rep_at, rep_count):
    if rep_count != 2:
        return (
            lax.all_gather(key, "ctx", axis=0, tiled=True),
            lax.all_gather(value, "ctx", axis=0, tiled=True),
        )
    payload = jnp.where(rep_at == 0, key, value)
    mine = lax.all_gather(payload, "ctx", axis=0, tiled=True)
    other = lax.ppermute(mine, "rep", [(0, 1), (1, 0)])
    first = rep_at == 0
    return jnp.where(first, mine, other), jnp.where(first, other, mine)


def local(query, key, value, out_weight, cotangent, response, segment_ids, masked_segments):
    ctx_count = lax.axis_size("ctx")
    rep_count = lax.axis_size("rep")
    ctx_at = lax.axis_index("ctx")
    rep_at = lax.axis_index("rep")
    query_count = query.shape[0]
    key_count = key.shape[0]
    kv_local = key.shape[1] // HD
    heads_local = query.shape[1] // HD
    group_size = heads_local // kv_local
    context_len = key_count * ctx_count
    query_base = context_len - query_count * ctx_count * rep_count
    base = (query_base + (ctx_at * rep_count + rep_at) * query_count).astype(jnp.int32)
    base = jnp.reshape(base, (1,))

    seg_all = lax.all_gather(segment_ids, "ctx", axis=0, tiled=True)
    kept = jnp.where(
        jnp.any(seg_all[:, None] == masked_segments[None, :], axis=1), 0.0, 1.0
    ).astype(jnp.float32)[None, :]
    key_all, value_all = gather_kv(key, value, rep_at, rep_count)

    grad_masked = jnp.where(response[:, None] > 0, cotangent, jnp.zeros_like(cotangent))
    grad_out = jnp.dot(grad_masked, out_weight.T, preferred_element_type=jnp.float32).astype(
        jnp.bfloat16
    )
    delta, attr = fused_attention(base, query, key_all, value_all, kept, grad_out, group_size)

    projected = jnp.dot(delta, out_weight, preferred_element_type=jnp.float32).astype(jnp.bfloat16)
    patch_effect = lax.psum_scatter(projected, "head", scatter_dimension=1, tiled=True)

    attr_all = lax.psum(attr[0], ("ctx", "head", "rep"))
    token_attr = lax.dynamic_slice_in_dim(attr_all, ctx_at * key_count, key_count, 0)
    onehot = (
        seg_all[:, None] == jnp.arange(SEG_DEV * ctx_count, dtype=jnp.int32)[None, :]
    ).astype(jnp.float32)
    segment_attr = jnp.dot(attr_all, onehot, precision=lax.Precision.HIGHEST)
    return (patch_effect, token_attr, segment_attr)


def solution(mesh):
    return jax.shard_map(
        local,
        mesh=mesh,
        in_specs=(
            P(("groups", "ctx", "rep"), "head"),
            P(("groups", "ctx"), "head"),
            P(("groups", "ctx"), "head"),
            P("head", None),
            P(("groups", "ctx", "rep"), None),
            P(("groups", "ctx", "rep")),
            P(("groups", "ctx")),
            P("groups"),
        ),
        out_specs=(P(("groups", "ctx", "rep"), "head"), P(("groups", "ctx")), P("groups")),
        check_vma=False,
    )
```

time: 225 us -> 167 us (0.74)
  matrix products: 61.2 us -> 22.8 us
  Pallas kernels: 0 us -> 31.2 us
  local copies, waits for them, and re-layouts: 21.4 us -> 0.68 us
  other arithmetic: 22.6 us -> 6.49 us
  waiting for transfers between devices: 64.7 us -> 49.6 us
  blocking collectives: 38.7 us -> 42.2 us
    dot_general x22 -> x2, matrix products: 49.7 us -> 10.4 us  [the longest x1 9.28 us: local(): jnp.dot(delta, out_weight, preferred_element_type=jnp.float32)]
    pallas_call x0 -> x1, Pallas kernels: none -> 31.2 us  [fused_attention(): pl.pallas_call(functools.partial(attention_kernel, tq=tq), grid_spec=pltp...]
    reduce_sum x5 -> x0, other arithmetic: 16.9 us -> none  [the longest x4 14.8 us: online_update(): row_total = row_total * shrink + jnp.sum(weights, axis=2)]
    all_gather x2 -> x1, waiting for transfers between devices: 64.7 us -> 49.5 us  [gather_kv(): mine = lax.all_gather(payload, 'ctx', axis=0, tiled=True)]
    psum x2 -> x1, blocking collectives: 15.6 us -> 30.3 us  [local(): attr_all = lax.psum(attr[0], ('ctx', 'head', 'rep'))]
    dynamic_slice x12 -> x1, local copies, waits for them, and re-layouts: 14 us -> 0.66 us  [local(): lax.dynamic_slice_in_dim(attr_all, ctx_at * key_count, key_count, 0)]
    unnamed x1 -> x0, blocking collectives: 9.39 us -> none
    select_n x0 -> x3, other arithmetic: none -> 6.38 us  [the longest x1 3.81 us: gather_kv(): return (jnp.where(first, mine, other), jnp.where(first, other, mine))]
  transfers between devices with their start and end apart: 3 -> 3, of which waited for: 2 -> 1; matrix products, arithmetic and copies ran while one was open for 16% -> 9% of each run, Pallas kernels for 0% -> 0%
where the time goes in v1:
time: 167 us
  waiting for transfers between devices  49.6 us (30%)
  blocking collectives  42.2 us (25%)
  Pallas kernels  31.2 us (19%)
  matrix products  22.8 us (14%)
  between operations  14.1 us (8%)
  other arithmetic  6.49 us (4%)
    all_gather x1, waiting for transfers between devices, gather_kv(): mine = lax.all_gather(payload, 'ctx', axis=0, tiled=True)  49.5 us
    pallas_call x1, Pallas kernels, fused_attention(): pl.pallas_call(functools.partial(attention_kernel, tq=tq), grid_spec=pltp...  31.2 us
    psum x1, blocking collectives, local(): attr_all = lax.psum(attr[0], ('ctx', 'head', 'rep'))  30.3 us
    dot_general x1, matrix products, local(): jnp.dot(grad_masked, out_weight.T, preferred_element_type=jnp.float32)  12.4 us
    all_gather x1, blocking collectives, local(): seg_all = lax.all_gather(segment_ids, 'ctx', axis=0, tiled=True)  11.9 us
    dot_general x1, matrix products, local(): jnp.dot(delta, out_weight, preferred_element_type=jnp.float32)  9.28 us
    select_n x1, other arithmetic, gather_kv(): return (jnp.where(first, mine, other), jnp.where(first, other, mine))  3.81 us
  transfers between devices with their start and end apart: 3, of which 1 were waited for; matrix products, arithmetic and copies ran while one was open for 9% of the time, Pallas kernels for 0%

profile of v1, /device:TPU:0, one launch (start us, length us, event | category | flops | bytes accessed | tf_op | source)
XLA Modules:
  0.0 167.1 jit_solution(1153247920302441825)
XLA Ops:
  7.2 0.0 copy-start.3
  7.2 0.0 copy-start.4
  7.2 0.0 copy-start.5
  7.2 0.0 copy-start.1
  7.2 0.0 all-gather.3.cloned.1.call-start
  7.3 2.0 %broadcast_select_fusion.2 = bf16[512,512]{1,0:T(8,128)(2,1)} fusion(bf16[512,512]{1,0:T(8,128)(2,1)} %param.9, bf16[512,512]{1,0:T(8,128)(2,1)} %param.10, pred[]{:T(512)S(6)} %eq.14), kind=kLoop, calls=%fused_computation.10 | loop fusion | flops 262144 | bytes 1572865 | tf_op jit(solution)/shard_map/jit(_where)/select_n | solution.py:109
  9.2 0.0 all-gather.3.cloned.1.call-update
  9.3 0.0 reduce-scatter.2.cloned.1.call-start
  9.3 49.5 %all-gather.3.cloned.1.call-done = bf16[2048,512]{1,0:T(8,128)(2,1)} async-done(((bf16[512,512]{1,0:T(8,128)(2,1)}), bf16[2048,512]{1,0:T(8,128)(2,1)}) %all-gather.3.cloned.1.call-update) | async-done | bytes 2097168 | tf_op jit(solution)/shard_map/all_gather | solution.py:110
  58.9 0.0 collective-permute-start
  58.9 0.0 copy-done.3
  58.9 11.9 %all-gather = s32[4,1,512]{2,1,0:T(1,128)S(1)} all-gather(s32[1,1,512]{2,1,0:T(1,128)S(1)} %bitcast.17), channel_id=1, replica_groups=mesh['groups'=2,'ctx'=4,'head'=2,'rep'=2] {'ctx'}, dimensions={0}, use_global_device_ids=true | all-gather | bytes 10240 | tf_op jit(solution)/shard_map/all_gather | solution.py:131
  70.7 0.0 copy-done.4
  70.7 0.1 compare_reduce_fusion
  70.8 0.0 copy-done.5
  70.9 0.6 broadcast_select_fusion.3
  71.4 0.0 copy-done.1
  71.5 0.0 copy-start
  71.5 12.4 %convolution_convert_fusion.1.do_ref = bf16[128,2048]{1,0:T(8,128)(2,1)} fusion(bf16[2048,4096]{1,0:T(8,128)(2,1)} %param.11, bf16[128,4096]{1,0:T(8,128)(2,1)S(1)} %copy-done.1, pred[128]{0:T(512)(128)(4,1)S(1)} %broadcast_compare_fusion), kind=kOutput, calls=%fused_computation.1 | convolution fusion | flops 2148270080 | bytes 18350208 | tf_op jit(solution)/shard_map/dot_general | solution.py:138
  83.9 0.0 collective-permute-done
  83.9 0.0 copy-done
  83.9 3.8 %broadcast_select_fusion = (bf16[2048,512]{1,0:T(8,128)(2,1)}, bf16[2048,512]{1,0:T(8,128)(2,1)}) fusion(bf16[2048,512]{1,0:T(8,128)(2,1)} %collective-permute-done, bf16[2048,512]{1,0:T(8,128)(2,1)S(1)} %copy-done, pred[]{:T(512)S(6)} %eq.14), kind=kLoop, calls=%fused_computation.2 | loop fusion | flops 2097152 | bytes 8388609 | tf_op jit(solution)/shard_map/jit(_where)/select_n | solution.py:113
  87.7 31.2 %shard_map.103 = (bf16[128,2048]{1,0:T(8,128)(2,1)}, f32[1,2048]{1,0:T(1,128)}) custom-call(s32[1]{0:T(128)} %bitcast.base_ref, bf16[128,2048]{1,0:T(8,128)(2,1)} %q_ref.1, bf16[2048,512]{1,0:T(8,128)(2,1)} %get-tuple-element.8.k_ref, bf16[2048,512]{1,0:T(8,128)(2,1)} %get-tuple-element.7.v_ref, f32[1,2048]{1,0:T(1,128)} %bitcast.15, ...), custom_call_target="tpu_custom_call" | custom-call | flops 4294967296 | bytes 5775360 | tf_op jit(solution)/shard_map/pallas_call | solution.py:75
  118.8 0.0 copy-start.2
  118.9 9.3 %convolution_convert_fusion = bf16[128,4096]{1,0:T(8,128)(2,1)} fusion(bf16[128,2048]{1,0:T(8,128)(2,1)} %get-tuple-element.5, bf16[2048,4096]{1,0:T(8,128)(2,1)} %param.11), kind=kOutput, calls=%fused_computation | convolution fusion | flops 2148007936 | bytes 18350080 | tf_op jit(solution)/shard_map/dot_general | solution.py:143
  128.1 0.0 reduce-scatter.2.cloned.1.call-update
  128.2 0.0 copy-done.2
  128.2 30.3 %psum.7 = f32[2048]{0:T(1024)S(1)} all-reduce(f32[2048]{0:T(1024)S(1)} %bitcast.16), channel_id=1, replica_groups=mesh['groups'=2,'ctx'=4,'head'=2,'rep'=2] {'ctx','head','rep'}, use_global_device_ids=true, to_apply=%region_2.3 | all-reduce | flops 2048 | bytes 16384 | tf_op jit(solution)/shard_map/psum | solution.py:146
  158.5 0.7 dynamic_slice.3
  159.2 1.1 convolution_bitcast_fusion
  160.3 0.0 reduce-scatter.2.cloned.1.call-done
  (1 shorter events, 0.0 us)
Async XLA Ops:
  7.2 51.7 %copy-start.3 = (s32[512]{0:T(512)S(1)}, s32[512]{0:T(512)}, u32[]{:S(2)}) copy-start(s32[512]{0:T(512)} %param.14) | copy-start | bytes 6148
  7.2 63.6 %copy-start.4 = (s32[4]{0:T(128)S(1)}, s32[4]{0:T(128)}, u32[]{:S(2)}) copy-start(s32[4]{0:T(128)} %param.15) | copy-start | bytes 52
  7.2 63.6 %copy-start.5 = (s32[128]{0:T(128)S(1)}, s32[128]{0:T(128)}, u32[]{:S(2)}) copy-start(s32[128]{0:T(128)} %param.13) | copy-start | bytes 1540
  7.2 64.3 %copy-start.1 = (bf16[128,4096]{1,0:T(8,128)(2,1)S(1)}, bf16[128,4096]{1,0:T(8,128)(2,1)}, u32[]{:S(2)}) copy-start(bf16[128,4096]{1,0:T(8,128)(2,1)} %param.12) | copy-start | bytes 3145732
  7.2 51.6 %all-gather.3.cloned.1.call-start = ((), (), s32[]{:S(2)}) async-start(), calls=%async_computation.1 | async-start | bytes 2621440 | tf_op jit(solution)/shard_map/all_gather | solution.py:110
  9.3 151.0 %reduce-scatter.2.cloned.1.call-start = ((), (), s32[]{:S(2)}) async-start(), calls=%async_computation.2 | async-start | bytes 1572864 | tf_op jit(solution)/shard_map/reduce_scatter | solution.py:144
  58.9 25.0 %collective-permute-start = (bf16[2048,512]{1,0:T(8,128)(2,1)}, bf16[2048,512]{1,0:T(8,128)(2,1)}, u32[]{:S(2)}, u32[]{:S(2)}) collective-permute-start(bf16[2048,512]{1,0:T(8,128)(2,1)} %all-gather.3.cloned.1.call-done), channel_id=1, source_target_pairs={{0,1},{1,0},{2,3},{3,2},{4,5},{5,4},{6,7},{7,6},{8,9},{9,8},{10,11... | collective-permute-start | bytes 6291464 | tf_op jit(solution)/shard_map/ppermute | solution.py:111
  71.5 12.4 %copy-start = (bf16[2048,512]{1,0:T(8,128)(2,1)S(1)}, bf16[2048,512]{1,0:T(8,128)(2,1)}, u32[]{:S(2)}) copy-start(bf16[2048,512]{1,0:T(8,128)(2,1)} %all-gather.3.cloned.1.call-done) | copy-start | bytes 6291460
  118.8 9.3 %copy-start.2 = (f32[1,2048]{1,0:T(1,128)S(1)}, f32[1,2048]{1,0:T(1,128)}, u32[]{:S(2)}) copy-start(f32[1,2048]{1,0:T(1,128)} %get-tuple-element.6) | copy-start | bytes 24580
Sparse Core Ops, SparseCore 0:
  10.2 48.6 all-gather.2
  128.3 19.4 reduce-scatter.1

commit v2 on v1

--- a/solution.py
+++ b/solution.py
@@ -13,7 +13,7 @@
 NT_DIMS = (((1,), (1,)), ((), ()))
 
 
-def attention_kernel(base_ref, q_ref, k_ref, v_ref, kept_ref, do_ref, delta_ref, attr_ref, *, tq):
+def attention_kernel(base_ref, kpos_ref, q_ref, k_ref, v_ref, kept_ref, do_ref, delta_ref, attr_ref, *, tq):
     r = pl.program_id(2)
     first = (pl.program_id(0) == 0) & (pl.program_id(1) == 0) & (r == 0)
 
@@ -27,8 +27,7 @@
     keys = k.shape[0]
     s = lax.dot_general(q, k, NT_DIMS, preferred_element_type=jnp.float32) * (HD ** -0.5)
     row_pos = base_ref[0] + r * tq + lax.broadcasted_iota(jnp.int32, (tq, keys), 0)
-    key_pos = lax.broadcasted_iota(jnp.int32, (tq, keys), 1)
-    vis = key_pos <= row_pos
+    vis = kpos_ref[...] <= row_pos
     kvis = jnp.logical_and(vis, kept_ref[...] > 0.0)
     m_c = jnp.max(jnp.where(vis, s, NEG_FILL), axis=1, keepdims=True)
     m_m = jnp.max(jnp.where(kvis, s, NEG_FILL), axis=1, keepdims=True)
@@ -48,7 +47,7 @@
     attr_ref[...] += jnp.sum(contrib, axis=0, keepdims=True)
 
 
-def fused_attention(base, query, key_all, value_all, kept, grad_out, group_size):
+def fused_attention(base, key_pos, query, key_all, value_all, kept, grad_out, group_size):
     qc, width = query.shape
     keys, kv_width = key_all.shape
     kv_local = kv_width // HD
@@ -78,6 +77,7 @@
             num_scalar_prefetch=1,
             grid=grid,
             in_specs=[
+                pl.BlockSpec((1, keys), fixed),
                 pl.BlockSpec((tq, HD), head_map),
                 pl.BlockSpec((keys, HD), kv_map),
                 pl.BlockSpec((keys, HD), kv_map),
@@ -97,27 +97,64 @@
             dimension_semantics=("arbitrary", "arbitrary", "arbitrary")
         ),
         cost_estimate=cost,
-    )(base, query, key_all, value_all, kept, grad_out)
-
-
-def gather_kv(key, value, rep_at, rep_count):
-    if rep_count != 2:
-        return (
-            lax.all_gather(key, "ctx", axis=0, tiled=True),
-            lax.all_gather(value, "ctx", axis=0, tiled=True),
-        )
-    payload = jnp.where(rep_at == 0, key, value)
-    mine = lax.all_gather(payload, "ctx", axis=0, tiled=True)
-    other = lax.ppermute(mine, "rep", [(0, 1), (1, 0)])
-    first = rep_at == 0
-    return jnp.where(first, mine, other), jnp.where(first, other, mine)
+    )(base, key_pos, query, key_all, value_all, kept, grad_out)
+
+
+def gather_kv(key, value, segment_ids, ctx_at, rep_at, rep_count):
+    n = lax.axis_size("ctx")
+    key_count, width = key.shape
+    seg_rows = -(-key_count // width)
+    seg_pad = -(-seg_rows // 16) * 16
+    seg_block = jnp.zeros((seg_pad * width,), jnp.bfloat16)
+    seg_block = seg_block.at[:key_count].set(segment_ids.astype(jnp.bfloat16))
+    seg_block = seg_block.reshape(seg_pad, width)
+    split = rep_count == 2
+    halves = [jnp.where(rep_at == 0, key, value)] if split else [key, value]
+    payloads = [jnp.concatenate([h, seg_block], axis=0) for h in halves]
+    gathered = []
+    for payload in payloads:
+        parts = [payload] + [
+            lax.ppermute(payload, "ctx", [(i, (i + d) % n) for i in range(n)]) for d in range(1, n)
+        ]
+        gathered.append(parts)
+    if split:
+        mine = gathered[0]
+        theirs = [lax.ppermute(p, "rep", [(0, 1), (1, 0)]) for p in mine]
+        first = rep_at == 0
+        key_parts = [jnp.where(first, a, b) for a, b in zip(mine, theirs)]
+        value_parts = [jnp.where(first, b, a) for a, b in zip(mine, theirs)]
+    else:
+        key_parts, value_parts = gathered
+    key_all = jnp.concatenate([p[:key_count] for p in key_parts], axis=0)
+    value_all = jnp.concatenate([p[:key_count] for p in value_parts], axis=0)
+    seg_all = jnp.concatenate(
+        [p[key_count:].reshape(-1)[:key_count] for p in key_parts], axis=0
+    ).astype(jnp.int32)
+    source = (ctx_at - jnp.arange(n, dtype=jnp.int32)) % n
+    key_pos = (source[:, None] * key_count + jnp.arange(key_count, dtype=jnp.int32)[None, :])
+    return key_all, value_all, seg_all, key_pos.reshape(1, -1), source
+
+
+def butterfly_sum(total, axes):
+    for axis in axes:
+        n = lax.axis_size(axis)
+        if n & (n - 1):
+            total = lax.psum(total, axis)
+            continue
+        bit = 1
+        while bit < n:
+            total = total + lax.ppermute(total, axis, [(i, i ^ bit) for i in range(n)])
+            bit *= 2
+    return total
 
 
 def local(query, key, value, out_weight, cotangent, response, segment_ids, masked_segments):
     ctx_count = lax.axis_size("ctx")
     rep_count = lax.axis_size("rep")
+    head_count = lax.axis_size("head")
     ctx_at = lax.axis_index("ctx")
     rep_at = lax.axis_index("rep")
+    head_at = lax.axis_index("head")
     query_count = query.shape[0]
     key_count = key.shape[0]
     kv_local = key.shape[1] // HD
@@ -128,25 +165,41 @@
     base = (query_base + (ctx_at * rep_count + rep_at) * query_count).astype(jnp.int32)
     base = jnp.reshape(base, (1,))
 
-    seg_all = lax.all_gather(segment_ids, "ctx", axis=0, tiled=True)
+    key_all, value_all, seg_shift, key_pos, source = gather_kv(
+        key, value, segment_ids, ctx_at, rep_at, rep_count
+    )
     kept = jnp.where(
-        jnp.any(seg_all[:, None] == masked_segments[None, :], axis=1), 0.0, 1.0
+        jnp.any(seg_shift[:, None] == masked_segments[None, :], axis=1), 0.0, 1.0
     ).astype(jnp.float32)[None, :]
-    key_all, value_all = gather_kv(key, value, rep_at, rep_count)
 
     grad_masked = jnp.where(response[:, None] > 0, cotangent, jnp.zeros_like(cotangent))
     grad_out = jnp.dot(grad_masked, out_weight.T, preferred_element_type=jnp.float32).astype(
         jnp.bfloat16
     )
-    delta, attr = fused_attention(base, query, key_all, value_all, kept, grad_out, group_size)
-
-    projected = jnp.dot(delta, out_weight, preferred_element_type=jnp.float32).astype(jnp.bfloat16)
-    patch_effect = lax.psum_scatter(projected, "head", scatter_dimension=1, tiled=True)
-
-    attr_all = lax.psum(attr[0], ("ctx", "head", "rep"))
+    delta, attr = fused_attention(
+        base, key_pos, query, key_all, value_all, kept, grad_out, group_size
+    )
+
+    inverse = (ctx_at - jnp.arange(ctx_count, dtype=jnp.int32)) % ctx_count
+    attr_abs = attr.reshape(ctx_count, key_count)[inverse].reshape(-1)
+    seg_abs = seg_shift.reshape(ctx_count, key_count)[inverse].reshape(-1)
+    attr_all = butterfly_sum(attr_abs, ("rep", "head", "ctx"))
+
+    projected = jnp.dot(delta, out_weight, preferred_element_type=jnp.float32)
+    if head_count == 2:
+        cols = projected.shape[1] // 2
+        keep = lax.dynamic_slice_in_dim(projected, head_at * cols, cols, 1)
+        send = lax.dynamic_slice_in_dim(projected, (1 - head_at) * cols, cols, 1)
+        got = lax.ppermute(send.astype(jnp.bfloat16), "head", [(0, 1), (1, 0)])
+        patch_effect = (keep + got.astype(jnp.float32)).astype(jnp.bfloat16)
+    else:
+        patch_effect = lax.psum_scatter(
+            projected.astype(jnp.bfloat16), "head", scatter_dimension=1, tiled=True
+        )
+
     token_attr = lax.dynamic_slice_in_dim(attr_all, ctx_at * key_count, key_count, 0)
     onehot = (
-        seg_all[:, None] == jnp.arange(SEG_DEV * ctx_count, dtype=jnp.int32)[None, :]
+        seg_abs[:, None] == jnp.arange(SEG_DEV * ctx_count, dtype=jnp.int32)[None, :]
     ).astype(jnp.float32)
     segment_attr = jnp.dot(attr_all, onehot, precision=lax.Precision.HIGHEST)
     return (patch_effect, token_attr, segment_attr)

time: 167 us -> 124 us (0.74)
  blocking collectives: 42.2 us -> 0 us
  starting transfers between devices: 0.08 us -> 25.2 us
  waiting for transfers between devices: 49.6 us -> 34.6 us
  between operations: 14.1 us -> 0.85 us
  local copies, waits for them, and re-layouts: 0.68 us -> 4.2 us
    all_gather x1 -> x0, waiting for transfers between devices: 49.5 us -> none  [gather_kv(): mine = lax.all_gather(payload, 'ctx', axis=0, tiled=True)]
    ppermute x1 -> x12, waiting for transfers between devices: 0.01 us -> 34.6 us  [the longest x3 19.2 us: gather_kv(): lax.ppermute(payload, 'ctx', [(i, (i + d) % n) for i in range(n)])]
    psum x1 -> x0, blocking collectives: 30.3 us -> none  [local(): attr_all = lax.psum(attr[0], ('ctx', 'head', 'rep'))]
    ppermute x1 -> x12, starting transfers between devices: 0.01 us -> 25.2 us  [the longest x4 14.7 us: butterfly_sum(): total = total + lax.ppermute(total, axis, [(i, i ^ bit) for i in range(n)])]
    all_gather x1 -> x0, blocking collectives: 11.9 us -> none  [local(): seg_all = lax.all_gather(segment_ids, 'ctx', axis=0, tiled=True)]
    select_n x3 -> x11, other arithmetic: 6.38 us -> 2.35 us  [the longest x1 1.11 us: gather_kv(): halves = [jnp.where(rep_at == 0, key, value)] if split else [key, value]]
    concatenate x0 -> x2, other arithmetic: none -> 2.18 us  [the longest x1 2.15 us: gather_kv(): key_all = jnp.concatenate([p[:key_count] for p in key_parts], axis=0)]
  transfers between devices with their start and end apart: 3 -> 12, of which waited for: 1 -> 8; matrix products, arithmetic and copies ran while one was open for 9% -> 14% of each run, Pallas kernels for 0% -> 0%
where the time goes in v2:
time: 124 us; the launch traced here: 123 us
  waiting for transfers between devices  34.6 us (28%)
  Pallas kernels  29.7 us (24%)
  starting transfers between devices  25.2 us (20%)
  matrix products  22 us (18%)
  other arithmetic  7.04 us (6%)
  local copies, waits for them, and re-layouts  4.2 us (3%)
    pallas_call x1, Pallas kernels, fused_attention(): pl.pallas_call(functools.partial(attention_kernel, tq=tq), grid_spec=pltp...  29.7 us
    ppermute x3, waiting for transfers between devices, gather_kv(): lax.ppermute(payload, 'ctx', [(i, (i + d) % n) for i in range(n)])  19.2 us
    ppermute x4, starting transfers between devices, butterfly_sum(): total = total + lax.ppermute(total, axis, [(i, i ^ bit) for i in range(n)])  14.7 us
    ppermute x4, waiting for transfers between devices, butterfly_sum(): total = total + lax.ppermute(total, axis, [(i, i ^ bit) for i in range(n)])  13 us
    dot_general x1, matrix products, local(): jnp.dot(grad_masked, out_weight.T, preferred_element_type=jnp.float32)  12.6 us
    dot_general x1, matrix products, local(): projected = jnp.dot(delta, out_weight, preferred_element_type=jnp.float32)  8.3 us
    ppermute x3, starting transfers between devices, gather_kv(): lax.ppermute(payload, 'ctx', [(i, (i + d) % n) for i in range(n)])  7.93 us
  transfers between devices with their start and end apart: 12, of which 8 were waited for; matrix products, arithmetic and copies ran while one was open for 14% of the time, Pallas kernels for 0%

profile of v2, /device:TPU:0, one launch (start us, length us, event | category | flops | bytes accessed | tf_op | source)
XLA Modules:
  0.0 123.5 jit_solution(17996355221159381871)
XLA Ops:
  0.6 0.0 copy-start.4
  0.6 0.7 convert_element_type.29
  1.4 1.1 broadcast_select_fusion.4
  2.5 4.1 %collective-permute-start.3 = (bf16[528,512]{1,0:T(8,128)(2,1)S(1)}, bf16[528,512]{1,0:T(8,128)(2,1)S(1)}, u32[]{:S(2)}, u32[]{:S(2)}) collective-permute-start(bf16[528,512]{1,0:T(8,128)(2,1)S(1)} %pad_maximum_fusion.2), channel_id=1, source_target_pairs={{0,8},{4,12},{8,0},{12,4},{1,9},{5,13},{9,1},{13,5},{2,10},{6,14},... | collective-permute-start | bytes 1622024 | tf_op jit(solution)/shard_map/ppermute | solution.py:117
  6.6 1.6 %collective-permute-start.1 = (bf16[528,512]{1,0:T(8,128)(2,1)S(1)}, bf16[528,512]{1,0:T(8,128)(2,1)S(1)}, u32[]{:S(2)}, u32[]{:S(2)}) collective-permute-start(bf16[528,512]{1,0:T(8,128)(2,1)S(1)} %pad_maximum_fusion.2), channel_id=1, source_target_pairs={{0,4},{4,8},{8,12},{12,0},{1,5},{5,9},{9,13},{13,1},{2,6},{6,10},{... | collective-permute-start | bytes 1622024 | tf_op jit(solution)/shard_map/ppermute | solution.py:117
  8.2 2.2 %collective-permute-start.5 = (bf16[528,512]{1,0:T(8,128)(2,1)S(1)}, bf16[528,512]{1,0:T(8,128)(2,1)S(1)}, u32[]{:S(2)}, u32[]{:S(2)}) collective-permute-start(bf16[528,512]{1,0:T(8,128)(2,1)S(1)} %pad_maximum_fusion.2), channel_id=1, source_target_pairs={{0,12},{4,0},{8,4},{12,8},{1,13},{5,1},{9,5},{13,9},{2,14},{6,2},{... | collective-permute-start | bytes 1622024 | tf_op jit(solution)/shard_map/ppermute | solution.py:117
  10.5 0.0 collective-permute-start
  10.5 0.0 copy-done.4
  10.5 12.6 %convolution_convert_fusion.do_ref = bf16[128,2048]{1,0:T(8,128)(2,1)} fusion(bf16[2048,4096]{1,0:T(8,128)(2,1)} %param.13, bf16[128,4096]{1,0:T(8,128)(2,1)} %param.14, pred[128]{0:T(512)(128)(4,1)S(1)} %broadcast_compare_fusion), kind=kOutput, calls=%fused_computation.2 | convolution fusion | flops 2148270080 | bytes 18350208 | tf_op jit(solution)/shard_map/dot_general | solution.py:176
  23.1 0.1 add_bitcast_fusion
  23.1 0.6 copy.11
  23.7 19.2 %collective-permute-done.3 = bf16[528,512]{1,0:T(8,128)(2,1)S(1)} collective-permute-done((bf16[528,512]{1,0:T(8,128)(2,1)S(1)}, bf16[528,512]{1,0:T(8,128)(2,1)S(1)}, u32[]{:S(2)}, u32[]{:S(2)}) %collective-permute-start.3) | collective-permute-done | bytes 540704 | tf_op jit(solution)/shard_map/ppermute | solution.py:117
  43.0 0.0 collective-permute-start.4
  43.0 0.0 collective-permute-done.1
  43.0 0.5 collective-permute-start.2
  43.5 0.0 collective-permute-done
  43.5 0.1 broadcast_select_fusion.3
  43.6 0.0 copy-start.1
  43.6 0.0 collective-permute-done.5
  43.7 0.1 collective-permute-start.6
  43.7 0.1 fusion.3
  43.9 1.0 collective-permute-done.4
  44.9 0.1 broadcast_select_fusion.1
  45.0 0.0 copy-done.1
  45.0 0.0 copy-start
  45.0 0.7 collective-permute-done.2
  45.7 0.1 broadcast_select_fusion.2
  45.7 0.0 copy-start.3
  45.8 0.6 collective-permute-done.6
  46.4 0.1 broadcast_select_fusion
  46.5 0.0 copy-done
  46.6 0.0 copy-done.3
  46.6 0.1 compare_reduce_fusion
  46.7 0.6 broadcast_select_fusion.5
  47.3 0.0 slice-start
  47.3 0.0 slice-start.1
  47.3 0.1 slice_select_fusion.1
  47.4 0.1 slice_select_fusion.2
  47.4 0.1 slice_select_fusion
  47.5 0.8 slice-done
  48.4 0.2 slice-done.1
  48.5 2.1 %pad_maximum_fusion = (bf16[2048,512]{1,0:T(8,128)(2,1)}, bf16[2048,512]{1,0:T(8,128)(2,1)}) fusion(bf16[512,512]{1,0:T(8,128)(2,1)S(1)} %slice.78, bf16[512,512]{1,0:T(8,128)(2,1)S(1)} %slice-done, bf16[512,512]{1,0:T(8,128)(2,1)S(1)} %slice.76, bf16[512,512]{1,0:T(8,128)(2,1)S(1)} %slice-done.1, bf16[512,512]{1,0:T(8,128)(2,1)S(1)} %slice_select_fusion, ...), kind=kLoop, calls=%fused_computation.3 | loop fusion | flops 16777216 | bytes 8388608 | tf_op jit(solution)/shard_map/concatenate | solution.py:128
  50.7 29.7 %shard_map.103 = (bf16[128,2048]{1,0:T(8,128)(2,1)}, f32[1,2048]{1,0:T(1,128)}) custom-call(s32[1]{0:T(128)} %bitcast.base_ref, s32[1,2048]{1,0:T(1,128)} %bitcast.25, bf16[128,2048]{1,0:T(8,128)(2,1)} %q_ref.1, bf16[2048,512]{1,0:T(8,128)(2,1)} %get-tuple-element.19.k_ref, bf16[2048,512]{1,0:T(8,128)(2,1)} %get-tuple-element.20.v_ref, f32[1,2048]{1,0:T(1,128)} %bitcast.24, ...), custom_call_target="tpu_custom_call" | custom-call | flops 4294967296 | bytes 5775360 | tf_op jit(solution)/shard_map/pallas_call | solution.py:74
  80.3 0.0 copy-start.2
  80.3 8.3 %fusion.11 = f32[128,4096]{1,0:T(8,128)S(1)} fusion(bf16[128,2048]{1,0:T(8,128)(2,1)} %get-tuple-element.17, bf16[2048,4096]{1,0:T(8,128)(2,1)} %param.13), kind=kOutput, calls=%fused_computation.47 | convolution fusion | flops 2147483648 | bytes 19398656 | tf_op jit(solution)/shard_map/dot_general | solution.py:188
  88.6 0.1 dynamic-slice_convert_fusion
  88.7 2.0 %collective-permute-start.7 = (bf16[128,2048]{1,0:T(8,128)(2,1)S(1)}, bf16[128,2048]{1,0:T(8,128)(2,1)S(1)}, u32[]{:S(2)}, u32[]{:S(2)}) collective-permute-start(bf16[128,2048]{1,0:T(8,128)(2,1)S(1)} %dynamic-slice_convert_fusion), channel_id=1, source_target_pairs={{0,2},{2,0},{1,3},{3,1},{4,6},{6,4},{5,7},{7,5},{8,10},{10,8},{9,1... | collective-permute-start | bytes 1572872 | tf_op jit(solution)/shard_map/ppermute | solution.py:193
  90.7 0.5 broadcast.152
  91.2 0.0 copy-done.2
  91.2 0.7 reduce.13
  91.9 0.6 gather_fusion
  92.5 0.1 collective-permute-start.8
  92.6 1.2 collective-permute-done.8
  93.7 0.1 collective-permute-start.9
  93.9 9.2 %collective-permute-done.9 = f32[2048]{0:T(1024)S(1)} collective-permute-done((f32[2048]{0:T(1024)S(1)}, f32[2048]{0:T(1024)S(1)}, u32[]{:S(2)}, u32[]{:S(2)}) %collective-permute-start.9) | collective-permute-done | bytes 8224 | tf_op jit(solution)/shard_map/ppermute | solution.py:146
  103.0 10.6 %collective-permute-start.10 = (f32[2048]{0:T(1024)S(1)}, f32[2048]{0:T(1024)S(1)}, u32[]{:S(2)}, u32[]{:S(2)}) collective-permute-start(f32[2048]{0:T(1024)S(1)} %add.97), channel_id=1, source_target_pairs={{0,4},{4,0},{8,12},{12,8},{1,5},{5,1},{9,13},{13,9},{2,6},{6,2},{1... | collective-permute-start | bytes 24584 | tf_op jit(solution)/shard_map/ppermute | solution.py:146
  113.6 1.6 %collective-permute-done.10 = f32[2048]{0:T(1024)S(1)} collective-permute-done((f32[2048]{0:T(1024)S(1)}, f32[2048]{0:T(1024)S(1)}, u32[]{:S(2)}, u32[]{:S(2)}) %collective-permute-start.10) | collective-permute-done | bytes 8224 | tf_op jit(solution)/shard_map/ppermute | solution.py:146
  115.2 3.9 %collective-permute-start.11 = (f32[2048]{0:T(1024)S(1)}, f32[2048]{0:T(1024)S(1)}, u32[]{:S(2)}, u32[]{:S(2)}) collective-permute-start(f32[2048]{0:T(1024)S(1)} %add.98), channel_id=1, source_target_pairs={{0,8},{4,12},{8,0},{12,4},{1,9},{5,13},{9,1},{13,5},{2,10},{6,14},... | collective-permute-start | bytes 24584 | tf_op jit(solution)/shard_map/ppermute | solution.py:146
  119.2 0.6 gather_fusion.1
  119.7 1.0 collective-permute-done.11
  120.8 0.7 dynamic_slice.11
  121.4 1.1 convolution_bitcast_fusion
  122.5 0.0 collective-permute-done.7
  122.5 0.9 add_convert_fusion
  (22 shorter events, 0.3 us)
Async XLA Ops:
  0.6 9.8 %copy-start.4 = (s32[128]{0:T(128)S(1)}, s32[128]{0:T(128)}, u32[]{:S(2)}) copy-start(s32[128]{0:T(128)} %param.15) | copy-start | bytes 1540
  2.5 40.4 %collective-permute-start.3 = (bf16[528,512]{1,0:T(8,128)(2,1)S(1)}, bf16[528,512]{1,0:T(8,128)(2,1)S(1)}, u32[]{:S(2)}, u32[]{:S(2)}) collective-permute-start(bf16[528,512]{1,0:T(8,128)(2,1)S(1)} %pad_maximum_fusion.2), channel_id=1, source_target_pairs={{0,8},{4,12},{8,0},{12,4},{1,9},{5,13},{9,1},{13,5},{2,10},{6,14},... | collective-permute-start | bytes 1622024 | tf_op jit(solution)/shard_map/ppermute | solution.py:117
  6.6 36.3 %collective-permute-start.1 = (bf16[528,512]{1,0:T(8,128)(2,1)S(1)}, bf16[528,512]{1,0:T(8,128)(2,1)S(1)}, u32[]{:S(2)}, u32[]{:S(2)}) collective-permute-start(bf16[528,512]{1,0:T(8,128)(2,1)S(1)} %pad_maximum_fusion.2), channel_id=1, source_target_pairs={{0,4},{4,8},{8,12},{12,0},{1,5},{5,9},{9,13},{13,1},{2,6},{6,10},{... | collective-permute-start | bytes 1622024 | tf_op jit(solution)/shard_map/ppermute | solution.py:117
  8.2 35.5 %collective-permute-start.5 = (bf16[528,512]{1,0:T(8,128)(2,1)S(1)}, bf16[528,512]{1,0:T(8,128)(2,1)S(1)}, u32[]{:S(2)}, u32[]{:S(2)}) collective-permute-start(bf16[528,512]{1,0:T(8,128)(2,1)S(1)} %pad_maximum_fusion.2), channel_id=1, source_target_pairs={{0,12},{4,0},{8,4},{12,8},{1,13},{5,1},{9,5},{13,9},{2,14},{6,2},{... | collective-permute-start | bytes 1622024 | tf_op jit(solution)/shard_map/ppermute | solution.py:117
  10.5 33.0 %collective-permute-start = (bf16[528,512]{1,0:T(8,128)(2,1)S(1)}, bf16[528,512]{1,0:T(8,128)(2,1)S(1)}, u32[]{:S(2)}, u32[]{:S(2)}) collective-permute-start(bf16[528,512]{1,0:T(8,128)(2,1)S(1)} %pad_maximum_fusion.2), channel_id=1, source_target_pairs={{0,1},{1,0},{2,3},{3,2},{4,5},{5,4},{6,7},{7,6},{8,9},{9,8},{10,11... | collective-permute-start | bytes 1622024 | tf_op jit(solution)/shard_map/ppermute | solution.py:122
  43.0 1.9 %collective-permute-start.4 = (bf16[528,512]{1,0:T(8,128)(2,1)S(1)}, bf16[528,512]{1,0:T(8,128)(2,1)S(1)}, u32[]{:S(2)}, u32[]{:S(2)}) collective-permute-start(bf16[528,512]{1,0:T(8,128)(2,1)S(1)} %collective-permute-done.3), channel_id=1, source_target_pairs={{0,1},{1,0},{2,3},{3,2},{4,5},{5,4},{6,7},{7,6},{8,9},{9,8},{10,11... | collective-permute-start | bytes 1622024 | tf_op jit(solution)/shard_map/ppermute | solution.py:122
  43.0 2.7 %collective-permute-start.2 = (bf16[528,512]{1,0:T(8,128)(2,1)S(1)}, bf16[528,512]{1,0:T(8,128)(2,1)S(1)}, u32[]{:S(2)}, u32[]{:S(2)}) collective-permute-start(bf16[528,512]{1,0:T(8,128)(2,1)S(1)} %collective-permute-done.1), channel_id=1, source_target_pairs={{0,1},{1,0},{2,3},{3,2},{4,5},{5,4},{6,7},{7,6},{8,9},{9,8},{10,11... | collective-permute-start | bytes 1622024 | tf_op jit(solution)/shard_map/ppermute | solution.py:122
  43.6 1.3 %copy-start.1 = (bf16[528,512]{1,0:T(8,128)(2,1)}, bf16[528,512]{1,0:T(8,128)(2,1)S(1)}, u32[]{:S(2)}) copy-start(bf16[528,512]{1,0:T(8,128)(2,1)S(1)} %broadcast_select_fusion.3) | copy-start | bytes 1622020
  43.7 2.8 %collective-permute-start.6 = (bf16[528,512]{1,0:T(8,128)(2,1)S(1)}, bf16[528,512]{1,0:T(8,128)(2,1)S(1)}, u32[]{:S(2)}, u32[]{:S(2)}) collective-permute-start(bf16[528,512]{1,0:T(8,128)(2,1)S(1)} %collective-permute-done.5), channel_id=1, source_target_pairs={{0,1},{1,0},{2,3},{3,2},{4,5},{5,4},{6,7},{7,6},{8,9},{9,8},{10,11... | collective-permute-start | bytes 1622024 | tf_op jit(solution)/shard_map/ppermute | solution.py:122
  45.0 1.5 %copy-start = (bf16[528,512]{1,0:T(8,128)(2,1)}, bf16[528,512]{1,0:T(8,128)(2,1)S(1)}, u32[]{:S(2)}) copy-start(bf16[528,512]{1,0:T(8,128)(2,1)S(1)} %broadcast_select_fusion.1) | copy-start | bytes 1622020
  45.7 0.9 copy-start.3
  47.3 1.0 slice-start
  47.3 1.2 slice-start.1
  80.3 10.9 %copy-start.2 = (f32[1,2048]{1,0:T(1,128)S(1)}, f32[1,2048]{1,0:T(1,128)}, u32[]{:S(2)}) copy-start(f32[1,2048]{1,0:T(1,128)} %get-tuple-element.18) | copy-start | bytes 24580
  88.7 33.8 %collective-permute-start.7 = (bf16[128,2048]{1,0:T(8,128)(2,1)S(1)}, bf16[128,2048]{1,0:T(8,128)(2,1)S(1)}, u32[]{:S(2)}, u32[]{:S(2)}) collective-permute-start(bf16[128,2048]{1,0:T(8,128)(2,1)S(1)} %dynamic-slice_convert_fusion), channel_id=1, source_target_pairs={{0,2},{2,0},{1,3},{3,1},{4,6},{6,4},{5,7},{7,5},{8,10},{10,8},{9,1... | collective-permute-start | bytes 1572872 | tf_op jit(solution)/shard_map/ppermute | solution.py:193
  92.5 1.2 %collective-permute-start.8 = (f32[2048]{0:T(1024)S(1)}, f32[2048]{0:T(1024)S(1)}, u32[]{:S(2)}, u32[]{:S(2)}) collective-permute-start(f32[2048]{0:T(1024)S(1)} %bitcast.19), channel_id=1, source_target_pairs={{0,1},{1,0},{2,3},{3,2},{4,5},{5,4},{6,7},{7,6},{8,9},{9,8},{10,11... | collective-permute-start | bytes 24584 | tf_op jit(solution)/shard_map/ppermute | solution.py:146
  93.7 9.3 %collective-permute-start.9 = (f32[2048]{0:T(1024)S(1)}, f32[2048]{0:T(1024)S(1)}, u32[]{:S(2)}, u32[]{:S(2)}) collective-permute-start(f32[2048]{0:T(1024)S(1)} %add.96), channel_id=1, source_target_pairs={{0,2},{2,0},{1,3},{3,1},{4,6},{6,4},{5,7},{7,5},{8,10},{10,8},{9,1... | collective-permute-start | bytes 24584 | tf_op jit(solution)/shard_map/ppermute | solution.py:146
  103.0 12.2 %collective-permute-start.10 = (f32[2048]{0:T(1024)S(1)}, f32[2048]{0:T(1024)S(1)}, u32[]{:S(2)}, u32[]{:S(2)}) collective-permute-start(f32[2048]{0:T(1024)S(1)} %add.97), channel_id=1, source_target_pairs={{0,4},{4,0},{8,12},{12,8},{1,5},{5,1},{9,13},{13,9},{2,6},{6,2},{1... | collective-permute-start | bytes 24584 | tf_op jit(solution)/shard_map/ppermute | solution.py:146
  115.2 5.6 %collective-permute-start.11 = (f32[2048]{0:T(1024)S(1)}, f32[2048]{0:T(1024)S(1)}, u32[]{:S(2)}, u32[]{:S(2)}) collective-permute-start(f32[2048]{0:T(1024)S(1)} %add.98), channel_id=1, source_target_pairs={{0,8},{4,12},{8,0},{12,4},{1,9},{5,13},{9,1},{13,5},{2,10},{6,14},... | collective-permute-start | bytes 24584 | tf_op jit(solution)/shard_map/ppermute | solution.py:146

commit v3 on v2

--- a/solution.py
+++ b/solution.py
@@ -13,21 +13,27 @@
 NT_DIMS = (((1,), (1,)), ((), ()))
 
 
-def attention_kernel(base_ref, kpos_ref, q_ref, k_ref, v_ref, kept_ref, do_ref, delta_ref, attr_ref, *, tq):
+def score_block(base_ref, kpos_ref, q_ref, k_ref, tq):
+    r = pl.program_id(2)
+    s = lax.dot_general(q_ref[...], k_ref[...], NT_DIMS, preferred_element_type=jnp.float32)
+    s = s * (HD ** -0.5)
+    row_pos = base_ref[0] + r * tq + lax.broadcasted_iota(jnp.int32, s.shape, 0)
+    return s, kpos_ref[...] <= row_pos
+
+
+def forward_kernel(
+    base_ref, kpos_ref, q_ref, k_ref, v_ref, kept_ref, do_ref, w_ref,
+    delta_ref, lse_ref, dot_ref, patch_ref, *, tq
+):
     r = pl.program_id(2)
     first = (pl.program_id(0) == 0) & (pl.program_id(1) == 0) & (r == 0)
 
     @pl.when(first)
     def _():
-        attr_ref[...] = jnp.zeros_like(attr_ref)
-
-    q = q_ref[...]
-    k = k_ref[...]
+        patch_ref[...] = jnp.zeros_like(patch_ref)
+
+    s, vis = score_block(base_ref, kpos_ref, q_ref, k_ref, tq)
     v = v_ref[...]
-    keys = k.shape[0]
-    s = lax.dot_general(q, k, NT_DIMS, preferred_element_type=jnp.float32) * (HD ** -0.5)
-    row_pos = base_ref[0] + r * tq + lax.broadcasted_iota(jnp.int32, (tq, keys), 0)
-    vis = kpos_ref[...] <= row_pos
     kvis = jnp.logical_and(vis, kept_ref[...] > 0.0)
     m_c = jnp.max(jnp.where(vis, s, NEG_FILL), axis=1, keepdims=True)
     m_m = jnp.max(jnp.where(kvis, s, NEG_FILL), axis=1, keepdims=True)
@@ -37,20 +43,38 @@
     l_m = jnp.sum(e_m, axis=1, keepdims=True)
     o_c = jnp.dot(e_c.astype(jnp.bfloat16), v, preferred_element_type=jnp.float32) / l_c
     o_m = jnp.dot(e_m.astype(jnp.bfloat16), v, preferred_element_type=jnp.float32) / l_m
-    delta_ref[...] = (o_m - o_c).astype(delta_ref.dtype)
-    g_rows = do_ref[...]
-    row_dot = jnp.sum(g_rows.astype(jnp.float32) * o_c, axis=1, keepdims=True)
-    d_p = lax.dot_general(g_rows, v, NT_DIMS, preferred_element_type=jnp.float32)
-    log_total = m_c + jnp.log(l_c)
-    prob = e_c * (1.0 / l_c)
-    contrib = prob * (d_p + (d_p - row_dot) * (s - log_total))
+    delta = (o_m - o_c).astype(jnp.bfloat16)
+    delta_ref[...] = delta
+    lse_ref[0] = m_c + jnp.log(l_c)
+    dot_ref[0] = jnp.sum(do_ref[...].astype(jnp.float32) * o_c, axis=1, keepdims=True)
+    rows = pl.ds(pl.multiple_of(r * tq, 8), tq)
+    patch_ref[rows, :] += jnp.dot(delta, w_ref[...], preferred_element_type=jnp.float32)
+
+
+def backward_kernel(
+    base_ref, kpos_ref, q_ref, k_ref, v_ref, do_ref, lse_ref, dot_ref, attr_ref, *, tq
+):
+    r = pl.program_id(2)
+    first = (pl.program_id(0) == 0) & (pl.program_id(1) == 0) & (r == 0)
+
+    @pl.when(first)
+    def _():
+        attr_ref[...] = jnp.zeros_like(attr_ref)
+
+    s, vis = score_block(base_ref, kpos_ref, q_ref, k_ref, tq)
+    shifted = s - lse_ref[0]
+    prob = jnp.where(vis, jnp.exp(shifted), 0.0)
+    d_p = lax.dot_general(do_ref[...], v_ref[...], NT_DIMS, preferred_element_type=jnp.float32)
+    contrib = prob * (d_p + (d_p - dot_ref[0]) * shifted)
     attr_ref[...] += jnp.sum(contrib, axis=0, keepdims=True)
 
 
-def fused_attention(base, key_pos, query, key_all, value_all, kept, grad_out, group_size):
+def fused_attention(base, key_pos, query, key_all, value_all, kept, grad_out, out_weight, group_size):
     qc, width = query.shape
     keys, kv_width = key_all.shape
     kv_local = kv_width // HD
+    heads_local = kv_local * group_size
+    model = out_weight.shape[1]
     tq = max(8, min(qc, (128 * 2048) // keys))
     n_rows = qc // tq
     grid = (kv_local, group_size, n_rows)
@@ -64,15 +88,16 @@
     def fixed(g, j, r, b):
         return (0, 0)
 
-    flops = 8 * qc * keys * HD * kv_local * group_size
-    cost = pl.CostEstimate(
-        flops=flops,
-        transcendentals=2 * qc * keys * kv_local * group_size,
-        bytes_accessed=2 * (query.size + key_all.size + value_all.size + grad_out.size + query.size)
-        + 4 * keys,
-    )
-    return pl.pallas_call(
-        functools.partial(attention_kernel, tq=tq),
+    def weight_map(g, j, r, b):
+        return (g * group_size + j, 0)
+
+    def stat_map(g, j, r, b):
+        return (g * group_size + j, r, 0)
+
+    params = pltpu.CompilerParams(dimension_semantics=("arbitrary", "arbitrary", "arbitrary"))
+    pair = qc * keys * HD * heads_local * 2
+    delta, lse, row_dot, patch = pl.pallas_call(
+        functools.partial(forward_kernel, tq=tq),
         grid_spec=pltpu.PrefetchScalarGridSpec(
             num_scalar_prefetch=1,
             grid=grid,
@@ -83,21 +108,54 @@
                 pl.BlockSpec((keys, HD), kv_map),
                 pl.BlockSpec((1, keys), fixed),
                 pl.BlockSpec((tq, HD), head_map),
+                pl.BlockSpec((HD, model), weight_map),
             ],
             out_specs=[
                 pl.BlockSpec((tq, HD), head_map),
-                pl.BlockSpec((1, keys), fixed),
+                pl.BlockSpec((1, tq, 1), stat_map),
+                pl.BlockSpec((1, tq, 1), stat_map),
+                pl.BlockSpec((qc, model), fixed),
             ],
         ),
         out_shape=[
             jax.ShapeDtypeStruct((qc, width), jnp.bfloat16),
-            jax.ShapeDtypeStruct((1, keys), jnp.float32),
+            jax.ShapeDtypeStruct((heads_local, qc, 1), jnp.float32),
+            jax.ShapeDtypeStruct((heads_local, qc, 1), jnp.float32),
+            jax.ShapeDtypeStruct((qc, model), jnp.float32),
         ],
-        compiler_params=pltpu.CompilerParams(
-            dimension_semantics=("arbitrary", "arbitrary", "arbitrary")
-        ),
-        cost_estimate=cost,
-    )(base, key_pos, query, key_all, value_all, kept, grad_out)
+        compiler_params=params,
+        cost_estimate=pl.CostEstimate(
+            flops=3 * pair + 2 * qc * width * model,
+            transcendentals=2 * qc * keys * heads_local,
+            bytes_accessed=2 * (3 * query.size + key_all.size + value_all.size + out_weight.size)
+            + 4 * qc * model,
+        ),
+    )(base, key_pos, query, key_all, value_all, kept, grad_out, out_weight)
+    attr = pl.pallas_call(
+        functools.partial(backward_kernel, tq=tq),
+        grid_spec=pltpu.PrefetchScalarGridSpec(
+            num_scalar_prefetch=1,
+            grid=grid,
+            in_specs=[
+                pl.BlockSpec((1, keys), fixed),
+                pl.BlockSpec((tq, HD), head_map),
+                pl.BlockSpec((keys, HD), kv_map),
+                pl.BlockSpec((keys, HD), kv_map),
+                pl.BlockSpec((tq, HD), head_map),
+                pl.BlockSpec((1, tq, 1), stat_map),
+                pl.BlockSpec((1, tq, 1), stat_map),
+            ],
+            out_specs=pl.BlockSpec((1, keys), fixed),
+        ),
+        out_shape=jax.ShapeDtypeStruct((1, keys), jnp.float32),
+        compiler_params=params,
+        cost_estimate=pl.CostEstimate(
+            flops=2 * pair,
+            transcendentals=qc * keys * heads_local,
+            bytes_accessed=2 * (2 * query.size + key_all.size + value_all.size) + 4 * keys,
+        ),
+    )(base, key_pos, query, key_all, value_all, grad_out, lse, row_dot)
+    return delta, attr, patch
 
 
 def gather_kv(key, value, segment_ids, ctx_at, rep_at, rep_count):
@@ -176,8 +234,8 @@
     grad_out = jnp.dot(grad_masked, out_weight.T, preferred_element_type=jnp.float32).astype(
         jnp.bfloat16
     )
-    delta, attr = fused_attention(
-        base, key_pos, query, key_all, value_all, kept, grad_out, group_size
+    delta, attr, projected = fused_attention(
+        base, key_pos, query, key_all, value_all, kept, grad_out, out_weight, group_size
     )
 
     inverse = (ctx_at - jnp.arange(ctx_count, dtype=jnp.int32)) % ctx_count
@@ -185,7 +243,6 @@
     seg_abs = seg_shift.reshape(ctx_count, key_count)[inverse].reshape(-1)
     attr_all = butterfly_sum(attr_abs, ("rep", "head", "ctx"))
 
-    projected = jnp.dot(delta, out_weight, preferred_element_type=jnp.float32)
     if head_count == 2:
         cols = projected.shape[1] // 2
         keep = lax.dynamic_slice_in_dim(projected, head_at * cols, cols, 1)

time: 124 us -> 130 us (1.048)
  Pallas kernels: 29.7 us -> 48.1 us
  matrix products: 22 us -> 13.7 us
  waiting for transfers between devices: 34.6 us -> 28.9 us
    pallas_call x1 -> x2, Pallas kernels: 29.7 us -> 48.1 us  [the longest x1 33.1 us: fused_attention(): pl.pallas_call(functools.partial(forward_kernel, tq=tq), grid_spec=pltpu....]
    dot_general x1 -> x0, matrix products: 8.3 us -> none  [local(): projected = jnp.dot(delta, out_weight, preferred_element_type=jnp.float32)]
    ppermute x4, waiting for transfers between devices: 13 us -> 7.38 us  [butterfly_sum(): total = total + lax.ppermute(total, axis, [(i, i ^ bit) for i in range(n)])]
  transfers between devices with their start and end apart: 12 -> 12, of which waited for: 8 -> 8; matrix products, arithmetic and copies ran while one was open for 14% -> 14% of each run, Pallas kernels for 0% -> 12%
where the time goes in v3:
time: 130 us
  Pallas kernels  48.1 us (37%)
  waiting for transfers between devices  28.9 us (22%)
  starting transfers between devices  24.9 us (19%)
  matrix products  13.7 us (11%)
  other arithmetic  7.73 us (6%)
  local copies, waits for them, and re-layouts  5.44 us (4%)
    pallas_call x1, Pallas kernels, fused_attention(): pl.pallas_call(functools.partial(forward_kernel, tq=tq), grid_spec=pltpu....  33.1 us
    ppermute x3, waiting for transfers between devices, gather_kv(): lax.ppermute(payload, 'ctx', [(i, (i + d) % n) for i in range(n)])  19.2 us
    pallas_call x1, Pallas kernels, fused_attention(): pl.pallas_call(functools.partial(backward_kernel, tq=tq), grid_spec=pltpu...  15 us
    ppermute x4, starting transfers between devices, butterfly_sum(): total = total + lax.ppermute(total, axis, [(i, i ^ bit) for i in range(n)])  14.4 us
    dot_general x1, matrix products, local(): jnp.dot(grad_masked, out_weight.T, preferred_element_type=jnp.float32)  12.6 us
    ppermute x3, starting transfers between devices, gather_kv(): lax.ppermute(payload, 'ctx', [(i, (i + d) % n) for i in range(n)])  7.93 us
    ppermute x4, waiting for transfers between devices, butterfly_sum(): total = total + lax.ppermute(total, axis, [(i, i ^ bit) for i in range(n)])  7.38 us
  transfers between devices with their start and end apart: 12, of which 8 were waited for; matrix products, arithmetic and copies ran while one was open for 14% of the time, Pallas kernels for 12%

profile of v3, /device:TPU:0, one launch (start us, length us, event | category | flops | bytes accessed | tf_op | source)
XLA Modules:
  0.0 129.6 jit_solution(9163351208360966780)
XLA Ops:
  0.6 0.0 copy-start.4
  0.6 0.7 convert_element_type.29
  1.4 1.1 broadcast_select_fusion.4
  2.5 4.1 %collective-permute-start.3 = (bf16[528,512]{1,0:T(8,128)(2,1)S(1)}, bf16[528,512]{1,0:T(8,128)(2,1)S(1)}, u32[]{:S(2)}, u32[]{:S(2)}) collective-permute-start(bf16[528,512]{1,0:T(8,128)(2,1)S(1)} %pad_maximum_fusion.2), channel_id=1, source_target_pairs={{0,8},{4,12},{8,0},{12,4},{1,9},{5,13},{9,1},{13,5},{2,10},{6,14},... | collective-permute-start | bytes 1622024 | tf_op jit(solution)/shard_map/ppermute | solution.py:175
  6.6 1.6 %collective-permute-start.1 = (bf16[528,512]{1,0:T(8,128)(2,1)S(1)}, bf16[528,512]{1,0:T(8,128)(2,1)S(1)}, u32[]{:S(2)}, u32[]{:S(2)}) collective-permute-start(bf16[528,512]{1,0:T(8,128)(2,1)S(1)} %pad_maximum_fusion.2), channel_id=1, source_target_pairs={{0,4},{4,8},{8,12},{12,0},{1,5},{5,9},{9,13},{13,1},{2,6},{6,10},{... | collective-permute-start | bytes 1622024 | tf_op jit(solution)/shard_map/ppermute | solution.py:175
  8.2 2.2 %collective-permute-start.5 = (bf16[528,512]{1,0:T(8,128)(2,1)S(1)}, bf16[528,512]{1,0:T(8,128)(2,1)S(1)}, u32[]{:S(2)}, u32[]{:S(2)}) collective-permute-start(bf16[528,512]{1,0:T(8,128)(2,1)S(1)} %pad_maximum_fusion.2), channel_id=1, source_target_pairs={{0,12},{4,0},{8,4},{12,8},{1,13},{5,1},{9,5},{13,9},{2,14},{6,2},{... | collective-permute-start | bytes 1622024 | tf_op jit(solution)/shard_map/ppermute | solution.py:175
  10.5 0.0 collective-permute-start
  10.5 0.0 copy-done.4
  10.5 12.6 %convolution_convert_fusion.do_ref = bf16[128,2048]{1,0:T(8,128)(2,1)} fusion(bf16[2048,4096]{1,0:T(8,128)(2,1)} %w_ref.1, bf16[128,4096]{1,0:T(8,128)(2,1)} %param.14, pred[128]{0:T(512)(128)(4,1)S(1)} %broadcast_compare_fusion), kind=kOutput, calls=%fused_computation.2 | convolution fusion | flops 2148270080 | bytes 18350208 | tf_op jit(solution)/shard_map/dot_general | solution.py:234
  23.1 0.1 add_bitcast_fusion
  23.1 0.6 copy.11
  23.8 19.2 %collective-permute-done.3 = bf16[528,512]{1,0:T(8,128)(2,1)S(1)} collective-permute-done((bf16[528,512]{1,0:T(8,128)(2,1)S(1)}, bf16[528,512]{1,0:T(8,128)(2,1)S(1)}, u32[]{:S(2)}, u32[]{:S(2)}) %collective-permute-start.3) | collective-permute-done | bytes 540704 | tf_op jit(solution)/shard_map/ppermute | solution.py:175
  43.0 0.0 collective-permute-start.4
  43.0 0.0 collective-permute-done.1
  43.0 0.5 collective-permute-start.2
  43.5 0.0 collective-permute-done
  43.5 0.1 broadcast_select_fusion.3
  43.6 0.0 copy-start.1
  43.6 0.0 collective-permute-done.5
  43.7 0.1 collective-permute-start.6
  43.7 0.1 fusion.3
  43.9 1.0 collective-permute-done.4
  44.9 0.1 broadcast_select_fusion.1
  45.0 0.0 copy-done.1
  45.0 0.0 copy-start
  45.0 0.7 collective-permute-done.2
  45.7 0.1 broadcast_select_fusion.2
  45.7 0.0 copy-start.3
  45.8 0.6 collective-permute-done.6
  46.4 0.1 broadcast_select_fusion
  46.5 0.0 copy-done
  46.6 0.0 copy-done.3
  46.6 0.1 compare_reduce_fusion
  46.7 0.6 broadcast_select_fusion.5
  47.3 0.0 slice-start
  47.3 0.0 slice-start.1
  47.3 0.1 slice_select_fusion.1
  47.4 0.1 slice_select_fusion.2
  47.4 0.1 slice_select_fusion
  47.5 0.8 slice-done
  48.3 0.2 slice-done.1
  48.5 2.1 %pad_maximum_fusion = (bf16[2048,512]{1,0:T(8,128)(2,1)}, bf16[2048,512]{1,0:T(8,128)(2,1)}) fusion(bf16[512,512]{1,0:T(8,128)(2,1)S(1)} %slice.78, bf16[512,512]{1,0:T(8,128)(2,1)S(1)} %slice-done, bf16[512,512]{1,0:T(8,128)(2,1)S(1)} %slice.76, bf16[512,512]{1,0:T(8,128)(2,1)S(1)} %slice-done.1, bf16[512,512]{1,0:T(8,128)(2,1)S(1)} %slice_select_fusion, ...), kind=kLoop, calls=%fused_computation.3 | loop fusion | flops 16777216 | bytes 8388608 | tf_op jit(solution)/shard_map/concatenate | solution.py:186
  50.7 33.1 %shard_map.103 = (bf16[128,2048]{1,0:T(8,128)(2,1)}, f32[16,128,1]{2,1,0:T(8,128)}, f32[16,128,1]{2,1,0:T(8,128)}, f32[128,4096]{1,0:T(8,128)}) custom-call(s32[1]{0:T(128)} %bitcast.base_ref, s32[1,2048]{1,0:T(1,128)} %bitcast.18, bf16[128,2048]{1,0:T(8,128)(2,1)} %q_ref.3, bf16[2048,512]{1,0:T(8,128)(2,1)} %get-tuple-element.21.k_ref, ...), custom_call_target="tpu_custom_call" | custom-call | flops 5368709120 | bytes 24641536 | tf_op jit(solution)/shard_map/pallas_call | solution.py:99
  83.7 1.3 dynamic-slice_convert_fusion
  85.0 2.0 %collective-permute-start.7 = (bf16[128,2048]{1,0:T(8,128)(2,1)S(1)}, bf16[128,2048]{1,0:T(8,128)(2,1)S(1)}, u32[]{:S(2)}, u32[]{:S(2)}) collective-permute-start(bf16[128,2048]{1,0:T(8,128)(2,1)S(1)} %dynamic-slice_convert_fusion), channel_id=1, source_target_pairs={{0,2},{2,0},{1,3},{3,1},{4,6},{6,4},{5,7},{7,5},{8,10},{10,8},{9,1... | collective-permute-start | bytes 1572872 | tf_op jit(solution)/shard_map/ppermute | solution.py:250
  87.0 0.0 copy-start.2
  87.1 15.0 %shard_map.104 = f32[1,2048]{1,0:T(1,128)} custom-call(s32[1]{0:T(128)} %bitcast.base_ref, s32[1,2048]{1,0:T(1,128)} %bitcast.19, bf16[128,2048]{1,0:T(8,128)(2,1)} %q_ref.3, bf16[2048,512]{1,0:T(8,128)(2,1)} %get-tuple-element.21.k_ref, bf16[2048,512]{1,0:T(8,128)(2,1)} %get-tuple-element.22.v_ref, bf16[128,2048]{1,0:T(8,128)(2,1)} %convolution_convert_fusion.do_ref, ...), custom_call_target="tpu_custom_call" | custom-call | flops 2147483648 | bytes 5251072 | tf_op jit(solution)/shard_map/pallas_call | solution.py:134
  102.1 0.5 broadcast.152
  102.6 1.4 %reduce.13 = f32[2048]{0:T(1024)S(1)} reduce(f32[1,2048]{1,0:T(1,128)} %shard_map.104, f32[]{:T(128)} %broadcast.152), dimensions={0}, to_apply=%pallas_call.15.reduce_sub_computation.3 | reduce | bytes 16388 | tf_op jit(solution)/shard_map/pallas_call | solution.py:134
  104.0 0.6 gather_fusion
  104.5 0.1 collective-permute-start.8
  104.6 1.2 collective-permute-done.8
  105.8 0.1 collective-permute-start.9
  105.9 3.5 %collective-permute-done.9 = f32[2048]{0:T(1024)S(1)} collective-permute-done((f32[2048]{0:T(1024)S(1)}, f32[2048]{0:T(1024)S(1)}, u32[]{:S(2)}, u32[]{:S(2)}) %collective-permute-start.9) | collective-permute-done | bytes 8224 | tf_op jit(solution)/shard_map/ppermute | solution.py:204
  109.4 10.3 %collective-permute-start.10 = (f32[2048]{0:T(1024)S(1)}, f32[2048]{0:T(1024)S(1)}, u32[]{:S(2)}, u32[]{:S(2)}) collective-permute-start(f32[2048]{0:T(1024)S(1)} %add.97), channel_id=1, source_target_pairs={{0,4},{4,0},{8,12},{12,8},{1,5},{5,1},{9,13},{13,9},{2,6},{6,2},{1... | collective-permute-start | bytes 24584 | tf_op jit(solution)/shard_map/ppermute | solution.py:204
  119.7 1.6 %collective-permute-done.10 = f32[2048]{0:T(1024)S(1)} collective-permute-done((f32[2048]{0:T(1024)S(1)}, f32[2048]{0:T(1024)S(1)}, u32[]{:S(2)}, u32[]{:S(2)}) %collective-permute-start.10) | collective-permute-done | bytes 8224 | tf_op jit(solution)/shard_map/ppermute | solution.py:204
  121.4 3.9 %collective-permute-start.11 = (f32[2048]{0:T(1024)S(1)}, f32[2048]{0:T(1024)S(1)}, u32[]{:S(2)}, u32[]{:S(2)}) collective-permute-start(f32[2048]{0:T(1024)S(1)} %add.98), channel_id=1, source_target_pairs={{0,8},{4,12},{8,0},{12,4},{1,9},{5,13},{9,1},{13,5},{2,10},{6,14},... | collective-permute-start | bytes 24584 | tf_op jit(solution)/shard_map/ppermute | solution.py:204
  125.3 0.6 gather_fusion.1
  125.9 1.0 collective-permute-done.11
  126.9 0.7 dynamic_slice.11
  127.6 1.1 convolution_bitcast_fusion
  128.7 0.0 collective-permute-done.7
  128.7 0.0 copy-done.2
  128.7 0.9 add_convert_fusion
  (22 shorter events, 0.3 us)
Async XLA Ops:
  0.6 9.8 %copy-start.4 = (s32[128]{0:T(128)S(1)}, s32[128]{0:T(128)}, u32[]{:S(2)}) copy-start(s32[128]{0:T(128)} %param.15) | copy-start | bytes 1540
  2.5 40.4 %collective-permute-start.3 = (bf16[528,512]{1,0:T(8,128)(2,1)S(1)}, bf16[528,512]{1,0:T(8,128)(2,1)S(1)}, u32[]{:S(2)}, u32[]{:S(2)}) collective-permute-start(bf16[528,512]{1,0:T(8,128)(2,1)S(1)} %pad_maximum_fusion.2), channel_id=1, source_target_pairs={{0,8},{4,12},{8,0},{12,4},{1,9},{5,13},{9,1},{13,5},{2,10},{6,14},... | collective-permute-start | bytes 1622024 | tf_op jit(solution)/shard_map/ppermute | solution.py:175
  6.6 36.3 %collective-permute-start.1 = (bf16[528,512]{1,0:T(8,128)(2,1)S(1)}, bf16[528,512]{1,0:T(8,128)(2,1)S(1)}, u32[]{:S(2)}, u32[]{:S(2)}) collective-permute-start(bf16[528,512]{1,0:T(8,128)(2,1)S(1)} %pad_maximum_fusion.2), channel_id=1, source_target_pairs={{0,4},{4,8},{8,12},{12,0},{1,5},{5,9},{9,13},{13,1},{2,6},{6,10},{... | collective-permute-start | bytes 1622024 | tf_op jit(solution)/shard_map/ppermute | solution.py:175
  8.2 35.5 %collective-permute-start.5 = (bf16[528,512]{1,0:T(8,128)(2,1)S(1)}, bf16[528,512]{1,0:T(8,128)(2,1)S(1)}, u32[]{:S(2)}, u32[]{:S(2)}) collective-permute-start(bf16[528,512]{1,0:T(8,128)(2,1)S(1)} %pad_maximum_fusion.2), channel_id=1, source_target_pairs={{0,12},{4,0},{8,4},{12,8},{1,13},{5,1},{9,5},{13,9},{2,14},{6,2},{... | collective-permute-start | bytes 1622024 | tf_op jit(solution)/shard_map/ppermute | solution.py:175
  10.5 33.0 %collective-permute-start = (bf16[528,512]{1,0:T(8,128)(2,1)S(1)}, bf16[528,512]{1,0:T(8,128)(2,1)S(1)}, u32[]{:S(2)}, u32[]{:S(2)}) collective-permute-start(bf16[528,512]{1,0:T(8,128)(2,1)S(1)} %pad_maximum_fusion.2), channel_id=1, source_target_pairs={{0,1},{1,0},{2,3},{3,2},{4,5},{5,4},{6,7},{7,6},{8,9},{9,8},{10,11... | collective-permute-start | bytes 1622024 | tf_op jit(solution)/shard_map/ppermute | solution.py:180
  43.0 1.9 %collective-permute-start.4 = (bf16[528,512]{1,0:T(8,128)(2,1)S(1)}, bf16[528,512]{1,0:T(8,128)(2,1)S(1)}, u32[]{:S(2)}, u32[]{:S(2)}) collective-permute-start(bf16[528,512]{1,0:T(8,128)(2,1)S(1)} %collective-permute-done.3), channel_id=1, source_target_pairs={{0,1},{1,0},{2,3},{3,2},{4,5},{5,4},{6,7},{7,6},{8,9},{9,8},{10,11... | collective-permute-start | bytes 1622024 | tf_op jit(solution)/shard_map/ppermute | solution.py:180
  43.0 2.7 %collective-permute-start.2 = (bf16[528,512]{1,0:T(8,128)(2,1)S(1)}, bf16[528,512]{1,0:T(8,128)(2,1)S(1)}, u32[]{:S(2)}, u32[]{:S(2)}) collective-permute-start(bf16[528,512]{1,0:T(8,128)(2,1)S(1)} %collective-permute-done.1), channel_id=1, source_target_pairs={{0,1},{1,0},{2,3},{3,2},{4,5},{5,4},{6,7},{7,6},{8,9},{9,8},{10,11... | collective-permute-start | bytes 1622024 | tf_op jit(solution)/shard_map/ppermute | solution.py:180
  43.6 1.3 %copy-start.1 = (bf16[528,512]{1,0:T(8,128)(2,1)}, bf16[528,512]{1,0:T(8,128)(2,1)S(1)}, u32[]{:S(2)}) copy-start(bf16[528,512]{1,0:T(8,128)(2,1)S(1)} %broadcast_select_fusion.3) | copy-start | bytes 1622020
  43.7 2.8 %collective-permute-start.6 = (bf16[528,512]{1,0:T(8,128)(2,1)S(1)}, bf16[528,512]{1,0:T(8,128)(2,1)S(1)}, u32[]{:S(2)}, u32[]{:S(2)}) collective-permute-start(bf16[528,512]{1,0:T(8,128)(2,1)S(1)} %collective-permute-done.5), channel_id=1, source_target_pairs={{0,1},{1,0},{2,3},{3,2},{4,5},{5,4},{6,7},{7,6},{8,9},{9,8},{10,11... | collective-permute-start | bytes 1622024 | tf_op jit(solution)/shard_map/ppermute | solution.py:180
  45.0 1.5 %copy-start = (bf16[528,512]{1,0:T(8,128)(2,1)}, bf16[528,512]{1,0:T(8,128)(2,1)S(1)}, u32[]{:S(2)}) copy-start(bf16[528,512]{1,0:T(8,128)(2,1)S(1)} %broadcast_select_fusion.1) | copy-start | bytes 1622020
  45.7 0.9 copy-start.3
  47.3 1.0 slice-start
  47.3 1.2 slice-start.1
  85.0 43.7 %collective-permute-start.7 = (bf16[128,2048]{1,0:T(8,128)(2,1)S(1)}, bf16[128,2048]{1,0:T(8,128)(2,1)S(1)}, u32[]{:S(2)}, u32[]{:S(2)}) collective-permute-start(bf16[128,2048]{1,0:T(8,128)(2,1)S(1)} %dynamic-slice_convert_fusion), channel_id=1, source_target_pairs={{0,2},{2,0},{1,3},{3,1},{4,6},{6,4},{5,7},{7,5},{8,10},{10,8},{9,1... | collective-permute-start | bytes 1572872 | tf_op jit(solution)/shard_map/ppermute | solution.py:250
  87.0 41.7 %copy-start.2 = (f32[128,4096]{1,0:T(8,128)S(1)}, f32[128,4096]{1,0:T(8,128)}, u32[]{:S(2)}) copy-start(f32[128,4096]{1,0:T(8,128)} %get-tuple-element.18) | copy-start | bytes 6291460
  104.5 1.2 collective-permute-start.8
  105.8 3.7 %collective-permute-start.9 = (f32[2048]{0:T(1024)S(1)}, f32[2048]{0:T(1024)S(1)}, u32[]{:S(2)}, u32[]{:S(2)}) collective-permute-start(f32[2048]{0:T(1024)S(1)} %add.96), channel_id=1, source_target_pairs={{0,2},{2,0},{1,3},{3,1},{4,6},{6,4},{5,7},{7,5},{8,10},{10,8},{9,1... | collective-permute-start | bytes 24584 | tf_op jit(solution)/shard_map/ppermute | solution.py:204
  109.4 11.9 %collective-permute-start.10 = (f32[2048]{0:T(1024)S(1)}, f32[2048]{0:T(1024)S(1)}, u32[]{:S(2)}, u32[]{:S(2)}) collective-permute-start(f32[2048]{0:T(1024)S(1)} %add.97), channel_id=1, source_target_pairs={{0,4},{4,0},{8,12},{12,8},{1,5},{5,1},{9,13},{13,9},{2,6},{6,2},{1... | collective-permute-start | bytes 24584 | tf_op jit(solution)/shard_map/ppermute | solution.py:204
  121.4 5.6 %collective-permute-start.11 = (f32[2048]{0:T(1024)S(1)}, f32[2048]{0:T(1024)S(1)}, u32[]{:S(2)}, u32[]{:S(2)}) collective-permute-start(f32[2048]{0:T(1024)S(1)} %add.98), channel_id=1, source_target_pairs={{0,8},{4,12},{8,0},{12,4},{1,9},{5,13},{9,1},{13,5},{2,10},{6,14},... | collective-permute-start | bytes 24584 | tf_op jit(solution)/shard_map/ppermute | solution.py:204

commit v4 on v2

--- a/solution.py
+++ b/solution.py
@@ -100,7 +100,22 @@
     )(base, key_pos, query, key_all, value_all, kept, grad_out)
 
 
-def gather_kv(key, value, segment_ids, ctx_at, rep_at, rep_count):
+def relay_gather(payload, needed, ctx_at):
+    n = lax.axis_size("ctx")
+    zero = jnp.zeros_like(payload)
+    forward, backward = [payload], [payload]
+    for k in range(1, n):
+        pairs = [(i, i + 1) for i in range(k - 1, n - 1) if needed(i + 1, i + 1 - k)]
+        forward.append(lax.ppermute(forward[-1], "ctx", pairs) if pairs else zero)
+        pairs = [(i + 1, i) for i in range(0, n - k) if needed(i, i + k)]
+        backward.append(lax.ppermute(backward[-1], "ctx", pairs) if pairs else zero)
+    parts = [payload]
+    for k in range(1, n):
+        parts.append(jnp.where(k <= ctx_at, forward[k], backward[n - k]))
+    return parts
+
+
+def gather_kv(key, value, segment_ids, ctx_at, rep_at, rep_count, needed):
     n = lax.axis_size("ctx")
     key_count, width = key.shape
     seg_rows = -(-key_count // width)
@@ -111,12 +126,7 @@
     split = rep_count == 2
     halves = [jnp.where(rep_at == 0, key, value)] if split else [key, value]
     payloads = [jnp.concatenate([h, seg_block], axis=0) for h in halves]
-    gathered = []
-    for payload in payloads:
-        parts = [payload] + [
-            lax.ppermute(payload, "ctx", [(i, (i + d) % n) for i in range(n)]) for d in range(1, n)
-        ]
-        gathered.append(parts)
+    gathered = [relay_gather(p, needed, ctx_at) for p in payloads]
     if split:
         mine = gathered[0]
         theirs = [lax.ppermute(p, "rep", [(0, 1), (1, 0)]) for p in mine]
@@ -165,8 +175,12 @@
     base = (query_base + (ctx_at * rep_count + rep_at) * query_count).astype(jnp.int32)
     base = jnp.reshape(base, (1,))
 
+    def needed(receiver, block):
+        last_query = query_base + (receiver * rep_count + rep_count) * query_count - 1
+        return block * key_count <= last_query
+
     key_all, value_all, seg_shift, key_pos, source = gather_kv(
-        key, value, segment_ids, ctx_at, rep_at, rep_count
+        key, value, segment_ids, ctx_at, rep_at, rep_count, needed
     )
     kept = jnp.where(
         jnp.any(seg_shift[:, None] == masked_segments[None, :], axis=1), 0.0, 1.0
@@ -183,7 +197,13 @@
     inverse = (ctx_at - jnp.arange(ctx_count, dtype=jnp.int32)) % ctx_count
     attr_abs = attr.reshape(ctx_count, key_count)[inverse].reshape(-1)
     seg_abs = seg_shift.reshape(ctx_count, key_count)[inverse].reshape(-1)
-    attr_all = butterfly_sum(attr_abs, ("rep", "head", "ctx"))
+    onehot = (
+        seg_abs[:, None] == jnp.arange(SEG_DEV * ctx_count, dtype=jnp.int32)[None, :]
+    ).astype(jnp.float32)
+    seg_part = jnp.dot(attr_abs, onehot, precision=lax.Precision.HIGHEST)
+    summed = butterfly_sum(jnp.concatenate([attr_abs, seg_part]), ("rep", "head", "ctx"))
+    attr_all = summed[:context_len]
+    segment_attr = summed[context_len:]
 
     projected = jnp.dot(delta, out_weight, preferred_element_type=jnp.float32)
     if head_count == 2:
@@ -198,10 +218,6 @@
         )
 
     token_attr = lax.dynamic_slice_in_dim(attr_all, ctx_at * key_count, key_count, 0)
-    onehot = (
-        seg_abs[:, None] == jnp.arange(SEG_DEV * ctx_count, dtype=jnp.int32)[None, :]
-    ).astype(jnp.float32)
-    segment_attr = jnp.dot(attr_all, onehot, precision=lax.Precision.HIGHEST)
     return (patch_effect, token_attr, segment_attr)
 
 

time: 124 us -> 125 us (level)
  starting transfers between devices: 25.2 us -> 26.8 us
  waiting for transfers between devices: 34.6 us -> 33.3 us
    ppermute x3 -> x5, waiting for transfers between devices: 19.2 us -> 17.3 us  [the longest x2 17.3 us: relay_gather(): backward.append(lax.ppermute(backward[-1], 'ctx', pairs) if pairs else zero)]
    ppermute x4, waiting for transfers between devices: 13 us -> 14.7 us  [butterfly_sum(): total = total + lax.ppermute(total, axis, [(i, i ^ bit) for i in range(n)])]
    ppermute x3 -> x5, starting transfers between devices: 7.93 us -> 8.9 us  [the longest x3 6.33 us: relay_gather(): forward.append(lax.ppermute(forward[-1], 'ctx', pairs) if pairs else zero)]
  transfers between devices with their start and end apart: 12 -> 14, of which waited for: 8 -> 7; matrix products, arithmetic and copies ran while one was open for 14% -> 14% of each run, Pallas kernels for 0% -> 0%
where the time goes in v4:
time: 125 us
  waiting for transfers between devices  33.3 us (27%)
  Pallas kernels  29.7 us (24%)
  starting transfers between devices  26.8 us (21%)
  matrix products  21.1 us (17%)
  other arithmetic  8.07 us (6%)
  local copies, waits for them, and re-layouts  4.52 us (4%)
    pallas_call x1, Pallas kernels, fused_attention(): pl.pallas_call(functools.partial(attention_kernel, tq=tq), grid_spec=pltp...  29.7 us
    ppermute x2, waiting for transfers between devices, relay_gather(): backward.append(lax.ppermute(backward[-1], 'ctx', pairs) if pairs else zero)  17.3 us
    ppermute x4, starting transfers between devices, butterfly_sum(): total = total + lax.ppermute(total, axis, [(i, i ^ bit) for i in range(n)])  15.2 us
    ppermute x4, waiting for transfers between devices, butterfly_sum(): total = total + lax.ppermute(total, axis, [(i, i ^ bit) for i in range(n)])  14.7 us
    dot_general x1, matrix products, local(): jnp.dot(grad_masked, out_weight.T, preferred_element_type=jnp.float32)  12.3 us
    dot_general x1, matrix products, local(): projected = jnp.dot(delta, out_weight, preferred_element_type=jnp.float32)  8.3 us
    ppermute x3, starting transfers between devices, relay_gather(): forward.append(lax.ppermute(forward[-1], 'ctx', pairs) if pairs else zero)  6.33 us
    ppermute x2, starting transfers between devices, relay_gather(): backward.append(lax.ppermute(backward[-1], 'ctx', pairs) if pairs else zero)  2.57 us
  transfers between devices with their start and end apart: 14, of which 7 were waited for; matrix products, arithmetic and copies ran while one was open for 14% of the time, Pallas kernels for 0%

profile of v4, /device:TPU:0, one launch (start us, length us, event | category | flops | bytes accessed | tf_op | source)
XLA Modules:
  0.0 124.5 jit_solution(5806511050446558643)
XLA Ops:
  0.6 0.0 copy-start.6
  0.6 0.0 copy-start.3
  0.7 0.8 convert_element_type.29
  1.5 1.1 broadcast_select_fusion.7
  2.6 0.8 pad_maximum_fusion.2
  3.4 4.9 %collective-permute-start.1 = (bf16[528,512]{1,0:T(8,128)(2,1)}, bf16[528,512]{1,0:T(8,128)(2,1)S(1)}, u32[]{:S(2)}, u32[]{:S(2)}) collective-permute-start(bf16[528,512]{1,0:T(8,128)(2,1)} %pad_maximum_fusion.2), channel_id=1, source_target_pairs={{0,4},{4,8},{8,12},{1,5},{5,9},{9,13},{2,6},{6,10},{10,14},{3,7},{... | collective-permute-start | bytes 1622024 | tf_op jit(solution)/shard_map/ppermute | solution.py:109
  8.4 1.3 %collective-permute-start.4 = (bf16[528,512]{1,0:T(8,128)(2,1)}, bf16[528,512]{1,0:T(8,128)(2,1)S(1)}, u32[]{:S(2)}, u32[]{:S(2)}) collective-permute-start(bf16[528,512]{1,0:T(8,128)(2,1)} %pad_maximum_fusion.2), channel_id=1, source_target_pairs={{4,0},{8,4},{12,8},{5,1},{9,5},{13,9},{6,2},{10,6},{14,10},{7,3},{... | collective-permute-start | bytes 1622024 | tf_op jit(solution)/shard_map/ppermute | solution.py:111
  9.7 0.1 collective-permute-start
  9.8 12.3 %convolution_convert_fusion.do_ref = bf16[128,2048]{1,0:T(8,128)(2,1)} fusion(bf16[2048,4096]{1,0:T(8,128)(2,1)} %param.13, bf16[128,4096]{1,0:T(8,128)(2,1)S(1)} %copy-done.3, pred[128]{0:T(512)(128)(4,1)S(1)} %broadcast_compare_fusion), kind=kOutput, calls=%fused_computation.2 | convolution fusion | flops 2148270080 | bytes 18350208 | tf_op jit(solution)/shard_map/dot_general | solution.py:190
  22.1 0.1 add_bitcast_fusion
  22.1 0.6 copy.11
  22.8 0.0 collective-permute-done.1
  22.8 0.5 collective-permute-start.2
  23.4 0.7 collective-permute-start.3
  24.0 0.2 collective-permute-done.4
  24.2 1.3 %collective-permute-start.5 = (bf16[528,512]{1,0:T(8,128)(2,1)S(1)}, bf16[528,512]{1,0:T(8,128)(2,1)S(1)}, u32[]{:S(2)}, u32[]{:S(2)}) collective-permute-start(bf16[528,512]{1,0:T(8,128)(2,1)S(1)} %collective-permute-done.4), channel_id=1, source_target_pairs={{4,0},{5,1},{6,2},{7,3},{20,16},{21,17},{22,18},{23,19}} | collective-permute-start | bytes 1622024 | tf_op jit(solution)/shard_map/ppermute | solution.py:111
  25.5 0.0 collective-permute-done
  25.5 0.1 broadcast_select_fusion.6
  25.7 0.1 fusion.3
  25.8 0.0 collective-permute-done.3
  25.9 17.1 %collective-permute-done.5 = bf16[528,512]{1,0:T(8,128)(2,1)S(1)} collective-permute-done((bf16[528,512]{1,0:T(8,128)(2,1)S(1)}, bf16[528,512]{1,0:T(8,128)(2,1)S(1)}, u32[]{:S(2)}, u32[]{:S(2)}) %collective-permute-start.5) | collective-permute-done | bytes 540704 | tf_op jit(solution)/shard_map/ppermute | solution.py:111
  43.0 0.1 broadcast_select_fusion.1
  43.0 0.1 collective-permute-start.6
  43.1 0.7 collective-permute-start.7
  43.8 0.0 collective-permute-done.2
  43.8 0.1 broadcast_select_fusion.5
  43.9 0.1 slice_select_fusion.2
  44.0 0.0 collective-permute-done.7
  44.0 0.1 broadcast_select_fusion
  44.1 0.6 copy-done.2
  44.7 0.5 collective-permute-start.8
  45.2 0.0 collective-permute-done.6
  45.2 0.1 broadcast_select_fusion.4
  45.3 0.1 slice_select_fusion.1
  45.3 0.0 slice-start
  45.4 0.0 slice-start.2
  45.4 1.4 %collective-permute-done.8 = bf16[528,512]{1,0:T(8,128)(2,1)S(1)} collective-permute-done((bf16[528,512]{1,0:T(8,128)(2,1)S(1)}, bf16[528,512]{1,0:T(8,128)(2,1)S(1)}, u32[]{:S(2)}, u32[]{:S(2)}) %collective-permute-start.8) | collective-permute-done | bytes 540704 | tf_op jit(solution)/shard_map/ppermute | solution.py:132
  46.7 0.1 broadcast_select_fusion.3
  46.9 0.1 compare_reduce_fusion
  47.0 0.6 broadcast_select_fusion.8
  47.6 0.1 slice_select_fusion
  47.7 0.2 slice-done.1
  47.9 2.1 %pad_maximum_fusion = (bf16[2048,512]{1,0:T(8,128)(2,1)}, bf16[2048,512]{1,0:T(8,128)(2,1)}) fusion(bf16[512,512]{1,0:T(8,128)(2,1)S(1)} %slice.86, bf16[512,512]{1,0:T(8,128)(2,1)S(1)} %slice-done.1, bf16[512,512]{1,0:T(8,128)(2,1)S(1)} %slice-done.2, bf16[512,512]{1,0:T(8,128)(2,1)S(1)} %slice-done, bf16[512,512]{1,0:T(8,128)(2,1)S(1)} %slice_select_fusion, ...), kind=kLoop, calls=%fused_computation.3 | loop fusion | flops 16777216 | bytes 8388608 | tf_op jit(solution)/shard_map/concatenate | solution.py:138
  50.0 29.7 %shard_map.103 = (bf16[128,2048]{1,0:T(8,128)(2,1)}, f32[1,2048]{1,0:T(1,128)}) custom-call(s32[1]{0:T(128)} %bitcast.base_ref, s32[1,2048]{1,0:T(1,128)} %bitcast.28, bf16[128,2048]{1,0:T(8,128)(2,1)} %q_ref.1, bf16[2048,512]{1,0:T(8,128)(2,1)} %get-tuple-element.19.k_ref, bf16[2048,512]{1,0:T(8,128)(2,1)} %get-tuple-element.20.v_ref, f32[1,2048]{1,0:T(1,128)} %bitcast.27, ...), custom_call_target="tpu_custom_call" | custom-call | flops 4294967296 | bytes 5775360 | tf_op jit(solution)/shard_map/pallas_call | solution.py:74
  79.7 8.3 %fusion.12 = f32[128,4096]{1,0:T(8,128)S(1)} fusion(bf16[128,2048]{1,0:T(8,128)(2,1)} %get-tuple-element.17, bf16[2048,4096]{1,0:T(8,128)(2,1)} %param.13), kind=kOutput, calls=%fused_computation.52 | convolution fusion | flops 2147483648 | bytes 19398656 | tf_op jit(solution)/shard_map/dot_general | solution.py:208
  88.0 0.1 dynamic-slice_convert_fusion
  88.1 1.6 %collective-permute-start.9 = (bf16[128,2048]{1,0:T(8,128)(2,1)S(1)}, bf16[128,2048]{1,0:T(8,128)(2,1)S(1)}, u32[]{:S(2)}, u32[]{:S(2)}) collective-permute-start(bf16[128,2048]{1,0:T(8,128)(2,1)S(1)} %dynamic-slice_convert_fusion), channel_id=1, source_target_pairs={{0,2},{2,0},{1,3},{3,1},{4,6},{6,4},{5,7},{7,5},{8,10},{10,8},{9,1... | collective-permute-start | bytes 1572872 | tf_op jit(solution)/shard_map/ppermute | solution.py:213
  89.7 0.5 broadcast.152
  90.2 0.7 reduce.13
  90.9 0.6 gather_fusion
  91.4 0.6 gather_fusion.1
  92.0 0.6 convolution_bitcast_fusion
  92.6 0.1 collective-permute-start.10
  92.8 1.1 collective-permute-done.10
  93.9 0.5 collective-permute-start.11
  94.4 8.2 %collective-permute-done.11 = f32[2080]{0:T(1024)S(1)} collective-permute-done((f32[2080]{0:T(1024)S(1)}, f32[2080]{0:T(1024)S(1)}, u32[]{:S(2)}, u32[]{:S(2)}) %collective-permute-start.11) | collective-permute-done | bytes 8352 | tf_op jit(solution)/shard_map/ppermute | solution.py:156
  102.6 0.0 collective-permute-start.12
  102.6 3.7 %collective-permute-done.12 = f32[2080]{0:T(1024)S(1)} collective-permute-done((f32[2080]{0:T(1024)S(1)}, f32[2080]{0:T(1024)S(1)}, u32[]{:S(2)}, u32[]{:S(2)}) %collective-permute-start.12) | collective-permute-done | bytes 8352 | tf_op jit(solution)/shard_map/ppermute | solution.py:156
  106.3 14.5 %collective-permute-start.13 = (f32[2080]{0:T(1024)S(1)}, f32[2080]{0:T(1024)S(1)}, u32[]{:S(2)}, u32[]{:S(2)}) collective-permute-start(f32[2080]{0:T(1024)S(1)} %add.98), channel_id=1, source_target_pairs={{0,8},{4,12},{8,0},{12,4},{1,9},{5,13},{9,1},{13,5},{2,10},{6,14},... | collective-permute-start | bytes 24968 | tf_op jit(solution)/shard_map/ppermute | solution.py:156
  120.8 1.7 %collective-permute-done.13 = f32[2080]{0:T(1024)S(1)} collective-permute-done((f32[2080]{0:T(1024)S(1)}, f32[2080]{0:T(1024)S(1)}, u32[]{:S(2)}, u32[]{:S(2)}) %collective-permute-start.13) | collective-permute-done | bytes 8352 | tf_op jit(solution)/shard_map/ppermute | solution.py:156
  122.5 0.5 slice.101
  123.0 0.7 dynamic_slice.11
  123.6 0.0 collective-permute-done.9
  123.6 0.9 add_convert_fusion
  (38 shorter events, 0.3 us)
Async XLA Ops:
  0.6 9.1 %copy-start.6 = (s32[128]{0:T(128)S(1)}, s32[128]{0:T(128)}, u32[]{:S(2)}) copy-start(s32[128]{0:T(128)} %param.15) | copy-start | bytes 1540
  0.6 9.1 %copy-start.3 = (bf16[128,4096]{1,0:T(8,128)(2,1)S(1)}, bf16[128,4096]{1,0:T(8,128)(2,1)}, u32[]{:S(2)}) copy-start(bf16[128,4096]{1,0:T(8,128)(2,1)} %param.14) | copy-start | bytes 3145732
  3.4 19.3 %collective-permute-start.1 = (bf16[528,512]{1,0:T(8,128)(2,1)}, bf16[528,512]{1,0:T(8,128)(2,1)S(1)}, u32[]{:S(2)}, u32[]{:S(2)}) collective-permute-start(bf16[528,512]{1,0:T(8,128)(2,1)} %pad_maximum_fusion.2), channel_id=1, source_target_pairs={{0,4},{4,8},{8,12},{1,5},{5,9},{9,13},{2,6},{6,10},{10,14},{3,7},{... | collective-permute-start | bytes 1622024 | tf_op jit(solution)/shard_map/ppermute | solution.py:109
  8.4 15.8 %collective-permute-start.4 = (bf16[528,512]{1,0:T(8,128)(2,1)}, bf16[528,512]{1,0:T(8,128)(2,1)S(1)}, u32[]{:S(2)}, u32[]{:S(2)}) collective-permute-start(bf16[528,512]{1,0:T(8,128)(2,1)} %pad_maximum_fusion.2), channel_id=1, source_target_pairs={{4,0},{8,4},{12,8},{5,1},{9,5},{13,9},{6,2},{10,6},{14,10},{7,3},{... | collective-permute-start | bytes 1622024 | tf_op jit(solution)/shard_map/ppermute | solution.py:111
  9.7 15.8 %collective-permute-start = (bf16[528,512]{1,0:T(8,128)(2,1)}, bf16[528,512]{1,0:T(8,128)(2,1)S(1)}, u32[]{:S(2)}, u32[]{:S(2)}) collective-permute-start(bf16[528,512]{1,0:T(8,128)(2,1)} %pad_maximum_fusion.2), channel_id=1, source_target_pairs={{0,1},{1,0},{2,3},{3,2},{4,5},{5,4},{6,7},{7,6},{8,9},{9,8},{10,11... | collective-permute-start | bytes 1622024 | tf_op jit(solution)/shard_map/ppermute | solution.py:132
  22.8 21.0 %collective-permute-start.2 = (bf16[528,512]{1,0:T(8,128)(2,1)S(1)}, bf16[528,512]{1,0:T(8,128)(2,1)S(1)}, u32[]{:S(2)}, u32[]{:S(2)}) collective-permute-start(bf16[528,512]{1,0:T(8,128)(2,1)S(1)} %broadcast_select_fusion.2), channel_id=1, source_target_pairs={{0,1},{1,0},{2,3},{3,2},{4,5},{5,4},{6,7},{7,6},{8,9},{9,8},{10,11... | collective-permute-start | bytes 1622024 | tf_op jit(solution)/shard_map/ppermute | solution.py:132
  23.4 2.5 %collective-permute-start.3 = (bf16[528,512]{1,0:T(8,128)(2,1)S(1)}, bf16[528,512]{1,0:T(8,128)(2,1)S(1)}, u32[]{:S(2)}, u32[]{:S(2)}) collective-permute-start(bf16[528,512]{1,0:T(8,128)(2,1)S(1)} %collective-permute-done.1), channel_id=1, source_target_pairs={{4,8},{8,12},{5,9},{9,13},{6,10},{10,14},{7,11},{11,15},{20,24},{2... | collective-permute-start | bytes 1622024 | tf_op jit(solution)/shard_map/ppermute | solution.py:109
  24.2 18.7 %collective-permute-start.5 = (bf16[528,512]{1,0:T(8,128)(2,1)S(1)}, bf16[528,512]{1,0:T(8,128)(2,1)S(1)}, u32[]{:S(2)}, u32[]{:S(2)}) collective-permute-start(bf16[528,512]{1,0:T(8,128)(2,1)S(1)} %collective-permute-done.4), channel_id=1, source_target_pairs={{4,0},{5,1},{6,2},{7,3},{20,16},{21,17},{22,18},{23,19}} | collective-permute-start | bytes 1622024 | tf_op jit(solution)/shard_map/ppermute | solution.py:111
  25.7 17.3 %copy-start = (bf16[528,512]{1,0:T(8,128)(2,1)}, bf16[528,512]{1,0:T(8,128)(2,1)S(1)}, u32[]{:S(2)}) copy-start(bf16[528,512]{1,0:T(8,128)(2,1)S(1)} %broadcast_select_fusion.6) | copy-start | bytes 1622020
  43.0 2.1 %collective-permute-start.6 = (bf16[528,512]{1,0:T(8,128)(2,1)S(1)}, bf16[528,512]{1,0:T(8,128)(2,1)S(1)}, u32[]{:S(2)}, u32[]{:S(2)}) collective-permute-start(bf16[528,512]{1,0:T(8,128)(2,1)S(1)} %broadcast_select_fusion.1), channel_id=1, source_target_pairs={{0,1},{1,0},{2,3},{3,2},{4,5},{5,4},{6,7},{7,6},{8,9},{9,8},{10,11... | collective-permute-start | bytes 1622024 | tf_op jit(solution)/shard_map/ppermute | solution.py:132
  43.1 0.9 collective-permute-start.7
  43.9 0.8 copy-start.2
  44.7 2.0 %collective-permute-start.8 = (bf16[528,512]{1,0:T(8,128)(2,1)S(1)}, bf16[528,512]{1,0:T(8,128)(2,1)S(1)}, u32[]{:S(2)}, u32[]{:S(2)}) collective-permute-start(bf16[528,512]{1,0:T(8,128)(2,1)S(1)} %broadcast_select_fusion), channel_id=1, source_target_pairs={{0,1},{1,0},{2,3},{3,2},{4,5},{5,4},{6,7},{7,6},{8,9},{9,8},{10,11... | collective-permute-start | bytes 1622024 | tf_op jit(solution)/shard_map/ppermute | solution.py:132
  45.2 1.6 %copy-start.1 = (bf16[528,512]{1,0:T(8,128)(2,1)}, bf16[528,512]{1,0:T(8,128)(2,1)S(1)}, u32[]{:S(2)}) copy-start(bf16[528,512]{1,0:T(8,128)(2,1)S(1)} %broadcast_select_fusion.4) | copy-start | bytes 1622020
  45.3 1.6 %copy-start.5 = (s32[4]{0:T(128)S(1)}, s32[4]{0:T(128)}, u32[]{:S(2)}) copy-start(s32[4]{0:T(128)} %param.17) | copy-start | bytes 52
  45.3 2.3 %slice-start = ((bf16[528,512]{1,0:T(8,128)(2,1)}), bf16[512,512]{1,0:T(8,128)(2,1)S(1)}, s32[]{:S(2)}) async-start(bf16[528,512]{1,0:T(8,128)(2,1)} %copy-done), calls=%async_computation | async-start | bytes 1048576 | tf_op jit(solution)/shard_map/slice | solution.py:138
  45.4 2.3 %slice-start.2 = ((bf16[528,512]{1,0:T(8,128)(2,1)}), bf16[512,512]{1,0:T(8,128)(2,1)S(1)}, s32[]{:S(2)}) async-start(bf16[528,512]{1,0:T(8,128)(2,1)} %copy-done.2), calls=%async_computation.2 | async-start | bytes 1048576 | tf_op jit(solution)/shard_map/slice | solution.py:138
  46.8 1.0 slice-start.1
  79.7 10.5 %copy-start.4 = (f32[1,2048]{1,0:T(1,128)S(1)}, f32[1,2048]{1,0:T(1,128)}, u32[]{:S(2)}) copy-start(f32[1,2048]{1,0:T(1,128)} %get-tuple-element.18) | copy-start | bytes 24580
  88.1 35.6 %collective-permute-start.9 = (bf16[128,2048]{1,0:T(8,128)(2,1)S(1)}, bf16[128,2048]{1,0:T(8,128)(2,1)S(1)}, u32[]{:S(2)}, u32[]{:S(2)}) collective-permute-start(bf16[128,2048]{1,0:T(8,128)(2,1)S(1)} %dynamic-slice_convert_fusion), channel_id=1, source_target_pairs={{0,2},{2,0},{1,3},{3,1},{4,6},{6,4},{5,7},{7,5},{8,10},{10,8},{9,1... | collective-permute-start | bytes 1572872 | tf_op jit(solution)/shard_map/ppermute | solution.py:213
  92.6 1.2 collective-permute-start.10
  93.9 8.7 %collective-permute-start.11 = (f32[2080]{0:T(1024)S(1)}, f32[2080]{0:T(1024)S(1)}, u32[]{:S(2)}, u32[]{:S(2)}) collective-permute-start(f32[2080]{0:T(1024)S(1)} %fusion.11), channel_id=1, source_target_pairs={{0,2},{2,0},{1,3},{3,1},{4,6},{6,4},{5,7},{7,5},{8,10},{10,8},{9,1... | collective-permute-start | bytes 24968 | tf_op jit(solution)/shard_map/ppermute | solution.py:156
  102.6 3.7 %collective-permute-start.12 = (f32[2080]{0:T(1024)S(1)}, f32[2080]{0:T(1024)S(1)}, u32[]{:S(2)}, u32[]{:S(2)}) collective-permute-start(f32[2080]{0:T(1024)S(1)} %add.97), channel_id=1, source_target_pairs={{0,4},{4,0},{8,12},{12,8},{1,5},{5,1},{9,13},{13,9},{2,6},{6,2},{1... | collective-permute-start | bytes 24968 | tf_op jit(solution)/shard_map/ppermute | solution.py:156
  106.3 16.1 %collective-permute-start.13 = (f32[2080]{0:T(1024)S(1)}, f32[2080]{0:T(1024)S(1)}, u32[]{:S(2)}, u32[]{:S(2)}) collective-permute-start(f32[2080]{0:T(1024)S(1)} %add.98), channel_id=1, source_target_pairs={{0,8},{4,12},{8,0},{12,4},{1,9},{5,13},{9,1},{13,5},{2,10},{6,14},... | collective-permute-start | bytes 24968 | tf_op jit(solution)/shard_map/ppermute | solution.py:156

commit v5 on v4

--- a/solution.py
+++ b/solution.py
@@ -105,10 +105,18 @@
     zero = jnp.zeros_like(payload)
     forward, backward = [payload], [payload]
     for k in range(1, n):
-        pairs = [(i, i + 1) for i in range(k - 1, n - 1) if needed(i + 1, i + 1 - k)]
-        forward.append(lax.ppermute(forward[-1], "ctx", pairs) if pairs else zero)
-        pairs = [(i + 1, i) for i in range(0, n - k) if needed(i, i + k)]
-        backward.append(lax.ppermute(backward[-1], "ctx", pairs) if pairs else zero)
+        fwd = [(i, i + k) for i in range(n - k) if needed(i + k, i)]
+        relay = [(i + k - 1, i + k) for i, _ in fwd]
+        if k > 2 and relay and all(needed(s, r - k) for s, r in relay):
+            forward.append(lax.ppermute(forward[-1], "ctx", relay))
+        else:
+            forward.append(lax.ppermute(payload, "ctx", fwd) if fwd else zero)
+        bwd = [(i + k, i) for i in range(n - k) if needed(i, i + k)]
+        relay = [(r + 1, r) for _, r in bwd]
+        if k > 2 and relay and all(needed(s, r + k) for s, r in relay):
+            backward.append(lax.ppermute(backward[-1], "ctx", relay))
+        else:
+            backward.append(lax.ppermute(payload, "ctx", bwd) if bwd else zero)
     parts = [payload]
     for k in range(1, n):
         parts.append(jnp.where(k <= ctx_at, forward[k], backward[n - k]))
@@ -201,7 +209,7 @@
         seg_abs[:, None] == jnp.arange(SEG_DEV * ctx_count, dtype=jnp.int32)[None, :]
     ).astype(jnp.float32)
     seg_part = jnp.dot(attr_abs, onehot, precision=lax.Precision.HIGHEST)
-    summed = butterfly_sum(jnp.concatenate([attr_abs, seg_part]), ("rep", "head", "ctx"))
+    summed = butterfly_sum(jnp.concatenate([attr_abs, seg_part]), ("rep", "ctx", "head"))
     attr_all = summed[:context_len]
     segment_attr = summed[context_len:]
 

time: 125 us -> 117 us (0.936)
  waiting for transfers between devices: 33.3 us -> 13.9 us
  starting transfers between devices: 26.8 us -> 36.6 us
  other arithmetic: 8.07 us -> 10.2 us
    ppermute x5, waiting for transfers between devices: 17.3 us -> 5.37 us  [the longest x2 4.72 us: relay_gather(): backward.append(lax.ppermute(payload, 'ctx', bwd) if bwd else zero)]
    ppermute x4, waiting for transfers between devices: 14.7 us -> 7.67 us  [butterfly_sum(): total = total + lax.ppermute(total, axis, [(i, i ^ bit) for i in range(n)])]
    ppermute x4, starting transfers between devices: 15.2 us -> 20.5 us  [butterfly_sum(): total = total + lax.ppermute(total, axis, [(i, i ^ bit) for i in range(n)])]
    ppermute x5, starting transfers between devices: 8.9 us -> 13.8 us  [the longest x2 10.5 us: relay_gather(): forward.append(lax.ppermute(payload, 'ctx', fwd) if fwd else zero)]
    select_n x3, other arithmetic: 0.16 us -> 2.25 us  [relay_gather(): parts.append(jnp.where(k <= ctx_at, forward[k], backward[n - k]))]
  transfers between devices with their start and end apart: 14 -> 14, of which waited for: 7 -> 7; matrix products, arithmetic and copies ran while one was open for 14% -> 17% of each run, Pallas kernels for 0% -> 0%
where the time goes in v5:
time: 117 us
  starting transfers between devices  36.6 us (31%)
  Pallas kernels  29.7 us (25%)
  matrix products  21.1 us (18%)
  waiting for transfers between devices  13.9 us (12%)
  other arithmetic  10.2 us (9%)
  local copies, waits for them, and re-layouts  4.62 us (4%)
    pallas_call x1, Pallas kernels, fused_attention(): pl.pallas_call(functools.partial(attention_kernel, tq=tq), grid_spec=pltp...  29.7 us
    ppermute x4, starting transfers between devices, butterfly_sum(): total = total + lax.ppermute(total, axis, [(i, i ^ bit) for i in range(n)])  20.5 us
    dot_general x1, matrix products, local(): jnp.dot(grad_masked, out_weight.T, preferred_element_type=jnp.float32)  12.3 us
    ppermute x2, starting transfers between devices, relay_gather(): forward.append(lax.ppermute(payload, 'ctx', fwd) if fwd else zero)  10.5 us
    dot_general x1, matrix products, local(): projected = jnp.dot(delta, out_weight, preferred_element_type=jnp.float32)  8.3 us
    ppermute x4, waiting for transfers between devices, butterfly_sum(): total = total + lax.ppermute(total, axis, [(i, i ^ bit) for i in range(n)])  7.67 us
    ppermute x2, waiting for transfers between devices, relay_gather(): backward.append(lax.ppermute(payload, 'ctx', bwd) if bwd else zero)  4.72 us
    ppermute x2, starting transfers between devices, relay_gather(): backward.append(lax.ppermute(payload, 'ctx', bwd) if bwd else zero)  2.58 us
  transfers between devices with their start and end apart: 14, of which 7 were waited for; matrix products, arithmetic and copies ran while one was open for 17% of the time, Pallas kernels for 0%

profile of v5, /device:TPU:0, one launch (start us, length us, event | category | flops | bytes accessed | tf_op | source)
XLA Modules:
  0.0 117.1 jit_solution(4077402965611266494)
XLA Ops:
  0.6 0.0 copy-start.6
  0.7 0.8 convert_element_type.29
  1.5 1.1 broadcast_select_fusion.7
  2.6 0.8 pad_maximum_fusion.2
  3.4 6.0 %collective-permute-start.3 = (bf16[528,512]{1,0:T(8,128)(2,1)}, bf16[528,512]{1,0:T(8,128)(2,1)S(1)}, u32[]{:S(2)}, u32[]{:S(2)}) collective-permute-start(bf16[528,512]{1,0:T(8,128)(2,1)} %pad_maximum_fusion.2), channel_id=1, source_target_pairs={{0,8},{4,12},{1,9},{5,13},{2,10},{6,14},{3,11},{7,15},{16,24},{20,... | collective-permute-start | bytes 1622024 | tf_op jit(solution)/shard_map/ppermute | solution.py:113
  9.4 1.3 %collective-permute-start.4 = (bf16[528,512]{1,0:T(8,128)(2,1)}, bf16[528,512]{1,0:T(8,128)(2,1)}, u32[]{:S(2)}, u32[]{:S(2)}) collective-permute-start(bf16[528,512]{1,0:T(8,128)(2,1)} %pad_maximum_fusion.2), channel_id=1, source_target_pairs={{8,0},{9,1},{10,2},{11,3},{24,16},{25,17},{26,18},{27,19}} | collective-permute-start | bytes 1622024 | tf_op jit(solution)/shard_map/ppermute | solution.py:119
  10.7 1.3 %collective-permute-start.7 = (bf16[528,512]{1,0:T(8,128)(2,1)}, bf16[528,512]{1,0:T(8,128)(2,1)}, u32[]{:S(2)}, u32[]{:S(2)}) collective-permute-start(bf16[528,512]{1,0:T(8,128)(2,1)} %pad_maximum_fusion.2), channel_id=1, source_target_pairs={{4,0},{8,4},{12,8},{5,1},{9,5},{13,9},{6,2},{10,6},{14,10},{7,3},{... | collective-permute-start | bytes 1622024 | tf_op jit(solution)/shard_map/ppermute | solution.py:119
  12.0 4.6 %collective-permute-start.1 = (bf16[528,512]{1,0:T(8,128)(2,1)}, bf16[528,512]{1,0:T(8,128)(2,1)S(1)}, u32[]{:S(2)}, u32[]{:S(2)}) collective-permute-start(bf16[528,512]{1,0:T(8,128)(2,1)} %pad_maximum_fusion.2), channel_id=1, source_target_pairs={{0,4},{4,8},{8,12},{1,5},{5,9},{9,13},{2,6},{6,10},{10,14},{3,7},{... | collective-permute-start | bytes 1622024 | tf_op jit(solution)/shard_map/ppermute | solution.py:113
  16.6 0.1 collective-permute-start
  16.7 0.0 copy-done.6
  16.7 12.3 %convolution_convert_fusion.do_ref = bf16[128,2048]{1,0:T(8,128)(2,1)} fusion(bf16[2048,4096]{1,0:T(8,128)(2,1)} %param.13, bf16[128,4096]{1,0:T(8,128)(2,1)S(1)} %copy-done.3, pred[128]{0:T(512)(128)(4,1)S(1)} %broadcast_compare_fusion), kind=kOutput, calls=%fused_computation.2 | convolution fusion | flops 2148270080 | bytes 18350208 | tf_op jit(solution)/shard_map/dot_general | solution.py:198
  28.9 0.1 add_bitcast_fusion
  29.0 0.6 copy.11
  29.6 0.0 collective-permute-done.3
  29.7 0.0 collective-permute-done.4
  29.7 1.1 broadcast_select_fusion.1
  30.8 0.5 collective-permute-start.5
  31.3 0.7 collective-permute-start.6
  32.0 0.0 collective-permute-done
  32.0 0.1 broadcast_select_fusion.6
  32.2 0.6 collective-permute-done.1
  32.9 0.1 collective-permute-start.2
  33.0 0.1 fusion.3
  33.1 4.7 %collective-permute-done.7 = bf16[528,512]{1,0:T(8,128)(2,1)} collective-permute-done((bf16[528,512]{1,0:T(8,128)(2,1)}, bf16[528,512]{1,0:T(8,128)(2,1)}, u32[]{:S(2)}, u32[]{:S(2)}) %collective-permute-start.7) | collective-permute-done | bytes 540704 | tf_op jit(solution)/shard_map/ppermute | solution.py:119
  37.8 0.0 collective-permute-done.6
  37.8 1.1 broadcast_select_fusion
  38.9 0.1 collective-permute-start.8
  39.0 0.0 collective-permute-done.5
  39.0 0.1 broadcast_select_fusion.4
  39.1 0.0 copy-start
  39.1 0.0 collective-permute-done.2
  39.1 0.1 broadcast_select_fusion.5
  39.2 0.1 slice_select_fusion.1
  39.3 0.6 copy-done
  39.9 0.1 slice_select_fusion.2
  40.0 0.1 copy-done.2
  40.1 0.8 collective-permute-done.8
  40.9 0.1 broadcast_select_fusion.3
  41.1 0.1 compare_reduce_fusion
  41.2 0.6 broadcast_select_fusion.8
  41.8 0.1 slice_select_fusion
  41.9 0.2 slice-done.2
  42.1 2.1 %pad_maximum_fusion = (bf16[2048,512]{1,0:T(8,128)(2,1)}, bf16[2048,512]{1,0:T(8,128)(2,1)}) fusion(bf16[512,512]{1,0:T(8,128)(2,1)S(1)} %slice.86, bf16[512,512]{1,0:T(8,128)(2,1)S(1)} %slice-done, bf16[512,512]{1,0:T(8,128)(2,1)S(1)} %slice-done.2, bf16[512,512]{1,0:T(8,128)(2,1)S(1)} %slice-done.1, bf16[512,512]{1,0:T(8,128)(2,1)S(1)} %slice_select_fusion, ...), kind=kLoop, calls=%fused_computation.3 | loop fusion | flops 16777216 | bytes 8388608 | tf_op jit(solution)/shard_map/concatenate | solution.py:146
  44.2 29.7 %shard_map.103 = (bf16[128,2048]{1,0:T(8,128)(2,1)}, f32[1,2048]{1,0:T(1,128)}) custom-call(s32[1]{0:T(128)} %bitcast.base_ref, s32[1,2048]{1,0:T(1,128)} %bitcast.28, bf16[128,2048]{1,0:T(8,128)(2,1)} %q_ref.1, bf16[2048,512]{1,0:T(8,128)(2,1)} %get-tuple-element.19.k_ref, bf16[2048,512]{1,0:T(8,128)(2,1)} %get-tuple-element.20.v_ref, f32[1,2048]{1,0:T(1,128)} %bitcast.27, ...), custom_call_target="tpu_custom_call" | custom-call | flops 4294967296 | bytes 5775360 | tf_op jit(solution)/shard_map/pallas_call | solution.py:74
  73.9 8.3 %fusion.12 = f32[128,4096]{1,0:T(8,128)S(1)} fusion(bf16[128,2048]{1,0:T(8,128)(2,1)} %get-tuple-element.17, bf16[2048,4096]{1,0:T(8,128)(2,1)} %param.13), kind=kOutput, calls=%fused_computation.52 | convolution fusion | flops 2147483648 | bytes 19398656 | tf_op jit(solution)/shard_map/dot_general | solution.py:216
  82.2 0.1 dynamic-slice_convert_fusion
  82.3 1.6 %collective-permute-start.9 = (bf16[128,2048]{1,0:T(8,128)(2,1)S(1)}, bf16[128,2048]{1,0:T(8,128)(2,1)S(1)}, u32[]{:S(2)}, u32[]{:S(2)}) collective-permute-start(bf16[128,2048]{1,0:T(8,128)(2,1)S(1)} %dynamic-slice_convert_fusion), channel_id=1, source_target_pairs={{0,2},{2,0},{1,3},{3,1},{4,6},{6,4},{5,7},{7,5},{8,10},{10,8},{9,1... | collective-permute-start | bytes 1572872 | tf_op jit(solution)/shard_map/ppermute | solution.py:221
  83.9 0.5 broadcast.152
  84.4 0.7 reduce.13
  85.1 0.6 gather_fusion
  85.6 0.6 gather_fusion.1
  86.2 0.6 convolution_bitcast_fusion
  86.8 0.1 collective-permute-start.10
  86.9 1.2 collective-permute-done.10
  88.1 8.5 %collective-permute-start.11 = (f32[2080]{0:T(1024)S(1)}, f32[2080]{0:T(1024)S(1)}, u32[]{:S(2)}, u32[]{:S(2)}) collective-permute-start(f32[2080]{0:T(1024)S(1)} %fusion.11), channel_id=1, source_target_pairs={{0,4},{4,0},{8,12},{12,8},{1,5},{5,1},{9,13},{13,9},{2,6},{6,2},{1... | collective-permute-start | bytes 24968 | tf_op jit(solution)/shard_map/ppermute | solution.py:164
  96.5 1.7 %collective-permute-done.11 = f32[2080]{0:T(1024)S(1)} collective-permute-done((f32[2080]{0:T(1024)S(1)}, f32[2080]{0:T(1024)S(1)}, u32[]{:S(2)}, u32[]{:S(2)}) %collective-permute-start.11) | collective-permute-done | bytes 8352 | tf_op jit(solution)/shard_map/ppermute | solution.py:164
  98.2 11.4 %collective-permute-start.12 = (f32[2080]{0:T(1024)S(1)}, f32[2080]{0:T(1024)S(1)}, u32[]{:S(2)}, u32[]{:S(2)}) collective-permute-start(f32[2080]{0:T(1024)S(1)} %add.97), channel_id=1, source_target_pairs={{0,8},{4,12},{8,0},{12,4},{1,9},{5,13},{9,1},{13,5},{2,10},{6,14},... | collective-permute-start | bytes 24968 | tf_op jit(solution)/shard_map/ppermute | solution.py:164
  109.6 1.7 %collective-permute-done.12 = f32[2080]{0:T(1024)S(1)} collective-permute-done((f32[2080]{0:T(1024)S(1)}, f32[2080]{0:T(1024)S(1)}, u32[]{:S(2)}, u32[]{:S(2)}) %collective-permute-start.12) | collective-permute-done | bytes 8352 | tf_op jit(solution)/shard_map/ppermute | solution.py:164
  111.3 0.5 collective-permute-start.13
  111.8 3.2 %collective-permute-done.13 = f32[2080]{0:T(1024)S(1)} collective-permute-done((f32[2080]{0:T(1024)S(1)}, f32[2080]{0:T(1024)S(1)}, u32[]{:S(2)}, u32[]{:S(2)}) %collective-permute-start.13) | collective-permute-done | bytes 8352 | tf_op jit(solution)/shard_map/ppermute | solution.py:164
  115.0 0.5 slice.101
  115.5 0.7 dynamic_slice.11
  116.1 0.0 collective-permute-done.9
  116.1 0.9 add_convert_fusion
  (38 shorter events, 0.3 us)
Async XLA Ops:
  0.6 16.0 %copy-start.6 = (s32[128]{0:T(128)S(1)}, s32[128]{0:T(128)}, u32[]{:S(2)}) copy-start(s32[128]{0:T(128)} %param.15) | copy-start | bytes 1540
  0.6 16.0 %copy-start.3 = (bf16[128,4096]{1,0:T(8,128)(2,1)S(1)}, bf16[128,4096]{1,0:T(8,128)(2,1)}, u32[]{:S(2)}) copy-start(bf16[128,4096]{1,0:T(8,128)(2,1)} %param.14) | copy-start | bytes 3145732
  3.4 26.2 %collective-permute-start.3 = (bf16[528,512]{1,0:T(8,128)(2,1)}, bf16[528,512]{1,0:T(8,128)(2,1)S(1)}, u32[]{:S(2)}, u32[]{:S(2)}) collective-permute-start(bf16[528,512]{1,0:T(8,128)(2,1)} %pad_maximum_fusion.2), channel_id=1, source_target_pairs={{0,8},{4,12},{1,9},{5,13},{2,10},{6,14},{3,11},{7,15},{16,24},{20,... | collective-permute-start | bytes 1622024 | tf_op jit(solution)/shard_map/ppermute | solution.py:113
  9.4 20.3 %collective-permute-start.4 = (bf16[528,512]{1,0:T(8,128)(2,1)}, bf16[528,512]{1,0:T(8,128)(2,1)}, u32[]{:S(2)}, u32[]{:S(2)}) collective-permute-start(bf16[528,512]{1,0:T(8,128)(2,1)} %pad_maximum_fusion.2), channel_id=1, source_target_pairs={{8,0},{9,1},{10,2},{11,3},{24,16},{25,17},{26,18},{27,19}} | collective-permute-start | bytes 1622024 | tf_op jit(solution)/shard_map/ppermute | solution.py:119
  10.7 27.1 %collective-permute-start.7 = (bf16[528,512]{1,0:T(8,128)(2,1)}, bf16[528,512]{1,0:T(8,128)(2,1)}, u32[]{:S(2)}, u32[]{:S(2)}) collective-permute-start(bf16[528,512]{1,0:T(8,128)(2,1)} %pad_maximum_fusion.2), channel_id=1, source_target_pairs={{4,0},{8,4},{12,8},{5,1},{9,5},{13,9},{6,2},{10,6},{14,10},{7,3},{... | collective-permute-start | bytes 1622024 | tf_op jit(solution)/shard_map/ppermute | solution.py:119
  12.0 20.8 %collective-permute-start.1 = (bf16[528,512]{1,0:T(8,128)(2,1)}, bf16[528,512]{1,0:T(8,128)(2,1)S(1)}, u32[]{:S(2)}, u32[]{:S(2)}) collective-permute-start(bf16[528,512]{1,0:T(8,128)(2,1)} %pad_maximum_fusion.2), channel_id=1, source_target_pairs={{0,4},{4,8},{8,12},{1,5},{5,9},{9,13},{2,6},{6,10},{10,14},{3,7},{... | collective-permute-start | bytes 1622024 | tf_op jit(solution)/shard_map/ppermute | solution.py:113
  16.6 15.4 %collective-permute-start = (bf16[528,512]{1,0:T(8,128)(2,1)}, bf16[528,512]{1,0:T(8,128)(2,1)S(1)}, u32[]{:S(2)}, u32[]{:S(2)}) collective-permute-start(bf16[528,512]{1,0:T(8,128)(2,1)} %pad_maximum_fusion.2), channel_id=1, source_target_pairs={{0,1},{1,0},{2,3},{3,2},{4,5},{5,4},{6,7},{7,6},{8,9},{9,8},{10,11... | collective-permute-start | bytes 1622024 | tf_op jit(solution)/shard_map/ppermute | solution.py:140
  30.8 8.3 %collective-permute-start.5 = (bf16[528,512]{1,0:T(8,128)(2,1)S(1)}, bf16[528,512]{1,0:T(8,128)(2,1)S(1)}, u32[]{:S(2)}, u32[]{:S(2)}) collective-permute-start(bf16[528,512]{1,0:T(8,128)(2,1)S(1)} %broadcast_select_fusion.1), channel_id=1, source_target_pairs={{0,1},{1,0},{2,3},{3,2},{4,5},{5,4},{6,7},{7,6},{8,9},{9,8},{10,11... | collective-permute-start | bytes 1622024 | tf_op jit(solution)/shard_map/ppermute | solution.py:140
  31.3 6.5 %collective-permute-start.6 = (bf16[528,512]{1,0:T(8,128)(2,1)S(1)}, bf16[528,512]{1,0:T(8,128)(2,1)S(1)}, u32[]{:S(2)}, u32[]{:S(2)}) collective-permute-start(bf16[528,512]{1,0:T(8,128)(2,1)S(1)} %collective-permute-done.3), channel_id=1, source_target_pairs={{8,12},{9,13},{10,14},{11,15},{24,28},{25,29},{26,30},{27,31}} | collective-permute-start | bytes 1622024 | tf_op jit(solution)/shard_map/ppermute | solution.py:111
  32.2 6.8 %copy-start.1 = (bf16[528,512]{1,0:T(8,128)(2,1)}, bf16[528,512]{1,0:T(8,128)(2,1)S(1)}, u32[]{:S(2)}) copy-start(bf16[528,512]{1,0:T(8,128)(2,1)S(1)} %broadcast_select_fusion.6) | copy-start | bytes 1622020
  32.9 6.3 %collective-permute-start.2 = (bf16[528,512]{1,0:T(8,128)(2,1)S(1)}, bf16[528,512]{1,0:T(8,128)(2,1)S(1)}, u32[]{:S(2)}, u32[]{:S(2)}) collective-permute-start(bf16[528,512]{1,0:T(8,128)(2,1)S(1)} %broadcast_select_fusion.2), channel_id=1, source_target_pairs={{0,1},{1,0},{2,3},{3,2},{4,5},{5,4},{6,7},{7,6},{8,9},{9,8},{10,11... | collective-permute-start | bytes 1622024 | tf_op jit(solution)/shard_map/ppermute | solution.py:140
  38.9 2.0 %collective-permute-start.8 = (bf16[528,512]{1,0:T(8,128)(2,1)S(1)}, bf16[528,512]{1,0:T(8,128)(2,1)S(1)}, u32[]{:S(2)}, u32[]{:S(2)}) collective-permute-start(bf16[528,512]{1,0:T(8,128)(2,1)S(1)} %broadcast_select_fusion), channel_id=1, source_target_pairs={{0,1},{1,0},{2,3},{3,2},{4,5},{5,4},{6,7},{7,6},{8,9},{9,8},{10,11... | collective-permute-start | bytes 1622024 | tf_op jit(solution)/shard_map/ppermute | solution.py:140
  39.1 0.8 copy-start
  39.2 0.9 copy-start.2
  39.9 1.1 copy-start.5
  40.1 1.8 %slice-start = ((bf16[528,512]{1,0:T(8,128)(2,1)}), bf16[512,512]{1,0:T(8,128)(2,1)S(1)}, s32[]{:S(2)}) async-start(bf16[528,512]{1,0:T(8,128)(2,1)} %copy-done), calls=%async_computation | async-start | bytes 1048576 | tf_op jit(solution)/shard_map/slice | solution.py:146
  40.1 1.8 %slice-start.1 = ((bf16[528,512]{1,0:T(8,128)(2,1)}), bf16[512,512]{1,0:T(8,128)(2,1)S(1)}, s32[]{:S(2)}) async-start(bf16[528,512]{1,0:T(8,128)(2,1)} %copy-done.1), calls=%async_computation.1 | async-start | bytes 1048576 | tf_op jit(solution)/shard_map/slice | solution.py:146
  40.9 1.1 slice-start.2
  73.9 10.5 %copy-start.4 = (f32[1,2048]{1,0:T(1,128)S(1)}, f32[1,2048]{1,0:T(1,128)}, u32[]{:S(2)}) copy-start(f32[1,2048]{1,0:T(1,128)} %get-tuple-element.18) | copy-start | bytes 24580
  82.3 33.9 %collective-permute-start.9 = (bf16[128,2048]{1,0:T(8,128)(2,1)S(1)}, bf16[128,2048]{1,0:T(8,128)(2,1)S(1)}, u32[]{:S(2)}, u32[]{:S(2)}) collective-permute-start(bf16[128,2048]{1,0:T(8,128)(2,1)S(1)} %dynamic-slice_convert_fusion), channel_id=1, source_target_pairs={{0,2},{2,0},{1,3},{3,1},{4,6},{6,4},{5,7},{7,5},{8,10},{10,8},{9,1... | collective-permute-start | bytes 1572872 | tf_op jit(solution)/shard_map/ppermute | solution.py:221
  86.8 1.2 %collective-permute-start.10 = (f32[2080]{0:T(1024)S(1)}, f32[2080]{0:T(1024)S(1)}, u32[]{:S(2)}, u32[]{:S(2)}) collective-permute-start(f32[2080]{0:T(1024)S(1)} %pad_maximum_fusion.3), channel_id=1, source_target_pairs={{0,1},{1,0},{2,3},{3,2},{4,5},{5,4},{6,7},{7,6},{8,9},{9,8},{10,11... | collective-permute-start | bytes 24968 | tf_op jit(solution)/shard_map/ppermute | solution.py:164
  88.1 10.1 %collective-permute-start.11 = (f32[2080]{0:T(1024)S(1)}, f32[2080]{0:T(1024)S(1)}, u32[]{:S(2)}, u32[]{:S(2)}) collective-permute-start(f32[2080]{0:T(1024)S(1)} %fusion.11), channel_id=1, source_target_pairs={{0,4},{4,0},{8,12},{12,8},{1,5},{5,1},{9,13},{13,9},{2,6},{6,2},{1... | collective-permute-start | bytes 24968 | tf_op jit(solution)/shard_map/ppermute | solution.py:164
  98.2 13.1 %collective-permute-start.12 = (f32[2080]{0:T(1024)S(1)}, f32[2080]{0:T(1024)S(1)}, u32[]{:S(2)}, u32[]{:S(2)}) collective-permute-start(f32[2080]{0:T(1024)S(1)} %add.97), channel_id=1, source_target_pairs={{0,8},{4,12},{8,0},{12,4},{1,9},{5,13},{9,1},{13,5},{2,10},{6,14},... | collective-permute-start | bytes 24968 | tf_op jit(solution)/shard_map/ppermute | solution.py:164
  111.3 3.7 %collective-permute-start.13 = (f32[2080]{0:T(1024)S(1)}, f32[2080]{0:T(1024)S(1)}, u32[]{:S(2)}, u32[]{:S(2)}) collective-permute-start(f32[2080]{0:T(1024)S(1)} %add.98), channel_id=1, source_target_pairs={{0,2},{2,0},{1,3},{3,1},{4,6},{6,4},{5,7},{7,5},{8,10},{10,8},{9,1... | collective-permute-start | bytes 24968 | tf_op jit(solution)/shard_map/ppermute | solution.py:164

commit v6 on v5

--- a/solution.py
+++ b/solution.py
@@ -13,7 +13,9 @@
 NT_DIMS = (((1,), (1,)), ((), ()))
 
 
-def attention_kernel(base_ref, kpos_ref, q_ref, k_ref, v_ref, kept_ref, do_ref, delta_ref, attr_ref, *, tq):
+def attention_kernel(
+    base_ref, kpos_ref, q_ref, k_ref, v_ref, kept_ref, gm_ref, w_ref, delta_ref, attr_ref, *, tq
+):
     r = pl.program_id(2)
     first = (pl.program_id(0) == 0) & (pl.program_id(1) == 0) & (r == 0)
 
@@ -28,17 +30,20 @@
     s = lax.dot_general(q, k, NT_DIMS, preferred_element_type=jnp.float32) * (HD ** -0.5)
     row_pos = base_ref[0] + r * tq + lax.broadcasted_iota(jnp.int32, (tq, keys), 0)
     vis = kpos_ref[...] <= row_pos
-    kvis = jnp.logical_and(vis, kept_ref[...] > 0.0)
-    m_c = jnp.max(jnp.where(vis, s, NEG_FILL), axis=1, keepdims=True)
-    m_m = jnp.max(jnp.where(kvis, s, NEG_FILL), axis=1, keepdims=True)
-    e_c = jnp.where(vis, jnp.exp(s - m_c), 0.0)
-    e_m = jnp.where(kvis, jnp.exp(s - m_m), 0.0)
+    s_c = jnp.where(vis, s, NEG_FILL)
+    s_m = jnp.where(kept_ref[...] > 0.0, s_c, NEG_FILL)
+    m_c = jnp.max(s_c, axis=1, keepdims=True)
+    m_m = jnp.max(s_m, axis=1, keepdims=True)
+    e_c = jnp.exp(s_c - m_c)
+    e_m = jnp.exp(s_m - m_m)
     l_c = jnp.sum(e_c, axis=1, keepdims=True)
     l_m = jnp.sum(e_m, axis=1, keepdims=True)
     o_c = jnp.dot(e_c.astype(jnp.bfloat16), v, preferred_element_type=jnp.float32) / l_c
     o_m = jnp.dot(e_m.astype(jnp.bfloat16), v, preferred_element_type=jnp.float32) / l_m
     delta_ref[...] = (o_m - o_c).astype(delta_ref.dtype)
-    g_rows = do_ref[...]
+    g_rows = lax.dot_general(
+        gm_ref[...], w_ref[...], NT_DIMS, preferred_element_type=jnp.float32
+    ).astype(jnp.bfloat16)
     row_dot = jnp.sum(g_rows.astype(jnp.float32) * o_c, axis=1, keepdims=True)
     d_p = lax.dot_general(g_rows, v, NT_DIMS, preferred_element_type=jnp.float32)
     log_total = m_c + jnp.log(l_c)
@@ -47,10 +52,11 @@
     attr_ref[...] += jnp.sum(contrib, axis=0, keepdims=True)
 
 
-def fused_attention(base, key_pos, query, key_all, value_all, kept, grad_out, group_size):
+def fused_attention(base, key_pos, query, key_all, value_all, kept, grad_rows, out_weight, group_size):
     qc, width = query.shape
     keys, kv_width = key_all.shape
     kv_local = kv_width // HD
+    model = out_weight.shape[1]
     tq = max(8, min(qc, (128 * 2048) // keys))
     n_rows = qc // tq
     grid = (kv_local, group_size, n_rows)
@@ -64,11 +70,17 @@
     def fixed(g, j, r, b):
         return (0, 0)
 
-    flops = 8 * qc * keys * HD * kv_local * group_size
+    def row_map(g, j, r, b):
+        return (r, 0)
+
+    def weight_map(g, j, r, b):
+        return (g * group_size + j, 0)
+
+    flops = 8 * qc * keys * HD * kv_local * group_size + 2 * qc * width * model
     cost = pl.CostEstimate(
         flops=flops,
         transcendentals=2 * qc * keys * kv_local * group_size,
-        bytes_accessed=2 * (query.size + key_all.size + value_all.size + grad_out.size + query.size)
+        bytes_accessed=2 * (2 * query.size + key_all.size + value_all.size + out_weight.size)
         + 4 * keys,
     )
     return pl.pallas_call(
@@ -82,7 +94,8 @@
                 pl.BlockSpec((keys, HD), kv_map),
                 pl.BlockSpec((keys, HD), kv_map),
                 pl.BlockSpec((1, keys), fixed),
-                pl.BlockSpec((tq, HD), head_map),
+                pl.BlockSpec((tq, model), row_map),
+                pl.BlockSpec((HD, model), weight_map),
             ],
             out_specs=[
                 pl.BlockSpec((tq, HD), head_map),
@@ -97,7 +110,7 @@
             dimension_semantics=("arbitrary", "arbitrary", "arbitrary")
         ),
         cost_estimate=cost,
-    )(base, key_pos, query, key_all, value_all, kept, grad_out)
+    )(base, key_pos, query, key_all, value_all, kept, grad_rows, out_weight)
 
 
 def relay_gather(payload, needed, ctx_at):
@@ -195,11 +208,8 @@
     ).astype(jnp.float32)[None, :]
 
     grad_masked = jnp.where(response[:, None] > 0, cotangent, jnp.zeros_like(cotangent))
-    grad_out = jnp.dot(grad_masked, out_weight.T, preferred_element_type=jnp.float32).astype(
-        jnp.bfloat16
-    )
     delta, attr = fused_attention(
-        base, key_pos, query, key_all, value_all, kept, grad_out, group_size
+        base, key_pos, query, key_all, value_all, kept, grad_masked, out_weight, group_size
     )
 
     inverse = (ctx_at - jnp.arange(ctx_count, dtype=jnp.int32)) % ctx_count

time: 117 us -> 125 us (1.068)
  matrix products: 21.1 us -> 8.87 us
  waiting for transfers between devices: 13.9 us -> 25.5 us
  Pallas kernels: 29.7 us -> 37 us
    dot_general x1 -> x0, matrix products: 12.3 us -> none  [local(): jnp.dot(grad_masked, out_weight.T, preferred_element_type=jnp.float32)]
    pallas_call x1, Pallas kernels: 29.7 us -> 37 us  [fused_attention(): pl.pallas_call(functools.partial(attention_kernel, tq=tq), grid_spec=pltp...]
    ppermute x2, waiting for transfers between devices: 0.64 us -> 6.88 us  [relay_gather(): forward.append(lax.ppermute(payload, 'ctx', fwd) if fwd else zero)]
    ppermute x2, waiting for transfers between devices: 4.72 us -> 10.1 us  [relay_gather(): backward.append(lax.ppermute(payload, 'ctx', bwd) if bwd else zero)]
  transfers between devices with their start and end apart: 14 -> 14, of which waited for: 7 -> 9; matrix products, arithmetic and copies ran while one was open for 17% -> 7% of each run, Pallas kernels for 0% -> 0%
where the time goes in v6:
time: 125 us; the launch traced here: 124 us
  Pallas kernels  37 us (30%)
  starting transfers between devices  36.1 us (29%)
  waiting for transfers between devices  25.5 us (20%)
  other arithmetic  11.3 us (9%)
  matrix products  8.87 us (7%)
  local copies, waits for them, and re-layouts  4.62 us (4%)
    pallas_call x1, Pallas kernels, fused_attention(): pl.pallas_call(functools.partial(attention_kernel, tq=tq), grid_spec=pltp...  37 us
    ppermute x4, starting transfers between devices, butterfly_sum(): total = total + lax.ppermute(total, axis, [(i, i ^ bit) for i in range(n)])  20.5 us
    ppermute x2, starting transfers between devices, relay_gather(): forward.append(lax.ppermute(payload, 'ctx', fwd) if fwd else zero)  10.5 us
    ppermute x2, waiting for transfers between devices, relay_gather(): backward.append(lax.ppermute(payload, 'ctx', bwd) if bwd else zero)  10.1 us
    dot_general x1, matrix products, local(): projected = jnp.dot(delta, out_weight, preferred_element_type=jnp.float32)  8.3 us
    ppermute x4, waiting for transfers between devices, butterfly_sum(): total = total + lax.ppermute(total, axis, [(i, i ^ bit) for i in range(n)])  7.67 us
    ppermute x2, waiting for transfers between devices, relay_gather(): forward.append(lax.ppermute(payload, 'ctx', fwd) if fwd else zero)  6.88 us
    ppermute x2, starting transfers between devices, relay_gather(): backward.append(lax.ppermute(payload, 'ctx', bwd) if bwd else zero)  2.58 us
  transfers between devices with their start and end apart: 14, of which 9 were waited for; matrix products, arithmetic and copies ran while one was open for 7% of the time, Pallas kernels for 0%

profile of v6, /device:TPU:0, one launch (start us, length us, event | category | flops | bytes accessed | tf_op | source)
XLA Modules:
  0.0 124.4 jit_solution(17063445818810551974)
XLA Ops:
  0.6 0.0 copy-start.6
  0.6 0.0 copy-start.3
  0.7 0.8 convert_element_type.26
  1.5 1.1 broadcast_select_fusion.8
  2.6 0.8 pad_maximum_fusion.2
  3.4 6.0 %collective-permute-start.3 = (bf16[528,512]{1,0:T(8,128)(2,1)}, bf16[528,512]{1,0:T(8,128)(2,1)S(1)}, u32[]{:S(2)}, u32[]{:S(2)}) collective-permute-start(bf16[528,512]{1,0:T(8,128)(2,1)} %pad_maximum_fusion.2), channel_id=1, source_target_pairs={{0,8},{4,12},{1,9},{5,13},{2,10},{6,14},{3,11},{7,15},{16,24},{20,... | collective-permute-start | bytes 1622024 | tf_op jit(solution)/shard_map/ppermute | solution.py:126
  9.4 1.3 %collective-permute-start.4 = (bf16[528,512]{1,0:T(8,128)(2,1)}, bf16[528,512]{1,0:T(8,128)(2,1)}, u32[]{:S(2)}, u32[]{:S(2)}) collective-permute-start(bf16[528,512]{1,0:T(8,128)(2,1)} %pad_maximum_fusion.2), channel_id=1, source_target_pairs={{8,0},{9,1},{10,2},{11,3},{24,16},{25,17},{26,18},{27,19}} | collective-permute-start | bytes 1622024 | tf_op jit(solution)/shard_map/ppermute | solution.py:132
  10.7 1.3 %collective-permute-start.7 = (bf16[528,512]{1,0:T(8,128)(2,1)}, bf16[528,512]{1,0:T(8,128)(2,1)}, u32[]{:S(2)}, u32[]{:S(2)}) collective-permute-start(bf16[528,512]{1,0:T(8,128)(2,1)} %pad_maximum_fusion.2), channel_id=1, source_target_pairs={{4,0},{8,4},{12,8},{5,1},{9,5},{13,9},{6,2},{10,6},{14,10},{7,3},{... | collective-permute-start | bytes 1622024 | tf_op jit(solution)/shard_map/ppermute | solution.py:132
  12.0 4.6 %collective-permute-start.1 = (bf16[528,512]{1,0:T(8,128)(2,1)}, bf16[528,512]{1,0:T(8,128)(2,1)S(1)}, u32[]{:S(2)}, u32[]{:S(2)}) collective-permute-start(bf16[528,512]{1,0:T(8,128)(2,1)} %pad_maximum_fusion.2), channel_id=1, source_target_pairs={{0,4},{4,8},{8,12},{1,5},{5,9},{9,13},{2,6},{6,10},{10,14},{3,7},{... | collective-permute-start | bytes 1622024 | tf_op jit(solution)/shard_map/ppermute | solution.py:126
  16.6 0.1 collective-permute-start
  16.7 0.0 copy-done.6
  16.7 1.1 broadcast_select_fusion.gm_ref
  17.8 0.1 add_bitcast_fusion
  17.9 0.6 copy.11
  18.5 3.9 %collective-permute-done.3 = bf16[528,512]{1,0:T(8,128)(2,1)S(1)} collective-permute-done((bf16[528,512]{1,0:T(8,128)(2,1)}, bf16[528,512]{1,0:T(8,128)(2,1)S(1)}, u32[]{:S(2)}, u32[]{:S(2)}) %collective-permute-start.3) | collective-permute-done | bytes 540704 | tf_op jit(solution)/shard_map/ppermute | solution.py:126
  22.4 5.4 %collective-permute-done.4 = bf16[528,512]{1,0:T(8,128)(2,1)} collective-permute-done((bf16[528,512]{1,0:T(8,128)(2,1)}, bf16[528,512]{1,0:T(8,128)(2,1)}, u32[]{:S(2)}, u32[]{:S(2)}) %collective-permute-start.4) | collective-permute-done | bytes 540704 | tf_op jit(solution)/shard_map/ppermute | solution.py:132
  27.8 1.1 broadcast_select_fusion.2
  28.9 0.1 collective-permute-start.5
  28.9 0.7 collective-permute-start.6
  29.6 0.0 collective-permute-done
  29.7 0.1 broadcast_select_fusion.7
  29.8 3.0 %collective-permute-done.1 = bf16[528,512]{1,0:T(8,128)(2,1)S(1)} collective-permute-done((bf16[528,512]{1,0:T(8,128)(2,1)}, bf16[528,512]{1,0:T(8,128)(2,1)S(1)}, u32[]{:S(2)}, u32[]{:S(2)}) %collective-permute-start.1) | collective-permute-done | bytes 540704 | tf_op jit(solution)/shard_map/ppermute | solution.py:126
  32.9 0.1 collective-permute-start.2
  33.0 0.1 fusion.1
  33.1 4.7 %collective-permute-done.7 = bf16[528,512]{1,0:T(8,128)(2,1)} collective-permute-done((bf16[528,512]{1,0:T(8,128)(2,1)}, bf16[528,512]{1,0:T(8,128)(2,1)}, u32[]{:S(2)}, u32[]{:S(2)}) %collective-permute-start.7) | collective-permute-done | bytes 540704 | tf_op jit(solution)/shard_map/ppermute | solution.py:132
  37.8 0.0 collective-permute-done.6
  37.8 1.1 broadcast_select_fusion.1
  39.0 0.1 collective-permute-start.8
  39.0 0.0 collective-permute-done.5
  39.0 0.1 broadcast_select_fusion.5
  39.1 0.0 collective-permute-done.2
  39.1 0.1 broadcast_select_fusion.6
  39.2 0.1 slice_select_fusion.1
  39.3 0.6 copy-done
  40.0 0.1 slice_select_fusion.2
  40.0 0.1 copy-done.2
  40.1 0.8 collective-permute-done.8
  41.0 0.1 broadcast_select_fusion.4
  41.1 0.1 compare_reduce_fusion
  41.2 0.6 broadcast_select_fusion.9
  41.8 0.1 slice_select_fusion
  41.9 0.2 slice-done.2
  42.1 2.1 %pad_maximum_fusion = (bf16[2048,512]{1,0:T(8,128)(2,1)}, bf16[2048,512]{1,0:T(8,128)(2,1)}) fusion(bf16[512,512]{1,0:T(8,128)(2,1)S(1)} %slice.86, bf16[512,512]{1,0:T(8,128)(2,1)S(1)} %slice-done, bf16[512,512]{1,0:T(8,128)(2,1)S(1)} %slice-done.2, bf16[512,512]{1,0:T(8,128)(2,1)S(1)} %slice-done.1, bf16[512,512]{1,0:T(8,128)(2,1)S(1)} %slice_select_fusion, ...), kind=kLoop, calls=%fused_computation.2 | loop fusion | flops 16777216 | bytes 8388608 | tf_op jit(solution)/shard_map/concatenate | solution.py:159
  44.2 37.0 %shard_map.103 = (bf16[128,2048]{1,0:T(8,128)(2,1)}, f32[1,2048]{1,0:T(1,128)}) custom-call(s32[1]{0:T(128)} %bitcast.base_ref, s32[1,2048]{1,0:T(1,128)} %bitcast.27, bf16[128,2048]{1,0:T(8,128)(2,1)} %q_ref.1, bf16[2048,512]{1,0:T(8,128)(2,1)} %get-tuple-element.19.k_ref, bf16[2048,512]{1,0:T(8,128)(2,1)} %get-tuple-element.20.v_ref, f32[1,2048]{1,0:T(1,128)} %bitcast.26, ...), custom_call_target="tpu_custom_call" | custom-call | flops 6442450944 | bytes 22028288 | tf_op jit(solution)/shard_map/pallas_call | solution.py:86
  81.2 8.3 %fusion.8 = f32[128,4096]{1,0:T(8,128)S(1)} fusion(bf16[128,2048]{1,0:T(8,128)(2,1)} %get-tuple-element.17, bf16[2048,4096]{1,0:T(8,128)(2,1)} %w_ref.1), kind=kOutput, calls=%fused_computation.48 | convolution fusion | flops 2147483648 | bytes 19398656 | tf_op jit(solution)/shard_map/dot_general | solution.py:226
  89.5 0.1 dynamic-slice_convert_fusion
  89.6 1.6 %collective-permute-start.9 = (bf16[128,2048]{1,0:T(8,128)(2,1)S(1)}, bf16[128,2048]{1,0:T(8,128)(2,1)S(1)}, u32[]{:S(2)}, u32[]{:S(2)}) collective-permute-start(bf16[128,2048]{1,0:T(8,128)(2,1)S(1)} %dynamic-slice_convert_fusion), channel_id=1, source_target_pairs={{0,2},{2,0},{1,3},{3,1},{4,6},{6,4},{5,7},{7,5},{8,10},{10,8},{9,1... | collective-permute-start | bytes 1572872 | tf_op jit(solution)/shard_map/ppermute | solution.py:231
  91.2 0.5 broadcast.152
  91.7 0.7 reduce.13
  92.4 0.6 gather_fusion
  92.9 0.6 gather_fusion.1
  93.5 0.6 convolution_bitcast_fusion
  94.1 0.1 collective-permute-start.10
  94.2 1.2 collective-permute-done.10
  95.4 8.5 %collective-permute-start.11 = (f32[2080]{0:T(1024)S(1)}, f32[2080]{0:T(1024)S(1)}, u32[]{:S(2)}, u32[]{:S(2)}) collective-permute-start(f32[2080]{0:T(1024)S(1)} %fusion.7), channel_id=1, source_target_pairs={{0,4},{4,0},{8,12},{12,8},{1,5},{5,1},{9,13},{13,9},{2,6},{6,2},{1... | collective-permute-start | bytes 24968 | tf_op jit(solution)/shard_map/ppermute | solution.py:177
  103.9 1.7 %collective-permute-done.11 = f32[2080]{0:T(1024)S(1)} collective-permute-done((f32[2080]{0:T(1024)S(1)}, f32[2080]{0:T(1024)S(1)}, u32[]{:S(2)}, u32[]{:S(2)}) %collective-permute-start.11) | collective-permute-done | bytes 8352 | tf_op jit(solution)/shard_map/ppermute | solution.py:177
  105.5 11.4 %collective-permute-start.12 = (f32[2080]{0:T(1024)S(1)}, f32[2080]{0:T(1024)S(1)}, u32[]{:S(2)}, u32[]{:S(2)}) collective-permute-start(f32[2080]{0:T(1024)S(1)} %add.97), channel_id=1, source_target_pairs={{0,8},{4,12},{8,0},{12,4},{1,9},{5,13},{9,1},{13,5},{2,10},{6,14},... | collective-permute-start | bytes 24968 | tf_op jit(solution)/shard_map/ppermute | solution.py:177
  116.9 1.7 %collective-permute-done.12 = f32[2080]{0:T(1024)S(1)} collective-permute-done((f32[2080]{0:T(1024)S(1)}, f32[2080]{0:T(1024)S(1)}, u32[]{:S(2)}, u32[]{:S(2)}) %collective-permute-start.12) | collective-permute-done | bytes 8352 | tf_op jit(solution)/shard_map/ppermute | solution.py:177
  118.6 0.5 collective-permute-start.13
  119.1 3.2 %collective-permute-done.13 = f32[2080]{0:T(1024)S(1)} collective-permute-done((f32[2080]{0:T(1024)S(1)}, f32[2080]{0:T(1024)S(1)}, u32[]{:S(2)}, u32[]{:S(2)}) %collective-permute-start.13) | collective-permute-done | bytes 8352 | tf_op jit(solution)/shard_map/ppermute | solution.py:177
  122.3 0.5 slice.101
  122.8 0.7 dynamic_slice.11
  123.5 0.0 collective-permute-done.9
  123.5 0.9 add_convert_fusion
  (38 shorter events, 0.3 us)
Async XLA Ops:
  0.6 16.0 %copy-start.6 = (s32[128]{0:T(128)S(1)}, s32[128]{0:T(128)}, u32[]{:S(2)}) copy-start(s32[128]{0:T(128)} %param.15) | copy-start | bytes 1540
  0.6 16.0 %copy-start.3 = (bf16[128,4096]{1,0:T(8,128)(2,1)S(1)}, bf16[128,4096]{1,0:T(8,128)(2,1)}, u32[]{:S(2)}) copy-start(bf16[128,4096]{1,0:T(8,128)(2,1)} %param.14) | copy-start | bytes 3145732
  3.4 19.0 %collective-permute-start.3 = (bf16[528,512]{1,0:T(8,128)(2,1)}, bf16[528,512]{1,0:T(8,128)(2,1)S(1)}, u32[]{:S(2)}, u32[]{:S(2)}) collective-permute-start(bf16[528,512]{1,0:T(8,128)(2,1)} %pad_maximum_fusion.2), channel_id=1, source_target_pairs={{0,8},{4,12},{1,9},{5,13},{2,10},{6,14},{3,11},{7,15},{16,24},{20,... | collective-permute-start | bytes 1622024 | tf_op jit(solution)/shard_map/ppermute | solution.py:126
  9.4 18.4 %collective-permute-start.4 = (bf16[528,512]{1,0:T(8,128)(2,1)}, bf16[528,512]{1,0:T(8,128)(2,1)}, u32[]{:S(2)}, u32[]{:S(2)}) collective-permute-start(bf16[528,512]{1,0:T(8,128)(2,1)} %pad_maximum_fusion.2), channel_id=1, source_target_pairs={{8,0},{9,1},{10,2},{11,3},{24,16},{25,17},{26,18},{27,19}} | collective-permute-start | bytes 1622024 | tf_op jit(solution)/shard_map/ppermute | solution.py:132
  10.7 27.1 %collective-permute-start.7 = (bf16[528,512]{1,0:T(8,128)(2,1)}, bf16[528,512]{1,0:T(8,128)(2,1)}, u32[]{:S(2)}, u32[]{:S(2)}) collective-permute-start(bf16[528,512]{1,0:T(8,128)(2,1)} %pad_maximum_fusion.2), channel_id=1, source_target_pairs={{4,0},{8,4},{12,8},{5,1},{9,5},{13,9},{6,2},{10,6},{14,10},{7,3},{... | collective-permute-start | bytes 1622024 | tf_op jit(solution)/shard_map/ppermute | solution.py:132
  12.0 20.8 %collective-permute-start.1 = (bf16[528,512]{1,0:T(8,128)(2,1)}, bf16[528,512]{1,0:T(8,128)(2,1)S(1)}, u32[]{:S(2)}, u32[]{:S(2)}) collective-permute-start(bf16[528,512]{1,0:T(8,128)(2,1)} %pad_maximum_fusion.2), channel_id=1, source_target_pairs={{0,4},{4,8},{8,12},{1,5},{5,9},{9,13},{2,6},{6,10},{10,14},{3,7},{... | collective-permute-start | bytes 1622024 | tf_op jit(solution)/shard_map/ppermute | solution.py:126
  16.6 13.1 %collective-permute-start = (bf16[528,512]{1,0:T(8,128)(2,1)}, bf16[528,512]{1,0:T(8,128)(2,1)S(1)}, u32[]{:S(2)}, u32[]{:S(2)}) collective-permute-start(bf16[528,512]{1,0:T(8,128)(2,1)} %pad_maximum_fusion.2), channel_id=1, source_target_pairs={{0,1},{1,0},{2,3},{3,2},{4,5},{5,4},{6,7},{7,6},{8,9},{9,8},{10,11... | collective-permute-start | bytes 1622024 | tf_op jit(solution)/shard_map/ppermute | solution.py:153
  28.9 10.2 %collective-permute-start.5 = (bf16[528,512]{1,0:T(8,128)(2,1)S(1)}, bf16[528,512]{1,0:T(8,128)(2,1)S(1)}, u32[]{:S(2)}, u32[]{:S(2)}) collective-permute-start(bf16[528,512]{1,0:T(8,128)(2,1)S(1)} %broadcast_select_fusion.2), channel_id=1, source_target_pairs={{0,1},{1,0},{2,3},{3,2},{4,5},{5,4},{6,7},{7,6},{8,9},{9,8},{10,11... | collective-permute-start | bytes 1622024 | tf_op jit(solution)/shard_map/ppermute | solution.py:153
  28.9 8.9 %collective-permute-start.6 = (bf16[528,512]{1,0:T(8,128)(2,1)S(1)}, bf16[528,512]{1,0:T(8,128)(2,1)S(1)}, u32[]{:S(2)}, u32[]{:S(2)}) collective-permute-start(bf16[528,512]{1,0:T(8,128)(2,1)S(1)} %collective-permute-done.3), channel_id=1, source_target_pairs={{8,12},{9,13},{10,14},{11,15},{24,28},{25,29},{26,30},{27,31}} | collective-permute-start | bytes 1622024 | tf_op jit(solution)/shard_map/ppermute | solution.py:124
  29.8 9.1 %copy-start.1 = (bf16[528,512]{1,0:T(8,128)(2,1)}, bf16[528,512]{1,0:T(8,128)(2,1)S(1)}, u32[]{:S(2)}) copy-start(bf16[528,512]{1,0:T(8,128)(2,1)S(1)} %broadcast_select_fusion.7) | copy-start | bytes 1622020
  32.9 6.3 %collective-permute-start.2 = (bf16[528,512]{1,0:T(8,128)(2,1)S(1)}, bf16[528,512]{1,0:T(8,128)(2,1)S(1)}, u32[]{:S(2)}, u32[]{:S(2)}) collective-permute-start(bf16[528,512]{1,0:T(8,128)(2,1)S(1)} %broadcast_select_fusion.3), channel_id=1, source_target_pairs={{0,1},{1,0},{2,3},{3,2},{4,5},{5,4},{6,7},{7,6},{8,9},{9,8},{10,11... | collective-permute-start | bytes 1622024 | tf_op jit(solution)/shard_map/ppermute | solution.py:153
  39.0 2.0 %collective-permute-start.8 = (bf16[528,512]{1,0:T(8,128)(2,1)S(1)}, bf16[528,512]{1,0:T(8,128)(2,1)S(1)}, u32[]{:S(2)}, u32[]{:S(2)}) collective-permute-start(bf16[528,512]{1,0:T(8,128)(2,1)S(1)} %broadcast_select_fusion.1), channel_id=1, source_target_pairs={{0,1},{1,0},{2,3},{3,2},{4,5},{5,4},{6,7},{7,6},{8,9},{9,8},{10,11... | collective-permute-start | bytes 1622024 | tf_op jit(solution)/shard_map/ppermute | solution.py:153
  39.1 0.8 copy-start
  39.2 0.9 copy-start.2
  40.0 1.1 copy-start.5
  40.1 1.8 %slice-start = ((bf16[528,512]{1,0:T(8,128)(2,1)}), bf16[512,512]{1,0:T(8,128)(2,1)S(1)}, s32[]{:S(2)}) async-start(bf16[528,512]{1,0:T(8,128)(2,1)} %copy-done), calls=%async_computation | async-start | bytes 1048576 | tf_op jit(solution)/shard_map/slice | solution.py:159
  40.1 1.8 %slice-start.1 = ((bf16[528,512]{1,0:T(8,128)(2,1)}), bf16[512,512]{1,0:T(8,128)(2,1)S(1)}, s32[]{:S(2)}) async-start(bf16[528,512]{1,0:T(8,128)(2,1)} %copy-done.1), calls=%async_computation.1 | async-start | bytes 1048576 | tf_op jit(solution)/shard_map/slice | solution.py:159
  41.0 1.1 slice-start.2
  81.2 10.5 %copy-start.4 = (f32[1,2048]{1,0:T(1,128)S(1)}, f32[1,2048]{1,0:T(1,128)}, u32[]{:S(2)}) copy-start(f32[1,2048]{1,0:T(1,128)} %get-tuple-element.18) | copy-start | bytes 24580
  89.6 33.9 %collective-permute-start.9 = (bf16[128,2048]{1,0:T(8,128)(2,1)S(1)}, bf16[128,2048]{1,0:T(8,128)(2,1)S(1)}, u32[]{:S(2)}, u32[]{:S(2)}) collective-permute-start(bf16[128,2048]{1,0:T(8,128)(2,1)S(1)} %dynamic-slice_convert_fusion), channel_id=1, source_target_pairs={{0,2},{2,0},{1,3},{3,1},{4,6},{6,4},{5,7},{7,5},{8,10},{10,8},{9,1... | collective-permute-start | bytes 1572872 | tf_op jit(solution)/shard_map/ppermute | solution.py:231
  94.1 1.2 collective-permute-start.10
  95.4 10.2 %collective-permute-start.11 = (f32[2080]{0:T(1024)S(1)}, f32[2080]{0:T(1024)S(1)}, u32[]{:S(2)}, u32[]{:S(2)}) collective-permute-start(f32[2080]{0:T(1024)S(1)} %fusion.7), channel_id=1, source_target_pairs={{0,4},{4,0},{8,12},{12,8},{1,5},{5,1},{9,13},{13,9},{2,6},{6,2},{1... | collective-permute-start | bytes 24968 | tf_op jit(solution)/shard_map/ppermute | solution.py:177
  105.5 13.0 %collective-permute-start.12 = (f32[2080]{0:T(1024)S(1)}, f32[2080]{0:T(1024)S(1)}, u32[]{:S(2)}, u32[]{:S(2)}) collective-permute-start(f32[2080]{0:T(1024)S(1)} %add.97), channel_id=1, source_target_pairs={{0,8},{4,12},{8,0},{12,4},{1,9},{5,13},{9,1},{13,5},{2,10},{6,14},... | collective-permute-start | bytes 24968 | tf_op jit(solution)/shard_map/ppermute | solution.py:177
  118.6 3.7 %collective-permute-start.13 = (f32[2080]{0:T(1024)S(1)}, f32[2080]{0:T(1024)S(1)}, u32[]{:S(2)}, u32[]{:S(2)}) collective-permute-start(f32[2080]{0:T(1024)S(1)} %add.98), channel_id=1, source_target_pairs={{0,2},{2,0},{1,3},{3,1},{4,6},{6,4},{5,7},{7,5},{8,10},{10,8},{9,1... | collective-permute-start | bytes 24968 | tf_op jit(solution)/shard_map/ppermute | solution.py:177

commit v7 on v5

--- a/solution.py
+++ b/solution.py
@@ -28,11 +28,12 @@
     s = lax.dot_general(q, k, NT_DIMS, preferred_element_type=jnp.float32) * (HD ** -0.5)
     row_pos = base_ref[0] + r * tq + lax.broadcasted_iota(jnp.int32, (tq, keys), 0)
     vis = kpos_ref[...] <= row_pos
-    kvis = jnp.logical_and(vis, kept_ref[...] > 0.0)
-    m_c = jnp.max(jnp.where(vis, s, NEG_FILL), axis=1, keepdims=True)
-    m_m = jnp.max(jnp.where(kvis, s, NEG_FILL), axis=1, keepdims=True)
-    e_c = jnp.where(vis, jnp.exp(s - m_c), 0.0)
-    e_m = jnp.where(kvis, jnp.exp(s - m_m), 0.0)
+    s_c = jnp.where(vis, s, NEG_FILL)
+    s_m = jnp.where(kept_ref[...] > 0.0, s_c, NEG_FILL)
+    m_c = jnp.max(s_c, axis=1, keepdims=True)
+    m_m = jnp.max(s_m, axis=1, keepdims=True)
+    e_c = jnp.exp(s_c - m_c)
+    e_m = jnp.exp(s_m - m_m)
     l_c = jnp.sum(e_c, axis=1, keepdims=True)
     l_m = jnp.sum(e_m, axis=1, keepdims=True)
     o_c = jnp.dot(e_c.astype(jnp.bfloat16), v, preferred_element_type=jnp.float32) / l_c
@@ -153,17 +154,26 @@
     return key_all, value_all, seg_all, key_pos.reshape(1, -1), source
 
 
-def butterfly_sum(total, axes):
-    for axis in axes:
-        n = lax.axis_size(axis)
-        if n & (n - 1):
-            total = lax.psum(total, axis)
-            continue
-        bit = 1
-        while bit < n:
-            total = total + lax.ppermute(total, axis, [(i, i ^ bit) for i in range(n)])
-            bit *= 2
-    return total
+def ordered_sum(total, axes):
+    sizes = [lax.axis_size(a) for a in axes]
+    count = 1
+    for size in sizes:
+        count *= size
+    if count > 16:
+        return lax.psum(total, axes)
+    at = 0
+    for axis, size in zip(axes, sizes):
+        at = at * size + lax.axis_index(axis)
+    got = [total] + [
+        lax.ppermute(total, axes, [(i, (i + d) % count) for i in range(count)])
+        for d in range(1, count)
+    ]
+    stacked = jnp.stack(got)
+    result = None
+    for a in range(count):
+        piece = lax.dynamic_index_in_dim(stacked, (at - a) % count, 0, keepdims=False)
+        result = piece if result is None else result + piece
+    return result
 
 
 def local(query, key, value, out_weight, cotangent, response, segment_ids, masked_segments):
@@ -209,7 +219,7 @@
         seg_abs[:, None] == jnp.arange(SEG_DEV * ctx_count, dtype=jnp.int32)[None, :]
     ).astype(jnp.float32)
     seg_part = jnp.dot(attr_abs, onehot, precision=lax.Precision.HIGHEST)
-    summed = butterfly_sum(jnp.concatenate([attr_abs, seg_part]), ("rep", "ctx", "head"))
+    summed = ordered_sum(jnp.concatenate([attr_abs, seg_part]), ("ctx", "head", "rep"))
     attr_all = summed[:context_len]
     segment_attr = summed[context_len:]
 

time: 117 us -> 134 us (1.15)
  starting transfers between devices: 36.6 us -> 53.9 us
  Pallas kernels: 29.7 us -> 24 us
  other arithmetic: 10.2 us -> 12.8 us
  waiting for transfers between devices: 13.9 us -> 15.8 us
    ppermute x4 -> x15, starting transfers between devices: 20.5 us -> 37.7 us  [ordered_sum(): lax.ppermute(total, axes, [(i, (i + d) % count) for i in range(count)])]
    ppermute x1, waiting for transfers between devices: 0.01 us -> 7.76 us  [local(): got = lax.ppermute(send.astype(jnp.bfloat16), 'head', [(0, 1), (1, 0)])]
    pallas_call x1, Pallas kernels: 29.7 us -> 24 us  [fused_attention(): pl.pallas_call(functools.partial(attention_kernel, tq=tq), grid_spec=pltp...]
    ppermute x2, waiting for transfers between devices: 4.72 us -> 0.01 us  [relay_gather(): backward.append(lax.ppermute(payload, 'ctx', bwd) if bwd else zero)]
    ppermute x4 -> x15, waiting for transfers between devices: 7.67 us -> 4.22 us  [ordered_sum(): lax.ppermute(total, axes, [(i, (i + d) % count) for i in range(count)])]
    ppermute x2, waiting for transfers between devices: 0.64 us -> 3.79 us  [relay_gather(): forward.append(lax.ppermute(payload, 'ctx', fwd) if fwd else zero)]
    select_n x4, other arithmetic: 0.3 us -> 2.03 us  [gather_kv(): value_parts = [jnp.where(first, b, a) for a, b in zip(mine, theirs)]]
  transfers between devices with their start and end apart: 14 -> 25, of which waited for: 7 -> 6; matrix products, arithmetic and copies ran while one was open for 17% -> 20% of each run, Pallas kernels for 0% -> 0%
where the time goes in v7:
time: 134 us
  starting transfers between devices  53.9 us (40%)
  Pallas kernels  24 us (18%)
  matrix products  21.1 us (16%)
  waiting for transfers between devices  15.8 us (12%)
  other arithmetic  12.8 us (10%)
  local copies, waits for them, and re-layouts  4.77 us (4%)
    ppermute x15, starting transfers between devices, ordered_sum(): lax.ppermute(total, axes, [(i, (i + d) % count) for i in range(count)])  37.7 us
    pallas_call x1, Pallas kernels, fused_attention(): pl.pallas_call(functools.partial(attention_kernel, tq=tq), grid_spec=pltp...  24 us
    dot_general x1, matrix products, local(): jnp.dot(grad_masked, out_weight.T, preferred_element_type=jnp.float32)  12.3 us
    ppermute x2, starting transfers between devices, relay_gather(): forward.append(lax.ppermute(payload, 'ctx', fwd) if fwd else zero)  9.66 us
    dot_general x1, matrix products, local(): projected = jnp.dot(delta, out_weight, preferred_element_type=jnp.float32)  8.29 us
    ppermute x1, waiting for transfers between devices, local(): got = lax.ppermute(send.astype(jnp.bfloat16), 'head', [(0, 1), (1, 0)])  7.76 us
    ppermute x15, waiting for transfers between devices, ordered_sum(): lax.ppermute(total, axes, [(i, (i + d) % count) for i in range(count)])  4.22 us
    ppermute x2, waiting for transfers between devices, relay_gather(): forward.append(lax.ppermute(payload, 'ctx', fwd) if fwd else zero)  3.79 us
  transfers between devices with their start and end apart: 25, of which 6 were waited for; matrix products, arithmetic and copies ran while one was open for 20% of the time, Pallas kernels for 0%

profile of v7, /device:TPU:0, one launch (start us, length us, event | category | flops | bytes accessed | tf_op | source)
XLA Modules:
  0.0 133.7 jit_solution(5925993947855543848)
XLA Ops:
  0.7 0.8 convert_element_type.29
  1.5 1.1 broadcast_select_fusion.7
  2.6 0.8 pad_maximum_fusion.2
  3.4 1.3 collective-permute-start.4
  4.7 6.8 %collective-permute-start.3 = (bf16[528,512]{1,0:T(8,128)(2,1)}, bf16[528,512]{1,0:T(8,128)(2,1)}, u32[]{:S(2)}, u32[]{:S(2)}) collective-permute-start(bf16[528,512]{1,0:T(8,128)(2,1)} %pad_maximum_fusion.2), channel_id=1, source_target_pairs={{0,8},{4,12},{1,9},{5,13},{2,10},{6,14},{3,11},{7,15},{16,24},{20,... | collective-permute-start | bytes 1622024 | tf_op jit(solution)/shard_map/ppermute | solution.py:114
  11.5 2.9 %collective-permute-start.1 = (bf16[528,512]{1,0:T(8,128)(2,1)}, bf16[528,512]{1,0:T(8,128)(2,1)S(1)}, u32[]{:S(2)}, u32[]{:S(2)}) collective-permute-start(bf16[528,512]{1,0:T(8,128)(2,1)} %pad_maximum_fusion.2), channel_id=1, source_target_pairs={{0,4},{4,8},{8,12},{1,5},{5,9},{9,13},{2,6},{6,10},{10,14},{3,7},{... | collective-permute-start | bytes 1622024 | tf_op jit(solution)/shard_map/ppermute | solution.py:114
  14.4 1.3 collective-permute-start.7
  15.7 0.1 collective-permute-start
  15.8 12.3 %convolution_convert_fusion.do_ref = bf16[128,2048]{1,0:T(8,128)(2,1)} fusion(bf16[2048,4096]{1,0:T(8,128)(2,1)} %param.13, bf16[128,4096]{1,0:T(8,128)(2,1)S(1)} %copy-done.3, pred[128]{0:T(512)(128)(4,1)S(1)} %broadcast_compare_fusion), kind=kOutput, calls=%fused_computation.2 | convolution fusion | flops 2148270080 | bytes 18350208 | tf_op jit(solution)/shard_map/dot_general | solution.py:208
  28.1 0.1 add_bitcast_fusion
  28.3 0.6 copy.11
  28.9 0.0 collective-permute-done.4
  28.9 0.0 collective-permute-done.3
  28.9 0.1 broadcast_select_fusion.1
  29.0 0.5 collective-permute-start.5
  29.5 0.7 collective-permute-start.6
  30.2 0.1 broadcast_select_fusion.6
  30.4 3.8 %collective-permute-done.1 = bf16[528,512]{1,0:T(8,128)(2,1)S(1)} collective-permute-done((bf16[528,512]{1,0:T(8,128)(2,1)}, bf16[528,512]{1,0:T(8,128)(2,1)S(1)}, u32[]{:S(2)}, u32[]{:S(2)}) %collective-permute-start.1) | collective-permute-done | bytes 540704 | tf_op jit(solution)/shard_map/ppermute | solution.py:114
  34.2 0.1 collective-permute-start.2
  34.3 0.1 fusion.3
  34.5 1.1 broadcast_select_fusion
  35.6 0.6 collective-permute-start.8
  36.1 0.0 collective-permute-done.5
  36.1 0.1 broadcast_select_fusion.4
  36.2 0.1 broadcast_select_fusion.5
  36.3 1.0 slice_select_fusion.1
  37.3 0.9 slice_select_fusion.2
  38.2 0.1 broadcast_select_fusion.3
  38.3 0.8 slice.88
  39.2 0.1 compare_reduce_fusion
  39.3 0.6 gather_fusion.1
  39.8 0.6 broadcast_select_fusion.8
  40.4 0.1 slice_select_fusion
  40.5 3.3 %pad_maximum_fusion = (bf16[2048,512]{1,0:T(8,128)(2,1)}, bf16[2048,512]{1,0:T(8,128)(2,1)}) fusion(bf16[512,512]{1,0:T(8,128)(2,1)} %slice.88, bf16[512,512]{1,0:T(8,128)(2,1)S(1)} %slice-done, bf16[512,512]{1,0:T(8,128)(2,1)S(1)} %slice-done.2, bf16[512,512]{1,0:T(8,128)(2,1)S(1)} %slice-done.1, bf16[512,512]{1,0:T(8,128)(2,1)S(1)} %slice_select_fusion, ...), kind=kLoop, calls=%fused_computation.3 | loop fusion | flops 16777216 | bytes 8388608 | tf_op jit(solution)/shard_map/concatenate | solution.py:147
  43.8 24.0 %shard_map.103 = (bf16[128,2048]{1,0:T(8,128)(2,1)}, f32[1,2048]{1,0:T(1,128)}) custom-call(s32[1]{0:T(128)} %bitcast.base_ref, s32[1,2048]{1,0:T(1,128)} %bitcast.30, bf16[128,2048]{1,0:T(8,128)(2,1)} %q_ref.1, bf16[2048,512]{1,0:T(8,128)(2,1)} %get-tuple-element.19.k_ref, bf16[2048,512]{1,0:T(8,128)(2,1)} %get-tuple-element.20.v_ref, f32[1,2048]{1,0:T(1,128)} %bitcast.29, ...), custom_call_target="tpu_custom_call" | custom-call | flops 4294967296 | bytes 5775360 | tf_op jit(solution)/shard_map/pallas_call | solution.py:75
  67.8 0.5 broadcast.168
  68.3 1.4 %reduce.13 = f32[2048]{0:T(1024)S(1)} reduce(f32[1,2048]{1,0:T(1,128)} %get-tuple-element.18, f32[]{:T(128)} %broadcast.168), dimensions={0}, to_apply=%get-tuple-element.18.reduce_sub_computation.3 | reduce | bytes 16388 | tf_op jit(solution)/shard_map/pallas_call | solution.py:75
  69.7 0.6 gather_fusion
  70.3 0.6 convolution_bitcast_fusion
  70.9 22.1 %collective-permute-start.24 = (f32[2080]{0:T(1024)S(1)}, f32[2080]{0:T(1024)S(1)}, u32[]{:S(2)}, u32[]{:S(2)}) collective-permute-start(f32[2080]{0:T(1024)S(1)} %pad_maximum_fusion.3), channel_id=1, source_target_pairs={{0,15},{1,0},{2,1},{3,2},{4,3},{5,4},{6,5},{7,6},{8,7},{9,8},{10,9... | collective-permute-start | bytes 24968 | tf_op jit(solution)/shard_map/ppermute | solution.py:168
  93.0 0.0 collective-permute-start.23
  93.0 0.5 collective-permute-start.22
  93.5 0.2 collective-permute-start.21
  93.7 0.7 collective-permute-done.24
  94.4 4.6 %collective-permute-start.19 = (f32[2080]{0:T(1024)S(1)}, f32[2080]{0:T(1024)S(1)}, u32[]{:S(2)}, u32[]{:S(2)}) collective-permute-start(f32[2080]{0:T(1024)S(1)} %pad_maximum_fusion.3), channel_id=1, source_target_pairs={{0,10},{1,11},{2,12},{3,13},{4,14},{5,15},{6,0},{7,1},{8,2},{9,3},... | collective-permute-start | bytes 24968 | tf_op jit(solution)/shard_map/ppermute | solution.py:168
  99.0 1.3 %collective-permute-start.17 = (f32[2080]{0:T(1024)S(1)}, f32[2080]{0:T(1024)S(1)}, u32[]{:S(2)}, u32[]{:S(2)}) collective-permute-start(f32[2080]{0:T(1024)S(1)} %pad_maximum_fusion.3), channel_id=1, source_target_pairs={{0,8},{1,9},{2,10},{3,11},{4,12},{5,13},{6,14},{7,15},{8,0},{9,1},... | collective-permute-start | bytes 24968 | tf_op jit(solution)/shard_map/ppermute | solution.py:168
  100.3 1.4 %collective-permute-start.16 = (f32[2080]{0:T(1024)S(1)}, f32[2080]{0:T(1024)S(1)}, u32[]{:S(2)}, u32[]{:S(2)}) collective-permute-start(f32[2080]{0:T(1024)S(1)} %pad_maximum_fusion.3), channel_id=1, source_target_pairs={{0,7},{1,8},{2,9},{3,10},{4,11},{5,12},{6,13},{7,14},{8,15},{9,0},... | collective-permute-start | bytes 24968 | tf_op jit(solution)/shard_map/ppermute | solution.py:168
  101.7 2.1 %collective-permute-start.15 = (f32[2080]{0:T(1024)S(1)}, f32[2080]{0:T(1024)S(1)}, u32[]{:S(2)}, u32[]{:S(2)}) collective-permute-start(f32[2080]{0:T(1024)S(1)} %pad_maximum_fusion.3), channel_id=1, source_target_pairs={{0,6},{1,7},{2,8},{3,9},{4,10},{5,11},{6,12},{7,13},{8,14},{9,15},... | collective-permute-start | bytes 24968 | tf_op jit(solution)/shard_map/ppermute | solution.py:168
  103.7 8.3 %fusion.11 = f32[128,4096]{1,0:T(8,128)S(1)} fusion(bf16[128,2048]{1,0:T(8,128)(2,1)} %get-tuple-element.17, bf16[2048,4096]{1,0:T(8,128)(2,1)} %param.13), kind=kOutput, calls=%fused_computation.54 | convolution fusion | flops 2147483648 | bytes 19398656 | tf_op jit(solution)/shard_map/dot_general | solution.py:226
  112.0 0.2 collective-permute-start.14
  112.3 2.1 %collective-permute-start.13 = (f32[2080]{0:T(1024)S(1)}, f32[2080]{0:T(1024)S(1)}, u32[]{:S(2)}, u32[]{:S(2)}) collective-permute-start(f32[2080]{0:T(1024)S(1)} %pad_maximum_fusion.3), channel_id=1, source_target_pairs={{0,4},{1,5},{2,6},{3,7},{4,8},{5,9},{6,10},{7,11},{8,12},{9,13},{1... | collective-permute-start | bytes 24968 | tf_op jit(solution)/shard_map/ppermute | solution.py:168
  114.4 2.1 %collective-permute-start.12 = (f32[2080]{0:T(1024)S(1)}, f32[2080]{0:T(1024)S(1)}, u32[]{:S(2)}, u32[]{:S(2)}) collective-permute-start(f32[2080]{0:T(1024)S(1)} %pad_maximum_fusion.3), channel_id=1, source_target_pairs={{0,3},{1,4},{2,5},{3,6},{4,7},{5,8},{6,9},{7,10},{8,11},{9,12},{10... | collective-permute-start | bytes 24968 | tf_op jit(solution)/shard_map/ppermute | solution.py:168
  116.5 1.1 collective-permute-start.11
  117.6 0.1 dynamic-slice_convert_fusion
  117.9 2.0 %collective-permute-start.9 = (bf16[128,2048]{1,0:T(8,128)(2,1)S(1)}, bf16[128,2048]{1,0:T(8,128)(2,1)S(1)}, u32[]{:S(2)}, u32[]{:S(2)}) collective-permute-start(bf16[128,2048]{1,0:T(8,128)(2,1)S(1)} %dynamic-slice_convert_fusion), channel_id=1, source_target_pairs={{0,2},{2,0},{1,3},{3,1},{4,6},{6,4},{5,7},{7,5},{8,10},{10,8},{9,1... | collective-permute-start | bytes 1572872 | tf_op jit(solution)/shard_map/ppermute | solution.py:231
  119.9 0.6 collective-permute-done.12
  120.5 2.5 %collective-permute-done.11 = f32[2080]{0:T(1024)S(1)} collective-permute-done((f32[2080]{0:T(1024)S(1)}, f32[2080]{0:T(1024)S(1)}, u32[]{:S(2)}, u32[]{:S(2)}) %collective-permute-start.11) | collective-permute-done | bytes 8352 | tf_op jit(solution)/shard_map/ppermute | solution.py:168
  123.0 0.5 collective-permute-done.10
  123.5 0.2 stack.67
  123.7 0.1 add_add_fusion
  123.9 0.6 constant_dynamic-slice_fusion
  124.4 0.5 slice_bitcast_fusion
  125.0 7.8 %collective-permute-done.9 = bf16[128,2048]{1,0:T(8,128)(2,1)S(1)} collective-permute-done((bf16[128,2048]{1,0:T(8,128)(2,1)S(1)}, bf16[128,2048]{1,0:T(8,128)(2,1)S(1)}, u32[]{:S(2)}, u32[]{:S(2)}) %collective-permute-start.9) | collective-permute-done | bytes 524320 | tf_op jit(solution)/shard_map/ppermute | solution.py:231
  132.7 0.9 add_convert_fusion
  (72 shorter events, 0.5 us)
Async XLA Ops:
  0.6 15.1 %copy-start.5 = (s32[128]{0:T(128)S(1)}, s32[128]{0:T(128)}, u32[]{:S(2)}) copy-start(s32[128]{0:T(128)} %param.15) | copy-start | bytes 1540
  0.6 15.1 %copy-start.3 = (bf16[128,4096]{1,0:T(8,128)(2,1)S(1)}, bf16[128,4096]{1,0:T(8,128)(2,1)}, u32[]{:S(2)}) copy-start(bf16[128,4096]{1,0:T(8,128)(2,1)} %param.14) | copy-start | bytes 3145732
  3.4 25.5 %collective-permute-start.4 = (bf16[528,512]{1,0:T(8,128)(2,1)}, bf16[528,512]{1,0:T(8,128)(2,1)S(1)}, u32[]{:S(2)}, u32[]{:S(2)}) collective-permute-start(bf16[528,512]{1,0:T(8,128)(2,1)} %pad_maximum_fusion.2), channel_id=1, source_target_pairs={{8,0},{9,1},{10,2},{11,3},{24,16},{25,17},{26,18},{27,19}} | collective-permute-start | bytes 1622024 | tf_op jit(solution)/shard_map/ppermute | solution.py:120
  4.7 24.2 %collective-permute-start.3 = (bf16[528,512]{1,0:T(8,128)(2,1)}, bf16[528,512]{1,0:T(8,128)(2,1)}, u32[]{:S(2)}, u32[]{:S(2)}) collective-permute-start(bf16[528,512]{1,0:T(8,128)(2,1)} %pad_maximum_fusion.2), channel_id=1, source_target_pairs={{0,8},{4,12},{1,9},{5,13},{2,10},{6,14},{3,11},{7,15},{16,24},{20,... | collective-permute-start | bytes 1622024 | tf_op jit(solution)/shard_map/ppermute | solution.py:114
  11.5 22.7 %collective-permute-start.1 = (bf16[528,512]{1,0:T(8,128)(2,1)}, bf16[528,512]{1,0:T(8,128)(2,1)S(1)}, u32[]{:S(2)}, u32[]{:S(2)}) collective-permute-start(bf16[528,512]{1,0:T(8,128)(2,1)} %pad_maximum_fusion.2), channel_id=1, source_target_pairs={{0,4},{4,8},{8,12},{1,5},{5,9},{9,13},{2,6},{6,10},{10,14},{3,7},{... | collective-permute-start | bytes 1622024 | tf_op jit(solution)/shard_map/ppermute | solution.py:114
  14.4 20.1 %collective-permute-start.7 = (bf16[528,512]{1,0:T(8,128)(2,1)}, bf16[528,512]{1,0:T(8,128)(2,1)}, u32[]{:S(2)}, u32[]{:S(2)}) collective-permute-start(bf16[528,512]{1,0:T(8,128)(2,1)} %pad_maximum_fusion.2), channel_id=1, source_target_pairs={{4,0},{8,4},{12,8},{5,1},{9,5},{13,9},{6,2},{10,6},{14,10},{7,3},{... | collective-permute-start | bytes 1622024 | tf_op jit(solution)/shard_map/ppermute | solution.py:120
  15.7 14.5 %collective-permute-start = (bf16[528,512]{1,0:T(8,128)(2,1)}, bf16[528,512]{1,0:T(8,128)(2,1)S(1)}, u32[]{:S(2)}, u32[]{:S(2)}) collective-permute-start(bf16[528,512]{1,0:T(8,128)(2,1)} %pad_maximum_fusion.2), channel_id=1, source_target_pairs={{0,1},{1,0},{2,3},{3,2},{4,5},{5,4},{6,7},{7,6},{8,9},{9,8},{10,11... | collective-permute-start | bytes 1622024 | tf_op jit(solution)/shard_map/ppermute | solution.py:141
  29.0 7.2 %collective-permute-start.5 = (bf16[528,512]{1,0:T(8,128)(2,1)S(1)}, bf16[528,512]{1,0:T(8,128)(2,1)S(1)}, u32[]{:S(2)}, u32[]{:S(2)}) collective-permute-start(bf16[528,512]{1,0:T(8,128)(2,1)S(1)} %broadcast_select_fusion.1), channel_id=1, source_target_pairs={{0,1},{1,0},{2,3},{3,2},{4,5},{5,4},{6,7},{7,6},{8,9},{9,8},{10,11... | collective-permute-start | bytes 1622024 | tf_op jit(solution)/shard_map/ppermute | solution.py:141
  29.5 4.9 %collective-permute-start.6 = (bf16[528,512]{1,0:T(8,128)(2,1)}, bf16[528,512]{1,0:T(8,128)(2,1)S(1)}, u32[]{:S(2)}, u32[]{:S(2)}) collective-permute-start(bf16[528,512]{1,0:T(8,128)(2,1)} %collective-permute-done.3), channel_id=1, source_target_pairs={{8,12},{9,13},{10,14},{11,15},{24,28},{25,29},{26,30},{27,31}} | collective-permute-start | bytes 1622024 | tf_op jit(solution)/shard_map/ppermute | solution.py:112
  30.4 5.2 %copy-start.1 = (bf16[528,512]{1,0:T(8,128)(2,1)}, bf16[528,512]{1,0:T(8,128)(2,1)S(1)}, u32[]{:S(2)}) copy-start(bf16[528,512]{1,0:T(8,128)(2,1)S(1)} %broadcast_select_fusion.6) | copy-start | bytes 1622020
  34.2 2.0 %collective-permute-start.2 = (bf16[528,512]{1,0:T(8,128)(2,1)S(1)}, bf16[528,512]{1,0:T(8,128)(2,1)S(1)}, u32[]{:S(2)}, u32[]{:S(2)}) collective-permute-start(bf16[528,512]{1,0:T(8,128)(2,1)S(1)} %broadcast_select_fusion.2), channel_id=1, source_target_pairs={{0,1},{1,0},{2,3},{3,2},{4,5},{5,4},{6,7},{7,6},{8,9},{9,8},{10,11... | collective-permute-start | bytes 1622024 | tf_op jit(solution)/shard_map/ppermute | solution.py:141
  35.6 2.6 %collective-permute-start.8 = (bf16[528,512]{1,0:T(8,128)(2,1)S(1)}, bf16[528,512]{1,0:T(8,128)(2,1)S(1)}, u32[]{:S(2)}, u32[]{:S(2)}) collective-permute-start(bf16[528,512]{1,0:T(8,128)(2,1)S(1)} %broadcast_select_fusion), channel_id=1, source_target_pairs={{0,1},{1,0},{2,3},{3,2},{4,5},{5,4},{6,7},{7,6},{8,9},{9,8},{10,11... | collective-permute-start | bytes 1622024 | tf_op jit(solution)/shard_map/ppermute | solution.py:141
  36.2 1.1 copy-start
  36.3 1.9 %copy-start.2 = (bf16[528,512]{1,0:T(8,128)(2,1)}, bf16[528,512]{1,0:T(8,128)(2,1)S(1)}, u32[]{:S(2)}) copy-start(bf16[528,512]{1,0:T(8,128)(2,1)S(1)} %broadcast_select_fusion.5) | copy-start | bytes 1622020
  37.3 1.8 %copy-start.4 = (s32[4]{0:T(128)S(1)}, s32[4]{0:T(128)}, u32[]{:S(2)}) copy-start(s32[4]{0:T(128)} %param.17) | copy-start | bytes 52
  38.2 2.3 %slice-start = ((bf16[528,512]{1,0:T(8,128)(2,1)}), bf16[512,512]{1,0:T(8,128)(2,1)S(1)}, s32[]{:S(2)}) async-start(bf16[528,512]{1,0:T(8,128)(2,1)} %copy-done), calls=%async_computation | async-start | bytes 1048576 | tf_op jit(solution)/shard_map/slice | solution.py:147
  38.2 2.3 %slice-start.1 = ((bf16[528,512]{1,0:T(8,128)(2,1)}), bf16[512,512]{1,0:T(8,128)(2,1)S(1)}, s32[]{:S(2)}) async-start(bf16[528,512]{1,0:T(8,128)(2,1)} %copy-done.1), calls=%async_computation.1 | async-start | bytes 1048576 | tf_op jit(solution)/shard_map/slice | solution.py:147
  38.2 2.3 %slice-start.2 = ((bf16[528,512]{1,0:T(8,128)(2,1)}), bf16[512,512]{1,0:T(8,128)(2,1)S(1)}, s32[]{:S(2)}) async-start(bf16[528,512]{1,0:T(8,128)(2,1)} %copy-done.2), calls=%async_computation.2 | async-start | bytes 1048576 | tf_op jit(solution)/shard_map/slice | solution.py:147
  70.9 23.5 %collective-permute-start.24 = (f32[2080]{0:T(1024)S(1)}, f32[2080]{0:T(1024)S(1)}, u32[]{:S(2)}, u32[]{:S(2)}) collective-permute-start(f32[2080]{0:T(1024)S(1)} %pad_maximum_fusion.3), channel_id=1, source_target_pairs={{0,15},{1,0},{2,1},{3,2},{4,3},{5,4},{6,5},{7,6},{8,7},{9,8},{10,9... | collective-permute-start | bytes 24968 | tf_op jit(solution)/shard_map/ppermute | solution.py:168
  93.0 6.0 %collective-permute-start.23 = (f32[2080]{0:T(1024)S(1)}, f32[2080]{0:T(1024)S(1)}, u32[]{:S(2)}, u32[]{:S(2)}) collective-permute-start(f32[2080]{0:T(1024)S(1)} %pad_maximum_fusion.3), channel_id=1, source_target_pairs={{0,14},{1,15},{2,0},{3,1},{4,2},{5,3},{6,4},{7,5},{8,6},{9,7},{10,... | collective-permute-start | bytes 24968 | tf_op jit(solution)/shard_map/ppermute | solution.py:168
  93.0 6.0 %collective-permute-start.22 = (f32[2080]{0:T(1024)S(1)}, f32[2080]{0:T(1024)S(1)}, u32[]{:S(2)}, u32[]{:S(2)}) collective-permute-start(f32[2080]{0:T(1024)S(1)} %pad_maximum_fusion.3), channel_id=1, source_target_pairs={{0,13},{1,14},{2,15},{3,0},{4,1},{5,2},{6,3},{7,4},{8,5},{9,6},{10... | collective-permute-start | bytes 24968 | tf_op jit(solution)/shard_map/ppermute | solution.py:168
  93.5 6.8 %collective-permute-start.21 = (f32[2080]{0:T(1024)S(1)}, f32[2080]{0:T(1024)S(1)}, u32[]{:S(2)}, u32[]{:S(2)}) collective-permute-start(f32[2080]{0:T(1024)S(1)} %pad_maximum_fusion.3), channel_id=1, source_target_pairs={{0,12},{1,13},{2,14},{3,15},{4,0},{5,1},{6,2},{7,3},{8,4},{9,5},{1... | collective-permute-start | bytes 24968 | tf_op jit(solution)/shard_map/ppermute | solution.py:168
  93.7 8.0 %collective-permute-start.20 = (f32[2080]{0:T(1024)S(1)}, f32[2080]{0:T(1024)S(1)}, u32[]{:S(2)}, u32[]{:S(2)}) collective-permute-start(f32[2080]{0:T(1024)S(1)} %pad_maximum_fusion.3), channel_id=1, source_target_pairs={{0,11},{1,12},{2,13},{3,14},{4,15},{5,0},{6,1},{7,2},{8,3},{9,4},{... | collective-permute-start | bytes 24968 | tf_op jit(solution)/shard_map/ppermute | solution.py:168
  94.4 17.7 %collective-permute-start.19 = (f32[2080]{0:T(1024)S(1)}, f32[2080]{0:T(1024)S(1)}, u32[]{:S(2)}, u32[]{:S(2)}) collective-permute-start(f32[2080]{0:T(1024)S(1)} %pad_maximum_fusion.3), channel_id=1, source_target_pairs={{0,10},{1,11},{2,12},{3,13},{4,14},{5,15},{6,0},{7,1},{8,2},{9,3},... | collective-permute-start | bytes 24968 | tf_op jit(solution)/shard_map/ppermute | solution.py:168
  98.9 13.3 %collective-permute-start.18 = (f32[2080]{0:T(1024)S(1)}, f32[2080]{0:T(1024)S(1)}, u32[]{:S(2)}, u32[]{:S(2)}) collective-permute-start(f32[2080]{0:T(1024)S(1)} %pad_maximum_fusion.3), channel_id=1, source_target_pairs={{0,9},{1,10},{2,11},{3,12},{4,13},{5,14},{6,15},{7,0},{8,1},{9,2},... | collective-permute-start | bytes 24968 | tf_op jit(solution)/shard_map/ppermute | solution.py:168
  99.0 15.5 %collective-permute-start.17 = (f32[2080]{0:T(1024)S(1)}, f32[2080]{0:T(1024)S(1)}, u32[]{:S(2)}, u32[]{:S(2)}) collective-permute-start(f32[2080]{0:T(1024)S(1)} %pad_maximum_fusion.3), channel_id=1, source_target_pairs={{0,8},{1,9},{2,10},{3,11},{4,12},{5,13},{6,14},{7,15},{8,0},{9,1},... | collective-permute-start | bytes 24968 | tf_op jit(solution)/shard_map/ppermute | solution.py:168
  100.3 16.2 %collective-permute-start.16 = (f32[2080]{0:T(1024)S(1)}, f32[2080]{0:T(1024)S(1)}, u32[]{:S(2)}, u32[]{:S(2)}) collective-permute-start(f32[2080]{0:T(1024)S(1)} %pad_maximum_fusion.3), channel_id=1, source_target_pairs={{0,7},{1,8},{2,9},{3,10},{4,11},{5,12},{6,13},{7,14},{8,15},{9,0},... | collective-permute-start | bytes 24968 | tf_op jit(solution)/shard_map/ppermute | solution.py:168
  101.7 16.0 %collective-permute-start.15 = (f32[2080]{0:T(1024)S(1)}, f32[2080]{0:T(1024)S(1)}, u32[]{:S(2)}, u32[]{:S(2)}) collective-permute-start(f32[2080]{0:T(1024)S(1)} %pad_maximum_fusion.3), channel_id=1, source_target_pairs={{0,6},{1,7},{2,8},{3,9},{4,10},{5,11},{6,12},{7,13},{8,14},{9,15},... | collective-permute-start | bytes 24968 | tf_op jit(solution)/shard_map/ppermute | solution.py:168
  112.0 5.8 %collective-permute-start.14 = (f32[2080]{0:T(1024)S(1)}, f32[2080]{0:T(1024)S(1)}, u32[]{:S(2)}, u32[]{:S(2)}) collective-permute-start(f32[2080]{0:T(1024)S(1)} %pad_maximum_fusion.3), channel_id=1, source_target_pairs={{0,5},{1,6},{2,7},{3,8},{4,9},{5,10},{6,11},{7,12},{8,13},{9,14},{... | collective-permute-start | bytes 24968 | tf_op jit(solution)/shard_map/ppermute | solution.py:168
  112.3 7.6 %collective-permute-start.13 = (f32[2080]{0:T(1024)S(1)}, f32[2080]{0:T(1024)S(1)}, u32[]{:S(2)}, u32[]{:S(2)}) collective-permute-start(f32[2080]{0:T(1024)S(1)} %pad_maximum_fusion.3), channel_id=1, source_target_pairs={{0,4},{1,5},{2,6},{3,7},{4,8},{5,9},{6,10},{7,11},{8,12},{9,13},{1... | collective-permute-start | bytes 24968 | tf_op jit(solution)/shard_map/ppermute | solution.py:168
  114.4 6.1 %collective-permute-start.12 = (f32[2080]{0:T(1024)S(1)}, f32[2080]{0:T(1024)S(1)}, u32[]{:S(2)}, u32[]{:S(2)}) collective-permute-start(f32[2080]{0:T(1024)S(1)} %pad_maximum_fusion.3), channel_id=1, source_target_pairs={{0,3},{1,4},{2,5},{3,6},{4,7},{5,8},{6,9},{7,10},{8,11},{9,12},{10... | collective-permute-start | bytes 24968 | tf_op jit(solution)/shard_map/ppermute | solution.py:168
  116.5 6.5 %collective-permute-start.11 = (f32[2080]{0:T(1024)S(1)}, f32[2080]{0:T(1024)S(1)}, u32[]{:S(2)}, u32[]{:S(2)}) collective-permute-start(f32[2080]{0:T(1024)S(1)} %pad_maximum_fusion.3), channel_id=1, source_target_pairs={{0,2},{1,3},{2,4},{3,5},{4,6},{5,7},{6,8},{7,9},{8,10},{9,11},{10,... | collective-permute-start | bytes 24968 | tf_op jit(solution)/shard_map/ppermute | solution.py:168
  117.6 5.8 %collective-permute-start.10 = (f32[2080]{0:T(1024)S(1)}, f32[2080]{0:T(1024)S(1)}, u32[]{:S(2)}, u32[]{:S(2)}) collective-permute-start(f32[2080]{0:T(1024)S(1)} %pad_maximum_fusion.3), channel_id=1, source_target_pairs={{0,1},{1,2},{2,3},{3,4},{4,5},{5,6},{6,7},{7,8},{8,9},{9,10},{10,1... | collective-permute-start | bytes 24968 | tf_op jit(solution)/shard_map/ppermute | solution.py:168
  117.9 14.8 %collective-permute-start.9 = (bf16[128,2048]{1,0:T(8,128)(2,1)S(1)}, bf16[128,2048]{1,0:T(8,128)(2,1)S(1)}, u32[]{:S(2)}, u32[]{:S(2)}) collective-permute-start(bf16[128,2048]{1,0:T(8,128)(2,1)S(1)} %dynamic-slice_convert_fusion), channel_id=1, source_target_pairs={{0,2},{2,0},{1,3},{3,1},{4,6},{6,4},{5,7},{7,5},{8,10},{10,8},{9,1... | collective-permute-start | bytes 1572872 | tf_op jit(solution)/shard_map/ppermute | solution.py:231

commit v8 on v5

--- a/solution.py
+++ b/solution.py
@@ -28,11 +28,12 @@
     s = lax.dot_general(q, k, NT_DIMS, preferred_element_type=jnp.float32) * (HD ** -0.5)
     row_pos = base_ref[0] + r * tq + lax.broadcasted_iota(jnp.int32, (tq, keys), 0)
     vis = kpos_ref[...] <= row_pos
-    kvis = jnp.logical_and(vis, kept_ref[...] > 0.0)
-    m_c = jnp.max(jnp.where(vis, s, NEG_FILL), axis=1, keepdims=True)
-    m_m = jnp.max(jnp.where(kvis, s, NEG_FILL), axis=1, keepdims=True)
-    e_c = jnp.where(vis, jnp.exp(s - m_c), 0.0)
-    e_m = jnp.where(kvis, jnp.exp(s - m_m), 0.0)
+    s_c = jnp.where(vis, s, NEG_FILL)
+    s_m = jnp.where(kept_ref[...] > 0.0, s_c, NEG_FILL)
+    m_c = jnp.max(s_c, axis=1, keepdims=True)
+    m_m = jnp.max(s_m, axis=1, keepdims=True)
+    e_c = jnp.exp(s_c - m_c)
+    e_m = jnp.exp(s_m - m_m)
     l_c = jnp.sum(e_c, axis=1, keepdims=True)
     l_m = jnp.sum(e_m, axis=1, keepdims=True)
     o_c = jnp.dot(e_c.astype(jnp.bfloat16), v, preferred_element_type=jnp.float32) / l_c

time: 117 us -> 112 us (0.957)
  Pallas kernels: 29.7 us -> 24 us
    pallas_call x1, Pallas kernels: 29.7 us -> 24 us  [fused_attention(): pl.pallas_call(functools.partial(attention_kernel, tq=tq), grid_spec=pltp...]
  transfers between devices with their start and end apart: 14 -> 14, of which waited for: 7 -> 7; matrix products, arithmetic and copies ran while one was open for 17% -> 18% of each run, Pallas kernels for 0% -> 0%
where the time goes in v8:
time: 112 us; the launch traced here: 111 us
  starting transfers between devices  36.6 us (33%)
  Pallas kernels  24 us (21%)
  matrix products  21.1 us (19%)
  waiting for transfers between devices  13.9 us (12%)
  other arithmetic  10.2 us (9%)
  local copies, waits for them, and re-layouts  4.62 us (4%)
    pallas_call x1, Pallas kernels, fused_attention(): pl.pallas_call(functools.partial(attention_kernel, tq=tq), grid_spec=pltp...  24 us
    ppermute x4, starting transfers between devices, butterfly_sum(): total = total + lax.ppermute(total, axis, [(i, i ^ bit) for i in range(n)])  20.5 us
    dot_general x1, matrix products, local(): jnp.dot(grad_masked, out_weight.T, preferred_element_type=jnp.float32)  12.3 us
    ppermute x2, starting transfers between devices, relay_gather(): forward.append(lax.ppermute(payload, 'ctx', fwd) if fwd else zero)  10.5 us
    dot_general x1, matrix products, local(): projected = jnp.dot(delta, out_weight, preferred_element_type=jnp.float32)  8.3 us
    ppermute x4, waiting for transfers between devices, butterfly_sum(): total = total + lax.ppermute(total, axis, [(i, i ^ bit) for i in range(n)])  7.68 us
    ppermute x2, waiting for transfers between devices, relay_gather(): backward.append(lax.ppermute(payload, 'ctx', bwd) if bwd else zero)  4.72 us
    ppermute x2, starting transfers between devices, relay_gather(): backward.append(lax.ppermute(payload, 'ctx', bwd) if bwd else zero)  2.58 us
  transfers between devices with their start and end apart: 14, of which 7 were waited for; matrix products, arithmetic and copies ran while one was open for 18% of the time, Pallas kernels for 0%

profile of v8, /device:TPU:0, one launch (start us, length us, event | category | flops | bytes accessed | tf_op | source)
XLA Modules:
  0.0 111.4 jit_solution(2818800753897682461)
XLA Ops:
  0.6 0.0 copy-start.6
  0.6 0.0 copy-start.3
  0.7 0.8 convert_element_type.29
  1.5 1.1 broadcast_select_fusion.7
  2.6 0.8 pad_maximum_fusion.2
  3.4 6.0 %collective-permute-start.3 = (bf16[528,512]{1,0:T(8,128)(2,1)}, bf16[528,512]{1,0:T(8,128)(2,1)S(1)}, u32[]{:S(2)}, u32[]{:S(2)}) collective-permute-start(bf16[528,512]{1,0:T(8,128)(2,1)} %pad_maximum_fusion.2), channel_id=1, source_target_pairs={{0,8},{4,12},{1,9},{5,13},{2,10},{6,14},{3,11},{7,15},{16,24},{20,... | collective-permute-start | bytes 1622024 | tf_op jit(solution)/shard_map/ppermute | solution.py:114
  9.4 1.3 %collective-permute-start.4 = (bf16[528,512]{1,0:T(8,128)(2,1)}, bf16[528,512]{1,0:T(8,128)(2,1)}, u32[]{:S(2)}, u32[]{:S(2)}) collective-permute-start(bf16[528,512]{1,0:T(8,128)(2,1)} %pad_maximum_fusion.2), channel_id=1, source_target_pairs={{8,0},{9,1},{10,2},{11,3},{24,16},{25,17},{26,18},{27,19}} | collective-permute-start | bytes 1622024 | tf_op jit(solution)/shard_map/ppermute | solution.py:120
  10.7 1.3 %collective-permute-start.7 = (bf16[528,512]{1,0:T(8,128)(2,1)}, bf16[528,512]{1,0:T(8,128)(2,1)}, u32[]{:S(2)}, u32[]{:S(2)}) collective-permute-start(bf16[528,512]{1,0:T(8,128)(2,1)} %pad_maximum_fusion.2), channel_id=1, source_target_pairs={{4,0},{8,4},{12,8},{5,1},{9,5},{13,9},{6,2},{10,6},{14,10},{7,3},{... | collective-permute-start | bytes 1622024 | tf_op jit(solution)/shard_map/ppermute | solution.py:120
  12.0 4.6 %collective-permute-start.1 = (bf16[528,512]{1,0:T(8,128)(2,1)}, bf16[528,512]{1,0:T(8,128)(2,1)S(1)}, u32[]{:S(2)}, u32[]{:S(2)}) collective-permute-start(bf16[528,512]{1,0:T(8,128)(2,1)} %pad_maximum_fusion.2), channel_id=1, source_target_pairs={{0,4},{4,8},{8,12},{1,5},{5,9},{9,13},{2,6},{6,10},{10,14},{3,7},{... | collective-permute-start | bytes 1622024 | tf_op jit(solution)/shard_map/ppermute | solution.py:114
  16.6 0.1 collective-permute-start
  16.7 0.0 copy-done.3
  16.7 12.3 %convolution_convert_fusion.do_ref = bf16[128,2048]{1,0:T(8,128)(2,1)} fusion(bf16[2048,4096]{1,0:T(8,128)(2,1)} %param.13, bf16[128,4096]{1,0:T(8,128)(2,1)S(1)} %copy-done.3, pred[128]{0:T(512)(128)(4,1)S(1)} %broadcast_compare_fusion), kind=kOutput, calls=%fused_computation.2 | convolution fusion | flops 2148270080 | bytes 18350208 | tf_op jit(solution)/shard_map/dot_general | solution.py:199
  28.9 0.1 add_bitcast_fusion
  29.0 0.6 copy.11
  29.6 0.0 collective-permute-done.3
  29.7 0.0 collective-permute-done.4
  29.7 1.1 broadcast_select_fusion.1
  30.8 0.5 collective-permute-start.5
  31.3 0.7 collective-permute-start.6
  32.0 0.0 collective-permute-done
  32.0 0.1 broadcast_select_fusion.6
  32.2 0.6 collective-permute-done.1
  32.9 0.1 collective-permute-start.2
  33.0 0.1 fusion.3
  33.1 4.7 %collective-permute-done.7 = bf16[528,512]{1,0:T(8,128)(2,1)} collective-permute-done((bf16[528,512]{1,0:T(8,128)(2,1)}, bf16[528,512]{1,0:T(8,128)(2,1)}, u32[]{:S(2)}, u32[]{:S(2)}) %collective-permute-start.7) | collective-permute-done | bytes 540704 | tf_op jit(solution)/shard_map/ppermute | solution.py:120
  37.8 0.0 collective-permute-done.6
  37.8 1.1 broadcast_select_fusion
  38.9 0.1 collective-permute-start.8
  39.0 0.0 collective-permute-done.5
  39.0 0.1 broadcast_select_fusion.4
  39.1 0.0 collective-permute-done.2
  39.1 0.1 broadcast_select_fusion.5
  39.2 0.1 slice_select_fusion.1
  39.3 0.6 copy-done
  39.9 0.1 slice_select_fusion.2
  40.0 0.1 copy-done.2
  40.1 0.8 collective-permute-done.8
  40.9 0.1 broadcast_select_fusion.3
  41.1 0.1 compare_reduce_fusion
  41.2 0.6 broadcast_select_fusion.8
  41.8 0.1 slice_select_fusion
  41.9 0.2 slice-done.2
  42.1 2.1 %pad_maximum_fusion = (bf16[2048,512]{1,0:T(8,128)(2,1)}, bf16[2048,512]{1,0:T(8,128)(2,1)}) fusion(bf16[512,512]{1,0:T(8,128)(2,1)S(1)} %slice.86, bf16[512,512]{1,0:T(8,128)(2,1)S(1)} %slice-done, bf16[512,512]{1,0:T(8,128)(2,1)S(1)} %slice-done.2, bf16[512,512]{1,0:T(8,128)(2,1)S(1)} %slice-done.1, bf16[512,512]{1,0:T(8,128)(2,1)S(1)} %slice_select_fusion, ...), kind=kLoop, calls=%fused_computation.3 | loop fusion | flops 16777216 | bytes 8388608 | tf_op jit(solution)/shard_map/concatenate | solution.py:147
  44.2 24.0 %shard_map.103 = (bf16[128,2048]{1,0:T(8,128)(2,1)}, f32[1,2048]{1,0:T(1,128)}) custom-call(s32[1]{0:T(128)} %bitcast.base_ref, s32[1,2048]{1,0:T(1,128)} %bitcast.28, bf16[128,2048]{1,0:T(8,128)(2,1)} %q_ref.1, bf16[2048,512]{1,0:T(8,128)(2,1)} %get-tuple-element.19.k_ref, bf16[2048,512]{1,0:T(8,128)(2,1)} %get-tuple-element.20.v_ref, f32[1,2048]{1,0:T(1,128)} %bitcast.27, ...), custom_call_target="tpu_custom_call" | custom-call | flops 4294967296 | bytes 5775360 | tf_op jit(solution)/shard_map/pallas_call | solution.py:75
  68.2 8.3 %fusion.12 = f32[128,4096]{1,0:T(8,128)S(1)} fusion(bf16[128,2048]{1,0:T(8,128)(2,1)} %get-tuple-element.17, bf16[2048,4096]{1,0:T(8,128)(2,1)} %param.13), kind=kOutput, calls=%fused_computation.52 | convolution fusion | flops 2147483648 | bytes 19398656 | tf_op jit(solution)/shard_map/dot_general | solution.py:217
  76.5 0.1 dynamic-slice_convert_fusion
  76.6 1.6 %collective-permute-start.9 = (bf16[128,2048]{1,0:T(8,128)(2,1)S(1)}, bf16[128,2048]{1,0:T(8,128)(2,1)S(1)}, u32[]{:S(2)}, u32[]{:S(2)}) collective-permute-start(bf16[128,2048]{1,0:T(8,128)(2,1)S(1)} %dynamic-slice_convert_fusion), channel_id=1, source_target_pairs={{0,2},{2,0},{1,3},{3,1},{4,6},{6,4},{5,7},{7,5},{8,10},{10,8},{9,1... | collective-permute-start | bytes 1572872 | tf_op jit(solution)/shard_map/ppermute | solution.py:222
  78.2 0.5 broadcast.152
  78.7 0.7 reduce.13
  79.4 0.6 gather_fusion
  80.0 0.6 gather_fusion.1
  80.6 0.6 convolution_bitcast_fusion
  81.1 0.1 collective-permute-start.10
  81.2 1.2 %collective-permute-done.10 = f32[2080]{0:T(1024)S(1)} collective-permute-done((f32[2080]{0:T(1024)S(1)}, f32[2080]{0:T(1024)S(1)}, u32[]{:S(2)}, u32[]{:S(2)}) %collective-permute-start.10) | collective-permute-done | bytes 8352 | tf_op jit(solution)/shard_map/ppermute | solution.py:165
  82.4 8.5 %collective-permute-start.11 = (f32[2080]{0:T(1024)S(1)}, f32[2080]{0:T(1024)S(1)}, u32[]{:S(2)}, u32[]{:S(2)}) collective-permute-start(f32[2080]{0:T(1024)S(1)} %fusion.11), channel_id=1, source_target_pairs={{0,4},{4,0},{8,12},{12,8},{1,5},{5,1},{9,13},{13,9},{2,6},{6,2},{1... | collective-permute-start | bytes 24968 | tf_op jit(solution)/shard_map/ppermute | solution.py:165
  90.9 1.7 %collective-permute-done.11 = f32[2080]{0:T(1024)S(1)} collective-permute-done((f32[2080]{0:T(1024)S(1)}, f32[2080]{0:T(1024)S(1)}, u32[]{:S(2)}, u32[]{:S(2)}) %collective-permute-start.11) | collective-permute-done | bytes 8352 | tf_op jit(solution)/shard_map/ppermute | solution.py:165
  92.6 11.4 %collective-permute-start.12 = (f32[2080]{0:T(1024)S(1)}, f32[2080]{0:T(1024)S(1)}, u32[]{:S(2)}, u32[]{:S(2)}) collective-permute-start(f32[2080]{0:T(1024)S(1)} %add.97), channel_id=1, source_target_pairs={{0,8},{4,12},{8,0},{12,4},{1,9},{5,13},{9,1},{13,5},{2,10},{6,14},... | collective-permute-start | bytes 24968 | tf_op jit(solution)/shard_map/ppermute | solution.py:165
  103.9 1.7 %collective-permute-done.12 = f32[2080]{0:T(1024)S(1)} collective-permute-done((f32[2080]{0:T(1024)S(1)}, f32[2080]{0:T(1024)S(1)}, u32[]{:S(2)}, u32[]{:S(2)}) %collective-permute-start.12) | collective-permute-done | bytes 8352 | tf_op jit(solution)/shard_map/ppermute | solution.py:165
  105.6 0.5 collective-permute-start.13
  106.2 3.2 %collective-permute-done.13 = f32[2080]{0:T(1024)S(1)} collective-permute-done((f32[2080]{0:T(1024)S(1)}, f32[2080]{0:T(1024)S(1)}, u32[]{:S(2)}, u32[]{:S(2)}) %collective-permute-start.13) | collective-permute-done | bytes 8352 | tf_op jit(solution)/shard_map/ppermute | solution.py:165
  109.3 0.5 slice.101
  109.8 0.7 dynamic_slice.11
  110.5 0.0 collective-permute-done.9
  110.5 0.9 add_convert_fusion
  (38 shorter events, 0.3 us)
Async XLA Ops:
  0.6 16.0 %copy-start.6 = (s32[128]{0:T(128)S(1)}, s32[128]{0:T(128)}, u32[]{:S(2)}) copy-start(s32[128]{0:T(128)} %param.15) | copy-start | bytes 1540
  0.6 16.0 %copy-start.3 = (bf16[128,4096]{1,0:T(8,128)(2,1)S(1)}, bf16[128,4096]{1,0:T(8,128)(2,1)}, u32[]{:S(2)}) copy-start(bf16[128,4096]{1,0:T(8,128)(2,1)} %param.14) | copy-start | bytes 3145732
  3.4 26.2 %collective-permute-start.3 = (bf16[528,512]{1,0:T(8,128)(2,1)}, bf16[528,512]{1,0:T(8,128)(2,1)S(1)}, u32[]{:S(2)}, u32[]{:S(2)}) collective-permute-start(bf16[528,512]{1,0:T(8,128)(2,1)} %pad_maximum_fusion.2), channel_id=1, source_target_pairs={{0,8},{4,12},{1,9},{5,13},{2,10},{6,14},{3,11},{7,15},{16,24},{20,... | collective-permute-start | bytes 1622024 | tf_op jit(solution)/shard_map/ppermute | solution.py:114
  9.4 20.3 %collective-permute-start.4 = (bf16[528,512]{1,0:T(8,128)(2,1)}, bf16[528,512]{1,0:T(8,128)(2,1)}, u32[]{:S(2)}, u32[]{:S(2)}) collective-permute-start(bf16[528,512]{1,0:T(8,128)(2,1)} %pad_maximum_fusion.2), channel_id=1, source_target_pairs={{8,0},{9,1},{10,2},{11,3},{24,16},{25,17},{26,18},{27,19}} | collective-permute-start | bytes 1622024 | tf_op jit(solution)/shard_map/ppermute | solution.py:120
  10.7 27.1 %collective-permute-start.7 = (bf16[528,512]{1,0:T(8,128)(2,1)}, bf16[528,512]{1,0:T(8,128)(2,1)}, u32[]{:S(2)}, u32[]{:S(2)}) collective-permute-start(bf16[528,512]{1,0:T(8,128)(2,1)} %pad_maximum_fusion.2), channel_id=1, source_target_pairs={{4,0},{8,4},{12,8},{5,1},{9,5},{13,9},{6,2},{10,6},{14,10},{7,3},{... | collective-permute-start | bytes 1622024 | tf_op jit(solution)/shard_map/ppermute | solution.py:120
  12.0 20.8 %collective-permute-start.1 = (bf16[528,512]{1,0:T(8,128)(2,1)}, bf16[528,512]{1,0:T(8,128)(2,1)S(1)}, u32[]{:S(2)}, u32[]{:S(2)}) collective-permute-start(bf16[528,512]{1,0:T(8,128)(2,1)} %pad_maximum_fusion.2), channel_id=1, source_target_pairs={{0,4},{4,8},{8,12},{1,5},{5,9},{9,13},{2,6},{6,10},{10,14},{3,7},{... | collective-permute-start | bytes 1622024 | tf_op jit(solution)/shard_map/ppermute | solution.py:114
  16.6 15.4 %collective-permute-start = (bf16[528,512]{1,0:T(8,128)(2,1)}, bf16[528,512]{1,0:T(8,128)(2,1)S(1)}, u32[]{:S(2)}, u32[]{:S(2)}) collective-permute-start(bf16[528,512]{1,0:T(8,128)(2,1)} %pad_maximum_fusion.2), channel_id=1, source_target_pairs={{0,1},{1,0},{2,3},{3,2},{4,5},{5,4},{6,7},{7,6},{8,9},{9,8},{10,11... | collective-permute-start | bytes 1622024 | tf_op jit(solution)/shard_map/ppermute | solution.py:141
  30.8 8.3 %collective-permute-start.5 = (bf16[528,512]{1,0:T(8,128)(2,1)S(1)}, bf16[528,512]{1,0:T(8,128)(2,1)S(1)}, u32[]{:S(2)}, u32[]{:S(2)}) collective-permute-start(bf16[528,512]{1,0:T(8,128)(2,1)S(1)} %broadcast_select_fusion.1), channel_id=1, source_target_pairs={{0,1},{1,0},{2,3},{3,2},{4,5},{5,4},{6,7},{7,6},{8,9},{9,8},{10,11... | collective-permute-start | bytes 1622024 | tf_op jit(solution)/shard_map/ppermute | solution.py:141
  31.3 6.5 %collective-permute-start.6 = (bf16[528,512]{1,0:T(8,128)(2,1)S(1)}, bf16[528,512]{1,0:T(8,128)(2,1)S(1)}, u32[]{:S(2)}, u32[]{:S(2)}) collective-permute-start(bf16[528,512]{1,0:T(8,128)(2,1)S(1)} %collective-permute-done.3), channel_id=1, source_target_pairs={{8,12},{9,13},{10,14},{11,15},{24,28},{25,29},{26,30},{27,31}} | collective-permute-start | bytes 1622024 | tf_op jit(solution)/shard_map/ppermute | solution.py:112
  32.2 6.8 %copy-start.1 = (bf16[528,512]{1,0:T(8,128)(2,1)}, bf16[528,512]{1,0:T(8,128)(2,1)S(1)}, u32[]{:S(2)}) copy-start(bf16[528,512]{1,0:T(8,128)(2,1)S(1)} %broadcast_select_fusion.6) | copy-start | bytes 1622020
  32.9 6.3 %collective-permute-start.2 = (bf16[528,512]{1,0:T(8,128)(2,1)S(1)}, bf16[528,512]{1,0:T(8,128)(2,1)S(1)}, u32[]{:S(2)}, u32[]{:S(2)}) collective-permute-start(bf16[528,512]{1,0:T(8,128)(2,1)S(1)} %broadcast_select_fusion.2), channel_id=1, source_target_pairs={{0,1},{1,0},{2,3},{3,2},{4,5},{5,4},{6,7},{7,6},{8,9},{9,8},{10,11... | collective-permute-start | bytes 1622024 | tf_op jit(solution)/shard_map/ppermute | solution.py:141
  38.9 2.0 %collective-permute-start.8 = (bf16[528,512]{1,0:T(8,128)(2,1)S(1)}, bf16[528,512]{1,0:T(8,128)(2,1)S(1)}, u32[]{:S(2)}, u32[]{:S(2)}) collective-permute-start(bf16[528,512]{1,0:T(8,128)(2,1)S(1)} %broadcast_select_fusion), channel_id=1, source_target_pairs={{0,1},{1,0},{2,3},{3,2},{4,5},{5,4},{6,7},{7,6},{8,9},{9,8},{10,11... | collective-permute-start | bytes 1622024 | tf_op jit(solution)/shard_map/ppermute | solution.py:141
  39.1 0.8 copy-start
  39.2 0.9 copy-start.2
  39.9 1.1 %copy-start.5 = (s32[4]{0:T(128)S(1)}, s32[4]{0:T(128)}, u32[]{:S(2)}) copy-start(s32[4]{0:T(128)} %param.17) | copy-start | bytes 52
  40.1 1.8 %slice-start = ((bf16[528,512]{1,0:T(8,128)(2,1)}), bf16[512,512]{1,0:T(8,128)(2,1)S(1)}, s32[]{:S(2)}) async-start(bf16[528,512]{1,0:T(8,128)(2,1)} %copy-done), calls=%async_computation | async-start | bytes 1048576 | tf_op jit(solution)/shard_map/slice | solution.py:147
  40.1 1.8 %slice-start.1 = ((bf16[528,512]{1,0:T(8,128)(2,1)}), bf16[512,512]{1,0:T(8,128)(2,1)S(1)}, s32[]{:S(2)}) async-start(bf16[528,512]{1,0:T(8,128)(2,1)} %copy-done.1), calls=%async_computation.1 | async-start | bytes 1048576 | tf_op jit(solution)/shard_map/slice | solution.py:147
  40.9 1.1 %slice-start.2 = ((bf16[528,512]{1,0:T(8,128)(2,1)}), bf16[512,512]{1,0:T(8,128)(2,1)S(1)}, s32[]{:S(2)}) async-start(bf16[528,512]{1,0:T(8,128)(2,1)} %copy-done.2), calls=%async_computation.2 | async-start | bytes 1048576 | tf_op jit(solution)/shard_map/slice | solution.py:147
  68.2 10.5 %copy-start.4 = (f32[1,2048]{1,0:T(1,128)S(1)}, f32[1,2048]{1,0:T(1,128)}, u32[]{:S(2)}) copy-start(f32[1,2048]{1,0:T(1,128)} %get-tuple-element.18) | copy-start | bytes 24580
  76.6 33.9 %collective-permute-start.9 = (bf16[128,2048]{1,0:T(8,128)(2,1)S(1)}, bf16[128,2048]{1,0:T(8,128)(2,1)S(1)}, u32[]{:S(2)}, u32[]{:S(2)}) collective-permute-start(bf16[128,2048]{1,0:T(8,128)(2,1)S(1)} %dynamic-slice_convert_fusion), channel_id=1, source_target_pairs={{0,2},{2,0},{1,3},{3,1},{4,6},{6,4},{5,7},{7,5},{8,10},{10,8},{9,1... | collective-permute-start | bytes 1572872 | tf_op jit(solution)/shard_map/ppermute | solution.py:222
  81.1 1.2 %collective-permute-start.10 = (f32[2080]{0:T(1024)S(1)}, f32[2080]{0:T(1024)S(1)}, u32[]{:S(2)}, u32[]{:S(2)}) collective-permute-start(f32[2080]{0:T(1024)S(1)} %pad_maximum_fusion.3), channel_id=1, source_target_pairs={{0,1},{1,0},{2,3},{3,2},{4,5},{5,4},{6,7},{7,6},{8,9},{9,8},{10,11... | collective-permute-start | bytes 24968 | tf_op jit(solution)/shard_map/ppermute | solution.py:165
  82.4 10.2 %collective-permute-start.11 = (f32[2080]{0:T(1024)S(1)}, f32[2080]{0:T(1024)S(1)}, u32[]{:S(2)}, u32[]{:S(2)}) collective-permute-start(f32[2080]{0:T(1024)S(1)} %fusion.11), channel_id=1, source_target_pairs={{0,4},{4,0},{8,12},{12,8},{1,5},{5,1},{9,13},{13,9},{2,6},{6,2},{1... | collective-permute-start | bytes 24968 | tf_op jit(solution)/shard_map/ppermute | solution.py:165
  92.6 13.1 %collective-permute-start.12 = (f32[2080]{0:T(1024)S(1)}, f32[2080]{0:T(1024)S(1)}, u32[]{:S(2)}, u32[]{:S(2)}) collective-permute-start(f32[2080]{0:T(1024)S(1)} %add.97), channel_id=1, source_target_pairs={{0,8},{4,12},{8,0},{12,4},{1,9},{5,13},{9,1},{13,5},{2,10},{6,14},... | collective-permute-start | bytes 24968 | tf_op jit(solution)/shard_map/ppermute | solution.py:165
  105.6 3.7 %collective-permute-start.13 = (f32[2080]{0:T(1024)S(1)}, f32[2080]{0:T(1024)S(1)}, u32[]{:S(2)}, u32[]{:S(2)}) collective-permute-start(f32[2080]{0:T(1024)S(1)} %add.98), channel_id=1, source_target_pairs={{0,2},{2,0},{1,3},{3,1},{4,6},{6,4},{5,7},{7,5},{8,10},{10,8},{9,1... | collective-permute-start | bytes 24968 | tf_op jit(solution)/shard_map/ppermute | solution.py:165

commit v9 on v5

--- a/solution.py
+++ b/solution.py
@@ -13,7 +13,7 @@
 NT_DIMS = (((1,), (1,)), ((), ()))
 
 
-def attention_kernel(base_ref, kpos_ref, q_ref, k_ref, v_ref, kept_ref, do_ref, delta_ref, attr_ref, *, tq):
+def attention_kernel(base_ref, kpos_ref, q_ref, k_ref, v_ref, kept_ref, do_ref, delta_ref, attr_ref, *, tq, hp):
     r = pl.program_id(2)
     first = (pl.program_id(0) == 0) & (pl.program_id(1) == 0) & (r == 0)
 
@@ -21,30 +21,36 @@
     def _():
         attr_ref[...] = jnp.zeros_like(attr_ref)
 
-    q = q_ref[...]
     k = k_ref[...]
     v = v_ref[...]
-    keys = k.shape[0]
-    s = lax.dot_general(q, k, NT_DIMS, preferred_element_type=jnp.float32) * (HD ** -0.5)
-    row_pos = base_ref[0] + r * tq + lax.broadcasted_iota(jnp.int32, (tq, keys), 0)
+    row_pos = base_ref[0] + r * tq + lax.broadcasted_iota(jnp.int32, (tq, 1), 0)
     vis = kpos_ref[...] <= row_pos
-    kvis = jnp.logical_and(vis, kept_ref[...] > 0.0)
-    m_c = jnp.max(jnp.where(vis, s, NEG_FILL), axis=1, keepdims=True)
-    m_m = jnp.max(jnp.where(kvis, s, NEG_FILL), axis=1, keepdims=True)
-    e_c = jnp.where(vis, jnp.exp(s - m_c), 0.0)
-    e_m = jnp.where(kvis, jnp.exp(s - m_m), 0.0)
-    l_c = jnp.sum(e_c, axis=1, keepdims=True)
-    l_m = jnp.sum(e_m, axis=1, keepdims=True)
-    o_c = jnp.dot(e_c.astype(jnp.bfloat16), v, preferred_element_type=jnp.float32) / l_c
-    o_m = jnp.dot(e_m.astype(jnp.bfloat16), v, preferred_element_type=jnp.float32) / l_m
-    delta_ref[...] = (o_m - o_c).astype(delta_ref.dtype)
-    g_rows = do_ref[...]
-    row_dot = jnp.sum(g_rows.astype(jnp.float32) * o_c, axis=1, keepdims=True)
-    d_p = lax.dot_general(g_rows, v, NT_DIMS, preferred_element_type=jnp.float32)
-    log_total = m_c + jnp.log(l_c)
-    prob = e_c * (1.0 / l_c)
-    contrib = prob * (d_p + (d_p - row_dot) * (s - log_total))
-    attr_ref[...] += jnp.sum(contrib, axis=0, keepdims=True)
+    kept = kept_ref[...] > 0.0
+    total = None
+    for h in range(hp):
+        cols = slice(h * HD, (h + 1) * HD)
+        s = lax.dot_general(q_ref[:, cols], k, NT_DIMS, preferred_element_type=jnp.float32)
+        s = s * (HD ** -0.5)
+        s_c = jnp.where(vis, s, NEG_FILL)
+        s_m = jnp.where(kept, s_c, NEG_FILL)
+        m_c = jnp.max(s_c, axis=1, keepdims=True)
+        m_m = jnp.max(s_m, axis=1, keepdims=True)
+        e_c = jnp.exp(s_c - m_c)
+        e_m = jnp.exp(s_m - m_m)
+        l_c = jnp.sum(e_c, axis=1, keepdims=True)
+        l_m = jnp.sum(e_m, axis=1, keepdims=True)
+        o_c = jnp.dot(e_c.astype(jnp.bfloat16), v, preferred_element_type=jnp.float32) / l_c
+        o_m = jnp.dot(e_m.astype(jnp.bfloat16), v, preferred_element_type=jnp.float32) / l_m
+        delta_ref[:, cols] = (o_m - o_c).astype(delta_ref.dtype)
+        g_rows = do_ref[:, cols]
+        row_dot = jnp.sum(g_rows.astype(jnp.float32) * o_c, axis=1, keepdims=True)
+        d_p = lax.dot_general(g_rows, v, NT_DIMS, preferred_element_type=jnp.float32)
+        log_total = m_c + jnp.log(l_c)
+        prob = e_c * (1.0 / l_c)
+        contrib = prob * (d_p + (d_p - row_dot) * (s - log_total))
+        part = jnp.sum(contrib, axis=0, keepdims=True)
+        total = part if total is None else total + part
+    attr_ref[...] += total
 
 
 def fused_attention(base, key_pos, query, key_all, value_all, kept, grad_out, group_size):
@@ -53,10 +59,12 @@
     kv_local = kv_width // HD
     tq = max(8, min(qc, (128 * 2048) // keys))
     n_rows = qc // tq
-    grid = (kv_local, group_size, n_rows)
+    hp = 2 if group_size % 2 == 0 else 1
+    steps = group_size // hp
+    grid = (kv_local, steps, n_rows)
 
     def head_map(g, j, r, b):
-        return (r, g * group_size + j)
+        return (r, g * steps + j)
 
     def kv_map(g, j, r, b):
         return (0, g)
@@ -72,20 +80,20 @@
         + 4 * keys,
     )
     return pl.pallas_call(
-        functools.partial(attention_kernel, tq=tq),
+        functools.partial(attention_kernel, tq=tq, hp=hp),
         grid_spec=pltpu.PrefetchScalarGridSpec(
             num_scalar_prefetch=1,
             grid=grid,
             in_specs=[
                 pl.BlockSpec((1, keys), fixed),
-                pl.BlockSpec((tq, HD), head_map),
+                pl.BlockSpec((tq, hp * HD), head_map),
                 pl.BlockSpec((keys, HD), kv_map),
                 pl.BlockSpec((keys, HD), kv_map),
                 pl.BlockSpec((1, keys), fixed),
-                pl.BlockSpec((tq, HD), head_map),
+                pl.BlockSpec((tq, hp * HD), head_map),
             ],
             out_specs=[
-                pl.BlockSpec((tq, HD), head_map),
+                pl.BlockSpec((tq, hp * HD), head_map),
                 pl.BlockSpec((1, keys), fixed),
             ],
         ),

time: 117 us -> 111 us (0.949)
  Pallas kernels: 29.7 us -> 23.1 us
    pallas_call x1, Pallas kernels: 29.7 us -> 23.1 us  [fused_attention(): pl.pallas_call(functools.partial(attention_kernel, tq=tq, hp=hp), grid_sp...]
  transfers between devices with their start and end apart: 14 -> 14, of which waited for: 7 -> 7; matrix products, arithmetic and copies ran while one was open for 17% -> 18% of each run, Pallas kernels for 0% -> 0%
where the time goes in v9:
time: 111 us
  starting transfers between devices  36.8 us (33%)
  Pallas kernels  23.1 us (21%)
  matrix products  21.1 us (19%)
  waiting for transfers between devices  13.7 us (12%)
  other arithmetic  10.2 us (9%)
  local copies, waits for them, and re-layouts  4.62 us (4%)
    pallas_call x1, Pallas kernels, fused_attention(): pl.pallas_call(functools.partial(attention_kernel, tq=tq, hp=hp), grid_sp...  23.1 us
    ppermute x4, starting transfers between devices, butterfly_sum(): total = total + lax.ppermute(total, axis, [(i, i ^ bit) for i in range(n)])  20.5 us
    dot_general x1, matrix products, local(): jnp.dot(grad_masked, out_weight.T, preferred_element_type=jnp.float32)  12.3 us
    ppermute x2, starting transfers between devices, relay_gather(): forward.append(lax.ppermute(payload, 'ctx', fwd) if fwd else zero)  10.5 us
    dot_general x1, matrix products, local(): projected = jnp.dot(delta, out_weight, preferred_element_type=jnp.float32)  8.3 us
    ppermute x4, waiting for transfers between devices, butterfly_sum(): total = total + lax.ppermute(total, axis, [(i, i ^ bit) for i in range(n)])  7.67 us
    ppermute x2, waiting for transfers between devices, relay_gather(): backward.append(lax.ppermute(payload, 'ctx', bwd) if bwd else zero)  4.72 us
    ppermute x2, starting transfers between devices, relay_gather(): backward.append(lax.ppermute(payload, 'ctx', bwd) if bwd else zero)  2.58 us
  transfers between devices with their start and end apart: 14, of which 7 were waited for; matrix products, arithmetic and copies ran while one was open for 18% of the time, Pallas kernels for 0%

profile of v9, /device:TPU:0, one launch (start us, length us, event | category | flops | bytes accessed | tf_op | source)
XLA Modules:
  0.0 110.5 jit_solution(5397332553113438688)
XLA Ops:
  0.6 0.0 copy-start.6
  0.7 0.8 convert_element_type.29
  1.5 1.1 %broadcast_select_fusion.7 = bf16[512,512]{1,0:T(8,128)(2,1)S(1)} fusion(bf16[512,512]{1,0:T(8,128)(2,1)} %param.11, bf16[512,512]{1,0:T(8,128)(2,1)} %param.12, pred[]{:T(512)S(6)} %eq.35), kind=kLoop, calls=%fused_computation.27 | loop fusion | flops 262144 | bytes 1572865 | tf_op jit(solution)/shard_map/jit(_where)/select_n | solution.py:143
  2.6 0.8 pad_maximum_fusion.2
  3.4 6.0 %collective-permute-start.3 = (bf16[528,512]{1,0:T(8,128)(2,1)}, bf16[528,512]{1,0:T(8,128)(2,1)S(1)}, u32[]{:S(2)}, u32[]{:S(2)}) collective-permute-start(bf16[528,512]{1,0:T(8,128)(2,1)} %pad_maximum_fusion.2), channel_id=1, source_target_pairs={{0,8},{4,12},{1,9},{5,13},{2,10},{6,14},{3,11},{7,15},{16,24},{20,... | collective-permute-start | bytes 1622024 | tf_op jit(solution)/shard_map/ppermute | solution.py:121
  9.4 1.3 %collective-permute-start.4 = (bf16[528,512]{1,0:T(8,128)(2,1)}, bf16[528,512]{1,0:T(8,128)(2,1)}, u32[]{:S(2)}, u32[]{:S(2)}) collective-permute-start(bf16[528,512]{1,0:T(8,128)(2,1)} %pad_maximum_fusion.2), channel_id=1, source_target_pairs={{8,0},{9,1},{10,2},{11,3},{24,16},{25,17},{26,18},{27,19}} | collective-permute-start | bytes 1622024 | tf_op jit(solution)/shard_map/ppermute | solution.py:127
  10.7 1.3 %collective-permute-start.7 = (bf16[528,512]{1,0:T(8,128)(2,1)}, bf16[528,512]{1,0:T(8,128)(2,1)}, u32[]{:S(2)}, u32[]{:S(2)}) collective-permute-start(bf16[528,512]{1,0:T(8,128)(2,1)} %pad_maximum_fusion.2), channel_id=1, source_target_pairs={{4,0},{8,4},{12,8},{5,1},{9,5},{13,9},{6,2},{10,6},{14,10},{7,3},{... | collective-permute-start | bytes 1622024 | tf_op jit(solution)/shard_map/ppermute | solution.py:127
  12.0 4.6 %collective-permute-start.1 = (bf16[528,512]{1,0:T(8,128)(2,1)}, bf16[528,512]{1,0:T(8,128)(2,1)S(1)}, u32[]{:S(2)}, u32[]{:S(2)}) collective-permute-start(bf16[528,512]{1,0:T(8,128)(2,1)} %pad_maximum_fusion.2), channel_id=1, source_target_pairs={{0,4},{4,8},{8,12},{1,5},{5,9},{9,13},{2,6},{6,10},{10,14},{3,7},{... | collective-permute-start | bytes 1622024 | tf_op jit(solution)/shard_map/ppermute | solution.py:121
  16.6 0.1 collective-permute-start
  16.7 12.3 %convolution_convert_fusion.do_ref = bf16[128,2048]{1,0:T(8,128)(2,1)} fusion(bf16[2048,4096]{1,0:T(8,128)(2,1)} %param.13, bf16[128,4096]{1,0:T(8,128)(2,1)S(1)} %copy-done.3, pred[128]{0:T(512)(128)(4,1)S(1)} %broadcast_compare_fusion), kind=kOutput, calls=%fused_computation.2 | convolution fusion | flops 2148270080 | bytes 18350208 | tf_op jit(solution)/shard_map/dot_general | solution.py:206
  29.0 0.1 add_bitcast_fusion
  29.1 0.6 copy.11
  29.7 0.0 collective-permute-done.3
  29.7 0.0 collective-permute-done.4
  29.7 1.1 %broadcast_select_fusion.1 = bf16[528,512]{1,0:T(8,128)(2,1)S(1)} fusion(bf16[528,512]{1,0:T(8,128)(2,1)S(1)} %collective-permute-done.3, bf16[528,512]{1,0:T(8,128)(2,1)} %collective-permute-done.4, pred[]{:T(512)S(6)} %ge.10), kind=kLoop, calls=%fused_computation.14 | loop fusion | flops 270336 | bytes 1622017 | tf_op jit(solution)/shard_map/jit(_where)/select_n | solution.py:130
  30.8 0.5 collective-permute-start.5
  31.3 0.9 collective-permute-start.6
  32.2 0.0 collective-permute-done
  32.2 0.1 broadcast_select_fusion.6
  32.4 0.5 collective-permute-done.1
  32.9 0.1 collective-permute-start.2
  33.0 0.1 fusion.3
  33.1 4.7 %collective-permute-done.7 = bf16[528,512]{1,0:T(8,128)(2,1)} collective-permute-done((bf16[528,512]{1,0:T(8,128)(2,1)}, bf16[528,512]{1,0:T(8,128)(2,1)}, u32[]{:S(2)}, u32[]{:S(2)}) %collective-permute-start.7) | collective-permute-done | bytes 540704 | tf_op jit(solution)/shard_map/ppermute | solution.py:127
  37.8 0.0 collective-permute-done.6
  37.8 1.1 %broadcast_select_fusion = bf16[528,512]{1,0:T(8,128)(2,1)S(1)} fusion(bf16[528,512]{1,0:T(8,128)(2,1)S(1)} %collective-permute-done.6, bf16[528,512]{1,0:T(8,128)(2,1)} %collective-permute-done.7, pred[]{:T(512)S(6)} %ge.11), kind=kLoop, calls=%fused_computation.13 | loop fusion | flops 270336 | bytes 1622017 | tf_op jit(solution)/shard_map/jit(_where)/select_n | solution.py:130
  38.9 0.1 collective-permute-start.8
  39.0 0.0 collective-permute-done.5
  39.0 0.1 broadcast_select_fusion.4
  39.1 0.0 copy-start
  39.1 0.0 collective-permute-done.2
  39.1 0.1 broadcast_select_fusion.5
  39.2 0.1 slice_select_fusion.1
  39.3 0.6 copy-done
  39.9 0.1 slice_select_fusion.2
  40.0 0.1 copy-done.2
  40.1 0.8 collective-permute-done.8
  40.9 0.1 broadcast_select_fusion.3
  41.1 0.0 copy-done.5
  41.1 0.1 compare_reduce_fusion
  41.2 0.6 broadcast_select_fusion.8
  41.8 0.1 slice_select_fusion
  41.9 0.2 slice-done.2
  42.1 2.1 %pad_maximum_fusion = (bf16[2048,512]{1,0:T(8,128)(2,1)}, bf16[2048,512]{1,0:T(8,128)(2,1)}) fusion(bf16[512,512]{1,0:T(8,128)(2,1)S(1)} %slice.86, bf16[512,512]{1,0:T(8,128)(2,1)S(1)} %slice-done, bf16[512,512]{1,0:T(8,128)(2,1)S(1)} %slice-done.2, bf16[512,512]{1,0:T(8,128)(2,1)S(1)} %slice-done.1, bf16[512,512]{1,0:T(8,128)(2,1)S(1)} %slice_select_fusion, ...), kind=kLoop, calls=%fused_computation.3 | loop fusion | flops 16777216 | bytes 8388608 | tf_op jit(solution)/shard_map/concatenate | solution.py:154
  44.2 23.1 %shard_map.103 = (bf16[128,2048]{1,0:T(8,128)(2,1)}, f32[1,2048]{1,0:T(1,128)}) custom-call(s32[1]{0:T(128)} %bitcast.base_ref, s32[1,2048]{1,0:T(1,128)} %bitcast.28, bf16[128,2048]{1,0:T(8,128)(2,1)} %q_ref.1, bf16[2048,512]{1,0:T(8,128)(2,1)} %get-tuple-element.19.k_ref, bf16[2048,512]{1,0:T(8,128)(2,1)} %get-tuple-element.20.v_ref, f32[1,2048]{1,0:T(1,128)} %bitcast.27, ...), custom_call_target="tpu_custom_call" | custom-call | flops 4294967296 | bytes 5775360 | tf_op jit(solution)/shard_map/pallas_call | solution.py:82
  67.4 8.3 %fusion.12 = f32[128,4096]{1,0:T(8,128)S(1)} fusion(bf16[128,2048]{1,0:T(8,128)(2,1)} %get-tuple-element.17, bf16[2048,4096]{1,0:T(8,128)(2,1)} %param.13), kind=kOutput, calls=%fused_computation.52 | convolution fusion | flops 2147483648 | bytes 19398656 | tf_op jit(solution)/shard_map/dot_general | solution.py:224
  75.7 0.1 dynamic-slice_convert_fusion
  75.8 1.6 %collective-permute-start.9 = (bf16[128,2048]{1,0:T(8,128)(2,1)S(1)}, bf16[128,2048]{1,0:T(8,128)(2,1)S(1)}, u32[]{:S(2)}, u32[]{:S(2)}) collective-permute-start(bf16[128,2048]{1,0:T(8,128)(2,1)S(1)} %dynamic-slice_convert_fusion), channel_id=1, source_target_pairs={{0,2},{2,0},{1,3},{3,1},{4,6},{6,4},{5,7},{7,5},{8,10},{10,8},{9,1... | collective-permute-start | bytes 1572872 | tf_op jit(solution)/shard_map/ppermute | solution.py:229
  77.3 0.5 broadcast.152
  77.8 0.7 reduce.13
  78.5 0.6 gather_fusion
  79.1 0.6 gather_fusion.1
  79.7 0.6 convolution_bitcast_fusion
  80.3 0.1 collective-permute-start.10
  80.4 1.2 %collective-permute-done.10 = f32[2080]{0:T(1024)S(1)} collective-permute-done((f32[2080]{0:T(1024)S(1)}, f32[2080]{0:T(1024)S(1)}, u32[]{:S(2)}, u32[]{:S(2)}) %collective-permute-start.10) | collective-permute-done | bytes 8352 | tf_op jit(solution)/shard_map/ppermute | solution.py:172
  81.5 8.5 %collective-permute-start.11 = (f32[2080]{0:T(1024)S(1)}, f32[2080]{0:T(1024)S(1)}, u32[]{:S(2)}, u32[]{:S(2)}) collective-permute-start(f32[2080]{0:T(1024)S(1)} %fusion.11), channel_id=1, source_target_pairs={{0,4},{4,0},{8,12},{12,8},{1,5},{5,1},{9,13},{13,9},{2,6},{6,2},{1... | collective-permute-start | bytes 24968 | tf_op jit(solution)/shard_map/ppermute | solution.py:172
  90.0 1.7 %collective-permute-done.11 = f32[2080]{0:T(1024)S(1)} collective-permute-done((f32[2080]{0:T(1024)S(1)}, f32[2080]{0:T(1024)S(1)}, u32[]{:S(2)}, u32[]{:S(2)}) %collective-permute-start.11) | collective-permute-done | bytes 8352 | tf_op jit(solution)/shard_map/ppermute | solution.py:172
  91.7 11.4 %collective-permute-start.12 = (f32[2080]{0:T(1024)S(1)}, f32[2080]{0:T(1024)S(1)}, u32[]{:S(2)}, u32[]{:S(2)}) collective-permute-start(f32[2080]{0:T(1024)S(1)} %add.97), channel_id=1, source_target_pairs={{0,8},{4,12},{8,0},{12,4},{1,9},{5,13},{9,1},{13,5},{2,10},{6,14},... | collective-permute-start | bytes 24968 | tf_op jit(solution)/shard_map/ppermute | solution.py:172
  103.1 1.7 %collective-permute-done.12 = f32[2080]{0:T(1024)S(1)} collective-permute-done((f32[2080]{0:T(1024)S(1)}, f32[2080]{0:T(1024)S(1)}, u32[]{:S(2)}, u32[]{:S(2)}) %collective-permute-start.12) | collective-permute-done | bytes 8352 | tf_op jit(solution)/shard_map/ppermute | solution.py:172
  104.7 0.5 collective-permute-start.13
  105.3 3.2 %collective-permute-done.13 = f32[2080]{0:T(1024)S(1)} collective-permute-done((f32[2080]{0:T(1024)S(1)}, f32[2080]{0:T(1024)S(1)}, u32[]{:S(2)}, u32[]{:S(2)}) %collective-permute-start.13) | collective-permute-done | bytes 8352 | tf_op jit(solution)/shard_map/ppermute | solution.py:172
  108.5 0.5 slice.101
  109.0 0.7 dynamic_slice.11
  109.6 0.0 collective-permute-done.9
  109.6 0.9 add_convert_fusion
  (38 shorter events, 0.3 us)
Async XLA Ops:
  0.6 16.0 %copy-start.6 = (s32[128]{0:T(128)S(1)}, s32[128]{0:T(128)}, u32[]{:S(2)}) copy-start(s32[128]{0:T(128)} %param.15) | copy-start | bytes 1540
  0.6 16.0 %copy-start.3 = (bf16[128,4096]{1,0:T(8,128)(2,1)S(1)}, bf16[128,4096]{1,0:T(8,128)(2,1)}, u32[]{:S(2)}) copy-start(bf16[128,4096]{1,0:T(8,128)(2,1)} %param.14) | copy-start | bytes 3145732
  3.4 26.2 %collective-permute-start.3 = (bf16[528,512]{1,0:T(8,128)(2,1)}, bf16[528,512]{1,0:T(8,128)(2,1)S(1)}, u32[]{:S(2)}, u32[]{:S(2)}) collective-permute-start(bf16[528,512]{1,0:T(8,128)(2,1)} %pad_maximum_fusion.2), channel_id=1, source_target_pairs={{0,8},{4,12},{1,9},{5,13},{2,10},{6,14},{3,11},{7,15},{16,24},{20,... | collective-permute-start | bytes 1622024 | tf_op jit(solution)/shard_map/ppermute | solution.py:121
  9.4 20.3 %collective-permute-start.4 = (bf16[528,512]{1,0:T(8,128)(2,1)}, bf16[528,512]{1,0:T(8,128)(2,1)}, u32[]{:S(2)}, u32[]{:S(2)}) collective-permute-start(bf16[528,512]{1,0:T(8,128)(2,1)} %pad_maximum_fusion.2), channel_id=1, source_target_pairs={{8,0},{9,1},{10,2},{11,3},{24,16},{25,17},{26,18},{27,19}} | collective-permute-start | bytes 1622024 | tf_op jit(solution)/shard_map/ppermute | solution.py:127
  10.7 27.1 %collective-permute-start.7 = (bf16[528,512]{1,0:T(8,128)(2,1)}, bf16[528,512]{1,0:T(8,128)(2,1)}, u32[]{:S(2)}, u32[]{:S(2)}) collective-permute-start(bf16[528,512]{1,0:T(8,128)(2,1)} %pad_maximum_fusion.2), channel_id=1, source_target_pairs={{4,0},{8,4},{12,8},{5,1},{9,5},{13,9},{6,2},{10,6},{14,10},{7,3},{... | collective-permute-start | bytes 1622024 | tf_op jit(solution)/shard_map/ppermute | solution.py:127
  12.0 20.8 %collective-permute-start.1 = (bf16[528,512]{1,0:T(8,128)(2,1)}, bf16[528,512]{1,0:T(8,128)(2,1)S(1)}, u32[]{:S(2)}, u32[]{:S(2)}) collective-permute-start(bf16[528,512]{1,0:T(8,128)(2,1)} %pad_maximum_fusion.2), channel_id=1, source_target_pairs={{0,4},{4,8},{8,12},{1,5},{5,9},{9,13},{2,6},{6,10},{10,14},{3,7},{... | collective-permute-start | bytes 1622024 | tf_op jit(solution)/shard_map/ppermute | solution.py:121
  16.6 15.6 %collective-permute-start = (bf16[528,512]{1,0:T(8,128)(2,1)}, bf16[528,512]{1,0:T(8,128)(2,1)S(1)}, u32[]{:S(2)}, u32[]{:S(2)}) collective-permute-start(bf16[528,512]{1,0:T(8,128)(2,1)} %pad_maximum_fusion.2), channel_id=1, source_target_pairs={{0,1},{1,0},{2,3},{3,2},{4,5},{5,4},{6,7},{7,6},{8,9},{9,8},{10,11... | collective-permute-start | bytes 1622024 | tf_op jit(solution)/shard_map/ppermute | solution.py:148
  30.8 8.3 %collective-permute-start.5 = (bf16[528,512]{1,0:T(8,128)(2,1)S(1)}, bf16[528,512]{1,0:T(8,128)(2,1)S(1)}, u32[]{:S(2)}, u32[]{:S(2)}) collective-permute-start(bf16[528,512]{1,0:T(8,128)(2,1)S(1)} %broadcast_select_fusion.1), channel_id=1, source_target_pairs={{0,1},{1,0},{2,3},{3,2},{4,5},{5,4},{6,7},{7,6},{8,9},{9,8},{10,11... | collective-permute-start | bytes 1622024 | tf_op jit(solution)/shard_map/ppermute | solution.py:148
  31.3 6.5 %collective-permute-start.6 = (bf16[528,512]{1,0:T(8,128)(2,1)S(1)}, bf16[528,512]{1,0:T(8,128)(2,1)S(1)}, u32[]{:S(2)}, u32[]{:S(2)}) collective-permute-start(bf16[528,512]{1,0:T(8,128)(2,1)S(1)} %collective-permute-done.3), channel_id=1, source_target_pairs={{8,12},{9,13},{10,14},{11,15},{24,28},{25,29},{26,30},{27,31}} | collective-permute-start | bytes 1622024 | tf_op jit(solution)/shard_map/ppermute | solution.py:119
  32.3 6.6 %copy-start.1 = (bf16[528,512]{1,0:T(8,128)(2,1)}, bf16[528,512]{1,0:T(8,128)(2,1)S(1)}, u32[]{:S(2)}) copy-start(bf16[528,512]{1,0:T(8,128)(2,1)S(1)} %broadcast_select_fusion.6) | copy-start | bytes 1622020
  32.9 6.3 %collective-permute-start.2 = (bf16[528,512]{1,0:T(8,128)(2,1)S(1)}, bf16[528,512]{1,0:T(8,128)(2,1)S(1)}, u32[]{:S(2)}, u32[]{:S(2)}) collective-permute-start(bf16[528,512]{1,0:T(8,128)(2,1)S(1)} %broadcast_select_fusion.2), channel_id=1, source_target_pairs={{0,1},{1,0},{2,3},{3,2},{4,5},{5,4},{6,7},{7,6},{8,9},{9,8},{10,11... | collective-permute-start | bytes 1622024 | tf_op jit(solution)/shard_map/ppermute | solution.py:148
  38.9 2.0 %collective-permute-start.8 = (bf16[528,512]{1,0:T(8,128)(2,1)S(1)}, bf16[528,512]{1,0:T(8,128)(2,1)S(1)}, u32[]{:S(2)}, u32[]{:S(2)}) collective-permute-start(bf16[528,512]{1,0:T(8,128)(2,1)S(1)} %broadcast_select_fusion), channel_id=1, source_target_pairs={{0,1},{1,0},{2,3},{3,2},{4,5},{5,4},{6,7},{7,6},{8,9},{9,8},{10,11... | collective-permute-start | bytes 1622024 | tf_op jit(solution)/shard_map/ppermute | solution.py:148
  39.1 0.8 copy-start
  39.2 0.9 copy-start.2
  39.9 1.1 %copy-start.5 = (s32[4]{0:T(128)S(1)}, s32[4]{0:T(128)}, u32[]{:S(2)}) copy-start(s32[4]{0:T(128)} %param.17) | copy-start | bytes 52
  40.1 1.8 %slice-start = ((bf16[528,512]{1,0:T(8,128)(2,1)}), bf16[512,512]{1,0:T(8,128)(2,1)S(1)}, s32[]{:S(2)}) async-start(bf16[528,512]{1,0:T(8,128)(2,1)} %copy-done), calls=%async_computation | async-start | bytes 1048576 | tf_op jit(solution)/shard_map/slice | solution.py:154
  40.1 1.8 %slice-start.1 = ((bf16[528,512]{1,0:T(8,128)(2,1)}), bf16[512,512]{1,0:T(8,128)(2,1)S(1)}, s32[]{:S(2)}) async-start(bf16[528,512]{1,0:T(8,128)(2,1)} %copy-done.1), calls=%async_computation.1 | async-start | bytes 1048576 | tf_op jit(solution)/shard_map/slice | solution.py:154
  40.9 1.1 %slice-start.2 = ((bf16[528,512]{1,0:T(8,128)(2,1)}), bf16[512,512]{1,0:T(8,128)(2,1)S(1)}, s32[]{:S(2)}) async-start(bf16[528,512]{1,0:T(8,128)(2,1)} %copy-done.2), calls=%async_computation.2 | async-start | bytes 1048576 | tf_op jit(solution)/shard_map/slice | solution.py:154
  67.4 10.5 %copy-start.4 = (f32[1,2048]{1,0:T(1,128)S(1)}, f32[1,2048]{1,0:T(1,128)}, u32[]{:S(2)}) copy-start(f32[1,2048]{1,0:T(1,128)} %get-tuple-element.18) | copy-start | bytes 24580
  75.8 33.9 %collective-permute-start.9 = (bf16[128,2048]{1,0:T(8,128)(2,1)S(1)}, bf16[128,2048]{1,0:T(8,128)(2,1)S(1)}, u32[]{:S(2)}, u32[]{:S(2)}) collective-permute-start(bf16[128,2048]{1,0:T(8,128)(2,1)S(1)} %dynamic-slice_convert_fusion), channel_id=1, source_target_pairs={{0,2},{2,0},{1,3},{3,1},{4,6},{6,4},{5,7},{7,5},{8,10},{10,8},{9,1... | collective-permute-start | bytes 1572872 | tf_op jit(solution)/shard_map/ppermute | solution.py:229
  80.3 1.2 %collective-permute-start.10 = (f32[2080]{0:T(1024)S(1)}, f32[2080]{0:T(1024)S(1)}, u32[]{:S(2)}, u32[]{:S(2)}) collective-permute-start(f32[2080]{0:T(1024)S(1)} %pad_maximum_fusion.3), channel_id=1, source_target_pairs={{0,1},{1,0},{2,3},{3,2},{4,5},{5,4},{6,7},{7,6},{8,9},{9,8},{10,11... | collective-permute-start | bytes 24968 | tf_op jit(solution)/shard_map/ppermute | solution.py:172
  81.5 10.2 %collective-permute-start.11 = (f32[2080]{0:T(1024)S(1)}, f32[2080]{0:T(1024)S(1)}, u32[]{:S(2)}, u32[]{:S(2)}) collective-permute-start(f32[2080]{0:T(1024)S(1)} %fusion.11), channel_id=1, source_target_pairs={{0,4},{4,0},{8,12},{12,8},{1,5},{5,1},{9,13},{13,9},{2,6},{6,2},{1... | collective-permute-start | bytes 24968 | tf_op jit(solution)/shard_map/ppermute | solution.py:172
  91.7 13.0 %collective-permute-start.12 = (f32[2080]{0:T(1024)S(1)}, f32[2080]{0:T(1024)S(1)}, u32[]{:S(2)}, u32[]{:S(2)}) collective-permute-start(f32[2080]{0:T(1024)S(1)} %add.97), channel_id=1, source_target_pairs={{0,8},{4,12},{8,0},{12,4},{1,9},{5,13},{9,1},{13,5},{2,10},{6,14},... | collective-permute-start | bytes 24968 | tf_op jit(solution)/shard_map/ppermute | solution.py:172
  104.7 3.7 %collective-permute-start.13 = (f32[2080]{0:T(1024)S(1)}, f32[2080]{0:T(1024)S(1)}, u32[]{:S(2)}, u32[]{:S(2)}) collective-permute-start(f32[2080]{0:T(1024)S(1)} %add.98), channel_id=1, source_target_pairs={{0,2},{2,0},{1,3},{3,1},{4,6},{6,4},{5,7},{7,5},{8,10},{10,8},{9,1... | collective-permute-start | bytes 24968 | tf_op jit(solution)/shard_map/ppermute | solution.py:172

commit v10 on v9

--- a/solution.py
+++ b/solution.py
@@ -201,6 +201,9 @@
     kept = jnp.where(
         jnp.any(seg_shift[:, None] == masked_segments[None, :], axis=1), 0.0, 1.0
     ).astype(jnp.float32)[None, :]
+    onehot = (
+        seg_shift[:, None] == jnp.arange(SEG_DEV * ctx_count, dtype=jnp.int32)[None, :]
+    ).astype(jnp.float32)
 
     grad_masked = jnp.where(response[:, None] > 0, cotangent, jnp.zeros_like(cotangent))
     grad_out = jnp.dot(grad_masked, out_weight.T, preferred_element_type=jnp.float32).astype(
@@ -212,23 +215,21 @@
 
     inverse = (ctx_at - jnp.arange(ctx_count, dtype=jnp.int32)) % ctx_count
     attr_abs = attr.reshape(ctx_count, key_count)[inverse].reshape(-1)
-    seg_abs = seg_shift.reshape(ctx_count, key_count)[inverse].reshape(-1)
-    onehot = (
-        seg_abs[:, None] == jnp.arange(SEG_DEV * ctx_count, dtype=jnp.int32)[None, :]
-    ).astype(jnp.float32)
-    seg_part = jnp.dot(attr_abs, onehot, precision=lax.Precision.HIGHEST)
+    seg_part = jnp.dot(attr[0], onehot, precision=lax.Precision.HIGHEST)
     summed = butterfly_sum(jnp.concatenate([attr_abs, seg_part]), ("rep", "ctx", "head"))
     attr_all = summed[:context_len]
     segment_attr = summed[context_len:]
 
-    projected = jnp.dot(delta, out_weight, preferred_element_type=jnp.float32)
     if head_count == 2:
-        cols = projected.shape[1] // 2
-        keep = lax.dynamic_slice_in_dim(projected, head_at * cols, cols, 1)
-        send = lax.dynamic_slice_in_dim(projected, (1 - head_at) * cols, cols, 1)
+        cols = out_weight.shape[1] // 2
+        send_w = lax.dynamic_slice_in_dim(out_weight, (1 - head_at) * cols, cols, 1)
+        send = jnp.dot(delta, send_w, preferred_element_type=jnp.float32)
         got = lax.ppermute(send.astype(jnp.bfloat16), "head", [(0, 1), (1, 0)])
+        keep_w = lax.dynamic_slice_in_dim(out_weight, head_at * cols, cols, 1)
+        keep = jnp.dot(delta, keep_w, preferred_element_type=jnp.float32)
         patch_effect = (keep + got.astype(jnp.float32)).astype(jnp.bfloat16)
     else:
+        projected = jnp.dot(delta, out_weight, preferred_element_type=jnp.float32)
         patch_effect = lax.psum_scatter(
             projected.astype(jnp.bfloat16), "head", scatter_dimension=1, tiled=True
         )

time: 111 us -> 109 us (0.982)
  other arithmetic: 10.2 us -> 7.75 us
  matrix products: 21.1 us -> 23.5 us
  local copies, waits for them, and re-layouts: 4.62 us -> 3.1 us
    select_n x3, other arithmetic: 2.25 us -> 0.15 us  [relay_gather(): parts.append(jnp.where(k <= ctx_at, forward[k], backward[n - k]))]
    dot_general x2 -> x3, matrix products: 8.87 us -> 10.9 us  [the longest x1 5.48 us: local(): keep = jnp.dot(delta, keep_w, preferred_element_type=jnp.float32)]
  transfers between devices with their start and end apart: 14 -> 14, of which waited for: 7 -> 7; matrix products, arithmetic and copies ran while one was open for 18% -> 17% of each run, Pallas kernels for 0% -> 0%
where the time goes in v10:
time: 109 us
  starting transfers between devices  35.8 us (33%)
  matrix products  23.5 us (22%)
  Pallas kernels  23.2 us (21%)
  waiting for transfers between devices  14.3 us (13%)
  other arithmetic  7.75 us (7%)
  local copies, waits for them, and re-layouts  3.1 us (3%)
    pallas_call x1, Pallas kernels, fused_attention(): pl.pallas_call(functools.partial(attention_kernel, tq=tq, hp=hp), grid_sp...  23.2 us
    ppermute x4, starting transfers between devices, butterfly_sum(): total = total + lax.ppermute(total, axis, [(i, i ^ bit) for i in range(n)])  19.5 us
    dot_general x1, matrix products, local(): jnp.dot(grad_masked, out_weight.T, preferred_element_type=jnp.float32)  12.6 us
    ppermute x2, starting transfers between devices, relay_gather(): forward.append(lax.ppermute(payload, 'ctx', fwd) if fwd else zero)  10.5 us
    ppermute x4, waiting for transfers between devices, butterfly_sum(): total = total + lax.ppermute(total, axis, [(i, i ^ bit) for i in range(n)])  7.68 us
    dot_general x1, matrix products, local(): keep = jnp.dot(delta, keep_w, preferred_element_type=jnp.float32)  5.48 us
    dot_general x1, matrix products, local(): send = jnp.dot(delta, send_w, preferred_element_type=jnp.float32)  4.87 us
    ppermute x2, waiting for transfers between devices, relay_gather(): backward.append(lax.ppermute(payload, 'ctx', bwd) if bwd else zero)  4.61 us
  transfers between devices with their start and end apart: 14, of which 7 were waited for; matrix products, arithmetic and copies ran while one was open for 17% of the time, Pallas kernels for 0%

profile of v10, /device:TPU:0, one launch (start us, length us, event | category | flops | bytes accessed | tf_op | source)
XLA Modules:
  0.0 108.6 jit_solution(18256395855004559573)
XLA Ops:
  0.6 0.7 convert_element_type.23
  1.4 1.1 %broadcast_select_fusion.7 = bf16[512,512]{1,0:T(8,128)(2,1)S(1)} fusion(bf16[512,512]{1,0:T(8,128)(2,1)} %param.11, bf16[512,512]{1,0:T(8,128)(2,1)} %param.12, pred[]{:T(512)S(6)} %eq.17), kind=kLoop, calls=%fused_computation.30 | loop fusion | flops 262144 | bytes 1572865 | tf_op jit(solution)/shard_map/jit(_where)/select_n | solution.py:143
  2.5 0.8 pad_maximum_fusion.2
  3.3 6.0 %collective-permute-start.3 = (bf16[528,512]{1,0:T(8,128)(2,1)}, bf16[528,512]{1,0:T(8,128)(2,1)S(1)}, u32[]{:S(2)}, u32[]{:S(2)}) collective-permute-start(bf16[528,512]{1,0:T(8,128)(2,1)} %pad_maximum_fusion.2), channel_id=1, source_target_pairs={{0,8},{4,12},{1,9},{5,13},{2,10},{6,14},{3,11},{7,15},{16,24},{20,... | collective-permute-start | bytes 1622024 | tf_op jit(solution)/shard_map/ppermute | solution.py:121
  9.3 1.3 %collective-permute-start.4 = (bf16[528,512]{1,0:T(8,128)(2,1)}, bf16[528,512]{1,0:T(8,128)(2,1)S(1)}, u32[]{:S(2)}, u32[]{:S(2)}) collective-permute-start(bf16[528,512]{1,0:T(8,128)(2,1)} %pad_maximum_fusion.2), channel_id=1, source_target_pairs={{8,0},{9,1},{10,2},{11,3},{24,16},{25,17},{26,18},{27,19}} | collective-permute-start | bytes 1622024 | tf_op jit(solution)/shard_map/ppermute | solution.py:127
  10.6 1.3 %collective-permute-start.7 = (bf16[528,512]{1,0:T(8,128)(2,1)}, bf16[528,512]{1,0:T(8,128)(2,1)S(1)}, u32[]{:S(2)}, u32[]{:S(2)}) collective-permute-start(bf16[528,512]{1,0:T(8,128)(2,1)} %pad_maximum_fusion.2), channel_id=1, source_target_pairs={{4,0},{8,4},{12,8},{5,1},{9,5},{13,9},{6,2},{10,6},{14,10},{7,3},{... | collective-permute-start | bytes 1622024 | tf_op jit(solution)/shard_map/ppermute | solution.py:127
  11.9 4.6 %collective-permute-start.1 = (bf16[528,512]{1,0:T(8,128)(2,1)}, bf16[528,512]{1,0:T(8,128)(2,1)S(1)}, u32[]{:S(2)}, u32[]{:S(2)}) collective-permute-start(bf16[528,512]{1,0:T(8,128)(2,1)} %pad_maximum_fusion.2), channel_id=1, source_target_pairs={{0,4},{4,8},{8,12},{1,5},{5,9},{9,13},{2,6},{6,10},{10,14},{3,7},{... | collective-permute-start | bytes 1622024 | tf_op jit(solution)/shard_map/ppermute | solution.py:121
  16.5 0.1 collective-permute-start
  16.5 0.7 broadcast_compare_fusion
  17.2 12.6 %convolution_convert_fusion.do_ref = bf16[128,2048]{1,0:T(8,128)(2,1)} fusion(bf16[2048,4096]{1,0:T(8,128)(2,1)} %param.13, bf16[128,4096]{1,0:T(8,128)(2,1)} %param.14, pred[128]{0:T(512)(128)(4,1)S(1)} %broadcast_compare_fusion), kind=kOutput, calls=%fused_computation.6 | convolution fusion | flops 2148270080 | bytes 18350208 | tf_op jit(solution)/shard_map/dot_general | solution.py:209
  29.8 0.1 add_bitcast_fusion
  29.9 0.6 copy.11
  30.5 0.0 collective-permute-done.3
  30.5 0.0 collective-permute-done.4
  30.5 0.1 broadcast_select_fusion.1
  30.6 0.6 collective-permute-start.5
  31.1 0.9 collective-permute-start.6
  32.0 0.0 collective-permute-done
  32.0 0.1 broadcast_select_fusion.6
  32.2 0.0 copy-start
  32.2 0.5 collective-permute-done.1
  32.8 0.1 collective-permute-start.2
  32.8 0.1 fusion.10
  33.0 4.6 %collective-permute-done.7 = bf16[528,512]{1,0:T(8,128)(2,1)S(1)} collective-permute-done((bf16[528,512]{1,0:T(8,128)(2,1)}, bf16[528,512]{1,0:T(8,128)(2,1)S(1)}, u32[]{:S(2)}, u32[]{:S(2)}) %collective-permute-start.7) | collective-permute-done | bytes 540704 | tf_op jit(solution)/shard_map/ppermute | solution.py:127
  37.6 0.0 collective-permute-done.6
  37.6 0.1 broadcast_select_fusion
  37.7 0.1 collective-permute-start.8
  37.8 0.0 collective-permute-done.5
  37.8 0.1 broadcast_select_fusion.4
  37.8 0.0 collective-permute-done.2
  37.9 0.1 broadcast_select_fusion.5
  37.9 0.0 copy-done
  37.9 0.0 copy-start.3
  38.0 0.0 slice-start
  38.1 0.1 slice_select_fusion.1
  38.1 0.1 slice_select_fusion.2
  38.2 1.5 %collective-permute-done.8 = bf16[528,512]{1,0:T(8,128)(2,1)S(1)} collective-permute-done((bf16[528,512]{1,0:T(8,128)(2,1)S(1)}, bf16[528,512]{1,0:T(8,128)(2,1)S(1)}, u32[]{:S(2)}, u32[]{:S(2)}) %collective-permute-start.8) | collective-permute-done | bytes 540704 | tf_op jit(solution)/shard_map/ppermute | solution.py:148
  39.7 0.1 broadcast_select_fusion.3
  39.8 0.0 copy-done.3
  39.8 0.1 compare_reduce_fusion
  39.9 0.6 broadcast_select_fusion.8
  40.5 0.1 slice_select_fusion
  40.6 0.0 slice-done
  40.6 2.2 %pad_maximum_fusion = (bf16[2048,512]{1,0:T(8,128)(2,1)}, bf16[2048,512]{1,0:T(8,128)(2,1)}) fusion(bf16[512,512]{1,0:T(8,128)(2,1)S(1)} %slice.84, bf16[512,512]{1,0:T(8,128)(2,1)S(1)} %slice.83, bf16[512,512]{1,0:T(8,128)(2,1)S(1)} %slice.82, bf16[512,512]{1,0:T(8,128)(2,1)S(1)} %slice-done, bf16[512,512]{1,0:T(8,128)(2,1)S(1)} %slice_select_fusion, ...), kind=kLoop, calls=%fused_computation.7 | loop fusion | flops 16777216 | bytes 8388608 | tf_op jit(solution)/shard_map/concatenate | solution.py:154
  42.8 23.2 %shard_map.103 = (bf16[128,2048]{1,0:T(8,128)(2,1)}, f32[1,2048]{1,0:T(1,128)}) custom-call(s32[1]{0:T(128)} %bitcast.base_ref, s32[1,2048]{1,0:T(1,128)} %bitcast.23, bf16[128,2048]{1,0:T(8,128)(2,1)} %q_ref.1, bf16[2048,512]{1,0:T(8,128)(2,1)} %get-tuple-element.19.k_ref, bf16[2048,512]{1,0:T(8,128)(2,1)} %get-tuple-element.20.v_ref, f32[1,2048]{1,0:T(1,128)} %bitcast.22, ...), custom_call_target="tpu_custom_call" | custom-call | flops 4294967296 | bytes 5775360 | tf_op jit(solution)/shard_map/pallas_call | solution.py:82
  65.9 0.0 copy-start.1
  65.9 4.9 %fusion.4 = bf16[128,2048]{1,0:T(8,128)(2,1)S(1)} fusion(bf16[128,2048]{1,0:T(8,128)(2,1)} %get-tuple-element.17, bf16[2048,4096]{1,0:T(8,128)(2,1)} %param.13, s32[]{:T(128)S(6)} %select_n.142), kind=kOutput, calls=%fused_computation.5 | convolution fusion | flops 1074003968 | bytes 9437188 | tf_op jit(solution)/shard_map/dot_general | solution.py:226
  70.8 1.6 %collective-permute-start.9 = (bf16[128,2048]{1,0:T(8,128)(2,1)S(1)}, bf16[128,2048]{1,0:T(8,128)(2,1)S(1)}, u32[]{:S(2)}, u32[]{:S(2)}) collective-permute-start(bf16[128,2048]{1,0:T(8,128)(2,1)S(1)} %fusion.4), channel_id=1, source_target_pairs={{0,2},{2,0},{1,3},{3,1},{4,6},{6,4},{5,7},{7,5},{8,10},{10,8},{9,1... | collective-permute-start | bytes 1572872 | tf_op jit(solution)/shard_map/ppermute | solution.py:227
  72.4 0.5 broadcast.150
  72.9 0.7 reduce.13
  73.6 0.6 gather_fusion
  74.2 0.6 convolution_bitcast_fusion
  74.7 0.1 collective-permute-start.10
  74.8 1.2 %collective-permute-done.10 = f32[2080]{0:T(1024)S(1)} collective-permute-done((f32[2080]{0:T(1024)S(1)}, f32[2080]{0:T(1024)S(1)}, u32[]{:S(2)}, u32[]{:S(2)}) %collective-permute-start.10) | collective-permute-done | bytes 8352 | tf_op jit(solution)/shard_map/ppermute | solution.py:172
  76.0 8.9 %collective-permute-start.11 = (f32[2080]{0:T(1024)S(1)}, f32[2080]{0:T(1024)S(1)}, u32[]{:S(2)}, u32[]{:S(2)}) collective-permute-start(f32[2080]{0:T(1024)S(1)} %fusion.23), channel_id=1, source_target_pairs={{0,4},{4,0},{8,12},{12,8},{1,5},{5,1},{9,13},{13,9},{2,6},{6,2},{1... | collective-permute-start | bytes 24968 | tf_op jit(solution)/shard_map/ppermute | solution.py:172
  84.9 1.7 %collective-permute-done.11 = f32[2080]{0:T(1024)S(1)} collective-permute-done((f32[2080]{0:T(1024)S(1)}, f32[2080]{0:T(1024)S(1)}, u32[]{:S(2)}, u32[]{:S(2)}) %collective-permute-start.11) | collective-permute-done | bytes 8352 | tf_op jit(solution)/shard_map/ppermute | solution.py:172
  86.6 9.9 %collective-permute-start.12 = (f32[2080]{0:T(1024)S(1)}, f32[2080]{0:T(1024)S(1)}, u32[]{:S(2)}, u32[]{:S(2)}) collective-permute-start(f32[2080]{0:T(1024)S(1)} %add.96), channel_id=1, source_target_pairs={{0,8},{4,12},{8,0},{12,4},{1,9},{5,13},{9,1},{13,5},{2,10},{6,14},... | collective-permute-start | bytes 24968 | tf_op jit(solution)/shard_map/ppermute | solution.py:172
  96.5 1.7 %collective-permute-done.12 = f32[2080]{0:T(1024)S(1)} collective-permute-done((f32[2080]{0:T(1024)S(1)}, f32[2080]{0:T(1024)S(1)}, u32[]{:S(2)}, u32[]{:S(2)}) %collective-permute-start.12) | collective-permute-done | bytes 8352 | tf_op jit(solution)/shard_map/ppermute | solution.py:172
  98.2 0.5 collective-permute-start.13
  98.8 3.2 %collective-permute-done.13 = f32[2080]{0:T(1024)S(1)} collective-permute-done((f32[2080]{0:T(1024)S(1)}, f32[2080]{0:T(1024)S(1)}, u32[]{:S(2)}, u32[]{:S(2)}) %collective-permute-start.13) | collective-permute-done | bytes 8352 | tf_op jit(solution)/shard_map/ppermute | solution.py:172
  101.9 0.5 slice.99
  102.4 0.7 dynamic_slice.11
  103.1 0.0 collective-permute-done.9
  103.1 5.5 %add_convert_fusion = bf16[128,2048]{1,0:T(8,128)(2,1)} fusion(bf16[128,2048]{1,0:T(8,128)(2,1)S(1)} %collective-permute-done.9, bf16[128,2048]{1,0:T(8,128)(2,1)S(1)} %copy-done.1, bf16[2048,4096]{1,0:T(8,128)(2,1)} %param.13, s32[]{:T(128)S(6)} %select_n.141), kind=kOutput, calls=%fused_computation.11 | convolution fusion | flops 1074528256 | bytes 9961476 | tf_op jit(solution)/shard_map/dot_general | solution.py:229
  (25 shorter events, 0.4 us)
Async XLA Ops:
  3.3 27.2 %collective-permute-start.3 = (bf16[528,512]{1,0:T(8,128)(2,1)}, bf16[528,512]{1,0:T(8,128)(2,1)S(1)}, u32[]{:S(2)}, u32[]{:S(2)}) collective-permute-start(bf16[528,512]{1,0:T(8,128)(2,1)} %pad_maximum_fusion.2), channel_id=1, source_target_pairs={{0,8},{4,12},{1,9},{5,13},{2,10},{6,14},{3,11},{7,15},{16,24},{20,... | collective-permute-start | bytes 1622024 | tf_op jit(solution)/shard_map/ppermute | solution.py:121
  9.3 21.2 %collective-permute-start.4 = (bf16[528,512]{1,0:T(8,128)(2,1)}, bf16[528,512]{1,0:T(8,128)(2,1)S(1)}, u32[]{:S(2)}, u32[]{:S(2)}) collective-permute-start(bf16[528,512]{1,0:T(8,128)(2,1)} %pad_maximum_fusion.2), channel_id=1, source_target_pairs={{8,0},{9,1},{10,2},{11,3},{24,16},{25,17},{26,18},{27,19}} | collective-permute-start | bytes 1622024 | tf_op jit(solution)/shard_map/ppermute | solution.py:127
  10.6 27.0 %collective-permute-start.7 = (bf16[528,512]{1,0:T(8,128)(2,1)}, bf16[528,512]{1,0:T(8,128)(2,1)S(1)}, u32[]{:S(2)}, u32[]{:S(2)}) collective-permute-start(bf16[528,512]{1,0:T(8,128)(2,1)} %pad_maximum_fusion.2), channel_id=1, source_target_pairs={{4,0},{8,4},{12,8},{5,1},{9,5},{13,9},{6,2},{10,6},{14,10},{7,3},{... | collective-permute-start | bytes 1622024 | tf_op jit(solution)/shard_map/ppermute | solution.py:127
  11.9 20.8 %collective-permute-start.1 = (bf16[528,512]{1,0:T(8,128)(2,1)}, bf16[528,512]{1,0:T(8,128)(2,1)S(1)}, u32[]{:S(2)}, u32[]{:S(2)}) collective-permute-start(bf16[528,512]{1,0:T(8,128)(2,1)} %pad_maximum_fusion.2), channel_id=1, source_target_pairs={{0,4},{4,8},{8,12},{1,5},{5,9},{9,13},{2,6},{6,10},{10,14},{3,7},{... | collective-permute-start | bytes 1622024 | tf_op jit(solution)/shard_map/ppermute | solution.py:121
  16.5 15.5 %collective-permute-start = (bf16[528,512]{1,0:T(8,128)(2,1)}, bf16[528,512]{1,0:T(8,128)(2,1)S(1)}, u32[]{:S(2)}, u32[]{:S(2)}) collective-permute-start(bf16[528,512]{1,0:T(8,128)(2,1)} %pad_maximum_fusion.2), channel_id=1, source_target_pairs={{0,1},{1,0},{2,3},{3,2},{4,5},{5,4},{6,7},{7,6},{8,9},{9,8},{10,11... | collective-permute-start | bytes 1622024 | tf_op jit(solution)/shard_map/ppermute | solution.py:148
  30.6 7.2 %collective-permute-start.5 = (bf16[528,512]{1,0:T(8,128)(2,1)S(1)}, bf16[528,512]{1,0:T(8,128)(2,1)S(1)}, u32[]{:S(2)}, u32[]{:S(2)}) collective-permute-start(bf16[528,512]{1,0:T(8,128)(2,1)S(1)} %broadcast_select_fusion.1), channel_id=1, source_target_pairs={{0,1},{1,0},{2,3},{3,2},{4,5},{5,4},{6,7},{7,6},{8,9},{9,8},{10,11... | collective-permute-start | bytes 1622024 | tf_op jit(solution)/shard_map/ppermute | solution.py:148
  31.1 6.5 %collective-permute-start.6 = (bf16[528,512]{1,0:T(8,128)(2,1)S(1)}, bf16[528,512]{1,0:T(8,128)(2,1)S(1)}, u32[]{:S(2)}, u32[]{:S(2)}) collective-permute-start(bf16[528,512]{1,0:T(8,128)(2,1)S(1)} %collective-permute-done.3), channel_id=1, source_target_pairs={{8,12},{9,13},{10,14},{11,15},{24,28},{25,29},{26,30},{27,31}} | collective-permute-start | bytes 1622024 | tf_op jit(solution)/shard_map/ppermute | solution.py:119
  32.2 5.8 %copy-start = (bf16[528,512]{1,0:T(8,128)(2,1)}, bf16[528,512]{1,0:T(8,128)(2,1)S(1)}, u32[]{:S(2)}) copy-start(bf16[528,512]{1,0:T(8,128)(2,1)S(1)} %broadcast_select_fusion.6) | copy-start | bytes 1622020
  32.8 5.1 %collective-permute-start.2 = (bf16[528,512]{1,0:T(8,128)(2,1)S(1)}, bf16[528,512]{1,0:T(8,128)(2,1)S(1)}, u32[]{:S(2)}, u32[]{:S(2)}) collective-permute-start(bf16[528,512]{1,0:T(8,128)(2,1)S(1)} %broadcast_select_fusion.2), channel_id=1, source_target_pairs={{0,1},{1,0},{2,3},{3,2},{4,5},{5,4},{6,7},{7,6},{8,9},{9,8},{10,11... | collective-permute-start | bytes 1622024 | tf_op jit(solution)/shard_map/ppermute | solution.py:148
  37.7 2.0 %collective-permute-start.8 = (bf16[528,512]{1,0:T(8,128)(2,1)S(1)}, bf16[528,512]{1,0:T(8,128)(2,1)S(1)}, u32[]{:S(2)}, u32[]{:S(2)}) collective-permute-start(bf16[528,512]{1,0:T(8,128)(2,1)S(1)} %broadcast_select_fusion), channel_id=1, source_target_pairs={{0,1},{1,0},{2,3},{3,2},{4,5},{5,4},{6,7},{7,6},{8,9},{9,8},{10,11... | collective-permute-start | bytes 1622024 | tf_op jit(solution)/shard_map/ppermute | solution.py:148
  37.9 1.9 %copy-start.3 = (s32[4]{0:T(128)S(1)}, s32[4]{0:T(128)}, u32[]{:S(2)}) copy-start(s32[4]{0:T(128)} %param.17) | copy-start | bytes 52
  38.0 2.6 %slice-start = ((bf16[528,512]{1,0:T(8,128)(2,1)}), bf16[512,512]{1,0:T(8,128)(2,1)S(1)}, s32[]{:S(2)}) async-start(bf16[528,512]{1,0:T(8,128)(2,1)} %copy-done), calls=%async_computation | async-start | bytes 1048576 | tf_op jit(solution)/shard_map/slice | solution.py:154
  65.9 7.0 %copy-start.2 = (f32[1,2048]{1,0:T(1,128)S(1)}, f32[1,2048]{1,0:T(1,128)}, u32[]{:S(2)}) copy-start(f32[1,2048]{1,0:T(1,128)} %get-tuple-element.18) | copy-start | bytes 24580
  65.9 37.2 %copy-start.1 = (bf16[128,2048]{1,0:T(8,128)(2,1)S(1)}, bf16[128,2048]{1,0:T(8,128)(2,1)}, u32[]{:S(2)}) copy-start(bf16[128,2048]{1,0:T(8,128)(2,1)} %get-tuple-element.17) | copy-start | bytes 1572868
  70.8 32.3 %collective-permute-start.9 = (bf16[128,2048]{1,0:T(8,128)(2,1)S(1)}, bf16[128,2048]{1,0:T(8,128)(2,1)S(1)}, u32[]{:S(2)}, u32[]{:S(2)}) collective-permute-start(bf16[128,2048]{1,0:T(8,128)(2,1)S(1)} %fusion.4), channel_id=1, source_target_pairs={{0,2},{2,0},{1,3},{3,1},{4,6},{6,4},{5,7},{7,5},{8,10},{10,8},{9,1... | collective-permute-start | bytes 1572872 | tf_op jit(solution)/shard_map/ppermute | solution.py:227
  74.7 1.2 %collective-permute-start.10 = (f32[2080]{0:T(1024)S(1)}, f32[2080]{0:T(1024)S(1)}, u32[]{:S(2)}, u32[]{:S(2)}) collective-permute-start(f32[2080]{0:T(1024)S(1)} %pad_maximum_fusion.3), channel_id=1, source_target_pairs={{0,1},{1,0},{2,3},{3,2},{4,5},{5,4},{6,7},{7,6},{8,9},{9,8},{10,11... | collective-permute-start | bytes 24968 | tf_op jit(solution)/shard_map/ppermute | solution.py:172
  76.0 10.6 %collective-permute-start.11 = (f32[2080]{0:T(1024)S(1)}, f32[2080]{0:T(1024)S(1)}, u32[]{:S(2)}, u32[]{:S(2)}) collective-permute-start(f32[2080]{0:T(1024)S(1)} %fusion.23), channel_id=1, source_target_pairs={{0,4},{4,0},{8,12},{12,8},{1,5},{5,1},{9,13},{13,9},{2,6},{6,2},{1... | collective-permute-start | bytes 24968 | tf_op jit(solution)/shard_map/ppermute | solution.py:172
  86.6 11.6 %collective-permute-start.12 = (f32[2080]{0:T(1024)S(1)}, f32[2080]{0:T(1024)S(1)}, u32[]{:S(2)}, u32[]{:S(2)}) collective-permute-start(f32[2080]{0:T(1024)S(1)} %add.96), channel_id=1, source_target_pairs={{0,8},{4,12},{8,0},{12,4},{1,9},{5,13},{9,1},{13,5},{2,10},{6,14},... | collective-permute-start | bytes 24968 | tf_op jit(solution)/shard_map/ppermute | solution.py:172
  98.2 3.7 %collective-permute-start.13 = (f32[2080]{0:T(1024)S(1)}, f32[2080]{0:T(1024)S(1)}, u32[]{:S(2)}, u32[]{:S(2)}) collective-permute-start(f32[2080]{0:T(1024)S(1)} %add.97), channel_id=1, source_target_pairs={{0,2},{2,0},{1,3},{3,1},{4,6},{6,4},{5,7},{7,5},{8,10},{10,8},{9,1... | collective-permute-start | bytes 24968 | tf_op jit(solution)/shard_map/ppermute | solution.py:172

commit v11 on v10

--- a/solution.py
+++ b/solution.py
@@ -226,7 +226,7 @@
         send = jnp.dot(delta, send_w, preferred_element_type=jnp.float32)
         got = lax.ppermute(send.astype(jnp.bfloat16), "head", [(0, 1), (1, 0)])
         keep_w = lax.dynamic_slice_in_dim(out_weight, head_at * cols, cols, 1)
-        keep = jnp.dot(delta, keep_w, preferred_element_type=jnp.float32)
+        keep = lax.optimization_barrier(jnp.dot(delta, keep_w, preferred_element_type=jnp.float32))
         patch_effect = (keep + got.astype(jnp.float32)).astype(jnp.bfloat16)
     else:
         projected = jnp.dot(delta, out_weight, preferred_element_type=jnp.float32)

time: 109 us -> 106 us (0.972)
  waiting for transfers between devices: 14.3 us -> 10.1 us
  other arithmetic: 7.75 us -> 9.35 us
    ppermute x4, waiting for transfers between devices: 7.68 us -> 3.47 us  [butterfly_sum(): total = total + lax.ppermute(total, axis, [(i, i ^ bit) for i in range(n)])]
  transfers between devices with their start and end apart: 14 -> 14, of which waited for: 7 -> 5; matrix products, arithmetic and copies ran while one was open for 17% -> 24% of each run, Pallas kernels for 0% -> 0%
where the time goes in v11:
time: 106 us
  starting transfers between devices  35.9 us (34%)
  matrix products  23.4 us (22%)
  Pallas kernels  23.1 us (22%)
  waiting for transfers between devices  10.1 us (10%)
  other arithmetic  9.35 us (9%)
  local copies, waits for them, and re-layouts  3.12 us (3%)
    pallas_call x1, Pallas kernels, fused_attention(): pl.pallas_call(functools.partial(attention_kernel, tq=tq, hp=hp), grid_sp...  23.1 us
    ppermute x4, starting transfers between devices, butterfly_sum(): total = total + lax.ppermute(total, axis, [(i, i ^ bit) for i in range(n)])  19.5 us
    dot_general x1, matrix products, local(): jnp.dot(grad_masked, out_weight.T, preferred_element_type=jnp.float32)  12.6 us
    ppermute x2, starting transfers between devices, relay_gather(): forward.append(lax.ppermute(payload, 'ctx', fwd) if fwd else zero)  10.5 us
    dot_general x1, matrix products, local(): send = jnp.dot(delta, send_w, preferred_element_type=jnp.float32)  4.86 us
    dot_general x1, matrix products, local(): jnp.dot(delta, keep_w, preferred_element_type=jnp.float32)  4.63 us
    ppermute x2, waiting for transfers between devices, relay_gather(): backward.append(lax.ppermute(payload, 'ctx', bwd) if bwd else zero)  4.61 us
    ppermute x4, waiting for transfers between devices, butterfly_sum(): total = total + lax.ppermute(total, axis, [(i, i ^ bit) for i in range(n)])  3.47 us
  transfers between devices with their start and end apart: 14, of which 5 were waited for; matrix products, arithmetic and copies ran while one was open for 24% of the time, Pallas kernels for 0%

profile of v11, /device:TPU:0, one launch (start us, length us, event | category | flops | bytes accessed | tf_op | source)
XLA Modules:
  0.0 105.9 jit_solution(11361314885672663544)
XLA Ops:
  0.6 0.7 convert_element_type.23
  1.4 1.1 %broadcast_select_fusion.7 = bf16[512,512]{1,0:T(8,128)(2,1)S(1)} fusion(bf16[512,512]{1,0:T(8,128)(2,1)} %param.11, bf16[512,512]{1,0:T(8,128)(2,1)} %param.12, pred[]{:T(512)S(6)} %eq.17), kind=kLoop, calls=%fused_computation.30 | loop fusion | flops 262144 | bytes 1572865 | tf_op jit(solution)/shard_map/jit(_where)/select_n | solution.py:143
  2.5 0.8 pad_maximum_fusion.2
  3.3 6.0 %collective-permute-start.3 = (bf16[528,512]{1,0:T(8,128)(2,1)}, bf16[528,512]{1,0:T(8,128)(2,1)S(1)}, u32[]{:S(2)}, u32[]{:S(2)}) collective-permute-start(bf16[528,512]{1,0:T(8,128)(2,1)} %pad_maximum_fusion.2), channel_id=1, source_target_pairs={{0,8},{4,12},{1,9},{5,13},{2,10},{6,14},{3,11},{7,15},{16,24},{20,... | collective-permute-start | bytes 1622024 | tf_op jit(solution)/shard_map/ppermute | solution.py:121
  9.3 1.3 %collective-permute-start.4 = (bf16[528,512]{1,0:T(8,128)(2,1)}, bf16[528,512]{1,0:T(8,128)(2,1)S(1)}, u32[]{:S(2)}, u32[]{:S(2)}) collective-permute-start(bf16[528,512]{1,0:T(8,128)(2,1)} %pad_maximum_fusion.2), channel_id=1, source_target_pairs={{8,0},{9,1},{10,2},{11,3},{24,16},{25,17},{26,18},{27,19}} | collective-permute-start | bytes 1622024 | tf_op jit(solution)/shard_map/ppermute | solution.py:127
  10.6 1.3 %collective-permute-start.7 = (bf16[528,512]{1,0:T(8,128)(2,1)}, bf16[528,512]{1,0:T(8,128)(2,1)S(1)}, u32[]{:S(2)}, u32[]{:S(2)}) collective-permute-start(bf16[528,512]{1,0:T(8,128)(2,1)} %pad_maximum_fusion.2), channel_id=1, source_target_pairs={{4,0},{8,4},{12,8},{5,1},{9,5},{13,9},{6,2},{10,6},{14,10},{7,3},{... | collective-permute-start | bytes 1622024 | tf_op jit(solution)/shard_map/ppermute | solution.py:127
  11.9 4.6 %collective-permute-start.1 = (bf16[528,512]{1,0:T(8,128)(2,1)}, bf16[528,512]{1,0:T(8,128)(2,1)S(1)}, u32[]{:S(2)}, u32[]{:S(2)}) collective-permute-start(bf16[528,512]{1,0:T(8,128)(2,1)} %pad_maximum_fusion.2), channel_id=1, source_target_pairs={{0,4},{4,8},{8,12},{1,5},{5,9},{9,13},{2,6},{6,10},{10,14},{3,7},{... | collective-permute-start | bytes 1622024 | tf_op jit(solution)/shard_map/ppermute | solution.py:121
  16.5 0.1 collective-permute-start
  16.5 0.7 broadcast_compare_fusion
  17.2 12.6 %convolution_convert_fusion.do_ref = bf16[128,2048]{1,0:T(8,128)(2,1)} fusion(bf16[2048,4096]{1,0:T(8,128)(2,1)} %param.13, bf16[128,4096]{1,0:T(8,128)(2,1)} %param.14, pred[128]{0:T(512)(128)(4,1)S(1)} %broadcast_compare_fusion), kind=kOutput, calls=%fused_computation.6 | convolution fusion | flops 2148270080 | bytes 18350208 | tf_op jit(solution)/shard_map/dot_general | solution.py:209
  29.8 0.1 add_bitcast_fusion
  29.9 0.6 copy.11
  30.5 0.0 collective-permute-done.3
  30.5 0.0 collective-permute-done.4
  30.5 0.1 broadcast_select_fusion.1
  30.6 0.6 collective-permute-start.5
  31.2 0.9 collective-permute-start.6
  32.0 0.0 collective-permute-done
  32.0 0.1 broadcast_select_fusion.6
  32.2 0.0 copy-start
  32.2 0.5 collective-permute-done.1
  32.8 0.1 collective-permute-start.2
  32.8 0.1 fusion.10
  33.0 4.6 %collective-permute-done.7 = bf16[528,512]{1,0:T(8,128)(2,1)S(1)} collective-permute-done((bf16[528,512]{1,0:T(8,128)(2,1)}, bf16[528,512]{1,0:T(8,128)(2,1)S(1)}, u32[]{:S(2)}, u32[]{:S(2)}) %collective-permute-start.7) | collective-permute-done | bytes 540704 | tf_op jit(solution)/shard_map/ppermute | solution.py:127
  37.6 0.0 collective-permute-done.6
  37.6 0.1 broadcast_select_fusion
  37.7 0.1 collective-permute-start.8
  37.8 0.0 collective-permute-done.5
  37.8 0.1 broadcast_select_fusion.4
  37.8 0.0 collective-permute-done.2
  37.9 0.1 broadcast_select_fusion.5
  37.9 0.0 copy-done
  37.9 0.0 copy-start.2
  38.0 0.0 slice-start
  38.1 0.1 slice_select_fusion.1
  38.1 0.1 slice_select_fusion.2
  38.2 1.5 %collective-permute-done.8 = bf16[528,512]{1,0:T(8,128)(2,1)S(1)} collective-permute-done((bf16[528,512]{1,0:T(8,128)(2,1)S(1)}, bf16[528,512]{1,0:T(8,128)(2,1)S(1)}, u32[]{:S(2)}, u32[]{:S(2)}) %collective-permute-start.8) | collective-permute-done | bytes 540704 | tf_op jit(solution)/shard_map/ppermute | solution.py:148
  39.7 0.1 broadcast_select_fusion.3
  39.8 0.0 copy-done.2
  39.8 0.1 compare_reduce_fusion
  39.9 0.6 broadcast_select_fusion.8
  40.5 0.1 slice_select_fusion
  40.6 0.0 slice-done
  40.6 2.2 %pad_maximum_fusion = (bf16[2048,512]{1,0:T(8,128)(2,1)}, bf16[2048,512]{1,0:T(8,128)(2,1)}) fusion(bf16[512,512]{1,0:T(8,128)(2,1)S(1)} %slice.84, bf16[512,512]{1,0:T(8,128)(2,1)S(1)} %slice.83, bf16[512,512]{1,0:T(8,128)(2,1)S(1)} %slice.82, bf16[512,512]{1,0:T(8,128)(2,1)S(1)} %slice-done, bf16[512,512]{1,0:T(8,128)(2,1)S(1)} %slice_select_fusion, ...), kind=kLoop, calls=%fused_computation.7 | loop fusion | flops 16777216 | bytes 8388608 | tf_op jit(solution)/shard_map/concatenate | solution.py:154
  42.8 23.1 %shard_map.103 = (bf16[128,2048]{1,0:T(8,128)(2,1)}, f32[1,2048]{1,0:T(1,128)}) custom-call(s32[1]{0:T(128)} %bitcast.base_ref, s32[1,2048]{1,0:T(1,128)} %bitcast.23, bf16[128,2048]{1,0:T(8,128)(2,1)} %q_ref.1, bf16[2048,512]{1,0:T(8,128)(2,1)} %get-tuple-element.19.k_ref, bf16[2048,512]{1,0:T(8,128)(2,1)} %get-tuple-element.20.v_ref, f32[1,2048]{1,0:T(1,128)} %bitcast.22, ...), custom_call_target="tpu_custom_call" | custom-call | flops 4294967296 | bytes 5775360 | tf_op jit(solution)/shard_map/pallas_call | solution.py:82
  65.9 1.3 %convolution_bitcast_fusion = f32[32]{0:T(128)S(1)} fusion(s32[2048]{0:T(1024)S(1)} %maximum_convert_fusion, f32[1,2048]{1,0:T(1,128)} %get-tuple-element.18), kind=kOutput, calls=%fused_computation.9 | convolution fusion | flops 851968 | bytes 16512 | tf_op jit(solution)/shard_map/dot_general | solution.py:218
  67.2 0.5 broadcast.150
  67.7 1.4 %reduce.13 = f32[2048]{0:T(1024)S(1)} reduce(f32[1,2048]{1,0:T(1,128)} %get-tuple-element.18, f32[]{:T(128)} %broadcast.150), dimensions={0}, to_apply=%get-tuple-element.18.reduce_sub_computation.3 | reduce | bytes 16388 | tf_op jit(solution)/shard_map/pallas_call | solution.py:82
  69.1 0.6 gather_fusion
  69.7 0.2 collective-permute-start.10
  69.9 4.9 %fusion.4 = bf16[128,2048]{1,0:T(8,128)(2,1)S(1)} fusion(bf16[128,2048]{1,0:T(8,128)(2,1)} %get-tuple-element.17, bf16[2048,4096]{1,0:T(8,128)(2,1)} %param.13, s32[]{:T(128)S(6)} %select_n.142), kind=kOutput, calls=%fused_computation.5 | convolution fusion | flops 1074003968 | bytes 9437188 | tf_op jit(solution)/shard_map/dot_general | solution.py:226
  74.7 1.6 %collective-permute-start.9 = (bf16[128,2048]{1,0:T(8,128)(2,1)S(1)}, bf16[128,2048]{1,0:T(8,128)(2,1)S(1)}, u32[]{:S(2)}, u32[]{:S(2)}) collective-permute-start(bf16[128,2048]{1,0:T(8,128)(2,1)S(1)} %fusion.4), channel_id=1, source_target_pairs={{0,2},{2,0},{1,3},{3,1},{4,6},{6,4},{5,7},{7,5},{8,10},{10,8},{9,1... | collective-permute-start | bytes 1572872 | tf_op jit(solution)/shard_map/ppermute | solution.py:227
  76.3 0.0 collective-permute-done.10
  76.3 9.0 %collective-permute-start.11 = (f32[2080]{0:T(1024)S(1)}, f32[2080]{0:T(1024)S(1)}, u32[]{:S(2)}, u32[]{:S(2)}) collective-permute-start(f32[2080]{0:T(1024)S(1)} %fusion.21), channel_id=1, source_target_pairs={{0,4},{4,0},{8,12},{12,8},{1,5},{5,1},{9,13},{13,9},{2,6},{6,2},{1... | collective-permute-start | bytes 24968 | tf_op jit(solution)/shard_map/ppermute | solution.py:172
  85.3 1.7 %collective-permute-done.11 = f32[2080]{0:T(1024)S(1)} collective-permute-done((f32[2080]{0:T(1024)S(1)}, f32[2080]{0:T(1024)S(1)}, u32[]{:S(2)}, u32[]{:S(2)}) %collective-permute-start.11) | collective-permute-done | bytes 8352 | tf_op jit(solution)/shard_map/ppermute | solution.py:172
  87.0 9.9 %collective-permute-start.12 = (f32[2080]{0:T(1024)S(1)}, f32[2080]{0:T(1024)S(1)}, u32[]{:S(2)}, u32[]{:S(2)}) collective-permute-start(f32[2080]{0:T(1024)S(1)} %add.96), channel_id=1, source_target_pairs={{0,8},{4,12},{8,0},{12,4},{1,9},{5,13},{9,1},{13,5},{2,10},{6,14},... | collective-permute-start | bytes 24968 | tf_op jit(solution)/shard_map/ppermute | solution.py:172
  96.9 1.8 %collective-permute-done.12 = f32[2080]{0:T(1024)S(1)} collective-permute-done((f32[2080]{0:T(1024)S(1)}, f32[2080]{0:T(1024)S(1)}, u32[]{:S(2)}, u32[]{:S(2)}) %collective-permute-start.12) | collective-permute-done | bytes 8352 | tf_op jit(solution)/shard_map/ppermute | solution.py:172
  98.7 0.4 collective-permute-start.13
  99.2 4.6 %fusion.2 = f32[128,2048]{1,0:T(8,128)S(1)} fusion(bf16[128,2048]{1,0:T(8,128)(2,1)S(1)} %copy-done.1, bf16[2048,4096]{1,0:T(8,128)(2,1)} %param.13, s32[]{:T(128)S(6)} %select_n.141), kind=kOutput, calls=%fused_computation.3 | convolution fusion | flops 1073741824 | bytes 9961476 | tf_op jit(solution)/shard_map/dot_general | solution.py:229
  103.8 0.0 collective-permute-done.13
  103.8 0.5 slice.99
  104.3 0.7 dynamic_slice.11
  105.0 0.0 collective-permute-done.9
  105.0 0.9 add_convert_fusion
  (24 shorter events, 0.4 us)
Async XLA Ops:
  3.3 27.2 %collective-permute-start.3 = (bf16[528,512]{1,0:T(8,128)(2,1)}, bf16[528,512]{1,0:T(8,128)(2,1)S(1)}, u32[]{:S(2)}, u32[]{:S(2)}) collective-permute-start(bf16[528,512]{1,0:T(8,128)(2,1)} %pad_maximum_fusion.2), channel_id=1, source_target_pairs={{0,8},{4,12},{1,9},{5,13},{2,10},{6,14},{3,11},{7,15},{16,24},{20,... | collective-permute-start | bytes 1622024 | tf_op jit(solution)/shard_map/ppermute | solution.py:121
  9.3 21.3 %collective-permute-start.4 = (bf16[528,512]{1,0:T(8,128)(2,1)}, bf16[528,512]{1,0:T(8,128)(2,1)S(1)}, u32[]{:S(2)}, u32[]{:S(2)}) collective-permute-start(bf16[528,512]{1,0:T(8,128)(2,1)} %pad_maximum_fusion.2), channel_id=1, source_target_pairs={{8,0},{9,1},{10,2},{11,3},{24,16},{25,17},{26,18},{27,19}} | collective-permute-start | bytes 1622024 | tf_op jit(solution)/shard_map/ppermute | solution.py:127
  10.6 27.0 %collective-permute-start.7 = (bf16[528,512]{1,0:T(8,128)(2,1)}, bf16[528,512]{1,0:T(8,128)(2,1)S(1)}, u32[]{:S(2)}, u32[]{:S(2)}) collective-permute-start(bf16[528,512]{1,0:T(8,128)(2,1)} %pad_maximum_fusion.2), channel_id=1, source_target_pairs={{4,0},{8,4},{12,8},{5,1},{9,5},{13,9},{6,2},{10,6},{14,10},{7,3},{... | collective-permute-start | bytes 1622024 | tf_op jit(solution)/shard_map/ppermute | solution.py:127
  11.9 20.8 %collective-permute-start.1 = (bf16[528,512]{1,0:T(8,128)(2,1)}, bf16[528,512]{1,0:T(8,128)(2,1)S(1)}, u32[]{:S(2)}, u32[]{:S(2)}) collective-permute-start(bf16[528,512]{1,0:T(8,128)(2,1)} %pad_maximum_fusion.2), channel_id=1, source_target_pairs={{0,4},{4,8},{8,12},{1,5},{5,9},{9,13},{2,6},{6,10},{10,14},{3,7},{... | collective-permute-start | bytes 1622024 | tf_op jit(solution)/shard_map/ppermute | solution.py:121
  16.5 15.6 %collective-permute-start = (bf16[528,512]{1,0:T(8,128)(2,1)}, bf16[528,512]{1,0:T(8,128)(2,1)S(1)}, u32[]{:S(2)}, u32[]{:S(2)}) collective-permute-start(bf16[528,512]{1,0:T(8,128)(2,1)} %pad_maximum_fusion.2), channel_id=1, source_target_pairs={{0,1},{1,0},{2,3},{3,2},{4,5},{5,4},{6,7},{7,6},{8,9},{9,8},{10,11... | collective-permute-start | bytes 1622024 | tf_op jit(solution)/shard_map/ppermute | solution.py:148
  30.6 7.2 %collective-permute-start.5 = (bf16[528,512]{1,0:T(8,128)(2,1)S(1)}, bf16[528,512]{1,0:T(8,128)(2,1)S(1)}, u32[]{:S(2)}, u32[]{:S(2)}) collective-permute-start(bf16[528,512]{1,0:T(8,128)(2,1)S(1)} %broadcast_select_fusion.1), channel_id=1, source_target_pairs={{0,1},{1,0},{2,3},{3,2},{4,5},{5,4},{6,7},{7,6},{8,9},{9,8},{10,11... | collective-permute-start | bytes 1622024 | tf_op jit(solution)/shard_map/ppermute | solution.py:148
  31.2 6.5 %collective-permute-start.6 = (bf16[528,512]{1,0:T(8,128)(2,1)S(1)}, bf16[528,512]{1,0:T(8,128)(2,1)S(1)}, u32[]{:S(2)}, u32[]{:S(2)}) collective-permute-start(bf16[528,512]{1,0:T(8,128)(2,1)S(1)} %collective-permute-done.3), channel_id=1, source_target_pairs={{8,12},{9,13},{10,14},{11,15},{24,28},{25,29},{26,30},{27,31}} | collective-permute-start | bytes 1622024 | tf_op jit(solution)/shard_map/ppermute | solution.py:119
  32.2 5.7 %copy-start = (bf16[528,512]{1,0:T(8,128)(2,1)}, bf16[528,512]{1,0:T(8,128)(2,1)S(1)}, u32[]{:S(2)}) copy-start(bf16[528,512]{1,0:T(8,128)(2,1)S(1)} %broadcast_select_fusion.6) | copy-start | bytes 1622020
  32.8 5.1 %collective-permute-start.2 = (bf16[528,512]{1,0:T(8,128)(2,1)S(1)}, bf16[528,512]{1,0:T(8,128)(2,1)S(1)}, u32[]{:S(2)}, u32[]{:S(2)}) collective-permute-start(bf16[528,512]{1,0:T(8,128)(2,1)S(1)} %broadcast_select_fusion.2), channel_id=1, source_target_pairs={{0,1},{1,0},{2,3},{3,2},{4,5},{5,4},{6,7},{7,6},{8,9},{9,8},{10,11... | collective-permute-start | bytes 1622024 | tf_op jit(solution)/shard_map/ppermute | solution.py:148
  37.7 2.0 %collective-permute-start.8 = (bf16[528,512]{1,0:T(8,128)(2,1)S(1)}, bf16[528,512]{1,0:T(8,128)(2,1)S(1)}, u32[]{:S(2)}, u32[]{:S(2)}) collective-permute-start(bf16[528,512]{1,0:T(8,128)(2,1)S(1)} %broadcast_select_fusion), channel_id=1, source_target_pairs={{0,1},{1,0},{2,3},{3,2},{4,5},{5,4},{6,7},{7,6},{8,9},{9,8},{10,11... | collective-permute-start | bytes 1622024 | tf_op jit(solution)/shard_map/ppermute | solution.py:148
  37.9 1.9 %copy-start.2 = (s32[4]{0:T(128)S(1)}, s32[4]{0:T(128)}, u32[]{:S(2)}) copy-start(s32[4]{0:T(128)} %param.17) | copy-start | bytes 52
  38.0 2.6 %slice-start = ((bf16[528,512]{1,0:T(8,128)(2,1)}), bf16[512,512]{1,0:T(8,128)(2,1)S(1)}, s32[]{:S(2)}) async-start(bf16[528,512]{1,0:T(8,128)(2,1)} %copy-done), calls=%async_computation | async-start | bytes 1048576 | tf_op jit(solution)/shard_map/slice | solution.py:154
  69.7 6.7 %collective-permute-start.10 = (f32[2080]{0:T(1024)S(1)}, f32[2080]{0:T(1024)S(1)}, u32[]{:S(2)}, u32[]{:S(2)}) collective-permute-start(f32[2080]{0:T(1024)S(1)} %pad_maximum_fusion.3), channel_id=1, source_target_pairs={{0,1},{1,0},{2,3},{3,2},{4,5},{5,4},{6,7},{7,6},{8,9},{9,8},{10,11... | collective-permute-start | bytes 24968 | tf_op jit(solution)/shard_map/ppermute | solution.py:172
  69.9 29.3 %copy-start.1 = (bf16[128,2048]{1,0:T(8,128)(2,1)S(1)}, bf16[128,2048]{1,0:T(8,128)(2,1)}, u32[]{:S(2)}) copy-start(bf16[128,2048]{1,0:T(8,128)(2,1)} %get-tuple-element.17) | copy-start | bytes 1572868
  74.7 30.3 %collective-permute-start.9 = (bf16[128,2048]{1,0:T(8,128)(2,1)S(1)}, bf16[128,2048]{1,0:T(8,128)(2,1)S(1)}, u32[]{:S(2)}, u32[]{:S(2)}) collective-permute-start(bf16[128,2048]{1,0:T(8,128)(2,1)S(1)} %fusion.4), channel_id=1, source_target_pairs={{0,2},{2,0},{1,3},{3,1},{4,6},{6,4},{5,7},{7,5},{8,10},{10,8},{9,1... | collective-permute-start | bytes 1572872 | tf_op jit(solution)/shard_map/ppermute | solution.py:227
  76.3 10.7 %collective-permute-start.11 = (f32[2080]{0:T(1024)S(1)}, f32[2080]{0:T(1024)S(1)}, u32[]{:S(2)}, u32[]{:S(2)}) collective-permute-start(f32[2080]{0:T(1024)S(1)} %fusion.21), channel_id=1, source_target_pairs={{0,4},{4,0},{8,12},{12,8},{1,5},{5,1},{9,13},{13,9},{2,6},{6,2},{1... | collective-permute-start | bytes 24968 | tf_op jit(solution)/shard_map/ppermute | solution.py:172
  87.0 11.7 %collective-permute-start.12 = (f32[2080]{0:T(1024)S(1)}, f32[2080]{0:T(1024)S(1)}, u32[]{:S(2)}, u32[]{:S(2)}) collective-permute-start(f32[2080]{0:T(1024)S(1)} %add.96), channel_id=1, source_target_pairs={{0,8},{4,12},{8,0},{12,4},{1,9},{5,13},{9,1},{13,5},{2,10},{6,14},... | collective-permute-start | bytes 24968 | tf_op jit(solution)/shard_map/ppermute | solution.py:172
  98.7 5.1 %collective-permute-start.13 = (f32[2080]{0:T(1024)S(1)}, f32[2080]{0:T(1024)S(1)}, u32[]{:S(2)}, u32[]{:S(2)}) collective-permute-start(f32[2080]{0:T(1024)S(1)} %add.97), channel_id=1, source_target_pairs={{0,2},{2,0},{1,3},{3,1},{4,6},{6,4},{5,7},{7,5},{8,10},{10,8},{9,1... | collective-permute-start | bytes 24968 | tf_op jit(solution)/shard_map/ppermute | solution.py:172

commit v12 on v11

--- a/solution.py
+++ b/solution.py
@@ -53,8 +53,9 @@
     attr_ref[...] += total
 
 
-def fused_attention(base, key_pos, query, key_all, value_all, kept, grad_out, group_size):
-    qc, width = query.shape
+def fused_attention(base, key_pos, query, key_all, value_all, kept, grad_out, group_size, col_off=0):
+    qc = query.shape[0]
+    width = key_all.shape[1] * group_size
     keys, kv_width = key_all.shape
     kv_local = kv_width // HD
     tq = max(8, min(qc, (128 * 2048) // keys))
@@ -64,6 +65,9 @@
     grid = (kv_local, steps, n_rows)
 
     def head_map(g, j, r, b):
+        return (r, col_off + g * steps + j)
+
+    def out_map(g, j, r, b):
         return (r, g * steps + j)
 
     def kv_map(g, j, r, b):
@@ -76,7 +80,7 @@
     cost = pl.CostEstimate(
         flops=flops,
         transcendentals=2 * qc * keys * kv_local * group_size,
-        bytes_accessed=2 * (query.size + key_all.size + value_all.size + grad_out.size + query.size)
+        bytes_accessed=2 * (3 * qc * width + key_all.size + value_all.size)
         + 4 * keys,
     )
     return pl.pallas_call(
@@ -93,7 +97,7 @@
                 pl.BlockSpec((tq, hp * HD), head_map),
             ],
             out_specs=[
-                pl.BlockSpec((tq, hp * HD), head_map),
+                pl.BlockSpec((tq, hp * HD), out_map),
                 pl.BlockSpec((1, keys), fixed),
             ],
         ),
@@ -195,9 +199,17 @@
         last_query = query_base + (receiver * rep_count + rep_count) * query_count - 1
         return block * key_count <= last_query
 
-    key_all, value_all, seg_shift, key_pos, source = gather_kv(
-        key, value, segment_ids, ctx_at, rep_at, rep_count, needed
-    )
+    parts = 2 if kv_local % 2 == 0 else 1
+    kv_cols = key.shape[1] // parts
+    gathered = [
+        gather_kv(
+            key[:, p * kv_cols:(p + 1) * kv_cols],
+            value[:, p * kv_cols:(p + 1) * kv_cols],
+            segment_ids, ctx_at, rep_at, rep_count, needed,
+        )
+        for p in range(parts)
+    ]
+    seg_shift, key_pos = gathered[0][2], gathered[0][3]
     kept = jnp.where(
         jnp.any(seg_shift[:, None] == masked_segments[None, :], axis=1), 0.0, 1.0
     ).astype(jnp.float32)[None, :]
@@ -209,9 +221,16 @@
     grad_out = jnp.dot(grad_masked, out_weight.T, preferred_element_type=jnp.float32).astype(
         jnp.bfloat16
     )
-    delta, attr = fused_attention(
-        base, key_pos, query, key_all, value_all, kept, grad_out, group_size
-    )
+    steps_per_part = (kv_local // parts) * (group_size // (2 if group_size % 2 == 0 else 1))
+    deltas, attr = [], None
+    for p in range(parts):
+        d_p, a_p = fused_attention(
+            base, key_pos, query, gathered[p][0], gathered[p][1], kept, grad_out, group_size,
+            col_off=p * steps_per_part,
+        )
+        deltas.append(d_p)
+        attr = a_p if attr is None else attr + a_p
+    delta = jnp.concatenate(deltas, axis=1) if parts > 1 else deltas[0]
 
     inverse = (ctx_at - jnp.arange(ctx_count, dtype=jnp.int32)) % ctx_count
     attr_abs = attr.reshape(ctx_count, key_count)[inverse].reshape(-1)

time: 106 us -> 124 us (1.17)
  starting transfers between devices: 35.9 us -> 48.7 us
  waiting for transfers between devices: 10.1 us -> 12.2 us
  Pallas kernels: 23.1 us -> 24.9 us
  local copies, waits for them, and re-layouts: 3.12 us -> 4.42 us
    ppermute x2 -> x4, starting transfers between devices: 10.5 us -> 19.5 us  [relay_gather(): forward.append(lax.ppermute(payload, 'ctx', fwd) if fwd else zero)]
    ppermute x2 -> x4, starting transfers between devices: 2.58 us -> 5.17 us  [relay_gather(): backward.append(lax.ppermute(payload, 'ctx', bwd) if bwd else zero)]
    pallas_call x1 -> x2, Pallas kernels: 23.1 us -> 24.9 us  [fused_attention(): pl.pallas_call(functools.partial(attention_kernel, tq=tq, hp=hp), grid_sp...]
    ppermute x2 -> x4, waiting for transfers between devices: 4.61 us -> 6.02 us  [relay_gather(): backward.append(lax.ppermute(payload, 'ctx', bwd) if bwd else zero)]
    pallas_call x1 -> x0, other arithmetic: 1.36 us -> none  [fused_attention(): pl.pallas_call(functools.partial(attention_kernel, tq=tq, hp=hp), grid_sp...]
    concatenate x1 -> x2, other arithmetic: 2.18 us -> 2.5 us  [gather_kv(): key_all = jnp.concatenate([p[:key_count] for p in key_parts], axis=0)]
  transfers between devices with their start and end apart: 14 -> 23, of which waited for: 5 -> 5; matrix products, arithmetic and copies ran while one was open for 24% -> 23% of each run, Pallas kernels for 0% -> 10%
where the time goes in v12:
time: 124 us; the launch traced here: 123 us
  starting transfers between devices  48.7 us (39%)
  Pallas kernels  24.9 us (20%)
  matrix products  22.8 us (18%)
  waiting for transfers between devices  12.2 us (10%)
  other arithmetic  8.99 us (7%)
  local copies, waits for them, and re-layouts  4.42 us (4%)
    pallas_call x2, Pallas kernels, fused_attention(): pl.pallas_call(functools.partial(attention_kernel, tq=tq, hp=hp), grid_sp...  24.9 us
    ppermute x4, starting transfers between devices, relay_gather(): forward.append(lax.ppermute(payload, 'ctx', fwd) if fwd else zero)  19.5 us
    ppermute x4, starting transfers between devices, butterfly_sum(): total = total + lax.ppermute(total, axis, [(i, i ^ bit) for i in range(n)])  18.9 us
    dot_general x1, matrix products, local(): jnp.dot(grad_masked, out_weight.T, preferred_element_type=jnp.float32)  12.3 us
    ppermute x4, waiting for transfers between devices, relay_gather(): backward.append(lax.ppermute(payload, 'ctx', bwd) if bwd else zero)  6.02 us
    ppermute x4, starting transfers between devices, relay_gather(): backward.append(lax.ppermute(payload, 'ctx', bwd) if bwd else zero)  5.17 us
    dot_general x1, matrix products, local(): send = jnp.dot(delta, send_w, preferred_element_type=jnp.float32)  4.64 us
    dot_general x1, matrix products, local(): jnp.dot(delta, keep_w, preferred_element_type=jnp.float32)  4.63 us
  transfers between devices with their start and end apart: 23, of which 5 were waited for; matrix products, arithmetic and copies ran while one was open for 23% of the time, Pallas kernels for 10%

profile of v12, /device:TPU:0, one launch (start us, length us, event | category | flops | bytes accessed | tf_op | source)
XLA Modules:
  0.0 123.2 jit_solution(2640271772020460812)
XLA Ops:
  0.7 0.8 convert_element_type.24
  1.5 1.4 %slice_select_fusion.3 = (bf16[512,256]{1,0:T(8,128)(2,1)S(1)}, bf16[512,256]{1,0:T(8,128)(2,1)S(1)}) fusion(bf16[512,512]{1,0:T(8,128)(2,1)} %param.14, bf16[512,512]{1,0:T(8,128)(2,1)} %param.13, pred[]{:T(512)S(6)} %eq.17), kind=kLoop, calls=%fused_computation.36 | loop fusion | flops 262144 | bytes 1572865 | tf_op jit(solution)/shard_map/jit(_where)/select_n | solution.py:147
  2.9 0.5 collective-permute-start
  3.4 5.5 %collective-permute-start.3 = (bf16[528,256]{1,0:T(8,128)(2,1)S(1)}, bf16[528,256]{1,0:T(8,128)(2,1)S(1)}, u32[]{:S(2)}, u32[]{:S(2)}) collective-permute-start(bf16[528,256]{1,0:T(8,128)(2,1)S(1)} %pad_maximum_fusion.5), channel_id=1, source_target_pairs={{0,8},{4,12},{1,9},{5,13},{2,10},{6,14},{3,11},{7,15},{16,24},{20,... | collective-permute-start | bytes 811016 | tf_op jit(solution)/shard_map/ppermute | solution.py:125
  8.9 1.3 %collective-permute-start.4 = (bf16[528,256]{1,0:T(8,128)(2,1)S(1)}, bf16[528,256]{1,0:T(8,128)(2,1)S(1)}, u32[]{:S(2)}, u32[]{:S(2)}) collective-permute-start(bf16[528,256]{1,0:T(8,128)(2,1)S(1)} %pad_maximum_fusion.5), channel_id=1, source_target_pairs={{8,0},{9,1},{10,2},{11,3},{24,16},{25,17},{26,18},{27,19}} | collective-permute-start | bytes 811016 | tf_op jit(solution)/shard_map/ppermute | solution.py:131
  10.2 1.3 %collective-permute-start.7 = (bf16[528,256]{1,0:T(8,128)(2,1)S(1)}, bf16[528,256]{1,0:T(8,128)(2,1)S(1)}, u32[]{:S(2)}, u32[]{:S(2)}) collective-permute-start(bf16[528,256]{1,0:T(8,128)(2,1)S(1)} %pad_maximum_fusion.5), channel_id=1, source_target_pairs={{4,0},{8,4},{12,8},{5,1},{9,5},{13,9},{6,2},{10,6},{14,10},{7,3},{... | collective-permute-start | bytes 811016 | tf_op jit(solution)/shard_map/ppermute | solution.py:131
  11.5 4.6 %collective-permute-start.1 = (bf16[528,256]{1,0:T(8,128)(2,1)S(1)}, bf16[528,256]{1,0:T(8,128)(2,1)S(1)}, u32[]{:S(2)}, u32[]{:S(2)}) collective-permute-start(bf16[528,256]{1,0:T(8,128)(2,1)S(1)} %pad_maximum_fusion.5), channel_id=1, source_target_pairs={{0,4},{4,8},{8,12},{1,5},{5,9},{9,13},{2,6},{6,10},{10,14},{3,7},{... | collective-permute-start | bytes 811016 | tf_op jit(solution)/shard_map/ppermute | solution.py:125
  16.1 12.3 %convolution_convert_fusion.do_ref = bf16[128,2048]{1,0:T(8,128)(2,1)} fusion(bf16[2048,4096]{1,0:T(8,128)(2,1)} %param.15, bf16[128,4096]{1,0:T(8,128)(2,1)S(1)} %copy-done.2, pred[128]{0:T(512)(128)(4,1)S(1)} %broadcast_compare_fusion), kind=kOutput, calls=%fused_computation.6 | convolution fusion | flops 2148270080 | bytes 18350208 | tf_op jit(solution)/shard_map/dot_general | solution.py:221
  28.4 0.1 add_bitcast_fusion
  28.5 0.6 copy.11
  29.1 0.0 collective-permute-done
  29.1 0.1 pad_maximum_fusion.4
  29.2 5.5 %collective-permute-start.12 = (bf16[528,256]{1,0:T(8,128)(2,1)S(1)}, bf16[528,256]{1,0:T(8,128)(2,1)S(1)}, u32[]{:S(2)}, u32[]{:S(2)}) collective-permute-start(bf16[528,256]{1,0:T(8,128)(2,1)S(1)} %get-tuple-element.42), channel_id=1, source_target_pairs={{0,8},{4,12},{1,9},{5,13},{2,10},{6,14},{3,11},{7,15},{16,24},{20,... | collective-permute-start | bytes 811016 | tf_op jit(solution)/shard_map/ppermute | solution.py:125
  34.7 1.3 %collective-permute-start.16 = (bf16[528,256]{1,0:T(8,128)(2,1)S(1)}, bf16[528,256]{1,0:T(8,128)(2,1)S(1)}, u32[]{:S(2)}, u32[]{:S(2)}) collective-permute-start(bf16[528,256]{1,0:T(8,128)(2,1)S(1)} %get-tuple-element.42), channel_id=1, source_target_pairs={{4,0},{8,4},{12,8},{5,1},{9,5},{13,9},{6,2},{10,6},{14,10},{7,3},{... | collective-permute-start | bytes 811016 | tf_op jit(solution)/shard_map/ppermute | solution.py:131
  36.0 0.0 collective-permute-done.3
  36.0 1.3 %collective-permute-start.13 = (bf16[528,256]{1,0:T(8,128)(2,1)S(1)}, bf16[528,256]{1,0:T(8,128)(2,1)S(1)}, u32[]{:S(2)}, u32[]{:S(2)}) collective-permute-start(bf16[528,256]{1,0:T(8,128)(2,1)S(1)} %get-tuple-element.42), channel_id=1, source_target_pairs={{8,0},{9,1},{10,2},{11,3},{24,16},{25,17},{26,18},{27,19}} | collective-permute-start | bytes 811016 | tf_op jit(solution)/shard_map/ppermute | solution.py:131
  37.3 0.0 collective-permute-done.4
  37.3 0.1 collective-permute-start.2
  37.5 1.4 %collective-permute-done.2 = bf16[528,256]{1,0:T(8,128)(2,1)S(1)} collective-permute-done((bf16[528,256]{1,0:T(8,128)(2,1)S(1)}, bf16[528,256]{1,0:T(8,128)(2,1)S(1)}, u32[]{:S(2)}, u32[]{:S(2)}) %collective-permute-start.2) | collective-permute-done | bytes 270368 | tf_op jit(solution)/shard_map/ppermute | solution.py:152
  39.0 3.9 %collective-permute-start.10 = (bf16[528,256]{1,0:T(8,128)(2,1)S(1)}, bf16[528,256]{1,0:T(8,128)(2,1)S(1)}, u32[]{:S(2)}, u32[]{:S(2)}) collective-permute-start(bf16[528,256]{1,0:T(8,128)(2,1)S(1)} %get-tuple-element.42), channel_id=1, source_target_pairs={{0,4},{4,8},{8,12},{1,5},{5,9},{9,13},{2,6},{6,10},{10,14},{3,7},{... | collective-permute-start | bytes 811016 | tf_op jit(solution)/shard_map/ppermute | solution.py:125
  43.0 0.0 collective-permute-done.12
  43.0 0.1 collective-permute-start.9
  43.1 6.0 %collective-permute-done.13 = bf16[528,256]{1,0:T(8,128)(2,1)S(1)} collective-permute-done((bf16[528,256]{1,0:T(8,128)(2,1)S(1)}, bf16[528,256]{1,0:T(8,128)(2,1)S(1)}, u32[]{:S(2)}, u32[]{:S(2)}) %collective-permute-start.13) | collective-permute-done | bytes 270368 | tf_op jit(solution)/shard_map/ppermute | solution.py:131
  49.1 0.7 collective-permute-start.6
  49.8 0.0 collective-permute-done.10
  49.8 0.1 collective-permute-start.5
  49.9 0.0 collective-permute-done.7
  49.9 0.6 collective-permute-start.14
  50.5 0.1 collective-permute-start.11
  50.6 0.8 collective-permute-done.5
  51.4 0.1 collective-permute-start.8
  51.7 0.0 copy-start.4
  51.7 0.0 collective-permute-done.9
  51.7 1.0 collective-permute-start.15
  52.7 0.2 broadcast_select_fusion.13
  52.9 0.0 collective-permute-done.16
  52.9 0.0 collective-permute-done.15
  53.0 0.0 slice-start
  53.0 0.4 collective-permute-start.17
  53.4 0.0 collective-permute-done.8
  53.5 0.1 compare_reduce_fusion
  53.7 1.0 pad_maximum_fusion.1.v_ref
  54.7 0.6 broadcast_select_fusion.18
  55.4 1.0 pad_maximum_fusion.k_ref
  56.4 12.5 %shard_map.103 = (bf16[128,1024]{1,0:T(8,128)(2,1)}, f32[1,2048]{1,0:T(1,128)}) custom-call(s32[1]{0:T(128)} %bitcast.base_ref, s32[1,2048]{1,0:T(1,128)} %bitcast.36, bf16[128,2048]{1,0:T(8,128)(2,1)} %q_ref.3, bf16[2048,256]{1,0:T(8,128)(2,1)} %pad_maximum_fusion.k_ref, bf16[2048,256]{1,0:T(8,128)(2,1)} %pad_maximum_fusion.1.v_ref, f32[1,2048]{1,0:T(1,128)} %bitcast.34, ...), custom_call_target="tpu_custom_call" | custom-call | flops 2147483648 | bytes 2891776 | tf_op jit(solution)/shard_map/pallas_call | solution.py:86
  68.9 1.0 constant_dynamic-update-slice_fusion.1
  70.0 1.5 %pad_maximum_fusion.2 = (bf16[2048,256]{1,0:T(8,128)(2,1)}, bf16[2048,256]{1,0:T(8,128)(2,1)}) fusion(bf16[512,256]{1,0:T(8,128)(2,1)S(1)} %get-tuple-element.40, bf16[512,256]{1,0:T(8,128)(2,1)S(1)} %get-tuple-element.38, bf16[512,256]{1,0:T(8,128)(2,1)S(1)} %get-tuple-element.36, bf16[512,256]{1,0:T(8,128)(2,1)S(1)} %get-tuple-element.34, ...), kind=kLoop, calls=%fused_computation.10 | loop fusion | flops 8388608 | bytes 4194304 | tf_op jit(solution)/shard_map/concatenate | solution.py:158
  71.5 12.4 %shard_map.104 = (bf16[128,1024]{1,0:T(8,128)(2,1)}, f32[1,2048]{1,0:T(1,128)}) custom-call(s32[1]{0:T(128)} %bitcast.base_ref, s32[1,2048]{1,0:T(1,128)} %bitcast.37, bf16[128,2048]{1,0:T(8,128)(2,1)} %q_ref.3, bf16[2048,256]{1,0:T(8,128)(2,1)} %get-tuple-element.44.k_ref, bf16[2048,256]{1,0:T(8,128)(2,1)} %get-tuple-element.45.v_ref, f32[1,2048]{1,0:T(1,128)} %bitcast.35, ...), custom_call_target="tpu_custom_call" | custom-call | flops 2147483648 | bytes 2891776 | tf_op jit(solution)/shard_map/pallas_call | solution.py:86
  83.9 0.7 add_reduce_fusion
  84.6 1.3 %convolution_bitcast_fusion = f32[32]{0:T(128)S(1)} fusion(s32[2048]{0:T(1024)S(1)} %maximum_convert_fusion, f32[1,2048]{1,0:T(1,128)S(1)} %copy-done.3, f32[1,2048]{1,0:T(1,128)} %get-tuple-element.30), kind=kOutput, calls=%fused_computation.7 | convolution fusion | flops 854016 | bytes 24704 | tf_op jit(solution)/shard_map/dot_general | solution.py:237
  85.9 0.6 gather_fusion
  86.5 0.2 collective-permute-start.19
  86.7 1.0 constant_dynamic-update-slice_fusion
  87.7 4.6 %fusion.4 = bf16[128,2048]{1,0:T(8,128)(2,1)S(1)} fusion(bf16[128,2048]{1,0:T(8,128)(2,1)S(1)} %constant_dynamic-update-slice_fusion, bf16[2048,4096]{1,0:T(8,128)(2,1)} %param.15, s32[]{:T(128)S(6)} %select_n.202), kind=kOutput, calls=%fused_computation.5 | convolution fusion | flops 1074003968 | bytes 9437188 | tf_op jit(solution)/shard_map/dot_general | solution.py:245
  92.3 1.6 %collective-permute-start.18 = (bf16[128,2048]{1,0:T(8,128)(2,1)S(1)}, bf16[128,2048]{1,0:T(8,128)(2,1)S(1)}, u32[]{:S(2)}, u32[]{:S(2)}) collective-permute-start(bf16[128,2048]{1,0:T(8,128)(2,1)S(1)} %fusion.4), channel_id=1, source_target_pairs={{0,2},{2,0},{1,3},{3,1},{4,6},{6,4},{5,7},{7,5},{8,10},{10,8},{9,1... | collective-permute-start | bytes 1572872 | tf_op jit(solution)/shard_map/ppermute | solution.py:246
  93.9 1.6 %collective-permute-start.20 = (f32[2080]{0:T(1024)S(1)}, f32[2080]{0:T(1024)S(1)}, u32[]{:S(2)}, u32[]{:S(2)}) collective-permute-start(f32[2080]{0:T(1024)S(1)} %fusion.20), channel_id=1, source_target_pairs={{0,4},{4,0},{8,12},{12,8},{1,5},{5,1},{9,13},{13,9},{2,6},{6,2},{1... | collective-permute-start | bytes 24968 | tf_op jit(solution)/shard_map/ppermute | solution.py:176
  95.5 2.2 %collective-permute-done.20 = f32[2080]{0:T(1024)S(1)} collective-permute-done((f32[2080]{0:T(1024)S(1)}, f32[2080]{0:T(1024)S(1)}, u32[]{:S(2)}, u32[]{:S(2)}) %collective-permute-start.20) | collective-permute-done | bytes 8352 | tf_op jit(solution)/shard_map/ppermute | solution.py:176
  97.7 16.6 %collective-permute-start.21 = (f32[2080]{0:T(1024)S(1)}, f32[2080]{0:T(1024)S(1)}, u32[]{:S(2)}, u32[]{:S(2)}) collective-permute-start(f32[2080]{0:T(1024)S(1)} %add.101), channel_id=1, source_target_pairs={{0,8},{4,12},{8,0},{12,4},{1,9},{5,13},{9,1},{13,5},{2,10},{6,14},... | collective-permute-start | bytes 24968 | tf_op jit(solution)/shard_map/ppermute | solution.py:176
  114.3 1.7 %collective-permute-done.21 = f32[2080]{0:T(1024)S(1)} collective-permute-done((f32[2080]{0:T(1024)S(1)}, f32[2080]{0:T(1024)S(1)}, u32[]{:S(2)}, u32[]{:S(2)}) %collective-permute-start.21) | collective-permute-done | bytes 8352 | tf_op jit(solution)/shard_map/ppermute | solution.py:176
  116.0 0.5 collective-permute-start.22
  116.5 4.6 %fusion.2 = f32[128,2048]{1,0:T(8,128)S(1)} fusion(bf16[128,2048]{1,0:T(8,128)(2,1)S(1)} %constant_dynamic-update-slice_fusion, bf16[2048,4096]{1,0:T(8,128)(2,1)} %param.15, s32[]{:T(128)S(6)} %select_n.201), kind=kOutput, calls=%fused_computation.3 | convolution fusion | flops 1073741824 | bytes 9961476 | tf_op jit(solution)/shard_map/dot_general | solution.py:248
  121.2 0.5 slice.171
  121.7 0.7 dynamic_slice.11
  122.3 0.9 add_convert_fusion
  (63 shorter events, 0.8 us)
Async XLA Ops:
  0.6 15.5 %copy-start.5 = (s32[128]{0:T(128)S(1)}, s32[128]{0:T(128)}, u32[]{:S(2)}) copy-start(s32[128]{0:T(128)} %param.17) | copy-start | bytes 1540
  0.6 15.5 %copy-start.2 = (bf16[128,4096]{1,0:T(8,128)(2,1)S(1)}, bf16[128,4096]{1,0:T(8,128)(2,1)}, u32[]{:S(2)}) copy-start(bf16[128,4096]{1,0:T(8,128)(2,1)} %param.16) | copy-start | bytes 3145732
  2.9 26.2 %collective-permute-start = (bf16[528,256]{1,0:T(8,128)(2,1)S(1)}, bf16[528,256]{1,0:T(8,128)(2,1)S(1)}, u32[]{:S(2)}, u32[]{:S(2)}) collective-permute-start(bf16[528,256]{1,0:T(8,128)(2,1)S(1)} %pad_maximum_fusion.5), channel_id=1, source_target_pairs={{0,1},{1,0},{2,3},{3,2},{4,5},{5,4},{6,7},{7,6},{8,9},{9,8},{10,11... | collective-permute-start | bytes 811016 | tf_op jit(solution)/shard_map/ppermute | solution.py:152
  3.4 32.6 %collective-permute-start.3 = (bf16[528,256]{1,0:T(8,128)(2,1)S(1)}, bf16[528,256]{1,0:T(8,128)(2,1)S(1)}, u32[]{:S(2)}, u32[]{:S(2)}) collective-permute-start(bf16[528,256]{1,0:T(8,128)(2,1)S(1)} %pad_maximum_fusion.5), channel_id=1, source_target_pairs={{0,8},{4,12},{1,9},{5,13},{2,10},{6,14},{3,11},{7,15},{16,24},{20,... | collective-permute-start | bytes 811016 | tf_op jit(solution)/shard_map/ppermute | solution.py:125
  8.9 28.4 %collective-permute-start.4 = (bf16[528,256]{1,0:T(8,128)(2,1)S(1)}, bf16[528,256]{1,0:T(8,128)(2,1)S(1)}, u32[]{:S(2)}, u32[]{:S(2)}) collective-permute-start(bf16[528,256]{1,0:T(8,128)(2,1)S(1)} %pad_maximum_fusion.5), channel_id=1, source_target_pairs={{8,0},{9,1},{10,2},{11,3},{24,16},{25,17},{26,18},{27,19}} | collective-permute-start | bytes 811016 | tf_op jit(solution)/shard_map/ppermute | solution.py:131
  10.2 39.7 %collective-permute-start.7 = (bf16[528,256]{1,0:T(8,128)(2,1)S(1)}, bf16[528,256]{1,0:T(8,128)(2,1)S(1)}, u32[]{:S(2)}, u32[]{:S(2)}) collective-permute-start(bf16[528,256]{1,0:T(8,128)(2,1)S(1)} %pad_maximum_fusion.5), channel_id=1, source_target_pairs={{4,0},{8,4},{12,8},{5,1},{9,5},{13,9},{6,2},{10,6},{14,10},{7,3},{... | collective-permute-start | bytes 811016 | tf_op jit(solution)/shard_map/ppermute | solution.py:131
  11.5 23.2 %collective-permute-start.1 = (bf16[528,256]{1,0:T(8,128)(2,1)S(1)}, bf16[528,256]{1,0:T(8,128)(2,1)S(1)}, u32[]{:S(2)}, u32[]{:S(2)}) collective-permute-start(bf16[528,256]{1,0:T(8,128)(2,1)S(1)} %pad_maximum_fusion.5), channel_id=1, source_target_pairs={{0,4},{4,8},{8,12},{1,5},{5,9},{9,13},{2,6},{6,10},{10,14},{3,7},{... | collective-permute-start | bytes 811016 | tf_op jit(solution)/shard_map/ppermute | solution.py:125
  29.2 13.8 %collective-permute-start.12 = (bf16[528,256]{1,0:T(8,128)(2,1)S(1)}, bf16[528,256]{1,0:T(8,128)(2,1)S(1)}, u32[]{:S(2)}, u32[]{:S(2)}) collective-permute-start(bf16[528,256]{1,0:T(8,128)(2,1)S(1)} %get-tuple-element.42), channel_id=1, source_target_pairs={{0,8},{4,12},{1,9},{5,13},{2,10},{6,14},{3,11},{7,15},{16,24},{20,... | collective-permute-start | bytes 811016 | tf_op jit(solution)/shard_map/ppermute | solution.py:125
  34.7 18.2 %collective-permute-start.16 = (bf16[528,256]{1,0:T(8,128)(2,1)S(1)}, bf16[528,256]{1,0:T(8,128)(2,1)S(1)}, u32[]{:S(2)}, u32[]{:S(2)}) collective-permute-start(bf16[528,256]{1,0:T(8,128)(2,1)S(1)} %get-tuple-element.42), channel_id=1, source_target_pairs={{4,0},{8,4},{12,8},{5,1},{9,5},{13,9},{6,2},{10,6},{14,10},{7,3},{... | collective-permute-start | bytes 811016 | tf_op jit(solution)/shard_map/ppermute | solution.py:131
  36.0 13.0 %collective-permute-start.13 = (bf16[528,256]{1,0:T(8,128)(2,1)S(1)}, bf16[528,256]{1,0:T(8,128)(2,1)S(1)}, u32[]{:S(2)}, u32[]{:S(2)}) collective-permute-start(bf16[528,256]{1,0:T(8,128)(2,1)S(1)} %get-tuple-element.42), channel_id=1, source_target_pairs={{8,0},{9,1},{10,2},{11,3},{24,16},{25,17},{26,18},{27,19}} | collective-permute-start | bytes 811016 | tf_op jit(solution)/shard_map/ppermute | solution.py:131
  37.3 1.6 %collective-permute-start.2 = (bf16[528,256]{1,0:T(8,128)(2,1)S(1)}, bf16[528,256]{1,0:T(8,128)(2,1)S(1)}, u32[]{:S(2)}, u32[]{:S(2)}) collective-permute-start(bf16[528,256]{1,0:T(8,128)(2,1)S(1)} %broadcast_select_fusion.5), channel_id=1, source_target_pairs={{0,1},{1,0},{2,3},{3,2},{4,5},{5,4},{6,7},{7,6},{8,9},{9,8},{10,11... | collective-permute-start | bytes 811016 | tf_op jit(solution)/shard_map/ppermute | solution.py:152
  39.0 10.9 %collective-permute-start.10 = (bf16[528,256]{1,0:T(8,128)(2,1)S(1)}, bf16[528,256]{1,0:T(8,128)(2,1)S(1)}, u32[]{:S(2)}, u32[]{:S(2)}) collective-permute-start(bf16[528,256]{1,0:T(8,128)(2,1)S(1)} %get-tuple-element.42), channel_id=1, source_target_pairs={{0,4},{4,8},{8,12},{1,5},{5,9},{9,13},{2,6},{6,10},{10,14},{3,7},{... | collective-permute-start | bytes 811016 | tf_op jit(solution)/shard_map/ppermute | solution.py:125
  43.0 9.9 %copy-start = (bf16[528,256]{1,0:T(8,128)(2,1)}, bf16[528,256]{1,0:T(8,128)(2,1)S(1)}, u32[]{:S(2)}) copy-start(bf16[528,256]{1,0:T(8,128)(2,1)S(1)} %broadcast_select_fusion.8) | copy-start | bytes 811012
  43.0 8.7 %collective-permute-start.9 = (bf16[528,256]{1,0:T(8,128)(2,1)S(1)}, bf16[528,256]{1,0:T(8,128)(2,1)S(1)}, u32[]{:S(2)}, u32[]{:S(2)}) collective-permute-start(bf16[528,256]{1,0:T(8,128)(2,1)S(1)} %get-tuple-element.42), channel_id=1, source_target_pairs={{0,1},{1,0},{2,3},{3,2},{4,5},{5,4},{6,7},{7,6},{8,9},{9,8},{10,11... | collective-permute-start | bytes 811016 | tf_op jit(solution)/shard_map/ppermute | solution.py:152
  49.1 1.4 %collective-permute-start.6 = (bf16[528,256]{1,0:T(8,128)(2,1)S(1)}, bf16[528,256]{1,0:T(8,128)(2,1)S(1)}, u32[]{:S(2)}, u32[]{:S(2)}) collective-permute-start(bf16[528,256]{1,0:T(8,128)(2,1)S(1)} %collective-permute-done.3), channel_id=1, source_target_pairs={{8,12},{9,13},{10,14},{11,15},{24,28},{25,29},{26,30},{27,31}} | collective-permute-start | bytes 811016 | tf_op jit(solution)/shard_map/ppermute | solution.py:123
  49.8 1.6 %collective-permute-start.5 = (bf16[528,256]{1,0:T(8,128)(2,1)S(1)}, bf16[528,256]{1,0:T(8,128)(2,1)S(1)}, u32[]{:S(2)}, u32[]{:S(2)}) collective-permute-start(bf16[528,256]{1,0:T(8,128)(2,1)S(1)} %broadcast_select_fusion.3), channel_id=1, source_target_pairs={{0,1},{1,0},{2,3},{3,2},{4,5},{5,4},{6,7},{7,6},{8,9},{9,8},{10,11... | collective-permute-start | bytes 811016 | tf_op jit(solution)/shard_map/ppermute | solution.py:152
  49.9 6.4 %collective-permute-start.14 = (bf16[528,256]{1,0:T(8,128)(2,1)S(1)}, bf16[528,256]{1,0:T(8,128)(2,1)S(1)}, u32[]{:S(2)}, u32[]{:S(2)}) collective-permute-start(bf16[528,256]{1,0:T(8,128)(2,1)S(1)} %broadcast_select_fusion.2), channel_id=1, source_target_pairs={{0,1},{1,0},{2,3},{3,2},{4,5},{5,4},{6,7},{7,6},{8,9},{9,8},{10,11... | collective-permute-start | bytes 811016 | tf_op jit(solution)/shard_map/ppermute | solution.py:152
  50.5 19.4 %collective-permute-start.11 = (bf16[528,256]{1,0:T(8,128)(2,1)S(1)}, bf16[528,256]{1,0:T(8,128)(2,1)S(1)}, u32[]{:S(2)}, u32[]{:S(2)}) collective-permute-start(bf16[528,256]{1,0:T(8,128)(2,1)S(1)} %broadcast_select_fusion.4), channel_id=1, source_target_pairs={{0,1},{1,0},{2,3},{3,2},{4,5},{5,4},{6,7},{7,6},{8,9},{9,8},{10,11... | collective-permute-start | bytes 811016 | tf_op jit(solution)/shard_map/ppermute | solution.py:152
  51.4 2.0 %collective-permute-start.8 = (bf16[528,256]{1,0:T(8,128)(2,1)S(1)}, bf16[528,256]{1,0:T(8,128)(2,1)S(1)}, u32[]{:S(2)}, u32[]{:S(2)}) collective-permute-start(bf16[528,256]{1,0:T(8,128)(2,1)S(1)} %broadcast_select_fusion.1), channel_id=1, source_target_pairs={{0,1},{1,0},{2,3},{3,2},{4,5},{5,4},{6,7},{7,6},{8,9},{9,8},{10,11... | collective-permute-start | bytes 811016 | tf_op jit(solution)/shard_map/ppermute | solution.py:152
  51.6 2.0 %copy-start.1 = (bf16[528,256]{1,0:T(8,128)(2,1)}, bf16[528,256]{1,0:T(8,128)(2,1)S(1)}, u32[]{:S(2)}) copy-start(bf16[528,256]{1,0:T(8,128)(2,1)S(1)} %broadcast_select_fusion.7) | copy-start | bytes 811012
  51.7 1.8 %copy-start.4 = (s32[4]{0:T(128)S(1)}, s32[4]{0:T(128)}, u32[]{:S(2)}) copy-start(s32[4]{0:T(128)} %param.19) | copy-start | bytes 52
  51.7 1.2 %collective-permute-start.15 = (bf16[528,256]{1,0:T(8,128)(2,1)S(1)}, bf16[528,256]{1,0:T(8,128)(2,1)S(1)}, u32[]{:S(2)}, u32[]{:S(2)}) collective-permute-start(bf16[528,256]{1,0:T(8,128)(2,1)S(1)} %collective-permute-done.12), channel_id=1, source_target_pairs={{8,12},{9,13},{10,14},{11,15},{24,28},{25,29},{26,30},{27,31}} | collective-permute-start | bytes 811016 | tf_op jit(solution)/shard_map/ppermute | solution.py:123
  53.0 2.4 %slice-start = ((bf16[528,256]{1,0:T(8,128)(2,1)}), bf16[512,256]{1,0:T(8,128)(2,1)S(1)}, s32[]{:S(2)}) async-start(bf16[528,256]{1,0:T(8,128)(2,1)} %copy-done), calls=%async_computation | async-start | bytes 524288 | tf_op jit(solution)/shard_map/slice | solution.py:158
  53.0 16.9 %collective-permute-start.17 = (bf16[528,256]{1,0:T(8,128)(2,1)S(1)}, bf16[528,256]{1,0:T(8,128)(2,1)S(1)}, u32[]{:S(2)}, u32[]{:S(2)}) collective-permute-start(bf16[528,256]{1,0:T(8,128)(2,1)S(1)} %broadcast_select_fusion), channel_id=1, source_target_pairs={{0,1},{1,0},{2,3},{3,2},{4,5},{5,4},{6,7},{7,6},{8,9},{9,8},{10,11... | collective-permute-start | bytes 811016 | tf_op jit(solution)/shard_map/ppermute | solution.py:152
  53.7 1.7 %slice-start.1 = ((bf16[528,256]{1,0:T(8,128)(2,1)}), bf16[512,256]{1,0:T(8,128)(2,1)S(1)}, s32[]{:S(2)}) async-start(bf16[528,256]{1,0:T(8,128)(2,1)} %copy-done.1), calls=%async_computation.1 | async-start | bytes 524288 | tf_op jit(solution)/shard_map/slice | solution.py:158
  71.5 12.5 %copy-start.3 = (f32[1,2048]{1,0:T(1,128)S(1)}, f32[1,2048]{1,0:T(1,128)}, u32[]{:S(2)}) copy-start(f32[1,2048]{1,0:T(1,128)} %get-tuple-element.29) | copy-start | bytes 24580
  86.5 7.4 %collective-permute-start.19 = (f32[2080]{0:T(1024)S(1)}, f32[2080]{0:T(1024)S(1)}, u32[]{:S(2)}, u32[]{:S(2)}) collective-permute-start(f32[2080]{0:T(1024)S(1)} %pad_maximum_fusion.6), channel_id=1, source_target_pairs={{0,1},{1,0},{2,3},{3,2},{4,5},{5,4},{6,7},{7,6},{8,9},{9,8},{10,11... | collective-permute-start | bytes 24968 | tf_op jit(solution)/shard_map/ppermute | solution.py:176
  92.3 30.0 %collective-permute-start.18 = (bf16[128,2048]{1,0:T(8,128)(2,1)S(1)}, bf16[128,2048]{1,0:T(8,128)(2,1)S(1)}, u32[]{:S(2)}, u32[]{:S(2)}) collective-permute-start(bf16[128,2048]{1,0:T(8,128)(2,1)S(1)} %fusion.4), channel_id=1, source_target_pairs={{0,2},{2,0},{1,3},{3,1},{4,6},{6,4},{5,7},{7,5},{8,10},{10,8},{9,1... | collective-permute-start | bytes 1572872 | tf_op jit(solution)/shard_map/ppermute | solution.py:246
  93.9 3.8 %collective-permute-start.20 = (f32[2080]{0:T(1024)S(1)}, f32[2080]{0:T(1024)S(1)}, u32[]{:S(2)}, u32[]{:S(2)}) collective-permute-start(f32[2080]{0:T(1024)S(1)} %fusion.20), channel_id=1, source_target_pairs={{0,4},{4,0},{8,12},{12,8},{1,5},{5,1},{9,13},{13,9},{2,6},{6,2},{1... | collective-permute-start | bytes 24968 | tf_op jit(solution)/shard_map/ppermute | solution.py:176
  97.7 18.2 %collective-permute-start.21 = (f32[2080]{0:T(1024)S(1)}, f32[2080]{0:T(1024)S(1)}, u32[]{:S(2)}, u32[]{:S(2)}) collective-permute-start(f32[2080]{0:T(1024)S(1)} %add.101), channel_id=1, source_target_pairs={{0,8},{4,12},{8,0},{12,4},{1,9},{5,13},{9,1},{13,5},{2,10},{6,14},... | collective-permute-start | bytes 24968 | tf_op jit(solution)/shard_map/ppermute | solution.py:176
  116.0 5.2 %collective-permute-start.22 = (f32[2080]{0:T(1024)S(1)}, f32[2080]{0:T(1024)S(1)}, u32[]{:S(2)}, u32[]{:S(2)}) collective-permute-start(f32[2080]{0:T(1024)S(1)} %add.102), channel_id=1, source_target_pairs={{0,2},{2,0},{1,3},{3,1},{4,6},{6,4},{5,7},{7,5},{8,10},{10,8},{9,1... | collective-permute-start | bytes 24968 | tf_op jit(solution)/shard_map/ppermute | solution.py:176

commit v13 on v11

--- a/solution.py
+++ b/solution.py
@@ -23,33 +23,36 @@
 
     k = k_ref[...]
     v = v_ref[...]
-    row_pos = base_ref[0] + r * tq + lax.broadcasted_iota(jnp.int32, (tq, 1), 0)
-    vis = kpos_ref[...] <= row_pos
     kept = kept_ref[...] > 0.0
+    sub = 32 if tq % 32 == 0 else tq
     total = None
     for h in range(hp):
         cols = slice(h * HD, (h + 1) * HD)
-        s = lax.dot_general(q_ref[:, cols], k, NT_DIMS, preferred_element_type=jnp.float32)
-        s = s * (HD ** -0.5)
-        s_c = jnp.where(vis, s, NEG_FILL)
-        s_m = jnp.where(kept, s_c, NEG_FILL)
-        m_c = jnp.max(s_c, axis=1, keepdims=True)
-        m_m = jnp.max(s_m, axis=1, keepdims=True)
-        e_c = jnp.exp(s_c - m_c)
-        e_m = jnp.exp(s_m - m_m)
-        l_c = jnp.sum(e_c, axis=1, keepdims=True)
-        l_m = jnp.sum(e_m, axis=1, keepdims=True)
-        o_c = jnp.dot(e_c.astype(jnp.bfloat16), v, preferred_element_type=jnp.float32) / l_c
-        o_m = jnp.dot(e_m.astype(jnp.bfloat16), v, preferred_element_type=jnp.float32) / l_m
-        delta_ref[:, cols] = (o_m - o_c).astype(delta_ref.dtype)
-        g_rows = do_ref[:, cols]
-        row_dot = jnp.sum(g_rows.astype(jnp.float32) * o_c, axis=1, keepdims=True)
-        d_p = lax.dot_general(g_rows, v, NT_DIMS, preferred_element_type=jnp.float32)
-        log_total = m_c + jnp.log(l_c)
-        prob = e_c * (1.0 / l_c)
-        contrib = prob * (d_p + (d_p - row_dot) * (s - log_total))
-        part = jnp.sum(contrib, axis=0, keepdims=True)
-        total = part if total is None else total + part
+        for rb in range(tq // sub):
+            rows = slice(rb * sub, (rb + 1) * sub)
+            row_pos = base_ref[0] + r * tq + rb * sub + lax.broadcasted_iota(jnp.int32, (sub, 1), 0)
+            vis = kpos_ref[...] <= row_pos
+            s = lax.dot_general(q_ref[rows, cols], k, NT_DIMS, preferred_element_type=jnp.float32)
+            s = s * (HD ** -0.5)
+            s_c = jnp.where(vis, s, NEG_FILL)
+            s_m = jnp.where(kept, s_c, NEG_FILL)
+            m_c = jnp.max(s_c, axis=1, keepdims=True)
+            m_m = jnp.max(s_m, axis=1, keepdims=True)
+            e_c = jnp.exp(s_c - m_c)
+            e_m = jnp.exp(s_m - m_m)
+            l_c = jnp.sum(e_c, axis=1, keepdims=True)
+            l_m = jnp.sum(e_m, axis=1, keepdims=True)
+            o_c = jnp.dot(e_c.astype(jnp.bfloat16), v, preferred_element_type=jnp.float32) / l_c
+            o_m = jnp.dot(e_m.astype(jnp.bfloat16), v, preferred_element_type=jnp.float32) / l_m
+            delta_ref[rows, cols] = (o_m - o_c).astype(delta_ref.dtype)
+            g_rows = do_ref[rows, cols]
+            row_dot = jnp.sum(g_rows.astype(jnp.float32) * o_c, axis=1, keepdims=True)
+            d_p = lax.dot_general(g_rows, v, NT_DIMS, preferred_element_type=jnp.float32)
+            log_total = m_c + jnp.log(l_c)
+            prob = e_c * (1.0 / l_c)
+            contrib = prob * (d_p + (d_p - row_dot) * (s - log_total))
+            part = jnp.sum(contrib, axis=0, keepdims=True)
+            total = part if total is None else total + part
     attr_ref[...] += total
 
 

time: 106 us -> 135 us (1.27)
  Pallas kernels: 23.1 us -> 51.8 us
    pallas_call x1, Pallas kernels: 23.1 us -> 51.8 us  [fused_attention(): pl.pallas_call(functools.partial(attention_kernel, tq=tq, hp=hp), grid_sp...]
  transfers between devices with their start and end apart: 14 -> 14, of which waited for: 5 -> 5; matrix products, arithmetic and copies ran while one was open for 24% -> 19% of each run, Pallas kernels for 0% -> 0%
where the time goes in v13:
time: 135 us
  Pallas kernels  51.8 us (38%)
  starting transfers between devices  35.9 us (27%)
  matrix products  23.4 us (17%)
  waiting for transfers between devices  10.1 us (7%)
  other arithmetic  9.35 us (7%)
  local copies, waits for them, and re-layouts  3.12 us (2%)
    pallas_call x1, Pallas kernels, fused_attention(): pl.pallas_call(functools.partial(attention_kernel, tq=tq, hp=hp), grid_sp...  51.8 us
    ppermute x4, starting transfers between devices, butterfly_sum(): total = total + lax.ppermute(total, axis, [(i, i ^ bit) for i in range(n)])  19.5 us
    dot_general x1, matrix products, local(): jnp.dot(grad_masked, out_weight.T, preferred_element_type=jnp.float32)  12.6 us
    ppermute x2, starting transfers between devices, relay_gather(): forward.append(lax.ppermute(payload, 'ctx', fwd) if fwd else zero)  10.5 us
    dot_general x1, matrix products, local(): send = jnp.dot(delta, send_w, preferred_element_type=jnp.float32)  4.86 us
    dot_general x1, matrix products, local(): jnp.dot(delta, keep_w, preferred_element_type=jnp.float32)  4.63 us
    ppermute x2, waiting for transfers between devices, relay_gather(): backward.append(lax.ppermute(payload, 'ctx', bwd) if bwd else zero)  4.61 us
    ppermute x4, waiting for transfers between devices, butterfly_sum(): total = total + lax.ppermute(total, axis, [(i, i ^ bit) for i in range(n)])  3.48 us
  transfers between devices with their start and end apart: 14, of which 5 were waited for; matrix products, arithmetic and copies ran while one was open for 19% of the time, Pallas kernels for 0%

profile of v13, /device:TPU:0, one launch (start us, length us, event | category | flops | bytes accessed | tf_op | source)
XLA Modules:
  0.0 134.5 jit_solution(12958677595241437655)
XLA Ops:
  0.6 0.7 convert_element_type.23
  1.4 1.1 broadcast_select_fusion.7
  2.5 0.8 pad_maximum_fusion.2
  3.3 6.0 %collective-permute-start.3 = (bf16[528,512]{1,0:T(8,128)(2,1)}, bf16[528,512]{1,0:T(8,128)(2,1)S(1)}, u32[]{:S(2)}, u32[]{:S(2)}) collective-permute-start(bf16[528,512]{1,0:T(8,128)(2,1)} %pad_maximum_fusion.2), channel_id=1, source_target_pairs={{0,8},{4,12},{1,9},{5,13},{2,10},{6,14},{3,11},{7,15},{16,24},{20,... | collective-permute-start | bytes 1622024 | tf_op jit(solution)/shard_map/ppermute | solution.py:124
  9.3 1.3 collective-permute-start.4
  10.6 1.3 collective-permute-start.7
  11.9 4.6 %collective-permute-start.1 = (bf16[528,512]{1,0:T(8,128)(2,1)}, bf16[528,512]{1,0:T(8,128)(2,1)S(1)}, u32[]{:S(2)}, u32[]{:S(2)}) collective-permute-start(bf16[528,512]{1,0:T(8,128)(2,1)} %pad_maximum_fusion.2), channel_id=1, source_target_pairs={{0,4},{4,8},{8,12},{1,5},{5,9},{9,13},{2,6},{6,10},{10,14},{3,7},{... | collective-permute-start | bytes 1622024 | tf_op jit(solution)/shard_map/ppermute | solution.py:124
  16.5 0.1 collective-permute-start
  16.5 0.7 broadcast_compare_fusion
  17.2 12.6 %convolution_convert_fusion.do_ref = bf16[128,2048]{1,0:T(8,128)(2,1)} fusion(bf16[2048,4096]{1,0:T(8,128)(2,1)} %param.13, bf16[128,4096]{1,0:T(8,128)(2,1)} %param.14, pred[128]{0:T(512)(128)(4,1)S(1)} %broadcast_compare_fusion), kind=kOutput, calls=%fused_computation.6 | convolution fusion | flops 2148270080 | bytes 18350208 | tf_op jit(solution)/shard_map/dot_general | solution.py:212
  29.8 0.1 add_bitcast_fusion
  29.9 0.6 copy.11
  30.5 0.0 collective-permute-done.3
  30.5 0.0 collective-permute-done.4
  30.5 0.1 broadcast_select_fusion.1
  30.6 0.6 collective-permute-start.5
  31.2 0.9 collective-permute-start.6
  32.0 0.0 collective-permute-done
  32.0 0.1 broadcast_select_fusion.6
  32.2 0.0 copy-start
  32.2 0.5 collective-permute-done.1
  32.8 0.1 collective-permute-start.2
  32.8 0.1 fusion.10
  33.0 4.6 %collective-permute-done.7 = bf16[528,512]{1,0:T(8,128)(2,1)S(1)} collective-permute-done((bf16[528,512]{1,0:T(8,128)(2,1)}, bf16[528,512]{1,0:T(8,128)(2,1)S(1)}, u32[]{:S(2)}, u32[]{:S(2)}) %collective-permute-start.7) | collective-permute-done | bytes 540704 | tf_op jit(solution)/shard_map/ppermute | solution.py:130
  37.6 0.0 collective-permute-done.6
  37.6 0.1 broadcast_select_fusion
  37.7 0.1 collective-permute-start.8
  37.8 0.0 collective-permute-done.5
  37.8 0.1 broadcast_select_fusion.4
  37.8 0.0 collective-permute-done.2
  37.9 0.1 broadcast_select_fusion.5
  37.9 0.0 copy-done
  37.9 0.0 copy-start.2
  38.0 0.0 slice-start
  38.1 0.1 slice_select_fusion.1
  38.1 0.1 slice_select_fusion.2
  38.2 1.5 %collective-permute-done.8 = bf16[528,512]{1,0:T(8,128)(2,1)S(1)} collective-permute-done((bf16[528,512]{1,0:T(8,128)(2,1)S(1)}, bf16[528,512]{1,0:T(8,128)(2,1)S(1)}, u32[]{:S(2)}, u32[]{:S(2)}) %collective-permute-start.8) | collective-permute-done | bytes 540704 | tf_op jit(solution)/shard_map/ppermute | solution.py:151
  39.7 0.1 broadcast_select_fusion.3
  39.8 0.0 copy-done.2
  39.8 0.1 compare_reduce_fusion
  39.9 0.6 broadcast_select_fusion.8
  40.5 0.1 slice_select_fusion
  40.6 0.0 slice-done
  40.6 2.2 %pad_maximum_fusion = (bf16[2048,512]{1,0:T(8,128)(2,1)}, bf16[2048,512]{1,0:T(8,128)(2,1)}) fusion(bf16[512,512]{1,0:T(8,128)(2,1)S(1)} %slice.84, bf16[512,512]{1,0:T(8,128)(2,1)S(1)} %slice.83, bf16[512,512]{1,0:T(8,128)(2,1)S(1)} %slice.82, bf16[512,512]{1,0:T(8,128)(2,1)S(1)} %slice-done, bf16[512,512]{1,0:T(8,128)(2,1)S(1)} %slice_select_fusion, ...), kind=kLoop, calls=%fused_computation.7 | loop fusion | flops 16777216 | bytes 8388608 | tf_op jit(solution)/shard_map/concatenate | solution.py:157
  42.8 51.8 %shard_map.103 = (bf16[128,2048]{1,0:T(8,128)(2,1)}, f32[1,2048]{1,0:T(1,128)}) custom-call(s32[1]{0:T(128)} %bitcast.base_ref, s32[1,2048]{1,0:T(1,128)} %bitcast.23, bf16[128,2048]{1,0:T(8,128)(2,1)} %q_ref.1, bf16[2048,512]{1,0:T(8,128)(2,1)} %get-tuple-element.19.k_ref, bf16[2048,512]{1,0:T(8,128)(2,1)} %get-tuple-element.20.v_ref, f32[1,2048]{1,0:T(1,128)} %bitcast.22, ...), custom_call_target="tpu_custom_call" | custom-call | flops 4294967296 | bytes 5775360 | tf_op jit(solution)/shard_map/pallas_call | solution.py:85
  94.5 1.3 convolution_bitcast_fusion
  95.8 0.5 broadcast.150
  96.3 1.4 %reduce.13 = f32[2048]{0:T(1024)S(1)} reduce(f32[1,2048]{1,0:T(1,128)} %get-tuple-element.18, f32[]{:T(128)} %broadcast.150), dimensions={0}, to_apply=%get-tuple-element.18.reduce_sub_computation.3 | reduce | bytes 16388 | tf_op jit(solution)/shard_map/pallas_call | solution.py:85
  97.7 0.6 gather_fusion
  98.3 0.2 collective-permute-start.10
  98.5 4.9 %fusion.4 = bf16[128,2048]{1,0:T(8,128)(2,1)S(1)} fusion(bf16[128,2048]{1,0:T(8,128)(2,1)} %get-tuple-element.17, bf16[2048,4096]{1,0:T(8,128)(2,1)} %param.13, s32[]{:T(128)S(6)} %select_n.142), kind=kOutput, calls=%fused_computation.5 | convolution fusion | flops 1074003968 | bytes 9437188 | tf_op jit(solution)/shard_map/dot_general | solution.py:229
  103.4 1.6 %collective-permute-start.9 = (bf16[128,2048]{1,0:T(8,128)(2,1)S(1)}, bf16[128,2048]{1,0:T(8,128)(2,1)S(1)}, u32[]{:S(2)}, u32[]{:S(2)}) collective-permute-start(bf16[128,2048]{1,0:T(8,128)(2,1)S(1)} %fusion.4), channel_id=1, source_target_pairs={{0,2},{2,0},{1,3},{3,1},{4,6},{6,4},{5,7},{7,5},{8,10},{10,8},{9,1... | collective-permute-start | bytes 1572872 | tf_op jit(solution)/shard_map/ppermute | solution.py:230
  104.9 0.0 collective-permute-done.10
  105.0 9.0 %collective-permute-start.11 = (f32[2080]{0:T(1024)S(1)}, f32[2080]{0:T(1024)S(1)}, u32[]{:S(2)}, u32[]{:S(2)}) collective-permute-start(f32[2080]{0:T(1024)S(1)} %fusion.21), channel_id=1, source_target_pairs={{0,4},{4,0},{8,12},{12,8},{1,5},{5,1},{9,13},{13,9},{2,6},{6,2},{1... | collective-permute-start | bytes 24968 | tf_op jit(solution)/shard_map/ppermute | solution.py:175
  113.9 1.7 %collective-permute-done.11 = f32[2080]{0:T(1024)S(1)} collective-permute-done((f32[2080]{0:T(1024)S(1)}, f32[2080]{0:T(1024)S(1)}, u32[]{:S(2)}, u32[]{:S(2)}) %collective-permute-start.11) | collective-permute-done | bytes 8352 | tf_op jit(solution)/shard_map/ppermute | solution.py:175
  115.6 9.9 %collective-permute-start.12 = (f32[2080]{0:T(1024)S(1)}, f32[2080]{0:T(1024)S(1)}, u32[]{:S(2)}, u32[]{:S(2)}) collective-permute-start(f32[2080]{0:T(1024)S(1)} %add.96), channel_id=1, source_target_pairs={{0,8},{4,12},{8,0},{12,4},{1,9},{5,13},{9,1},{13,5},{2,10},{6,14},... | collective-permute-start | bytes 24968 | tf_op jit(solution)/shard_map/ppermute | solution.py:175
  125.6 1.8 %collective-permute-done.12 = f32[2080]{0:T(1024)S(1)} collective-permute-done((f32[2080]{0:T(1024)S(1)}, f32[2080]{0:T(1024)S(1)}, u32[]{:S(2)}, u32[]{:S(2)}) %collective-permute-start.12) | collective-permute-done | bytes 8352 | tf_op jit(solution)/shard_map/ppermute | solution.py:175
  127.4 0.4 collective-permute-start.13
  127.8 4.6 %fusion.2 = f32[128,2048]{1,0:T(8,128)S(1)} fusion(bf16[128,2048]{1,0:T(8,128)(2,1)S(1)} %copy-done.1, bf16[2048,4096]{1,0:T(8,128)(2,1)} %param.13, s32[]{:T(128)S(6)} %select_n.141), kind=kOutput, calls=%fused_computation.3 | convolution fusion | flops 1073741824 | bytes 9961476 | tf_op jit(solution)/shard_map/dot_general | solution.py:232
  132.4 0.0 collective-permute-done.13
  132.5 0.5 slice.99
  133.0 0.7 dynamic_slice.11
  133.6 0.0 collective-permute-done.9
  133.6 0.9 add_convert_fusion
  (24 shorter events, 0.4 us)
Async XLA Ops:
  3.3 27.2 %collective-permute-start.3 = (bf16[528,512]{1,0:T(8,128)(2,1)}, bf16[528,512]{1,0:T(8,128)(2,1)S(1)}, u32[]{:S(2)}, u32[]{:S(2)}) collective-permute-start(bf16[528,512]{1,0:T(8,128)(2,1)} %pad_maximum_fusion.2), channel_id=1, source_target_pairs={{0,8},{4,12},{1,9},{5,13},{2,10},{6,14},{3,11},{7,15},{16,24},{20,... | collective-permute-start | bytes 1622024 | tf_op jit(solution)/shard_map/ppermute | solution.py:124
  9.3 21.3 %collective-permute-start.4 = (bf16[528,512]{1,0:T(8,128)(2,1)}, bf16[528,512]{1,0:T(8,128)(2,1)S(1)}, u32[]{:S(2)}, u32[]{:S(2)}) collective-permute-start(bf16[528,512]{1,0:T(8,128)(2,1)} %pad_maximum_fusion.2), channel_id=1, source_target_pairs={{8,0},{9,1},{10,2},{11,3},{24,16},{25,17},{26,18},{27,19}} | collective-permute-start | bytes 1622024 | tf_op jit(solution)/shard_map/ppermute | solution.py:130
  10.6 27.0 %collective-permute-start.7 = (bf16[528,512]{1,0:T(8,128)(2,1)}, bf16[528,512]{1,0:T(8,128)(2,1)S(1)}, u32[]{:S(2)}, u32[]{:S(2)}) collective-permute-start(bf16[528,512]{1,0:T(8,128)(2,1)} %pad_maximum_fusion.2), channel_id=1, source_target_pairs={{4,0},{8,4},{12,8},{5,1},{9,5},{13,9},{6,2},{10,6},{14,10},{7,3},{... | collective-permute-start | bytes 1622024 | tf_op jit(solution)/shard_map/ppermute | solution.py:130
  11.9 20.8 %collective-permute-start.1 = (bf16[528,512]{1,0:T(8,128)(2,1)}, bf16[528,512]{1,0:T(8,128)(2,1)S(1)}, u32[]{:S(2)}, u32[]{:S(2)}) collective-permute-start(bf16[528,512]{1,0:T(8,128)(2,1)} %pad_maximum_fusion.2), channel_id=1, source_target_pairs={{0,4},{4,8},{8,12},{1,5},{5,9},{9,13},{2,6},{6,10},{10,14},{3,7},{... | collective-permute-start | bytes 1622024 | tf_op jit(solution)/shard_map/ppermute | solution.py:124
  16.5 15.6 %collective-permute-start = (bf16[528,512]{1,0:T(8,128)(2,1)}, bf16[528,512]{1,0:T(8,128)(2,1)S(1)}, u32[]{:S(2)}, u32[]{:S(2)}) collective-permute-start(bf16[528,512]{1,0:T(8,128)(2,1)} %pad_maximum_fusion.2), channel_id=1, source_target_pairs={{0,1},{1,0},{2,3},{3,2},{4,5},{5,4},{6,7},{7,6},{8,9},{9,8},{10,11... | collective-permute-start | bytes 1622024 | tf_op jit(solution)/shard_map/ppermute | solution.py:151
  30.6 7.2 %collective-permute-start.5 = (bf16[528,512]{1,0:T(8,128)(2,1)S(1)}, bf16[528,512]{1,0:T(8,128)(2,1)S(1)}, u32[]{:S(2)}, u32[]{:S(2)}) collective-permute-start(bf16[528,512]{1,0:T(8,128)(2,1)S(1)} %broadcast_select_fusion.1), channel_id=1, source_target_pairs={{0,1},{1,0},{2,3},{3,2},{4,5},{5,4},{6,7},{7,6},{8,9},{9,8},{10,11... | collective-permute-start | bytes 1622024 | tf_op jit(solution)/shard_map/ppermute | solution.py:151
  31.2 6.5 %collective-permute-start.6 = (bf16[528,512]{1,0:T(8,128)(2,1)S(1)}, bf16[528,512]{1,0:T(8,128)(2,1)S(1)}, u32[]{:S(2)}, u32[]{:S(2)}) collective-permute-start(bf16[528,512]{1,0:T(8,128)(2,1)S(1)} %collective-permute-done.3), channel_id=1, source_target_pairs={{8,12},{9,13},{10,14},{11,15},{24,28},{25,29},{26,30},{27,31}} | collective-permute-start | bytes 1622024 | tf_op jit(solution)/shard_map/ppermute | solution.py:122
  32.2 5.7 %copy-start = (bf16[528,512]{1,0:T(8,128)(2,1)}, bf16[528,512]{1,0:T(8,128)(2,1)S(1)}, u32[]{:S(2)}) copy-start(bf16[528,512]{1,0:T(8,128)(2,1)S(1)} %broadcast_select_fusion.6) | copy-start | bytes 1622020
  32.8 5.1 %collective-permute-start.2 = (bf16[528,512]{1,0:T(8,128)(2,1)S(1)}, bf16[528,512]{1,0:T(8,128)(2,1)S(1)}, u32[]{:S(2)}, u32[]{:S(2)}) collective-permute-start(bf16[528,512]{1,0:T(8,128)(2,1)S(1)} %broadcast_select_fusion.2), channel_id=1, source_target_pairs={{0,1},{1,0},{2,3},{3,2},{4,5},{5,4},{6,7},{7,6},{8,9},{9,8},{10,11... | collective-permute-start | bytes 1622024 | tf_op jit(solution)/shard_map/ppermute | solution.py:151
  37.7 2.0 %collective-permute-start.8 = (bf16[528,512]{1,0:T(8,128)(2,1)S(1)}, bf16[528,512]{1,0:T(8,128)(2,1)S(1)}, u32[]{:S(2)}, u32[]{:S(2)}) collective-permute-start(bf16[528,512]{1,0:T(8,128)(2,1)S(1)} %broadcast_select_fusion), channel_id=1, source_target_pairs={{0,1},{1,0},{2,3},{3,2},{4,5},{5,4},{6,7},{7,6},{8,9},{9,8},{10,11... | collective-permute-start | bytes 1622024 | tf_op jit(solution)/shard_map/ppermute | solution.py:151
  37.9 1.9 %copy-start.2 = (s32[4]{0:T(128)S(1)}, s32[4]{0:T(128)}, u32[]{:S(2)}) copy-start(s32[4]{0:T(128)} %param.17) | copy-start | bytes 52
  38.0 2.6 %slice-start = ((bf16[528,512]{1,0:T(8,128)(2,1)}), bf16[512,512]{1,0:T(8,128)(2,1)S(1)}, s32[]{:S(2)}) async-start(bf16[528,512]{1,0:T(8,128)(2,1)} %copy-done), calls=%async_computation | async-start | bytes 1048576 | tf_op jit(solution)/shard_map/slice | solution.py:157
  98.3 6.7 %collective-permute-start.10 = (f32[2080]{0:T(1024)S(1)}, f32[2080]{0:T(1024)S(1)}, u32[]{:S(2)}, u32[]{:S(2)}) collective-permute-start(f32[2080]{0:T(1024)S(1)} %pad_maximum_fusion.3), channel_id=1, source_target_pairs={{0,1},{1,0},{2,3},{3,2},{4,5},{5,4},{6,7},{7,6},{8,9},{9,8},{10,11... | collective-permute-start | bytes 24968 | tf_op jit(solution)/shard_map/ppermute | solution.py:175
  98.5 29.3 %copy-start.1 = (bf16[128,2048]{1,0:T(8,128)(2,1)S(1)}, bf16[128,2048]{1,0:T(8,128)(2,1)}, u32[]{:S(2)}) copy-start(bf16[128,2048]{1,0:T(8,128)(2,1)} %get-tuple-element.17) | copy-start | bytes 1572868
  103.4 30.2 %collective-permute-start.9 = (bf16[128,2048]{1,0:T(8,128)(2,1)S(1)}, bf16[128,2048]{1,0:T(8,128)(2,1)S(1)}, u32[]{:S(2)}, u32[]{:S(2)}) collective-permute-start(bf16[128,2048]{1,0:T(8,128)(2,1)S(1)} %fusion.4), channel_id=1, source_target_pairs={{0,2},{2,0},{1,3},{3,1},{4,6},{6,4},{5,7},{7,5},{8,10},{10,8},{9,1... | collective-permute-start | bytes 1572872 | tf_op jit(solution)/shard_map/ppermute | solution.py:230
  105.0 10.7 %collective-permute-start.11 = (f32[2080]{0:T(1024)S(1)}, f32[2080]{0:T(1024)S(1)}, u32[]{:S(2)}, u32[]{:S(2)}) collective-permute-start(f32[2080]{0:T(1024)S(1)} %fusion.21), channel_id=1, source_target_pairs={{0,4},{4,0},{8,12},{12,8},{1,5},{5,1},{9,13},{13,9},{2,6},{6,2},{1... | collective-permute-start | bytes 24968 | tf_op jit(solution)/shard_map/ppermute | solution.py:175
  115.6 11.7 %collective-permute-start.12 = (f32[2080]{0:T(1024)S(1)}, f32[2080]{0:T(1024)S(1)}, u32[]{:S(2)}, u32[]{:S(2)}) collective-permute-start(f32[2080]{0:T(1024)S(1)} %add.96), channel_id=1, source_target_pairs={{0,8},{4,12},{8,0},{12,4},{1,9},{5,13},{9,1},{13,5},{2,10},{6,14},... | collective-permute-start | bytes 24968 | tf_op jit(solution)/shard_map/ppermute | solution.py:175
  127.4 5.1 %collective-permute-start.13 = (f32[2080]{0:T(1024)S(1)}, f32[2080]{0:T(1024)S(1)}, u32[]{:S(2)}, u32[]{:S(2)}) collective-permute-start(f32[2080]{0:T(1024)S(1)} %add.97), channel_id=1, source_target_pairs={{0,2},{2,0},{1,3},{3,1},{4,6},{6,4},{5,7},{7,5},{8,10},{10,8},{9,1... | collective-permute-start | bytes 24968 | tf_op jit(solution)/shard_map/ppermute | solution.py:175

commit v14 on v11

--- a/solution.py
+++ b/solution.py
@@ -23,33 +23,36 @@
 
     k = k_ref[...]
     v = v_ref[...]
-    row_pos = base_ref[0] + r * tq + lax.broadcasted_iota(jnp.int32, (tq, 1), 0)
+    rows = hp * tq
+    row_pos = base_ref[0] + r * tq + lax.broadcasted_iota(jnp.int32, (rows, 1), 0) % tq
     vis = kpos_ref[...] <= row_pos
     kept = kept_ref[...] > 0.0
-    total = None
+    if hp > 1:
+        q = jnp.concatenate([q_ref[:, h * HD:(h + 1) * HD] for h in range(hp)], axis=0)
+        g_rows = jnp.concatenate([do_ref[:, h * HD:(h + 1) * HD] for h in range(hp)], axis=0)
+    else:
+        q = q_ref[...]
+        g_rows = do_ref[...]
+    s = lax.dot_general(q, k, NT_DIMS, preferred_element_type=jnp.float32) * (HD ** -0.5)
+    s_c = jnp.where(vis, s, NEG_FILL)
+    s_m = jnp.where(kept, s_c, NEG_FILL)
+    m_c = jnp.max(s_c, axis=1, keepdims=True)
+    m_m = jnp.max(s_m, axis=1, keepdims=True)
+    e_c = jnp.exp(s_c - m_c)
+    e_m = jnp.exp(s_m - m_m)
+    l_c = jnp.sum(e_c, axis=1, keepdims=True)
+    l_m = jnp.sum(e_m, axis=1, keepdims=True)
+    o_c = jnp.dot(e_c.astype(jnp.bfloat16), v, preferred_element_type=jnp.float32) / l_c
+    o_m = jnp.dot(e_m.astype(jnp.bfloat16), v, preferred_element_type=jnp.float32) / l_m
+    delta = (o_m - o_c).astype(delta_ref.dtype)
     for h in range(hp):
-        cols = slice(h * HD, (h + 1) * HD)
-        s = lax.dot_general(q_ref[:, cols], k, NT_DIMS, preferred_element_type=jnp.float32)
-        s = s * (HD ** -0.5)
-        s_c = jnp.where(vis, s, NEG_FILL)
-        s_m = jnp.where(kept, s_c, NEG_FILL)
-        m_c = jnp.max(s_c, axis=1, keepdims=True)
-        m_m = jnp.max(s_m, axis=1, keepdims=True)
-        e_c = jnp.exp(s_c - m_c)
-        e_m = jnp.exp(s_m - m_m)
-        l_c = jnp.sum(e_c, axis=1, keepdims=True)
-        l_m = jnp.sum(e_m, axis=1, keepdims=True)
-        o_c = jnp.dot(e_c.astype(jnp.bfloat16), v, preferred_element_type=jnp.float32) / l_c
-        o_m = jnp.dot(e_m.astype(jnp.bfloat16), v, preferred_element_type=jnp.float32) / l_m
-        delta_ref[:, cols] = (o_m - o_c).astype(delta_ref.dtype)
-        g_rows = do_ref[:, cols]
-        row_dot = jnp.sum(g_rows.astype(jnp.float32) * o_c, axis=1, keepdims=True)
-        d_p = lax.dot_general(g_rows, v, NT_DIMS, preferred_element_type=jnp.float32)
-        log_total = m_c + jnp.log(l_c)
-        prob = e_c * (1.0 / l_c)
-        contrib = prob * (d_p + (d_p - row_dot) * (s - log_total))
-        part = jnp.sum(contrib, axis=0, keepdims=True)
-        total = part if total is None else total + part
+        delta_ref[:, h * HD:(h + 1) * HD] = delta[h * tq:(h + 1) * tq]
+    row_dot = jnp.sum(g_rows.astype(jnp.float32) * o_c, axis=1, keepdims=True)
+    d_p = lax.dot_general(g_rows, v, NT_DIMS, preferred_element_type=jnp.float32)
+    log_total = m_c + jnp.log(l_c)
+    prob = e_c * (1.0 / l_c)
+    contrib = prob * (d_p + (d_p - row_dot) * (s - log_total))
+    total = jnp.sum(contrib, axis=0, keepdims=True)
     attr_ref[...] += total
 
 

time: 106 us -> 105 us (level)
  Pallas kernels: 23.1 us -> 21.3 us
    pallas_call x1, Pallas kernels: 23.1 us -> 21.3 us  [fused_attention(): pl.pallas_call(functools.partial(attention_kernel, tq=tq, hp=hp), grid_sp...]
where the time goes in v14:
time: 105 us; the launch traced here: 104 us
  starting transfers between devices  35.9 us (34%)
  matrix products  23.3 us (22%)
  Pallas kernels  21.3 us (20%)
  waiting for transfers between devices  10.1 us (10%)
  other arithmetic  9.35 us (9%)
  local copies, waits for them, and re-layouts  3.12 us (3%)
    pallas_call x1, Pallas kernels, fused_attention(): pl.pallas_call(functools.partial(attention_kernel, tq=tq, hp=hp), grid_sp...  21.3 us
    ppermute x4, starting transfers between devices, butterfly_sum(): total = total + lax.ppermute(total, axis, [(i, i ^ bit) for i in range(n)])  19.5 us
    dot_general x1, matrix products, local(): jnp.dot(grad_masked, out_weight.T, preferred_element_type=jnp.float32)  12.6 us
    ppermute x2, starting transfers between devices, relay_gather(): forward.append(lax.ppermute(payload, 'ctx', fwd) if fwd else zero)  10.5 us
    dot_general x1, matrix products, local(): send = jnp.dot(delta, send_w, preferred_element_type=jnp.float32)  4.86 us
    dot_general x1, matrix products, local(): jnp.dot(delta, keep_w, preferred_element_type=jnp.float32)  4.63 us
    ppermute x2, waiting for transfers between devices, relay_gather(): backward.append(lax.ppermute(payload, 'ctx', bwd) if bwd else zero)  4.61 us
    ppermute x4, waiting for transfers between devices, butterfly_sum(): total = total + lax.ppermute(total, axis, [(i, i ^ bit) for i in range(n)])  3.48 us
  transfers between devices with their start and end apart: 14, of which 5 were waited for; matrix products, arithmetic and copies ran while one was open for 24% of the time, Pallas kernels for 0%

profile of v14, /device:TPU:0, one launch (start us, length us, event | category | flops | bytes accessed | tf_op | source)
XLA Modules:
  0.0 104.1 jit_solution(4921787056760768321)
XLA Ops:
  0.6 0.7 convert_element_type.23
  1.4 1.1 %broadcast_select_fusion.7 = bf16[512,512]{1,0:T(8,128)(2,1)S(1)} fusion(bf16[512,512]{1,0:T(8,128)(2,1)} %param.11, bf16[512,512]{1,0:T(8,128)(2,1)} %param.12, pred[]{:T(512)S(6)} %eq.17), kind=kLoop, calls=%fused_computation.30 | loop fusion | flops 262144 | bytes 1572865 | tf_op jit(solution)/shard_map/jit(_where)/select_n | solution.py:146
  2.5 0.8 pad_maximum_fusion.2
  3.3 6.0 %collective-permute-start.3 = (bf16[528,512]{1,0:T(8,128)(2,1)}, bf16[528,512]{1,0:T(8,128)(2,1)S(1)}, u32[]{:S(2)}, u32[]{:S(2)}) collective-permute-start(bf16[528,512]{1,0:T(8,128)(2,1)} %pad_maximum_fusion.2), channel_id=1, source_target_pairs={{0,8},{4,12},{1,9},{5,13},{2,10},{6,14},{3,11},{7,15},{16,24},{20,... | collective-permute-start | bytes 1622024 | tf_op jit(solution)/shard_map/ppermute | solution.py:124
  9.3 1.3 %collective-permute-start.4 = (bf16[528,512]{1,0:T(8,128)(2,1)}, bf16[528,512]{1,0:T(8,128)(2,1)S(1)}, u32[]{:S(2)}, u32[]{:S(2)}) collective-permute-start(bf16[528,512]{1,0:T(8,128)(2,1)} %pad_maximum_fusion.2), channel_id=1, source_target_pairs={{8,0},{9,1},{10,2},{11,3},{24,16},{25,17},{26,18},{27,19}} | collective-permute-start | bytes 1622024 | tf_op jit(solution)/shard_map/ppermute | solution.py:130
  10.6 1.3 %collective-permute-start.7 = (bf16[528,512]{1,0:T(8,128)(2,1)}, bf16[528,512]{1,0:T(8,128)(2,1)S(1)}, u32[]{:S(2)}, u32[]{:S(2)}) collective-permute-start(bf16[528,512]{1,0:T(8,128)(2,1)} %pad_maximum_fusion.2), channel_id=1, source_target_pairs={{4,0},{8,4},{12,8},{5,1},{9,5},{13,9},{6,2},{10,6},{14,10},{7,3},{... | collective-permute-start | bytes 1622024 | tf_op jit(solution)/shard_map/ppermute | solution.py:130
  11.9 4.6 %collective-permute-start.1 = (bf16[528,512]{1,0:T(8,128)(2,1)}, bf16[528,512]{1,0:T(8,128)(2,1)S(1)}, u32[]{:S(2)}, u32[]{:S(2)}) collective-permute-start(bf16[528,512]{1,0:T(8,128)(2,1)} %pad_maximum_fusion.2), channel_id=1, source_target_pairs={{0,4},{4,8},{8,12},{1,5},{5,9},{9,13},{2,6},{6,10},{10,14},{3,7},{... | collective-permute-start | bytes 1622024 | tf_op jit(solution)/shard_map/ppermute | solution.py:124
  16.5 0.1 collective-permute-start
  16.5 0.7 broadcast_compare_fusion
  17.2 12.6 %convolution_convert_fusion.do_ref = bf16[128,2048]{1,0:T(8,128)(2,1)} fusion(bf16[2048,4096]{1,0:T(8,128)(2,1)} %param.13, bf16[128,4096]{1,0:T(8,128)(2,1)} %param.14, pred[128]{0:T(512)(128)(4,1)S(1)} %broadcast_compare_fusion), kind=kOutput, calls=%fused_computation.6 | convolution fusion | flops 2148270080 | bytes 18350208 | tf_op jit(solution)/shard_map/dot_general | solution.py:212
  29.8 0.1 add_bitcast_fusion
  29.9 0.6 copy.11
  30.5 0.0 collective-permute-done.3
  30.5 0.0 collective-permute-done.4
  30.5 0.1 broadcast_select_fusion.1
  30.6 0.6 collective-permute-start.5
  31.2 0.9 collective-permute-start.6
  32.0 0.0 collective-permute-done
  32.0 0.1 broadcast_select_fusion.6
  32.2 0.0 copy-start
  32.2 0.5 collective-permute-done.1
  32.8 0.1 collective-permute-start.2
  32.8 0.1 fusion.10
  33.0 4.6 %collective-permute-done.7 = bf16[528,512]{1,0:T(8,128)(2,1)S(1)} collective-permute-done((bf16[528,512]{1,0:T(8,128)(2,1)}, bf16[528,512]{1,0:T(8,128)(2,1)S(1)}, u32[]{:S(2)}, u32[]{:S(2)}) %collective-permute-start.7) | collective-permute-done | bytes 540704 | tf_op jit(solution)/shard_map/ppermute | solution.py:130
  37.6 0.0 collective-permute-done.6
  37.6 0.1 broadcast_select_fusion
  37.7 0.1 collective-permute-start.8
  37.8 0.0 collective-permute-done.5
  37.8 0.1 broadcast_select_fusion.4
  37.8 0.0 collective-permute-done.2
  37.9 0.1 broadcast_select_fusion.5
  37.9 0.0 copy-done
  37.9 0.0 copy-start.2
  38.0 0.0 slice-start
  38.1 0.1 slice_select_fusion.1
  38.1 0.1 slice_select_fusion.2
  38.2 1.5 %collective-permute-done.8 = bf16[528,512]{1,0:T(8,128)(2,1)S(1)} collective-permute-done((bf16[528,512]{1,0:T(8,128)(2,1)S(1)}, bf16[528,512]{1,0:T(8,128)(2,1)S(1)}, u32[]{:S(2)}, u32[]{:S(2)}) %collective-permute-start.8) | collective-permute-done | bytes 540704 | tf_op jit(solution)/shard_map/ppermute | solution.py:151
  39.7 0.1 broadcast_select_fusion.3
  39.8 0.0 copy-done.2
  39.8 0.1 compare_reduce_fusion
  39.9 0.6 broadcast_select_fusion.8
  40.5 0.1 slice_select_fusion
  40.6 0.0 slice-done
  40.6 2.2 %pad_maximum_fusion = (bf16[2048,512]{1,0:T(8,128)(2,1)}, bf16[2048,512]{1,0:T(8,128)(2,1)}) fusion(bf16[512,512]{1,0:T(8,128)(2,1)S(1)} %slice.84, bf16[512,512]{1,0:T(8,128)(2,1)S(1)} %slice.83, bf16[512,512]{1,0:T(8,128)(2,1)S(1)} %slice.82, bf16[512,512]{1,0:T(8,128)(2,1)S(1)} %slice-done, bf16[512,512]{1,0:T(8,128)(2,1)S(1)} %slice_select_fusion, ...), kind=kLoop, calls=%fused_computation.7 | loop fusion | flops 16777216 | bytes 8388608 | tf_op jit(solution)/shard_map/concatenate | solution.py:157
  42.8 21.3 %shard_map.103 = (bf16[128,2048]{1,0:T(8,128)(2,1)}, f32[1,2048]{1,0:T(1,128)}) custom-call(s32[1]{0:T(128)} %bitcast.base_ref, s32[1,2048]{1,0:T(1,128)} %bitcast.23, bf16[128,2048]{1,0:T(8,128)(2,1)} %q_ref.1, bf16[2048,512]{1,0:T(8,128)(2,1)} %get-tuple-element.19.k_ref, bf16[2048,512]{1,0:T(8,128)(2,1)} %get-tuple-element.20.v_ref, f32[1,2048]{1,0:T(1,128)} %bitcast.22, ...), custom_call_target="tpu_custom_call" | custom-call | flops 4294967296 | bytes 5775360 | tf_op jit(solution)/shard_map/pallas_call | solution.py:85
  64.1 1.3 %convolution_bitcast_fusion = f32[32]{0:T(128)S(1)} fusion(s32[2048]{0:T(1024)S(1)} %maximum_convert_fusion, f32[1,2048]{1,0:T(1,128)} %get-tuple-element.18), kind=kOutput, calls=%fused_computation.9 | convolution fusion | flops 851968 | bytes 16512 | tf_op jit(solution)/shard_map/dot_general | solution.py:221
  65.4 0.5 broadcast.150
  65.9 1.4 %reduce.13 = f32[2048]{0:T(1024)S(1)} reduce(f32[1,2048]{1,0:T(1,128)} %get-tuple-element.18, f32[]{:T(128)} %broadcast.150), dimensions={0}, to_apply=%get-tuple-element.18.reduce_sub_computation.3 | reduce | bytes 16388 | tf_op jit(solution)/shard_map/pallas_call | solution.py:85
  67.3 0.6 gather_fusion
  67.9 0.2 collective-permute-start.10
  68.1 4.9 %fusion.4 = bf16[128,2048]{1,0:T(8,128)(2,1)S(1)} fusion(bf16[128,2048]{1,0:T(8,128)(2,1)} %get-tuple-element.17, bf16[2048,4096]{1,0:T(8,128)(2,1)} %param.13, s32[]{:T(128)S(6)} %select_n.142), kind=kOutput, calls=%fused_computation.5 | convolution fusion | flops 1074003968 | bytes 9437188 | tf_op jit(solution)/shard_map/dot_general | solution.py:229
  72.9 1.6 %collective-permute-start.9 = (bf16[128,2048]{1,0:T(8,128)(2,1)S(1)}, bf16[128,2048]{1,0:T(8,128)(2,1)S(1)}, u32[]{:S(2)}, u32[]{:S(2)}) collective-permute-start(bf16[128,2048]{1,0:T(8,128)(2,1)S(1)} %fusion.4), channel_id=1, source_target_pairs={{0,2},{2,0},{1,3},{3,1},{4,6},{6,4},{5,7},{7,5},{8,10},{10,8},{9,1... | collective-permute-start | bytes 1572872 | tf_op jit(solution)/shard_map/ppermute | solution.py:230
  74.5 0.0 collective-permute-done.10
  74.5 9.0 %collective-permute-start.11 = (f32[2080]{0:T(1024)S(1)}, f32[2080]{0:T(1024)S(1)}, u32[]{:S(2)}, u32[]{:S(2)}) collective-permute-start(f32[2080]{0:T(1024)S(1)} %fusion.21), channel_id=1, source_target_pairs={{0,4},{4,0},{8,12},{12,8},{1,5},{5,1},{9,13},{13,9},{2,6},{6,2},{1... | collective-permute-start | bytes 24968 | tf_op jit(solution)/shard_map/ppermute | solution.py:175
  83.5 1.7 %collective-permute-done.11 = f32[2080]{0:T(1024)S(1)} collective-permute-done((f32[2080]{0:T(1024)S(1)}, f32[2080]{0:T(1024)S(1)}, u32[]{:S(2)}, u32[]{:S(2)}) %collective-permute-start.11) | collective-permute-done | bytes 8352 | tf_op jit(solution)/shard_map/ppermute | solution.py:175
  85.2 9.9 %collective-permute-start.12 = (f32[2080]{0:T(1024)S(1)}, f32[2080]{0:T(1024)S(1)}, u32[]{:S(2)}, u32[]{:S(2)}) collective-permute-start(f32[2080]{0:T(1024)S(1)} %add.96), channel_id=1, source_target_pairs={{0,8},{4,12},{8,0},{12,4},{1,9},{5,13},{9,1},{13,5},{2,10},{6,14},... | collective-permute-start | bytes 24968 | tf_op jit(solution)/shard_map/ppermute | solution.py:175
  95.1 1.8 %collective-permute-done.12 = f32[2080]{0:T(1024)S(1)} collective-permute-done((f32[2080]{0:T(1024)S(1)}, f32[2080]{0:T(1024)S(1)}, u32[]{:S(2)}, u32[]{:S(2)}) %collective-permute-start.12) | collective-permute-done | bytes 8352 | tf_op jit(solution)/shard_map/ppermute | solution.py:175
  96.9 0.4 collective-permute-start.13
  97.3 4.6 %fusion.2 = f32[128,2048]{1,0:T(8,128)S(1)} fusion(bf16[128,2048]{1,0:T(8,128)(2,1)S(1)} %copy-done.1, bf16[2048,4096]{1,0:T(8,128)(2,1)} %param.13, s32[]{:T(128)S(6)} %select_n.141), kind=kOutput, calls=%fused_computation.3 | convolution fusion | flops 1073741824 | bytes 9961476 | tf_op jit(solution)/shard_map/dot_general | solution.py:232
  102.0 0.0 collective-permute-done.13
  102.0 0.5 slice.99
  102.5 0.7 dynamic_slice.11
  103.2 0.0 collective-permute-done.9
  103.2 0.9 add_convert_fusion
  (24 shorter events, 0.4 us)
Async XLA Ops:
  3.3 27.2 %collective-permute-start.3 = (bf16[528,512]{1,0:T(8,128)(2,1)}, bf16[528,512]{1,0:T(8,128)(2,1)S(1)}, u32[]{:S(2)}, u32[]{:S(2)}) collective-permute-start(bf16[528,512]{1,0:T(8,128)(2,1)} %pad_maximum_fusion.2), channel_id=1, source_target_pairs={{0,8},{4,12},{1,9},{5,13},{2,10},{6,14},{3,11},{7,15},{16,24},{20,... | collective-permute-start | bytes 1622024 | tf_op jit(solution)/shard_map/ppermute | solution.py:124
  9.3 21.3 %collective-permute-start.4 = (bf16[528,512]{1,0:T(8,128)(2,1)}, bf16[528,512]{1,0:T(8,128)(2,1)S(1)}, u32[]{:S(2)}, u32[]{:S(2)}) collective-permute-start(bf16[528,512]{1,0:T(8,128)(2,1)} %pad_maximum_fusion.2), channel_id=1, source_target_pairs={{8,0},{9,1},{10,2},{11,3},{24,16},{25,17},{26,18},{27,19}} | collective-permute-start | bytes 1622024 | tf_op jit(solution)/shard_map/ppermute | solution.py:130
  10.6 27.0 %collective-permute-start.7 = (bf16[528,512]{1,0:T(8,128)(2,1)}, bf16[528,512]{1,0:T(8,128)(2,1)S(1)}, u32[]{:S(2)}, u32[]{:S(2)}) collective-permute-start(bf16[528,512]{1,0:T(8,128)(2,1)} %pad_maximum_fusion.2), channel_id=1, source_target_pairs={{4,0},{8,4},{12,8},{5,1},{9,5},{13,9},{6,2},{10,6},{14,10},{7,3},{... | collective-permute-start | bytes 1622024 | tf_op jit(solution)/shard_map/ppermute | solution.py:130
  11.9 20.8 %collective-permute-start.1 = (bf16[528,512]{1,0:T(8,128)(2,1)}, bf16[528,512]{1,0:T(8,128)(2,1)S(1)}, u32[]{:S(2)}, u32[]{:S(2)}) collective-permute-start(bf16[528,512]{1,0:T(8,128)(2,1)} %pad_maximum_fusion.2), channel_id=1, source_target_pairs={{0,4},{4,8},{8,12},{1,5},{5,9},{9,13},{2,6},{6,10},{10,14},{3,7},{... | collective-permute-start | bytes 1622024 | tf_op jit(solution)/shard_map/ppermute | solution.py:124
  16.5 15.6 %collective-permute-start = (bf16[528,512]{1,0:T(8,128)(2,1)}, bf16[528,512]{1,0:T(8,128)(2,1)S(1)}, u32[]{:S(2)}, u32[]{:S(2)}) collective-permute-start(bf16[528,512]{1,0:T(8,128)(2,1)} %pad_maximum_fusion.2), channel_id=1, source_target_pairs={{0,1},{1,0},{2,3},{3,2},{4,5},{5,4},{6,7},{7,6},{8,9},{9,8},{10,11... | collective-permute-start | bytes 1622024 | tf_op jit(solution)/shard_map/ppermute | solution.py:151
  30.6 7.2 %collective-permute-start.5 = (bf16[528,512]{1,0:T(8,128)(2,1)S(1)}, bf16[528,512]{1,0:T(8,128)(2,1)S(1)}, u32[]{:S(2)}, u32[]{:S(2)}) collective-permute-start(bf16[528,512]{1,0:T(8,128)(2,1)S(1)} %broadcast_select_fusion.1), channel_id=1, source_target_pairs={{0,1},{1,0},{2,3},{3,2},{4,5},{5,4},{6,7},{7,6},{8,9},{9,8},{10,11... | collective-permute-start | bytes 1622024 | tf_op jit(solution)/shard_map/ppermute | solution.py:151
  31.2 6.5 %collective-permute-start.6 = (bf16[528,512]{1,0:T(8,128)(2,1)S(1)}, bf16[528,512]{1,0:T(8,128)(2,1)S(1)}, u32[]{:S(2)}, u32[]{:S(2)}) collective-permute-start(bf16[528,512]{1,0:T(8,128)(2,1)S(1)} %collective-permute-done.3), channel_id=1, source_target_pairs={{8,12},{9,13},{10,14},{11,15},{24,28},{25,29},{26,30},{27,31}} | collective-permute-start | bytes 1622024 | tf_op jit(solution)/shard_map/ppermute | solution.py:122
  32.2 5.7 %copy-start = (bf16[528,512]{1,0:T(8,128)(2,1)}, bf16[528,512]{1,0:T(8,128)(2,1)S(1)}, u32[]{:S(2)}) copy-start(bf16[528,512]{1,0:T(8,128)(2,1)S(1)} %broadcast_select_fusion.6) | copy-start | bytes 1622020
  32.8 5.1 %collective-permute-start.2 = (bf16[528,512]{1,0:T(8,128)(2,1)S(1)}, bf16[528,512]{1,0:T(8,128)(2,1)S(1)}, u32[]{:S(2)}, u32[]{:S(2)}) collective-permute-start(bf16[528,512]{1,0:T(8,128)(2,1)S(1)} %broadcast_select_fusion.2), channel_id=1, source_target_pairs={{0,1},{1,0},{2,3},{3,2},{4,5},{5,4},{6,7},{7,6},{8,9},{9,8},{10,11... | collective-permute-start | bytes 1622024 | tf_op jit(solution)/shard_map/ppermute | solution.py:151
  37.7 2.0 %collective-permute-start.8 = (bf16[528,512]{1,0:T(8,128)(2,1)S(1)}, bf16[528,512]{1,0:T(8,128)(2,1)S(1)}, u32[]{:S(2)}, u32[]{:S(2)}) collective-permute-start(bf16[528,512]{1,0:T(8,128)(2,1)S(1)} %broadcast_select_fusion), channel_id=1, source_target_pairs={{0,1},{1,0},{2,3},{3,2},{4,5},{5,4},{6,7},{7,6},{8,9},{9,8},{10,11... | collective-permute-start | bytes 1622024 | tf_op jit(solution)/shard_map/ppermute | solution.py:151
  37.9 1.9 %copy-start.2 = (s32[4]{0:T(128)S(1)}, s32[4]{0:T(128)}, u32[]{:S(2)}) copy-start(s32[4]{0:T(128)} %param.17) | copy-start | bytes 52
  38.0 2.6 %slice-start = ((bf16[528,512]{1,0:T(8,128)(2,1)}), bf16[512,512]{1,0:T(8,128)(2,1)S(1)}, s32[]{:S(2)}) async-start(bf16[528,512]{1,0:T(8,128)(2,1)} %copy-done), calls=%async_computation | async-start | bytes 1048576 | tf_op jit(solution)/shard_map/slice | solution.py:157
  67.9 6.7 %collective-permute-start.10 = (f32[2080]{0:T(1024)S(1)}, f32[2080]{0:T(1024)S(1)}, u32[]{:S(2)}, u32[]{:S(2)}) collective-permute-start(f32[2080]{0:T(1024)S(1)} %pad_maximum_fusion.3), channel_id=1, source_target_pairs={{0,1},{1,0},{2,3},{3,2},{4,5},{5,4},{6,7},{7,6},{8,9},{9,8},{10,11... | collective-permute-start | bytes 24968 | tf_op jit(solution)/shard_map/ppermute | solution.py:175
  68.1 29.3 %copy-start.1 = (bf16[128,2048]{1,0:T(8,128)(2,1)S(1)}, bf16[128,2048]{1,0:T(8,128)(2,1)}, u32[]{:S(2)}) copy-start(bf16[128,2048]{1,0:T(8,128)(2,1)} %get-tuple-element.17) | copy-start | bytes 1572868
  72.9 30.2 %collective-permute-start.9 = (bf16[128,2048]{1,0:T(8,128)(2,1)S(1)}, bf16[128,2048]{1,0:T(8,128)(2,1)S(1)}, u32[]{:S(2)}, u32[]{:S(2)}) collective-permute-start(bf16[128,2048]{1,0:T(8,128)(2,1)S(1)} %fusion.4), channel_id=1, source_target_pairs={{0,2},{2,0},{1,3},{3,1},{4,6},{6,4},{5,7},{7,5},{8,10},{10,8},{9,1... | collective-permute-start | bytes 1572872 | tf_op jit(solution)/shard_map/ppermute | solution.py:230
  74.5 10.7 %collective-permute-start.11 = (f32[2080]{0:T(1024)S(1)}, f32[2080]{0:T(1024)S(1)}, u32[]{:S(2)}, u32[]{:S(2)}) collective-permute-start(f32[2080]{0:T(1024)S(1)} %fusion.21), channel_id=1, source_target_pairs={{0,4},{4,0},{8,12},{12,8},{1,5},{5,1},{9,13},{13,9},{2,6},{6,2},{1... | collective-permute-start | bytes 24968 | tf_op jit(solution)/shard_map/ppermute | solution.py:175
  85.2 11.7 %collective-permute-start.12 = (f32[2080]{0:T(1024)S(1)}, f32[2080]{0:T(1024)S(1)}, u32[]{:S(2)}, u32[]{:S(2)}) collective-permute-start(f32[2080]{0:T(1024)S(1)} %add.96), channel_id=1, source_target_pairs={{0,8},{4,12},{8,0},{12,4},{1,9},{5,13},{9,1},{13,5},{2,10},{6,14},... | collective-permute-start | bytes 24968 | tf_op jit(solution)/shard_map/ppermute | solution.py:175
  96.9 5.1 %collective-permute-start.13 = (f32[2080]{0:T(1024)S(1)}, f32[2080]{0:T(1024)S(1)}, u32[]{:S(2)}, u32[]{:S(2)}) collective-permute-start(f32[2080]{0:T(1024)S(1)} %add.97), channel_id=1, source_target_pairs={{0,2},{2,0},{1,3},{3,1},{4,6},{6,4},{5,7},{7,5},{8,10},{10,8},{9,1... | collective-permute-start | bytes 24968 | tf_op jit(solution)/shard_map/ppermute | solution.py:175

commit v15 on v14

--- a/solution.py
+++ b/solution.py
@@ -62,7 +62,7 @@
     kv_local = kv_width // HD
     tq = max(8, min(qc, (128 * 2048) // keys))
     n_rows = qc // tq
-    hp = 2 if group_size % 2 == 0 else 1
+    hp = group_size
     steps = group_size // hp
     grid = (kv_local, steps, n_rows)
 

time: 105 us -> 104 us (level)
  transfers between devices with their start and end apart: 14 -> 14, of which waited for: 5 -> 5; matrix products, arithmetic and copies ran while one was open for 24% -> 25% of each run, Pallas kernels for 0% -> 0%
where the time goes in v15:
time: 104 us; the launch traced here: 103 us
  starting transfers between devices  35.9 us (35%)
  matrix products  23.4 us (22%)
  Pallas kernels  20.3 us (20%)
  waiting for transfers between devices  10.1 us (10%)
  other arithmetic  9.35 us (9%)
  local copies, waits for them, and re-layouts  3.12 us (3%)
    pallas_call x1, Pallas kernels, fused_attention(): pl.pallas_call(functools.partial(attention_kernel, tq=tq, hp=hp), grid_sp...  20.3 us
    ppermute x4, starting transfers between devices, butterfly_sum(): total = total + lax.ppermute(total, axis, [(i, i ^ bit) for i in range(n)])  19.6 us
    dot_general x1, matrix products, local(): jnp.dot(grad_masked, out_weight.T, preferred_element_type=jnp.float32)  12.6 us
    ppermute x2, starting transfers between devices, relay_gather(): forward.append(lax.ppermute(payload, 'ctx', fwd) if fwd else zero)  10.5 us
    dot_general x1, matrix products, local(): send = jnp.dot(delta, send_w, preferred_element_type=jnp.float32)  4.86 us
    dot_general x1, matrix products, local(): jnp.dot(delta, keep_w, preferred_element_type=jnp.float32)  4.63 us
    ppermute x2, waiting for transfers between devices, relay_gather(): backward.append(lax.ppermute(payload, 'ctx', bwd) if bwd else zero)  4.61 us
    ppermute x4, waiting for transfers between devices, butterfly_sum(): total = total + lax.ppermute(total, axis, [(i, i ^ bit) for i in range(n)])  3.48 us
  transfers between devices with their start and end apart: 14, of which 5 were waited for; matrix products, arithmetic and copies ran while one was open for 25% of the time, Pallas kernels for 0%

profile of v15, /device:TPU:0, one launch (start us, length us, event | category | flops | bytes accessed | tf_op | source)
XLA Modules:
  0.0 103.1 jit_solution(10188784859373529635)
XLA Ops:
  0.6 0.7 convert_element_type.23
  1.4 1.1 %broadcast_select_fusion.7 = bf16[512,512]{1,0:T(8,128)(2,1)S(1)} fusion(bf16[512,512]{1,0:T(8,128)(2,1)} %param.11, bf16[512,512]{1,0:T(8,128)(2,1)} %param.12, pred[]{:T(512)S(6)} %eq.17), kind=kLoop, calls=%fused_computation.30 | loop fusion | flops 262144 | bytes 1572865 | tf_op jit(solution)/shard_map/jit(_where)/select_n | solution.py:146
  2.5 0.8 pad_maximum_fusion.2
  3.3 6.0 %collective-permute-start.3 = (bf16[528,512]{1,0:T(8,128)(2,1)}, bf16[528,512]{1,0:T(8,128)(2,1)S(1)}, u32[]{:S(2)}, u32[]{:S(2)}) collective-permute-start(bf16[528,512]{1,0:T(8,128)(2,1)} %pad_maximum_fusion.2), channel_id=1, source_target_pairs={{0,8},{4,12},{1,9},{5,13},{2,10},{6,14},{3,11},{7,15},{16,24},{20,... | collective-permute-start | bytes 1622024 | tf_op jit(solution)/shard_map/ppermute | solution.py:124
  9.3 1.3 %collective-permute-start.4 = (bf16[528,512]{1,0:T(8,128)(2,1)}, bf16[528,512]{1,0:T(8,128)(2,1)S(1)}, u32[]{:S(2)}, u32[]{:S(2)}) collective-permute-start(bf16[528,512]{1,0:T(8,128)(2,1)} %pad_maximum_fusion.2), channel_id=1, source_target_pairs={{8,0},{9,1},{10,2},{11,3},{24,16},{25,17},{26,18},{27,19}} | collective-permute-start | bytes 1622024 | tf_op jit(solution)/shard_map/ppermute | solution.py:130
  10.6 1.3 %collective-permute-start.7 = (bf16[528,512]{1,0:T(8,128)(2,1)}, bf16[528,512]{1,0:T(8,128)(2,1)S(1)}, u32[]{:S(2)}, u32[]{:S(2)}) collective-permute-start(bf16[528,512]{1,0:T(8,128)(2,1)} %pad_maximum_fusion.2), channel_id=1, source_target_pairs={{4,0},{8,4},{12,8},{5,1},{9,5},{13,9},{6,2},{10,6},{14,10},{7,3},{... | collective-permute-start | bytes 1622024 | tf_op jit(solution)/shard_map/ppermute | solution.py:130
  11.9 4.6 %collective-permute-start.1 = (bf16[528,512]{1,0:T(8,128)(2,1)}, bf16[528,512]{1,0:T(8,128)(2,1)S(1)}, u32[]{:S(2)}, u32[]{:S(2)}) collective-permute-start(bf16[528,512]{1,0:T(8,128)(2,1)} %pad_maximum_fusion.2), channel_id=1, source_target_pairs={{0,4},{4,8},{8,12},{1,5},{5,9},{9,13},{2,6},{6,10},{10,14},{3,7},{... | collective-permute-start | bytes 1622024 | tf_op jit(solution)/shard_map/ppermute | solution.py:124
  16.5 0.1 collective-permute-start
  16.5 0.7 broadcast_compare_fusion
  17.2 12.6 %convolution_convert_fusion.do_ref = bf16[128,2048]{1,0:T(8,128)(2,1)} fusion(bf16[2048,4096]{1,0:T(8,128)(2,1)} %param.13, bf16[128,4096]{1,0:T(8,128)(2,1)} %param.14, pred[128]{0:T(512)(128)(4,1)S(1)} %broadcast_compare_fusion), kind=kOutput, calls=%fused_computation.6 | convolution fusion | flops 2148270080 | bytes 18350208 | tf_op jit(solution)/shard_map/dot_general | solution.py:212
  29.8 0.1 add_bitcast_fusion
  29.9 0.6 copy.11
  30.5 0.0 collective-permute-done.3
  30.5 0.0 collective-permute-done.4
  30.5 0.1 broadcast_select_fusion.1
  30.6 0.6 collective-permute-start.5
  31.2 0.9 collective-permute-start.6
  32.0 0.0 collective-permute-done
  32.0 0.1 broadcast_select_fusion.6
  32.2 0.0 copy-start
  32.2 0.5 collective-permute-done.1
  32.8 0.1 collective-permute-start.2
  32.8 0.1 fusion.10
  33.0 4.6 %collective-permute-done.7 = bf16[528,512]{1,0:T(8,128)(2,1)S(1)} collective-permute-done((bf16[528,512]{1,0:T(8,128)(2,1)}, bf16[528,512]{1,0:T(8,128)(2,1)S(1)}, u32[]{:S(2)}, u32[]{:S(2)}) %collective-permute-start.7) | collective-permute-done | bytes 540704 | tf_op jit(solution)/shard_map/ppermute | solution.py:130
  37.6 0.0 collective-permute-done.6
  37.6 0.1 broadcast_select_fusion
  37.7 0.1 collective-permute-start.8
  37.8 0.0 collective-permute-done.5
  37.8 0.1 broadcast_select_fusion.4
  37.8 0.0 collective-permute-done.2
  37.9 0.1 broadcast_select_fusion.5
  37.9 0.0 copy-done
  37.9 0.0 copy-start.2
  38.0 0.0 slice-start
  38.1 0.1 slice_select_fusion.1
  38.1 0.1 slice_select_fusion.2
  38.2 1.5 %collective-permute-done.8 = bf16[528,512]{1,0:T(8,128)(2,1)S(1)} collective-permute-done((bf16[528,512]{1,0:T(8,128)(2,1)S(1)}, bf16[528,512]{1,0:T(8,128)(2,1)S(1)}, u32[]{:S(2)}, u32[]{:S(2)}) %collective-permute-start.8) | collective-permute-done | bytes 540704 | tf_op jit(solution)/shard_map/ppermute | solution.py:151
  39.7 0.1 broadcast_select_fusion.3
  39.8 0.0 copy-done.2
  39.8 0.1 compare_reduce_fusion
  39.9 0.6 broadcast_select_fusion.8
  40.5 0.1 slice_select_fusion
  40.6 0.0 slice-done
  40.6 2.2 %pad_maximum_fusion = (bf16[2048,512]{1,0:T(8,128)(2,1)}, bf16[2048,512]{1,0:T(8,128)(2,1)}) fusion(bf16[512,512]{1,0:T(8,128)(2,1)S(1)} %slice.84, bf16[512,512]{1,0:T(8,128)(2,1)S(1)} %slice.83, bf16[512,512]{1,0:T(8,128)(2,1)S(1)} %slice.82, bf16[512,512]{1,0:T(8,128)(2,1)S(1)} %slice-done, bf16[512,512]{1,0:T(8,128)(2,1)S(1)} %slice_select_fusion, ...), kind=kLoop, calls=%fused_computation.7 | loop fusion | flops 16777216 | bytes 8388608 | tf_op jit(solution)/shard_map/concatenate | solution.py:157
  42.8 20.3 %shard_map.103 = (bf16[128,2048]{1,0:T(8,128)(2,1)}, f32[1,2048]{1,0:T(1,128)}) custom-call(s32[1]{0:T(128)} %bitcast.base_ref, s32[1,2048]{1,0:T(1,128)} %bitcast.23, bf16[128,2048]{1,0:T(8,128)(2,1)} %q_ref.1, bf16[2048,512]{1,0:T(8,128)(2,1)} %get-tuple-element.19.k_ref, bf16[2048,512]{1,0:T(8,128)(2,1)} %get-tuple-element.20.v_ref, f32[1,2048]{1,0:T(1,128)} %bitcast.22, ...), custom_call_target="tpu_custom_call" | custom-call | flops 4294967296 | bytes 5775360 | tf_op jit(solution)/shard_map/pallas_call | solution.py:85
  63.1 1.3 %convolution_bitcast_fusion = f32[32]{0:T(128)S(1)} fusion(s32[2048]{0:T(1024)S(1)} %maximum_convert_fusion, f32[1,2048]{1,0:T(1,128)} %get-tuple-element.18), kind=kOutput, calls=%fused_computation.9 | convolution fusion | flops 851968 | bytes 16512 | tf_op jit(solution)/shard_map/dot_general | solution.py:221
  64.4 0.5 broadcast.150
  64.9 1.4 %reduce.13 = f32[2048]{0:T(1024)S(1)} reduce(f32[1,2048]{1,0:T(1,128)} %get-tuple-element.18, f32[]{:T(128)} %broadcast.150), dimensions={0}, to_apply=%get-tuple-element.18.reduce_sub_computation.3 | reduce | bytes 16388 | tf_op jit(solution)/shard_map/pallas_call | solution.py:85
  66.3 0.6 gather_fusion
  66.9 0.2 collective-permute-start.10
  67.1 4.9 %fusion.4 = bf16[128,2048]{1,0:T(8,128)(2,1)S(1)} fusion(bf16[128,2048]{1,0:T(8,128)(2,1)} %get-tuple-element.17, bf16[2048,4096]{1,0:T(8,128)(2,1)} %param.13, s32[]{:T(128)S(6)} %select_n.142), kind=kOutput, calls=%fused_computation.5 | convolution fusion | flops 1074003968 | bytes 9437188 | tf_op jit(solution)/shard_map/dot_general | solution.py:229
  72.0 1.6 %collective-permute-start.9 = (bf16[128,2048]{1,0:T(8,128)(2,1)S(1)}, bf16[128,2048]{1,0:T(8,128)(2,1)S(1)}, u32[]{:S(2)}, u32[]{:S(2)}) collective-permute-start(bf16[128,2048]{1,0:T(8,128)(2,1)S(1)} %fusion.4), channel_id=1, source_target_pairs={{0,2},{2,0},{1,3},{3,1},{4,6},{6,4},{5,7},{7,5},{8,10},{10,8},{9,1... | collective-permute-start | bytes 1572872 | tf_op jit(solution)/shard_map/ppermute | solution.py:230
  73.5 0.0 collective-permute-done.10
  73.5 9.0 %collective-permute-start.11 = (f32[2080]{0:T(1024)S(1)}, f32[2080]{0:T(1024)S(1)}, u32[]{:S(2)}, u32[]{:S(2)}) collective-permute-start(f32[2080]{0:T(1024)S(1)} %fusion.21), channel_id=1, source_target_pairs={{0,4},{4,0},{8,12},{12,8},{1,5},{5,1},{9,13},{13,9},{2,6},{6,2},{1... | collective-permute-start | bytes 24968 | tf_op jit(solution)/shard_map/ppermute | solution.py:175
  82.5 1.7 %collective-permute-done.11 = f32[2080]{0:T(1024)S(1)} collective-permute-done((f32[2080]{0:T(1024)S(1)}, f32[2080]{0:T(1024)S(1)}, u32[]{:S(2)}, u32[]{:S(2)}) %collective-permute-start.11) | collective-permute-done | bytes 8352 | tf_op jit(solution)/shard_map/ppermute | solution.py:175
  84.2 9.9 %collective-permute-start.12 = (f32[2080]{0:T(1024)S(1)}, f32[2080]{0:T(1024)S(1)}, u32[]{:S(2)}, u32[]{:S(2)}) collective-permute-start(f32[2080]{0:T(1024)S(1)} %add.96), channel_id=1, source_target_pairs={{0,8},{4,12},{8,0},{12,4},{1,9},{5,13},{9,1},{13,5},{2,10},{6,14},... | collective-permute-start | bytes 24968 | tf_op jit(solution)/shard_map/ppermute | solution.py:175
  94.1 1.8 %collective-permute-done.12 = f32[2080]{0:T(1024)S(1)} collective-permute-done((f32[2080]{0:T(1024)S(1)}, f32[2080]{0:T(1024)S(1)}, u32[]{:S(2)}, u32[]{:S(2)}) %collective-permute-start.12) | collective-permute-done | bytes 8352 | tf_op jit(solution)/shard_map/ppermute | solution.py:175
  95.9 0.4 collective-permute-start.13
  96.3 4.6 %fusion.2 = f32[128,2048]{1,0:T(8,128)S(1)} fusion(bf16[128,2048]{1,0:T(8,128)(2,1)S(1)} %copy-done.1, bf16[2048,4096]{1,0:T(8,128)(2,1)} %param.13, s32[]{:T(128)S(6)} %select_n.141), kind=kOutput, calls=%fused_computation.3 | convolution fusion | flops 1073741824 | bytes 9961476 | tf_op jit(solution)/shard_map/dot_general | solution.py:232
  101.0 0.0 collective-permute-done.13
  101.0 0.5 slice.99
  101.5 0.7 dynamic_slice.11
  102.2 0.0 collective-permute-done.9
  102.2 0.9 add_convert_fusion
  (24 shorter events, 0.4 us)
Async XLA Ops:
  3.3 27.2 %collective-permute-start.3 = (bf16[528,512]{1,0:T(8,128)(2,1)}, bf16[528,512]{1,0:T(8,128)(2,1)S(1)}, u32[]{:S(2)}, u32[]{:S(2)}) collective-permute-start(bf16[528,512]{1,0:T(8,128)(2,1)} %pad_maximum_fusion.2), channel_id=1, source_target_pairs={{0,8},{4,12},{1,9},{5,13},{2,10},{6,14},{3,11},{7,15},{16,24},{20,... | collective-permute-start | bytes 1622024 | tf_op jit(solution)/shard_map/ppermute | solution.py:124
  9.3 21.3 %collective-permute-start.4 = (bf16[528,512]{1,0:T(8,128)(2,1)}, bf16[528,512]{1,0:T(8,128)(2,1)S(1)}, u32[]{:S(2)}, u32[]{:S(2)}) collective-permute-start(bf16[528,512]{1,0:T(8,128)(2,1)} %pad_maximum_fusion.2), channel_id=1, source_target_pairs={{8,0},{9,1},{10,2},{11,3},{24,16},{25,17},{26,18},{27,19}} | collective-permute-start | bytes 1622024 | tf_op jit(solution)/shard_map/ppermute | solution.py:130
  10.6 27.0 %collective-permute-start.7 = (bf16[528,512]{1,0:T(8,128)(2,1)}, bf16[528,512]{1,0:T(8,128)(2,1)S(1)}, u32[]{:S(2)}, u32[]{:S(2)}) collective-permute-start(bf16[528,512]{1,0:T(8,128)(2,1)} %pad_maximum_fusion.2), channel_id=1, source_target_pairs={{4,0},{8,4},{12,8},{5,1},{9,5},{13,9},{6,2},{10,6},{14,10},{7,3},{... | collective-permute-start | bytes 1622024 | tf_op jit(solution)/shard_map/ppermute | solution.py:130
  11.9 20.8 %collective-permute-start.1 = (bf16[528,512]{1,0:T(8,128)(2,1)}, bf16[528,512]{1,0:T(8,128)(2,1)S(1)}, u32[]{:S(2)}, u32[]{:S(2)}) collective-permute-start(bf16[528,512]{1,0:T(8,128)(2,1)} %pad_maximum_fusion.2), channel_id=1, source_target_pairs={{0,4},{4,8},{8,12},{1,5},{5,9},{9,13},{2,6},{6,10},{10,14},{3,7},{... | collective-permute-start | bytes 1622024 | tf_op jit(solution)/shard_map/ppermute | solution.py:124
  16.5 15.6 %collective-permute-start = (bf16[528,512]{1,0:T(8,128)(2,1)}, bf16[528,512]{1,0:T(8,128)(2,1)S(1)}, u32[]{:S(2)}, u32[]{:S(2)}) collective-permute-start(bf16[528,512]{1,0:T(8,128)(2,1)} %pad_maximum_fusion.2), channel_id=1, source_target_pairs={{0,1},{1,0},{2,3},{3,2},{4,5},{5,4},{6,7},{7,6},{8,9},{9,8},{10,11... | collective-permute-start | bytes 1622024 | tf_op jit(solution)/shard_map/ppermute | solution.py:151
  30.6 7.2 %collective-permute-start.5 = (bf16[528,512]{1,0:T(8,128)(2,1)S(1)}, bf16[528,512]{1,0:T(8,128)(2,1)S(1)}, u32[]{:S(2)}, u32[]{:S(2)}) collective-permute-start(bf16[528,512]{1,0:T(8,128)(2,1)S(1)} %broadcast_select_fusion.1), channel_id=1, source_target_pairs={{0,1},{1,0},{2,3},{3,2},{4,5},{5,4},{6,7},{7,6},{8,9},{9,8},{10,11... | collective-permute-start | bytes 1622024 | tf_op jit(solution)/shard_map/ppermute | solution.py:151
  31.2 6.5 %collective-permute-start.6 = (bf16[528,512]{1,0:T(8,128)(2,1)S(1)}, bf16[528,512]{1,0:T(8,128)(2,1)S(1)}, u32[]{:S(2)}, u32[]{:S(2)}) collective-permute-start(bf16[528,512]{1,0:T(8,128)(2,1)S(1)} %collective-permute-done.3), channel_id=1, source_target_pairs={{8,12},{9,13},{10,14},{11,15},{24,28},{25,29},{26,30},{27,31}} | collective-permute-start | bytes 1622024 | tf_op jit(solution)/shard_map/ppermute | solution.py:122
  32.2 5.7 %copy-start = (bf16[528,512]{1,0:T(8,128)(2,1)}, bf16[528,512]{1,0:T(8,128)(2,1)S(1)}, u32[]{:S(2)}) copy-start(bf16[528,512]{1,0:T(8,128)(2,1)S(1)} %broadcast_select_fusion.6) | copy-start | bytes 1622020
  32.8 5.1 %collective-permute-start.2 = (bf16[528,512]{1,0:T(8,128)(2,1)S(1)}, bf16[528,512]{1,0:T(8,128)(2,1)S(1)}, u32[]{:S(2)}, u32[]{:S(2)}) collective-permute-start(bf16[528,512]{1,0:T(8,128)(2,1)S(1)} %broadcast_select_fusion.2), channel_id=1, source_target_pairs={{0,1},{1,0},{2,3},{3,2},{4,5},{5,4},{6,7},{7,6},{8,9},{9,8},{10,11... | collective-permute-start | bytes 1622024 | tf_op jit(solution)/shard_map/ppermute | solution.py:151
  37.7 2.0 %collective-permute-start.8 = (bf16[528,512]{1,0:T(8,128)(2,1)S(1)}, bf16[528,512]{1,0:T(8,128)(2,1)S(1)}, u32[]{:S(2)}, u32[]{:S(2)}) collective-permute-start(bf16[528,512]{1,0:T(8,128)(2,1)S(1)} %broadcast_select_fusion), channel_id=1, source_target_pairs={{0,1},{1,0},{2,3},{3,2},{4,5},{5,4},{6,7},{7,6},{8,9},{9,8},{10,11... | collective-permute-start | bytes 1622024 | tf_op jit(solution)/shard_map/ppermute | solution.py:151
  37.9 1.9 %copy-start.2 = (s32[4]{0:T(128)S(1)}, s32[4]{0:T(128)}, u32[]{:S(2)}) copy-start(s32[4]{0:T(128)} %param.17) | copy-start | bytes 52
  38.0 2.6 %slice-start = ((bf16[528,512]{1,0:T(8,128)(2,1)}), bf16[512,512]{1,0:T(8,128)(2,1)S(1)}, s32[]{:S(2)}) async-start(bf16[528,512]{1,0:T(8,128)(2,1)} %copy-done), calls=%async_computation | async-start | bytes 1048576 | tf_op jit(solution)/shard_map/slice | solution.py:157
  66.9 6.7 %collective-permute-start.10 = (f32[2080]{0:T(1024)S(1)}, f32[2080]{0:T(1024)S(1)}, u32[]{:S(2)}, u32[]{:S(2)}) collective-permute-start(f32[2080]{0:T(1024)S(1)} %pad_maximum_fusion.3), channel_id=1, source_target_pairs={{0,1},{1,0},{2,3},{3,2},{4,5},{5,4},{6,7},{7,6},{8,9},{9,8},{10,11... | collective-permute-start | bytes 24968 | tf_op jit(solution)/shard_map/ppermute | solution.py:175
  67.1 29.3 %copy-start.1 = (bf16[128,2048]{1,0:T(8,128)(2,1)S(1)}, bf16[128,2048]{1,0:T(8,128)(2,1)}, u32[]{:S(2)}) copy-start(bf16[128,2048]{1,0:T(8,128)(2,1)} %get-tuple-element.17) | copy-start | bytes 1572868
  72.0 30.2 %collective-permute-start.9 = (bf16[128,2048]{1,0:T(8,128)(2,1)S(1)}, bf16[128,2048]{1,0:T(8,128)(2,1)S(1)}, u32[]{:S(2)}, u32[]{:S(2)}) collective-permute-start(bf16[128,2048]{1,0:T(8,128)(2,1)S(1)} %fusion.4), channel_id=1, source_target_pairs={{0,2},{2,0},{1,3},{3,1},{4,6},{6,4},{5,7},{7,5},{8,10},{10,8},{9,1... | collective-permute-start | bytes 1572872 | tf_op jit(solution)/shard_map/ppermute | solution.py:230
  73.5 10.7 %collective-permute-start.11 = (f32[2080]{0:T(1024)S(1)}, f32[2080]{0:T(1024)S(1)}, u32[]{:S(2)}, u32[]{:S(2)}) collective-permute-start(f32[2080]{0:T(1024)S(1)} %fusion.21), channel_id=1, source_target_pairs={{0,4},{4,0},{8,12},{12,8},{1,5},{5,1},{9,13},{13,9},{2,6},{6,2},{1... | collective-permute-start | bytes 24968 | tf_op jit(solution)/shard_map/ppermute | solution.py:175
  84.2 11.7 %collective-permute-start.12 = (f32[2080]{0:T(1024)S(1)}, f32[2080]{0:T(1024)S(1)}, u32[]{:S(2)}, u32[]{:S(2)}) collective-permute-start(f32[2080]{0:T(1024)S(1)} %add.96), channel_id=1, source_target_pairs={{0,8},{4,12},{8,0},{12,4},{1,9},{5,13},{9,1},{13,5},{2,10},{6,14},... | collective-permute-start | bytes 24968 | tf_op jit(solution)/shard_map/ppermute | solution.py:175
  95.9 5.0 %collective-permute-start.13 = (f32[2080]{0:T(1024)S(1)}, f32[2080]{0:T(1024)S(1)}, u32[]{:S(2)}, u32[]{:S(2)}) collective-permute-start(f32[2080]{0:T(1024)S(1)} %add.97), channel_id=1, source_target_pairs={{0,2},{2,0},{1,3},{3,1},{4,6},{6,4},{5,7},{7,5},{8,10},{10,8},{9,1... | collective-permute-start | bytes 24968 | tf_op jit(solution)/shard_map/ppermute | solution.py:175

commit v16 on v15

--- a/solution.py
+++ b/solution.py
@@ -13,16 +13,9 @@
 NT_DIMS = (((1,), (1,)), ((), ()))
 
 
-def attention_kernel(base_ref, kpos_ref, q_ref, k_ref, v_ref, kept_ref, do_ref, delta_ref, attr_ref, *, tq, hp):
+def attention_body(base_ref, kpos_ref, q_ref, kept_ref, do_ref, k_refs, v_refs, delta_ref, attr_ref, tq, hp):
     r = pl.program_id(2)
-    first = (pl.program_id(0) == 0) & (pl.program_id(1) == 0) & (r == 0)
-
-    @pl.when(first)
-    def _():
-        attr_ref[...] = jnp.zeros_like(attr_ref)
-
-    k = k_ref[...]
-    v = v_ref[...]
+    kc = k_refs[0].shape[0]
     rows = hp * tq
     row_pos = base_ref[0] + r * tq + lax.broadcasted_iota(jnp.int32, (rows, 1), 0) % tq
     vis = kpos_ref[...] <= row_pos
@@ -33,7 +26,10 @@
     else:
         q = q_ref[...]
         g_rows = do_ref[...]
-    s = lax.dot_general(q, k, NT_DIMS, preferred_element_type=jnp.float32) * (HD ** -0.5)
+    s = jnp.concatenate(
+        [lax.dot_general(q, kr[...], NT_DIMS, preferred_element_type=jnp.float32) for kr in k_refs],
+        axis=1,
+    ) * (HD ** -0.5)
     s_c = jnp.where(vis, s, NEG_FILL)
     s_m = jnp.where(kept, s_c, NEG_FILL)
     m_c = jnp.max(s_c, axis=1, keepdims=True)
@@ -42,32 +38,70 @@
     e_m = jnp.exp(s_m - m_m)
     l_c = jnp.sum(e_c, axis=1, keepdims=True)
     l_m = jnp.sum(e_m, axis=1, keepdims=True)
-    o_c = jnp.dot(e_c.astype(jnp.bfloat16), v, preferred_element_type=jnp.float32) / l_c
-    o_m = jnp.dot(e_m.astype(jnp.bfloat16), v, preferred_element_type=jnp.float32) / l_m
+    eb_c = e_c.astype(jnp.bfloat16)
+    eb_m = e_m.astype(jnp.bfloat16)
+    o_c = None
+    o_m = None
+    for i, vr in enumerate(v_refs):
+        v = vr[...]
+        pc = jnp.dot(eb_c[:, i * kc:(i + 1) * kc], v, preferred_element_type=jnp.float32)
+        pm = jnp.dot(eb_m[:, i * kc:(i + 1) * kc], v, preferred_element_type=jnp.float32)
+        o_c = pc if o_c is None else o_c + pc
+        o_m = pm if o_m is None else o_m + pm
+    o_c = o_c / l_c
+    o_m = o_m / l_m
     delta = (o_m - o_c).astype(delta_ref.dtype)
     for h in range(hp):
         delta_ref[:, h * HD:(h + 1) * HD] = delta[h * tq:(h + 1) * tq]
     row_dot = jnp.sum(g_rows.astype(jnp.float32) * o_c, axis=1, keepdims=True)
-    d_p = lax.dot_general(g_rows, v, NT_DIMS, preferred_element_type=jnp.float32)
+    d_p = jnp.concatenate(
+        [lax.dot_general(g_rows, vr[...], NT_DIMS, preferred_element_type=jnp.float32) for vr in v_refs],
+        axis=1,
+    )
     log_total = m_c + jnp.log(l_c)
     prob = e_c * (1.0 / l_c)
     contrib = prob * (d_p + (d_p - row_dot) * (s - log_total))
-    total = jnp.sum(contrib, axis=0, keepdims=True)
-    attr_ref[...] += total
-
-
-def fused_attention(base, key_pos, query, key_all, value_all, kept, grad_out, group_size):
-    qc, width = query.shape
-    keys, kv_width = key_all.shape
+    attr_ref[...] += jnp.sum(contrib, axis=0, keepdims=True)
+
+
+def attention_kernel(base_ref, kpos_ref, q_ref, kept_ref, do_ref, *refs, tq, hp, n, split):
+    mine, theirs = refs[:n], refs[n:2 * n]
+    delta_ref, attr_ref = refs[2 * n:]
+    first = (pl.program_id(0) == 0) & (pl.program_id(1) == 0) & (pl.program_id(2) == 0)
+
+    @pl.when(first)
+    def _():
+        attr_ref[...] = jnp.zeros_like(attr_ref)
+
+    args = (base_ref, kpos_ref, q_ref, kept_ref, do_ref)
+    if not split:
+        attention_body(*args, mine, theirs, delta_ref, attr_ref, tq, hp)
+        return
+
+    @pl.when(base_ref[1] == 0)
+    def _():
+        attention_body(*args, mine, theirs, delta_ref, attr_ref, tq, hp)
+
+    @pl.when(base_ref[1] != 0)
+    def _():
+        attention_body(*args, theirs, mine, delta_ref, attr_ref, tq, hp)
+
+
+def fused_attention(base, key_pos, query, mine, theirs, kept, grad_out, group_size, split):
+    qc = query.shape[0]
+    n = len(mine)
+    kc = key_pos.shape[1] // n
+    keys = kc * n
+    kv_width = mine[0].shape[1]
+    width = kv_width * group_size
     kv_local = kv_width // HD
     tq = max(8, min(qc, (128 * 2048) // keys))
     n_rows = qc // tq
     hp = group_size
-    steps = group_size // hp
-    grid = (kv_local, steps, n_rows)
+    grid = (kv_local, 1, n_rows)
 
     def head_map(g, j, r, b):
-        return (r, g * steps + j)
+        return (r, g + j)
 
     def kv_map(g, j, r, b):
         return (0, g)
@@ -79,22 +113,20 @@
     cost = pl.CostEstimate(
         flops=flops,
         transcendentals=2 * qc * keys * kv_local * group_size,
-        bytes_accessed=2 * (query.size + key_all.size + value_all.size + grad_out.size + query.size)
-        + 4 * keys,
-    )
+        bytes_accessed=2 * (3 * qc * width + 2 * keys * kv_width) + 4 * keys,
+    )
+    part_spec = pl.BlockSpec((kc, HD), kv_map)
     return pl.pallas_call(
-        functools.partial(attention_kernel, tq=tq, hp=hp),
+        functools.partial(attention_kernel, tq=tq, hp=hp, n=n, split=split),
         grid_spec=pltpu.PrefetchScalarGridSpec(
             num_scalar_prefetch=1,
             grid=grid,
             in_specs=[
                 pl.BlockSpec((1, keys), fixed),
                 pl.BlockSpec((tq, hp * HD), head_map),
-                pl.BlockSpec((keys, HD), kv_map),
-                pl.BlockSpec((keys, HD), kv_map),
                 pl.BlockSpec((1, keys), fixed),
                 pl.BlockSpec((tq, hp * HD), head_map),
-            ],
+            ] + [part_spec] * (2 * n),
             out_specs=[
                 pl.BlockSpec((tq, hp * HD), head_map),
                 pl.BlockSpec((1, keys), fixed),
@@ -108,7 +140,7 @@
             dimension_semantics=("arbitrary", "arbitrary", "arbitrary")
         ),
         cost_estimate=cost,
-    )(base, key_pos, query, key_all, value_all, kept, grad_out)
+    )(base, key_pos, query, kept, grad_out, *mine, *theirs)
 
 
 def relay_gather(payload, needed, ctx_at):
@@ -149,19 +181,16 @@
     if split:
         mine = gathered[0]
         theirs = [lax.ppermute(p, "rep", [(0, 1), (1, 0)]) for p in mine]
-        first = rep_at == 0
-        key_parts = [jnp.where(first, a, b) for a, b in zip(mine, theirs)]
-        value_parts = [jnp.where(first, b, a) for a, b in zip(mine, theirs)]
+        key_parts = [jnp.where(rep_at == 0, a, b) for a, b in zip(mine, theirs)]
     else:
-        key_parts, value_parts = gathered
-    key_all = jnp.concatenate([p[:key_count] for p in key_parts], axis=0)
-    value_all = jnp.concatenate([p[:key_count] for p in value_parts], axis=0)
+        mine, theirs = gathered
+        key_parts = mine
     seg_all = jnp.concatenate(
         [p[key_count:].reshape(-1)[:key_count] for p in key_parts], axis=0
     ).astype(jnp.int32)
     source = (ctx_at - jnp.arange(n, dtype=jnp.int32)) % n
     key_pos = (source[:, None] * key_count + jnp.arange(key_count, dtype=jnp.int32)[None, :])
-    return key_all, value_all, seg_all, key_pos.reshape(1, -1), source
+    return mine, theirs, seg_all, key_pos.reshape(1, -1), split
 
 
 def butterfly_sum(total, axes):
@@ -192,13 +221,13 @@
     context_len = key_count * ctx_count
     query_base = context_len - query_count * ctx_count * rep_count
     base = (query_base + (ctx_at * rep_count + rep_at) * query_count).astype(jnp.int32)
-    base = jnp.reshape(base, (1,))
+    base = jnp.stack([base, rep_at.astype(jnp.int32)])
 
     def needed(receiver, block):
         last_query = query_base + (receiver * rep_count + rep_count) * query_count - 1
         return block * key_count <= last_query
 
-    key_all, value_all, seg_shift, key_pos, source = gather_kv(
+    mine, theirs, seg_shift, key_pos, split = gather_kv(
         key, value, segment_ids, ctx_at, rep_at, rep_count, needed
     )
     kept = jnp.where(
@@ -213,7 +242,7 @@
         jnp.bfloat16
     )
     delta, attr = fused_attention(
-        base, key_pos, query, key_all, value_all, kept, grad_out, group_size
+        base, key_pos, query, mine, theirs, kept, grad_out, group_size, split
     )
 
     inverse = (ctx_at - jnp.arange(ctx_count, dtype=jnp.int32)) % ctx_count

time: 104 us -> 103 us (level)
  waiting for transfers between devices: 10.1 us -> 8.61 us
  other arithmetic: 9.35 us -> 8 us
    concatenate x1 -> x0, other arithmetic: 2.18 us -> none  [gather_kv(): key_all = jnp.concatenate([p[:key_count] for p in key_parts], axis=0)]
  transfers between devices with their start and end apart: 14 -> 14, of which waited for: 5 -> 4; matrix products, arithmetic and copies ran while one was open for 25% -> 26% of each run, Pallas kernels for 0% -> 0%
where the time goes in v16:
time: 103 us; the launch traced here: 102 us
  starting transfers between devices  36.8 us (36%)
  matrix products  23.5 us (23%)
  Pallas kernels  21.3 us (21%)
  waiting for transfers between devices  8.61 us (8%)
  other arithmetic  8 us (8%)
  local copies, waits for them, and re-layouts  2.94 us (3%)
    pallas_call x1, Pallas kernels, fused_attention(): pl.pallas_call(functools.partial(attention_kernel, tq=tq, hp=hp, n=n, spl...  21.3 us
    ppermute x4, starting transfers between devices, butterfly_sum(): total = total + lax.ppermute(total, axis, [(i, i ^ bit) for i in range(n)])  19.7 us
    dot_general x1, matrix products, local(): jnp.dot(grad_masked, out_weight.T, preferred_element_type=jnp.float32)  12.6 us
    ppermute x2, starting transfers between devices, relay_gather(): forward.append(lax.ppermute(payload, 'ctx', fwd) if fwd else zero)  11.3 us
    dot_general x1, matrix products, local(): send = jnp.dot(delta, send_w, preferred_element_type=jnp.float32)  4.82 us
    dot_general x1, matrix products, local(): jnp.dot(delta, keep_w, preferred_element_type=jnp.float32)  4.82 us
    ppermute x2, waiting for transfers between devices, relay_gather(): backward.append(lax.ppermute(payload, 'ctx', bwd) if bwd else zero)  4.72 us
    ppermute x4, waiting for transfers between devices, butterfly_sum(): total = total + lax.ppermute(total, axis, [(i, i ^ bit) for i in range(n)])  3.4 us
  transfers between devices with their start and end apart: 14, of which 4 were waited for; matrix products, arithmetic and copies ran while one was open for 26% of the time, Pallas kernels for 0%

profile of v16, /device:TPU:0, one launch (start us, length us, event | category | flops | bytes accessed | tf_op | source)
XLA Modules:
  0.0 102.0 jit_solution(16864100050590187822)
XLA Ops:
  0.6 0.0 copy-start.3
  0.6 0.7 convert_element_type.23
  1.4 1.1 %broadcast_select_fusion.3 = bf16[512,512]{1,0:T(8,128)(2,1)S(1)} fusion(bf16[512,512]{1,0:T(8,128)(2,1)} %param.11, bf16[512,512]{1,0:T(8,128)(2,1)} %param.12, pred[]{:T(512)S(6)} %eq.17), kind=kLoop, calls=%fused_computation.19 | loop fusion | flops 262144 | bytes 1572865 | tf_op jit(solution)/shard_map/jit(_where)/select_n | solution.py:178
  2.5 0.8 pad_maximum_fusion.refs_0_
  3.3 6.0 %collective-permute-start.3 = (bf16[528,512]{1,0:T(8,128)(2,1)}, bf16[528,512]{1,0:T(8,128)(2,1)S(1)}, u32[]{:S(2)}, u32[]{:S(2)}) collective-permute-start(bf16[528,512]{1,0:T(8,128)(2,1)} %pad_maximum_fusion.refs_0_), channel_id=1, source_target_pairs={{0,8},{4,12},{1,9},{5,13},{2,10},{6,14},{3,11},{7,15},{16,24},{20,... | collective-permute-start | bytes 1622024 | tf_op jit(solution)/shard_map/ppermute | solution.py:156
  9.3 1.3 %collective-permute-start.4 = (bf16[528,512]{1,0:T(8,128)(2,1)}, bf16[528,512]{1,0:T(8,128)(2,1)S(1)}, u32[]{:S(2)}, u32[]{:S(2)}) collective-permute-start(bf16[528,512]{1,0:T(8,128)(2,1)} %pad_maximum_fusion.refs_0_), channel_id=1, source_target_pairs={{8,0},{9,1},{10,2},{11,3},{24,16},{25,17},{26,18},{27,19}} | collective-permute-start | bytes 1622024 | tf_op jit(solution)/shard_map/ppermute | solution.py:162
  10.6 1.3 %collective-permute-start.7 = (bf16[528,512]{1,0:T(8,128)(2,1)}, bf16[528,512]{1,0:T(8,128)(2,1)S(1)}, u32[]{:S(2)}, u32[]{:S(2)}) collective-permute-start(bf16[528,512]{1,0:T(8,128)(2,1)} %pad_maximum_fusion.refs_0_), channel_id=1, source_target_pairs={{4,0},{8,4},{12,8},{5,1},{9,5},{13,9},{6,2},{10,6},{14,10},{7,3},{... | collective-permute-start | bytes 1622024 | tf_op jit(solution)/shard_map/ppermute | solution.py:162
  11.9 5.4 %collective-permute-start.1 = (bf16[528,512]{1,0:T(8,128)(2,1)}, bf16[528,512]{1,0:T(8,128)(2,1)}, u32[]{:S(2)}, u32[]{:S(2)}) collective-permute-start(bf16[528,512]{1,0:T(8,128)(2,1)} %pad_maximum_fusion.refs_0_), channel_id=1, source_target_pairs={{0,4},{4,8},{8,12},{1,5},{5,9},{9,13},{2,6},{6,10},{10,14},{3,7},{... | collective-permute-start | bytes 1622024 | tf_op jit(solution)/shard_map/ppermute | solution.py:156
  17.2 0.0 collective-permute-start
  17.2 0.7 broadcast_compare_fusion
  17.9 12.6 %convolution_convert_fusion.do_ref = bf16[128,2048]{1,0:T(8,128)(2,1)} fusion(bf16[2048,4096]{1,0:T(8,128)(2,1)} %param.13, bf16[128,4096]{1,0:T(8,128)(2,1)} %param.14, pred[128]{0:T(512)(128)(4,1)S(1)} %broadcast_compare_fusion), kind=kOutput, calls=%fused_computation.6 | convolution fusion | flops 2148270080 | bytes 18350208 | tf_op jit(solution)/shard_map/dot_general | solution.py:241
  30.5 0.1 add_bitcast_fusion
  30.6 0.0 collective-permute-done.3
  30.6 0.9 collective-permute-start.6
  31.5 0.6 copy.11
  32.1 0.0 collective-permute-done.4
  32.1 0.1 broadcast_select_fusion.1.refs_2_
  32.2 0.0 copy-start
  32.2 0.6 collective-permute-start.5
  32.7 0.0 collective-permute-done.1
  32.8 0.0 copy-start.2
  32.8 0.1 collective-permute-start.2
  32.9 4.7 %collective-permute-done.7 = bf16[528,512]{1,0:T(8,128)(2,1)S(1)} collective-permute-done((bf16[528,512]{1,0:T(8,128)(2,1)}, bf16[528,512]{1,0:T(8,128)(2,1)S(1)}, u32[]{:S(2)}, u32[]{:S(2)}) %collective-permute-start.7) | collective-permute-done | bytes 540704 | tf_op jit(solution)/shard_map/ppermute | solution.py:162
  37.6 0.0 collective-permute-done.6
  37.6 0.1 broadcast_select_fusion.refs_3_
  37.7 0.0 copy-start.1
  37.7 0.1 collective-permute-start.8
  37.8 0.6 pad_add_fusion.base_ref
  38.4 0.0 collective-permute-done.refs_4_
  38.4 0.7 fusion.16
  39.1 0.0 collective-permute-done.5.refs_6_
  39.1 0.0 copy-start.4
  39.2 0.0 collective-permute-done.2.refs_5_
  39.2 0.0 copy-start.5
  39.2 0.5 collective-permute-done.8.refs_7_
  39.7 0.0 copy-done.3
  39.7 0.1 compare_reduce_fusion
  39.8 0.6 broadcast_select_fusion.4
  40.5 0.0 copy-done.4
  40.5 0.0 copy-done.5
  40.5 0.0 copy-done
  40.5 0.0 copy-done.2
  40.5 0.0 copy-done.1
  40.5 0.0 copy-done.6
  40.5 21.3 %shard_map.103 = (bf16[128,2048]{1,0:T(8,128)(2,1)}, f32[1,2048]{1,0:T(1,128)}) custom-call(s32[2]{0:T(128)} %pad_add_fusion.base_ref, s32[1,2048]{1,0:T(1,128)} %bitcast.24, bf16[128,2048]{1,0:T(8,128)(2,1)} %q_ref.1, f32[1,2048]{1,0:T(1,128)} %bitcast.23, bf16[128,2048]{1,0:T(8,128)(2,1)} %convolution_convert_fusion.do_ref, ...), custom_call_target="tpu_custom_call" | custom-call | flops 4294967296 | bytes 5775360 | tf_op jit(solution)/shard_map/pallas_call | solution.py:119
  61.8 1.3 %convolution_bitcast_fusion = f32[32]{0:T(128)S(1)} fusion(s32[2048]{0:T(1024)S(1)} %maximum_convert_fusion, f32[1,2048]{1,0:T(1,128)} %get-tuple-element.18), kind=kOutput, calls=%fused_computation.7 | convolution fusion | flops 851968 | bytes 16512 | tf_op jit(solution)/shard_map/dot_general | solution.py:250
  63.1 0.5 broadcast.150
  63.6 1.4 %reduce.13 = f32[2048]{0:T(1024)S(1)} reduce(f32[1,2048]{1,0:T(1,128)} %get-tuple-element.18, f32[]{:T(128)} %broadcast.150), dimensions={0}, to_apply=%get-tuple-element.18.reduce_sub_computation.3 | reduce | bytes 16388 | tf_op jit(solution)/shard_map/pallas_call | solution.py:119
  65.0 0.6 gather_fusion
  65.6 0.3 collective-permute-start.10
  65.9 4.8 %fusion.4 = bf16[128,2048]{1,0:T(8,128)(2,1)S(1)} fusion(bf16[128,2048]{1,0:T(8,128)(2,1)} %get-tuple-element.17, bf16[2048,4096]{1,0:T(8,128)(2,1)} %param.13, s32[]{:T(128)S(6)} %select_n.122), kind=kOutput, calls=%fused_computation.5 | convolution fusion | flops 1074003968 | bytes 9437188 | tf_op jit(solution)/shard_map/dot_general | solution.py:258
  70.7 1.6 %collective-permute-start.9 = (bf16[128,2048]{1,0:T(8,128)(2,1)S(1)}, bf16[128,2048]{1,0:T(8,128)(2,1)S(1)}, u32[]{:S(2)}, u32[]{:S(2)}) collective-permute-start(bf16[128,2048]{1,0:T(8,128)(2,1)S(1)} %fusion.4), channel_id=1, source_target_pairs={{0,2},{2,0},{1,3},{3,1},{4,6},{6,4},{5,7},{7,5},{8,10},{10,8},{9,1... | collective-permute-start | bytes 1572872 | tf_op jit(solution)/shard_map/ppermute | solution.py:259
  72.3 0.0 collective-permute-done.10
  72.3 9.9 %collective-permute-start.11 = (f32[2080]{0:T(1024)S(1)}, f32[2080]{0:T(1024)S(1)}, u32[]{:S(2)}, u32[]{:S(2)}) collective-permute-start(f32[2080]{0:T(1024)S(1)} %fusion.24), channel_id=1, source_target_pairs={{0,4},{4,0},{8,12},{12,8},{1,5},{5,1},{9,13},{13,9},{2,6},{6,2},{1... | collective-permute-start | bytes 24968 | tf_op jit(solution)/shard_map/ppermute | solution.py:204
  82.2 1.7 %collective-permute-done.11 = f32[2080]{0:T(1024)S(1)} collective-permute-done((f32[2080]{0:T(1024)S(1)}, f32[2080]{0:T(1024)S(1)}, u32[]{:S(2)}, u32[]{:S(2)}) %collective-permute-start.11) | collective-permute-done | bytes 8352 | tf_op jit(solution)/shard_map/ppermute | solution.py:204
  83.9 9.0 %collective-permute-start.12 = (f32[2080]{0:T(1024)S(1)}, f32[2080]{0:T(1024)S(1)}, u32[]{:S(2)}, u32[]{:S(2)}) collective-permute-start(f32[2080]{0:T(1024)S(1)} %add.96), channel_id=1, source_target_pairs={{0,8},{4,12},{8,0},{12,4},{1,9},{5,13},{9,1},{13,5},{2,10},{6,14},... | collective-permute-start | bytes 24968 | tf_op jit(solution)/shard_map/ppermute | solution.py:204
  92.9 1.7 %collective-permute-done.12 = f32[2080]{0:T(1024)S(1)} collective-permute-done((f32[2080]{0:T(1024)S(1)}, f32[2080]{0:T(1024)S(1)}, u32[]{:S(2)}, u32[]{:S(2)}) %collective-permute-start.12) | collective-permute-done | bytes 8352 | tf_op jit(solution)/shard_map/ppermute | solution.py:204
  94.6 0.5 collective-permute-start.13
  95.1 4.8 %fusion.2 = f32[128,2048]{1,0:T(8,128)S(1)} fusion(bf16[128,2048]{1,0:T(8,128)(2,1)} %get-tuple-element.17, bf16[2048,4096]{1,0:T(8,128)(2,1)} %param.13, s32[]{:T(128)S(6)} %select_n.121), kind=kOutput, calls=%fused_computation.3 | convolution fusion | flops 1073741824 | bytes 9961476 | tf_op jit(solution)/shard_map/dot_general | solution.py:261
  99.9 0.0 collective-permute-done.13
  100.0 0.5 slice.59
  100.5 0.7 dynamic_slice.11
  101.1 0.0 collective-permute-done.9
  101.1 0.9 add_convert_fusion
  (19 shorter events, 0.2 us)
Async XLA Ops:
  0.6 39.1 %copy-start.3 = (s32[4]{0:T(128)S(1)}, s32[4]{0:T(128)}, u32[]{:S(2)}) copy-start(s32[4]{0:T(128)} %param.17) | copy-start | bytes 52
  3.3 27.3 %collective-permute-start.3 = (bf16[528,512]{1,0:T(8,128)(2,1)}, bf16[528,512]{1,0:T(8,128)(2,1)S(1)}, u32[]{:S(2)}, u32[]{:S(2)}) collective-permute-start(bf16[528,512]{1,0:T(8,128)(2,1)} %pad_maximum_fusion.refs_0_), channel_id=1, source_target_pairs={{0,8},{4,12},{1,9},{5,13},{2,10},{6,14},{3,11},{7,15},{16,24},{20,... | collective-permute-start | bytes 1622024 | tf_op jit(solution)/shard_map/ppermute | solution.py:156
  9.3 22.8 %collective-permute-start.4 = (bf16[528,512]{1,0:T(8,128)(2,1)}, bf16[528,512]{1,0:T(8,128)(2,1)S(1)}, u32[]{:S(2)}, u32[]{:S(2)}) collective-permute-start(bf16[528,512]{1,0:T(8,128)(2,1)} %pad_maximum_fusion.refs_0_), channel_id=1, source_target_pairs={{8,0},{9,1},{10,2},{11,3},{24,16},{25,17},{26,18},{27,19}} | collective-permute-start | bytes 1622024 | tf_op jit(solution)/shard_map/ppermute | solution.py:162
  10.6 27.0 %collective-permute-start.7 = (bf16[528,512]{1,0:T(8,128)(2,1)}, bf16[528,512]{1,0:T(8,128)(2,1)S(1)}, u32[]{:S(2)}, u32[]{:S(2)}) collective-permute-start(bf16[528,512]{1,0:T(8,128)(2,1)} %pad_maximum_fusion.refs_0_), channel_id=1, source_target_pairs={{4,0},{8,4},{12,8},{5,1},{9,5},{13,9},{6,2},{10,6},{14,10},{7,3},{... | collective-permute-start | bytes 1622024 | tf_op jit(solution)/shard_map/ppermute | solution.py:162
  11.9 20.9 %collective-permute-start.1 = (bf16[528,512]{1,0:T(8,128)(2,1)}, bf16[528,512]{1,0:T(8,128)(2,1)}, u32[]{:S(2)}, u32[]{:S(2)}) collective-permute-start(bf16[528,512]{1,0:T(8,128)(2,1)} %pad_maximum_fusion.refs_0_), channel_id=1, source_target_pairs={{0,4},{4,8},{8,12},{1,5},{5,9},{9,13},{2,6},{6,10},{10,14},{3,7},{... | collective-permute-start | bytes 1622024 | tf_op jit(solution)/shard_map/ppermute | solution.py:156
  17.2 21.2 %collective-permute-start = (bf16[528,512]{1,0:T(8,128)(2,1)}, bf16[528,512]{1,0:T(8,128)(2,1)}, u32[]{:S(2)}, u32[]{:S(2)}) collective-permute-start(bf16[528,512]{1,0:T(8,128)(2,1)} %pad_maximum_fusion.refs_0_), channel_id=1, source_target_pairs={{0,1},{1,0},{2,3},{3,2},{4,5},{5,4},{6,7},{7,6},{8,9},{9,8},{10,11... | collective-permute-start | bytes 1622024 | tf_op jit(solution)/shard_map/ppermute | solution.py:183
  30.6 7.0 %collective-permute-start.6 = (bf16[528,512]{1,0:T(8,128)(2,1)S(1)}, bf16[528,512]{1,0:T(8,128)(2,1)S(1)}, u32[]{:S(2)}, u32[]{:S(2)}) collective-permute-start(bf16[528,512]{1,0:T(8,128)(2,1)S(1)} %collective-permute-done.3), channel_id=1, source_target_pairs={{8,12},{9,13},{10,14},{11,15},{24,28},{25,29},{26,30},{27,31}} | collective-permute-start | bytes 1622024 | tf_op jit(solution)/shard_map/ppermute | solution.py:154
  32.2 8.3 %copy-start = (bf16[528,512]{1,0:T(8,128)(2,1)}, bf16[528,512]{1,0:T(8,128)(2,1)S(1)}, u32[]{:S(2)}) copy-start(bf16[528,512]{1,0:T(8,128)(2,1)S(1)} %broadcast_select_fusion.1.refs_2_) | copy-start | bytes 1622020
  32.2 7.0 %collective-permute-start.5 = (bf16[528,512]{1,0:T(8,128)(2,1)S(1)}, bf16[528,512]{1,0:T(8,128)(2,1)S(1)}, u32[]{:S(2)}, u32[]{:S(2)}) collective-permute-start(bf16[528,512]{1,0:T(8,128)(2,1)S(1)} %broadcast_select_fusion.1.refs_2_), channel_id=1, source_target_pairs={{0,1},{1,0},{2,3},{3,2},{4,5},{5,4},{6,7},{7,6},{8,9},{9,8},{10,11... | collective-permute-start | bytes 1622024 | tf_op jit(solution)/shard_map/ppermute | solution.py:183
  32.8 7.7 %copy-start.2 = (bf16[528,512]{1,0:T(8,128)(2,1)}, bf16[528,512]{1,0:T(8,128)(2,1)S(1)}, u32[]{:S(2)}) copy-start(bf16[528,512]{1,0:T(8,128)(2,1)S(1)} %broadcast_select_fusion.2.refs_1_) | copy-start | bytes 1622020
  32.8 6.4 %collective-permute-start.2 = (bf16[528,512]{1,0:T(8,128)(2,1)S(1)}, bf16[528,512]{1,0:T(8,128)(2,1)S(1)}, u32[]{:S(2)}, u32[]{:S(2)}) collective-permute-start(bf16[528,512]{1,0:T(8,128)(2,1)S(1)} %broadcast_select_fusion.2.refs_1_), channel_id=1, source_target_pairs={{0,1},{1,0},{2,3},{3,2},{4,5},{5,4},{6,7},{7,6},{8,9},{9,8},{10,11... | collective-permute-start | bytes 1622024 | tf_op jit(solution)/shard_map/ppermute | solution.py:183
  37.7 2.8 %copy-start.1 = (bf16[528,512]{1,0:T(8,128)(2,1)}, bf16[528,512]{1,0:T(8,128)(2,1)S(1)}, u32[]{:S(2)}) copy-start(bf16[528,512]{1,0:T(8,128)(2,1)S(1)} %broadcast_select_fusion.refs_3_) | copy-start | bytes 1622020
  37.7 2.0 %collective-permute-start.8 = (bf16[528,512]{1,0:T(8,128)(2,1)S(1)}, bf16[528,512]{1,0:T(8,128)(2,1)S(1)}, u32[]{:S(2)}, u32[]{:S(2)}) collective-permute-start(bf16[528,512]{1,0:T(8,128)(2,1)S(1)} %broadcast_select_fusion.refs_3_), channel_id=1, source_target_pairs={{0,1},{1,0},{2,3},{3,2},{4,5},{5,4},{6,7},{7,6},{8,9},{9,8},{10,11... | collective-permute-start | bytes 1622024 | tf_op jit(solution)/shard_map/ppermute | solution.py:183
  39.1 1.3 %copy-start.4 = (bf16[528,512]{1,0:T(8,128)(2,1)}, bf16[528,512]{1,0:T(8,128)(2,1)S(1)}, u32[]{:S(2)}) copy-start(bf16[528,512]{1,0:T(8,128)(2,1)S(1)} %collective-permute-done.5.refs_6_) | copy-start | bytes 1622020
  39.2 1.3 %copy-start.5 = (bf16[528,512]{1,0:T(8,128)(2,1)}, bf16[528,512]{1,0:T(8,128)(2,1)S(1)}, u32[]{:S(2)}) copy-start(bf16[528,512]{1,0:T(8,128)(2,1)S(1)} %collective-permute-done.2.refs_5_) | copy-start | bytes 1622020
  39.7 0.8 copy-start.6
  65.6 6.7 %collective-permute-start.10 = (f32[2080]{0:T(1024)S(1)}, f32[2080]{0:T(1024)S(1)}, u32[]{:S(2)}, u32[]{:S(2)}) collective-permute-start(f32[2080]{0:T(1024)S(1)} %pad_maximum_fusion.1), channel_id=1, source_target_pairs={{0,1},{1,0},{2,3},{3,2},{4,5},{5,4},{6,7},{7,6},{8,9},{9,8},{10,11... | collective-permute-start | bytes 24968 | tf_op jit(solution)/shard_map/ppermute | solution.py:204
  70.7 30.4 %collective-permute-start.9 = (bf16[128,2048]{1,0:T(8,128)(2,1)S(1)}, bf16[128,2048]{1,0:T(8,128)(2,1)S(1)}, u32[]{:S(2)}, u32[]{:S(2)}) collective-permute-start(bf16[128,2048]{1,0:T(8,128)(2,1)S(1)} %fusion.4), channel_id=1, source_target_pairs={{0,2},{2,0},{1,3},{3,1},{4,6},{6,4},{5,7},{7,5},{8,10},{10,8},{9,1... | collective-permute-start | bytes 1572872 | tf_op jit(solution)/shard_map/ppermute | solution.py:259
  72.3 11.6 %collective-permute-start.11 = (f32[2080]{0:T(1024)S(1)}, f32[2080]{0:T(1024)S(1)}, u32[]{:S(2)}, u32[]{:S(2)}) collective-permute-start(f32[2080]{0:T(1024)S(1)} %fusion.24), channel_id=1, source_target_pairs={{0,4},{4,0},{8,12},{12,8},{1,5},{5,1},{9,13},{13,9},{2,6},{6,2},{1... | collective-permute-start | bytes 24968 | tf_op jit(solution)/shard_map/ppermute | solution.py:204
  83.9 10.7 %collective-permute-start.12 = (f32[2080]{0:T(1024)S(1)}, f32[2080]{0:T(1024)S(1)}, u32[]{:S(2)}, u32[]{:S(2)}) collective-permute-start(f32[2080]{0:T(1024)S(1)} %add.96), channel_id=1, source_target_pairs={{0,8},{4,12},{8,0},{12,4},{1,9},{5,13},{9,1},{13,5},{2,10},{6,14},... | collective-permute-start | bytes 24968 | tf_op jit(solution)/shard_map/ppermute | solution.py:204
  94.6 5.3 %collective-permute-start.13 = (f32[2080]{0:T(1024)S(1)}, f32[2080]{0:T(1024)S(1)}, u32[]{:S(2)}, u32[]{:S(2)}) collective-permute-start(f32[2080]{0:T(1024)S(1)} %add.97), channel_id=1, source_target_pairs={{0,2},{2,0},{1,3},{3,1},{4,6},{6,4},{5,7},{7,5},{8,10},{10,8},{9,1... | collective-permute-start | bytes 24968 | tf_op jit(solution)/shard_map/ppermute | solution.py:204

commit v17 on v16

--- a/solution.py
+++ b/solution.py
@@ -246,11 +246,12 @@
     )
 
     inverse = (ctx_at - jnp.arange(ctx_count, dtype=jnp.int32)) % ctx_count
-    attr_abs = attr.reshape(ctx_count, key_count)[inverse].reshape(-1)
-    seg_part = jnp.dot(attr[0], onehot, precision=lax.Precision.HIGHEST)
-    summed = butterfly_sum(jnp.concatenate([attr_abs, seg_part]), ("rep", "ctx", "head"))
-    attr_all = summed[:context_len]
-    segment_attr = summed[context_len:]
+    order = (inverse[:, None] * key_count + jnp.arange(key_count, dtype=jnp.int32)[None, :]).reshape(-1)
+    attr_abs = jnp.take(attr, order, axis=1)
+    seg_part = jnp.dot(attr, onehot, precision=lax.Precision.HIGHEST)
+    summed = butterfly_sum(jnp.concatenate([attr_abs, seg_part], axis=1), ("rep", "ctx", "head"))
+    attr_all = summed[0, :context_len]
+    segment_attr = summed[0, context_len:]
 
     if head_count == 2:
         cols = out_weight.shape[1] // 2

time: 103 us -> 117 us (1.14)
  local copies, waits for them, and re-layouts: 2.94 us -> 11.7 us
  waiting for transfers between devices: 8.61 us -> 14.7 us
    gather x1, local copies, waits for them, and re-layouts: 0.56 us -> 10.5 us  [local(): attr_abs = jnp.take(attr, order, axis=1)]
    ppermute x4, waiting for transfers between devices: 3.4 us -> 8.95 us  [butterfly_sum(): total = total + lax.ppermute(total, axis, [(i, i ^ bit) for i in range(n)])]
    pallas_call x1 -> x0, other arithmetic: 1.36 us -> none  [fused_attention(): pl.pallas_call(functools.partial(attention_kernel, tq=tq, hp=hp, n=n, spl...]
  transfers between devices with their start and end apart: 14 -> 14, of which waited for: 4 -> 5; matrix products, arithmetic and copies ran while one was open for 26% -> 22% of each run, Pallas kernels for 0% -> 0%
where the time goes in v17:
time: 117 us; the launch traced here: 116 us
  starting transfers between devices  36.9 us (32%)
  matrix products  23.4 us (20%)
  Pallas kernels  21.3 us (18%)
  waiting for transfers between devices  14.7 us (13%)
  local copies, waits for them, and re-layouts  11.7 us (10%)
  other arithmetic  7.35 us (6%)
    pallas_call x1, Pallas kernels, fused_attention(): pl.pallas_call(functools.partial(attention_kernel, tq=tq, hp=hp, n=n, spl...  21.3 us
    ppermute x4, starting transfers between devices, butterfly_sum(): total = total + lax.ppermute(total, axis, [(i, i ^ bit) for i in range(n)])  19.8 us
    dot_general x1, matrix products, local(): jnp.dot(grad_masked, out_weight.T, preferred_element_type=jnp.float32)  12.6 us
    ppermute x2, starting transfers between devices, relay_gather(): forward.append(lax.ppermute(payload, 'ctx', fwd) if fwd else zero)  11.3 us
    gather x1, local copies, waits for them, and re-layouts, local(): attr_abs = jnp.take(attr, order, axis=1)  10.5 us
    ppermute x4, waiting for transfers between devices, butterfly_sum(): total = total + lax.ppermute(total, axis, [(i, i ^ bit) for i in range(n)])  8.95 us
    dot_general x1, matrix products, local(): send = jnp.dot(delta, send_w, preferred_element_type=jnp.float32)  4.82 us
    ppermute x2, waiting for transfers between devices, relay_gather(): backward.append(lax.ppermute(payload, 'ctx', bwd) if bwd else zero)  4.72 us
  transfers between devices with their start and end apart: 14, of which 5 were waited for; matrix products, arithmetic and copies ran while one was open for 22% of the time, Pallas kernels for 0%

profile of v17, /device:TPU:0, one launch (start us, length us, event | category | flops | bytes accessed | tf_op | source)
XLA Modules:
  0.0 116.3 jit_solution(11404051931211694276)
XLA Ops:
  0.6 0.0 copy-start.5
  0.6 0.7 convert_element_type.23
  1.4 1.1 broadcast_select_fusion.3
  2.5 0.8 pad_maximum_fusion.refs_0_
  3.3 6.0 %collective-permute-start.3 = (bf16[528,512]{1,0:T(8,128)(2,1)}, bf16[528,512]{1,0:T(8,128)(2,1)S(1)}, u32[]{:S(2)}, u32[]{:S(2)}) collective-permute-start(bf16[528,512]{1,0:T(8,128)(2,1)} %pad_maximum_fusion.refs_0_), channel_id=1, source_target_pairs={{0,8},{4,12},{1,9},{5,13},{2,10},{6,14},{3,11},{7,15},{16,24},{20,... | collective-permute-start | bytes 1622024 | tf_op jit(solution)/shard_map/ppermute | solution.py:156
  9.3 1.3 %collective-permute-start.4 = (bf16[528,512]{1,0:T(8,128)(2,1)}, bf16[528,512]{1,0:T(8,128)(2,1)S(1)}, u32[]{:S(2)}, u32[]{:S(2)}) collective-permute-start(bf16[528,512]{1,0:T(8,128)(2,1)} %pad_maximum_fusion.refs_0_), channel_id=1, source_target_pairs={{8,0},{9,1},{10,2},{11,3},{24,16},{25,17},{26,18},{27,19}} | collective-permute-start | bytes 1622024 | tf_op jit(solution)/shard_map/ppermute | solution.py:162
  10.6 1.3 %collective-permute-start.7 = (bf16[528,512]{1,0:T(8,128)(2,1)}, bf16[528,512]{1,0:T(8,128)(2,1)S(1)}, u32[]{:S(2)}, u32[]{:S(2)}) collective-permute-start(bf16[528,512]{1,0:T(8,128)(2,1)} %pad_maximum_fusion.refs_0_), channel_id=1, source_target_pairs={{4,0},{8,4},{12,8},{5,1},{9,5},{13,9},{6,2},{10,6},{14,10},{7,3},{... | collective-permute-start | bytes 1622024 | tf_op jit(solution)/shard_map/ppermute | solution.py:162
  11.9 5.4 %collective-permute-start.1 = (bf16[528,512]{1,0:T(8,128)(2,1)}, bf16[528,512]{1,0:T(8,128)(2,1)}, u32[]{:S(2)}, u32[]{:S(2)}) collective-permute-start(bf16[528,512]{1,0:T(8,128)(2,1)} %pad_maximum_fusion.refs_0_), channel_id=1, source_target_pairs={{0,4},{4,8},{8,12},{1,5},{5,9},{9,13},{2,6},{6,10},{10,14},{3,7},{... | collective-permute-start | bytes 1622024 | tf_op jit(solution)/shard_map/ppermute | solution.py:156
  17.3 0.0 collective-permute-start
  17.3 0.7 broadcast_compare_fusion
  17.9 12.6 %convolution_convert_fusion.do_ref = bf16[128,2048]{1,0:T(8,128)(2,1)} fusion(bf16[2048,4096]{1,0:T(8,128)(2,1)} %param.13, bf16[128,4096]{1,0:T(8,128)(2,1)} %param.14, pred[128]{0:T(512)(128)(4,1)S(1)} %broadcast_compare_fusion), kind=kOutput, calls=%fused_computation.6 | convolution fusion | flops 2148270080 | bytes 18350208 | tf_op jit(solution)/shard_map/dot_general | solution.py:241
  30.5 0.1 add_bitcast_fusion
  30.6 0.0 collective-permute-done.3
  30.6 0.9 collective-permute-start.6
  31.5 0.6 pad_add_fusion.base_ref
  32.1 0.0 collective-permute-done.4
  32.1 0.1 broadcast_select_fusion.1.refs_2_
  32.2 0.0 copy-start.1
  32.2 0.6 collective-permute-start.5
  32.7 0.0 collective-permute-done.1
  32.8 0.0 copy-start.3
  32.8 0.1 collective-permute-start.2
  32.9 4.7 %collective-permute-done.7 = bf16[528,512]{1,0:T(8,128)(2,1)S(1)} collective-permute-done((bf16[528,512]{1,0:T(8,128)(2,1)}, bf16[528,512]{1,0:T(8,128)(2,1)S(1)}, u32[]{:S(2)}, u32[]{:S(2)}) %collective-permute-start.7) | collective-permute-done | bytes 540704 | tf_op jit(solution)/shard_map/ppermute | solution.py:162
  37.6 0.0 collective-permute-done.6
  37.6 0.1 broadcast_select_fusion.refs_3_
  37.7 0.0 copy-start.2
  37.7 0.1 collective-permute-start.8
  37.8 0.0 collective-permute-done.refs_4_
  37.8 0.8 fusion.17
  38.6 0.0 collective-permute-done.5.refs_6_
  38.6 0.0 copy-start.6
  38.6 0.0 collective-permute-done.2.refs_5_
  38.6 0.0 copy-start.7
  38.6 1.1 collective-permute-done.8.refs_7_
  39.7 0.0 copy-done.5
  39.7 0.1 compare_reduce_fusion
  39.8 0.6 broadcast_select_fusion.4
  40.5 0.0 copy-done.6
  40.5 0.0 copy-done.7
  40.5 0.0 copy-done.4
  40.5 0.0 copy-done.1
  40.5 0.0 copy-done.3
  40.5 0.0 copy-done.2
  40.5 21.3 %shard_map.103 = (bf16[128,2048]{1,0:T(8,128)(2,1)}, f32[1,2048]{1,0:T(1,128)}) custom-call(s32[2]{0:T(128)} %pad_add_fusion.base_ref, s32[1,2048]{1,0:T(1,128)} %bitcast.26, bf16[128,2048]{1,0:T(8,128)(2,1)} %q_ref.1, f32[1,2048]{1,0:T(1,128)} %bitcast.30, bf16[128,2048]{1,0:T(8,128)(2,1)} %convolution_convert_fusion.do_ref, ...), custom_call_target="tpu_custom_call" | custom-call | flops 4294967296 | bytes 5775360 | tf_op jit(solution)/shard_map/pallas_call | solution.py:119
  61.8 0.0 copy-start
  61.8 1.3 %fusion.9 = f32[1,32]{1,0:T(1,128)S(1)} fusion(s32[2048]{0:T(1024)S(1)} %maximum_convert_fusion, f32[1,2048]{1,0:T(1,128)} %get-tuple-element.18), kind=kOutput, calls=%fused_computation.11 | convolution fusion | flops 851968 | bytes 16512 | tf_op jit(solution)/shard_map/dot_general | solution.py:251
  63.2 10.5 %gather_fusion = f32[2048]{0:T(1024)S(1)} fusion(f32[2048]{0:T(1024)} %bitcast.24, s32[2048]{0:T(1024)S(1)} %broadcast_clamp_fusion), kind=kCustom, calls=%fused_computation | custom fusion | bytes 24576 | tf_op jit(solution)/shard_map/jit(_take)/gather | solution.py:250
  73.7 0.7 and_select_fusion
  74.4 0.2 collective-permute-start.10
  74.6 1.0 collective-permute-done.10
  75.6 10.0 %collective-permute-start.11 = (f32[1,2080]{1,0:T(1,128)S(1)}, f32[1,2080]{1,0:T(1,128)S(1)}, u32[]{:S(2)}, u32[]{:S(2)}) collective-permute-start(f32[1,2080]{1,0:T(1,128)S(1)} %fusion.23), channel_id=1, source_target_pairs={{0,4},{4,0},{8,12},{12,8},{1,5},{5,1},{9,13},{13,9},{2,6},{6,2},{1... | collective-permute-start | bytes 24968 | tf_op jit(solution)/shard_map/ppermute | solution.py:204
  85.7 1.6 %collective-permute-done.11 = f32[1,2080]{1,0:T(1,128)S(1)} collective-permute-done((f32[1,2080]{1,0:T(1,128)S(1)}, f32[1,2080]{1,0:T(1,128)S(1)}, u32[]{:S(2)}, u32[]{:S(2)}) %collective-permute-start.11) | collective-permute-done | bytes 8352 | tf_op jit(solution)/shard_map/ppermute | solution.py:204
  87.3 9.0 %collective-permute-start.12 = (f32[1,2080]{1,0:T(1,128)S(1)}, f32[1,2080]{1,0:T(1,128)S(1)}, u32[]{:S(2)}, u32[]{:S(2)}) collective-permute-start(f32[1,2080]{1,0:T(1,128)S(1)} %add.133), channel_id=1, source_target_pairs={{0,8},{4,12},{8,0},{12,4},{1,9},{5,13},{9,1},{13,5},{2,10},{6,14},... | collective-permute-start | bytes 24968 | tf_op jit(solution)/shard_map/ppermute | solution.py:204
  96.3 4.8 %fusion.4 = bf16[128,2048]{1,0:T(8,128)(2,1)S(1)} fusion(bf16[128,2048]{1,0:T(8,128)(2,1)} %get-tuple-element.17, bf16[2048,4096]{1,0:T(8,128)(2,1)} %param.13, s32[]{:T(128)S(6)} %select_n.139), kind=kOutput, calls=%fused_computation.5 | convolution fusion | flops 1074003968 | bytes 9437188 | tf_op jit(solution)/shard_map/dot_general | solution.py:259
  101.1 1.6 %collective-permute-start.9 = (bf16[128,2048]{1,0:T(8,128)(2,1)S(1)}, bf16[128,2048]{1,0:T(8,128)(2,1)S(1)}, u32[]{:S(2)}, u32[]{:S(2)}) collective-permute-start(bf16[128,2048]{1,0:T(8,128)(2,1)S(1)} %fusion.4), channel_id=1, source_target_pairs={{0,2},{2,0},{1,3},{3,1},{4,6},{6,4},{5,7},{7,5},{8,10},{10,8},{9,1... | collective-permute-start | bytes 1572872 | tf_op jit(solution)/shard_map/ppermute | solution.py:260
  102.7 0.0 collective-permute-done.12
  102.7 0.6 collective-permute-start.13
  103.3 0.0 copy-done
  103.3 4.6 %fusion.2 = f32[128,2048]{1,0:T(8,128)S(1)} fusion(bf16[128,2048]{1,0:T(8,128)(2,1)S(1)} %copy-done, bf16[2048,4096]{1,0:T(8,128)(2,1)} %param.13, s32[]{:T(128)S(6)} %select_n.138), kind=kOutput, calls=%fused_computation.3 | convolution fusion | flops 1073741824 | bytes 9961476 | tf_op jit(solution)/shard_map/dot_general | solution.py:262
  107.9 6.3 %collective-permute-done.13 = f32[1,2080]{1,0:T(1,128)S(1)} collective-permute-done((f32[1,2080]{1,0:T(1,128)S(1)}, f32[1,2080]{1,0:T(1,128)S(1)}, u32[]{:S(2)}, u32[]{:S(2)}) %collective-permute-start.13) | collective-permute-done | bytes 8352 | tf_op jit(solution)/shard_map/ppermute | solution.py:204
  114.3 0.6 constant_dynamic-slice_fusion
  114.8 0.5 slice_bitcast_fusion
  115.4 0.0 collective-permute-done.9
  115.4 0.9 add_convert_fusion
  (20 shorter events, 0.3 us)
Async XLA Ops:
  0.6 39.1 %copy-start.5 = (s32[4]{0:T(128)S(1)}, s32[4]{0:T(128)}, u32[]{:S(2)}) copy-start(s32[4]{0:T(128)} %param.17) | copy-start | bytes 52
  3.3 27.3 %collective-permute-start.3 = (bf16[528,512]{1,0:T(8,128)(2,1)}, bf16[528,512]{1,0:T(8,128)(2,1)S(1)}, u32[]{:S(2)}, u32[]{:S(2)}) collective-permute-start(bf16[528,512]{1,0:T(8,128)(2,1)} %pad_maximum_fusion.refs_0_), channel_id=1, source_target_pairs={{0,8},{4,12},{1,9},{5,13},{2,10},{6,14},{3,11},{7,15},{16,24},{20,... | collective-permute-start | bytes 1622024 | tf_op jit(solution)/shard_map/ppermute | solution.py:156
  9.3 22.8 %collective-permute-start.4 = (bf16[528,512]{1,0:T(8,128)(2,1)}, bf16[528,512]{1,0:T(8,128)(2,1)S(1)}, u32[]{:S(2)}, u32[]{:S(2)}) collective-permute-start(bf16[528,512]{1,0:T(8,128)(2,1)} %pad_maximum_fusion.refs_0_), channel_id=1, source_target_pairs={{8,0},{9,1},{10,2},{11,3},{24,16},{25,17},{26,18},{27,19}} | collective-permute-start | bytes 1622024 | tf_op jit(solution)/shard_map/ppermute | solution.py:162
  10.6 27.0 %collective-permute-start.7 = (bf16[528,512]{1,0:T(8,128)(2,1)}, bf16[528,512]{1,0:T(8,128)(2,1)S(1)}, u32[]{:S(2)}, u32[]{:S(2)}) collective-permute-start(bf16[528,512]{1,0:T(8,128)(2,1)} %pad_maximum_fusion.refs_0_), channel_id=1, source_target_pairs={{4,0},{8,4},{12,8},{5,1},{9,5},{13,9},{6,2},{10,6},{14,10},{7,3},{... | collective-permute-start | bytes 1622024 | tf_op jit(solution)/shard_map/ppermute | solution.py:162
  11.9 20.9 %collective-permute-start.1 = (bf16[528,512]{1,0:T(8,128)(2,1)}, bf16[528,512]{1,0:T(8,128)(2,1)}, u32[]{:S(2)}, u32[]{:S(2)}) collective-permute-start(bf16[528,512]{1,0:T(8,128)(2,1)} %pad_maximum_fusion.refs_0_), channel_id=1, source_target_pairs={{0,4},{4,8},{8,12},{1,5},{5,9},{9,13},{2,6},{6,10},{10,14},{3,7},{... | collective-permute-start | bytes 1622024 | tf_op jit(solution)/shard_map/ppermute | solution.py:156
  17.3 20.5 %collective-permute-start = (bf16[528,512]{1,0:T(8,128)(2,1)}, bf16[528,512]{1,0:T(8,128)(2,1)}, u32[]{:S(2)}, u32[]{:S(2)}) collective-permute-start(bf16[528,512]{1,0:T(8,128)(2,1)} %pad_maximum_fusion.refs_0_), channel_id=1, source_target_pairs={{0,1},{1,0},{2,3},{3,2},{4,5},{5,4},{6,7},{7,6},{8,9},{9,8},{10,11... | collective-permute-start | bytes 1622024 | tf_op jit(solution)/shard_map/ppermute | solution.py:183
  30.6 9.9 %copy-start.4 = (s32[1,1,4,512]{3,1,2,0:T(1,128)}, s32[1,1,4,512]{3,1,2,0:T(1,128)S(1)}, u32[]{:S(2)}) copy-start(s32[1,1,4,512]{3,1,2,0:T(1,128)S(1)} %copy.11) | copy-start | bytes 24580
  30.6 7.0 %collective-permute-start.6 = (bf16[528,512]{1,0:T(8,128)(2,1)S(1)}, bf16[528,512]{1,0:T(8,128)(2,1)S(1)}, u32[]{:S(2)}, u32[]{:S(2)}) collective-permute-start(bf16[528,512]{1,0:T(8,128)(2,1)S(1)} %collective-permute-done.3), channel_id=1, source_target_pairs={{8,12},{9,13},{10,14},{11,15},{24,28},{25,29},{26,30},{27,31}} | collective-permute-start | bytes 1622024 | tf_op jit(solution)/shard_map/ppermute | solution.py:154
  32.2 8.3 %copy-start.1 = (bf16[528,512]{1,0:T(8,128)(2,1)}, bf16[528,512]{1,0:T(8,128)(2,1)S(1)}, u32[]{:S(2)}) copy-start(bf16[528,512]{1,0:T(8,128)(2,1)S(1)} %broadcast_select_fusion.1.refs_2_) | copy-start | bytes 1622020
  32.2 6.4 %collective-permute-start.5 = (bf16[528,512]{1,0:T(8,128)(2,1)S(1)}, bf16[528,512]{1,0:T(8,128)(2,1)S(1)}, u32[]{:S(2)}, u32[]{:S(2)}) collective-permute-start(bf16[528,512]{1,0:T(8,128)(2,1)S(1)} %broadcast_select_fusion.1.refs_2_), channel_id=1, source_target_pairs={{0,1},{1,0},{2,3},{3,2},{4,5},{5,4},{6,7},{7,6},{8,9},{9,8},{10,11... | collective-permute-start | bytes 1622024 | tf_op jit(solution)/shard_map/ppermute | solution.py:183
  32.8 7.7 %copy-start.3 = (bf16[528,512]{1,0:T(8,128)(2,1)}, bf16[528,512]{1,0:T(8,128)(2,1)S(1)}, u32[]{:S(2)}) copy-start(bf16[528,512]{1,0:T(8,128)(2,1)S(1)} %broadcast_select_fusion.2.refs_1_) | copy-start | bytes 1622020
  32.8 5.8 %collective-permute-start.2 = (bf16[528,512]{1,0:T(8,128)(2,1)S(1)}, bf16[528,512]{1,0:T(8,128)(2,1)S(1)}, u32[]{:S(2)}, u32[]{:S(2)}) collective-permute-start(bf16[528,512]{1,0:T(8,128)(2,1)S(1)} %broadcast_select_fusion.2.refs_1_), channel_id=1, source_target_pairs={{0,1},{1,0},{2,3},{3,2},{4,5},{5,4},{6,7},{7,6},{8,9},{9,8},{10,11... | collective-permute-start | bytes 1622024 | tf_op jit(solution)/shard_map/ppermute | solution.py:183
  37.7 2.8 %copy-start.2 = (bf16[528,512]{1,0:T(8,128)(2,1)}, bf16[528,512]{1,0:T(8,128)(2,1)S(1)}, u32[]{:S(2)}) copy-start(bf16[528,512]{1,0:T(8,128)(2,1)S(1)} %broadcast_select_fusion.refs_3_) | copy-start | bytes 1622020
  37.7 2.0 %collective-permute-start.8 = (bf16[528,512]{1,0:T(8,128)(2,1)S(1)}, bf16[528,512]{1,0:T(8,128)(2,1)S(1)}, u32[]{:S(2)}, u32[]{:S(2)}) collective-permute-start(bf16[528,512]{1,0:T(8,128)(2,1)S(1)} %broadcast_select_fusion.refs_3_), channel_id=1, source_target_pairs={{0,1},{1,0},{2,3},{3,2},{4,5},{5,4},{6,7},{7,6},{8,9},{9,8},{10,11... | collective-permute-start | bytes 1622024 | tf_op jit(solution)/shard_map/ppermute | solution.py:183
  38.6 1.9 %copy-start.6 = (bf16[528,512]{1,0:T(8,128)(2,1)}, bf16[528,512]{1,0:T(8,128)(2,1)S(1)}, u32[]{:S(2)}) copy-start(bf16[528,512]{1,0:T(8,128)(2,1)S(1)} %collective-permute-done.5.refs_6_) | copy-start | bytes 1622020
  38.6 1.9 %copy-start.7 = (bf16[528,512]{1,0:T(8,128)(2,1)}, bf16[528,512]{1,0:T(8,128)(2,1)S(1)}, u32[]{:S(2)}) copy-start(bf16[528,512]{1,0:T(8,128)(2,1)S(1)} %collective-permute-done.2.refs_5_) | copy-start | bytes 1622020
  39.7 0.8 copy-start.8
  61.8 41.5 %copy-start = (bf16[128,2048]{1,0:T(8,128)(2,1)S(1)}, bf16[128,2048]{1,0:T(8,128)(2,1)}, u32[]{:S(2)}) copy-start(bf16[128,2048]{1,0:T(8,128)(2,1)} %get-tuple-element.17) | copy-start | bytes 1572868
  74.4 1.2 %collective-permute-start.10 = (f32[1,2080]{1,0:T(1,128)S(1)}, f32[1,2080]{1,0:T(1,128)S(1)}, u32[]{:S(2)}, u32[]{:S(2)}) collective-permute-start(f32[1,2080]{1,0:T(1,128)S(1)} %pad_maximum_fusion.1), channel_id=1, source_target_pairs={{0,1},{1,0},{2,3},{3,2},{4,5},{5,4},{6,7},{7,6},{8,9},{9,8},{10,11... | collective-permute-start | bytes 24968 | tf_op jit(solution)/shard_map/ppermute | solution.py:204
  75.6 11.7 %collective-permute-start.11 = (f32[1,2080]{1,0:T(1,128)S(1)}, f32[1,2080]{1,0:T(1,128)S(1)}, u32[]{:S(2)}, u32[]{:S(2)}) collective-permute-start(f32[1,2080]{1,0:T(1,128)S(1)} %fusion.23), channel_id=1, source_target_pairs={{0,4},{4,0},{8,12},{12,8},{1,5},{5,1},{9,13},{13,9},{2,6},{6,2},{1... | collective-permute-start | bytes 24968 | tf_op jit(solution)/shard_map/ppermute | solution.py:204
  87.3 15.4 %collective-permute-start.12 = (f32[1,2080]{1,0:T(1,128)S(1)}, f32[1,2080]{1,0:T(1,128)S(1)}, u32[]{:S(2)}, u32[]{:S(2)}) collective-permute-start(f32[1,2080]{1,0:T(1,128)S(1)} %add.133), channel_id=1, source_target_pairs={{0,8},{4,12},{8,0},{12,4},{1,9},{5,13},{9,1},{13,5},{2,10},{6,14},... | collective-permute-start | bytes 24968 | tf_op jit(solution)/shard_map/ppermute | solution.py:204
  101.1 14.2 %collective-permute-start.9 = (bf16[128,2048]{1,0:T(8,128)(2,1)S(1)}, bf16[128,2048]{1,0:T(8,128)(2,1)S(1)}, u32[]{:S(2)}, u32[]{:S(2)}) collective-permute-start(bf16[128,2048]{1,0:T(8,128)(2,1)S(1)} %fusion.4), channel_id=1, source_target_pairs={{0,2},{2,0},{1,3},{3,1},{4,6},{6,4},{5,7},{7,5},{8,10},{10,8},{9,1... | collective-permute-start | bytes 1572872 | tf_op jit(solution)/shard_map/ppermute | solution.py:260
  102.7 11.5 %collective-permute-start.13 = (f32[1,2080]{1,0:T(1,128)S(1)}, f32[1,2080]{1,0:T(1,128)S(1)}, u32[]{:S(2)}, u32[]{:S(2)}) collective-permute-start(f32[1,2080]{1,0:T(1,128)S(1)} %add.134), channel_id=1, source_target_pairs={{0,2},{2,0},{1,3},{3,1},{4,6},{6,4},{5,7},{7,5},{8,10},{10,8},{9,1... | collective-permute-start | bytes 24968 | tf_op jit(solution)/shard_map/ppermute | solution.py:204

commit v18 on v16

--- a/solution.py
+++ b/solution.py
@@ -18,34 +18,34 @@
     kc = k_refs[0].shape[0]
     rows = hp * tq
     row_pos = base_ref[0] + r * tq + lax.broadcasted_iota(jnp.int32, (rows, 1), 0) % tq
-    vis = kpos_ref[...] <= row_pos
-    kept = kept_ref[...] > 0.0
     if hp > 1:
         q = jnp.concatenate([q_ref[:, h * HD:(h + 1) * HD] for h in range(hp)], axis=0)
         g_rows = jnp.concatenate([do_ref[:, h * HD:(h + 1) * HD] for h in range(hp)], axis=0)
     else:
         q = q_ref[...]
         g_rows = do_ref[...]
-    s = jnp.concatenate(
-        [lax.dot_general(q, kr[...], NT_DIMS, preferred_element_type=jnp.float32) for kr in k_refs],
-        axis=1,
-    ) * (HD ** -0.5)
-    s_c = jnp.where(vis, s, NEG_FILL)
-    s_m = jnp.where(kept, s_c, NEG_FILL)
-    m_c = jnp.max(s_c, axis=1, keepdims=True)
-    m_m = jnp.max(s_m, axis=1, keepdims=True)
-    e_c = jnp.exp(s_c - m_c)
-    e_m = jnp.exp(s_m - m_m)
-    l_c = jnp.sum(e_c, axis=1, keepdims=True)
-    l_m = jnp.sum(e_m, axis=1, keepdims=True)
-    eb_c = e_c.astype(jnp.bfloat16)
-    eb_m = e_m.astype(jnp.bfloat16)
+    spans = [slice(i * kc, (i + 1) * kc) for i in range(len(k_refs))]
+    s_l, sc_l, sm_l = [], [], []
+    for i, kr in enumerate(k_refs):
+        s_i = lax.dot_general(q, kr[...], NT_DIMS, preferred_element_type=jnp.float32)
+        s_i = s_i * (HD ** -0.5)
+        sc_i = jnp.where(kpos_ref[:, spans[i]] <= row_pos, s_i, NEG_FILL)
+        sm_i = jnp.where(kept_ref[:, spans[i]] > 0.0, sc_i, NEG_FILL)
+        s_l.append(s_i)
+        sc_l.append(sc_i)
+        sm_l.append(sm_i)
+    m_c = functools.reduce(jnp.maximum, [jnp.max(x, axis=1, keepdims=True) for x in sc_l])
+    m_m = functools.reduce(jnp.maximum, [jnp.max(x, axis=1, keepdims=True) for x in sm_l])
+    ec_l = [jnp.exp(x - m_c) for x in sc_l]
+    em_l = [jnp.exp(x - m_m) for x in sm_l]
+    l_c = functools.reduce(jnp.add, [jnp.sum(x, axis=1, keepdims=True) for x in ec_l])
+    l_m = functools.reduce(jnp.add, [jnp.sum(x, axis=1, keepdims=True) for x in em_l])
     o_c = None
     o_m = None
     for i, vr in enumerate(v_refs):
         v = vr[...]
-        pc = jnp.dot(eb_c[:, i * kc:(i + 1) * kc], v, preferred_element_type=jnp.float32)
-        pm = jnp.dot(eb_m[:, i * kc:(i + 1) * kc], v, preferred_element_type=jnp.float32)
+        pc = jnp.dot(ec_l[i].astype(jnp.bfloat16), v, preferred_element_type=jnp.float32)
+        pm = jnp.dot(em_l[i].astype(jnp.bfloat16), v, preferred_element_type=jnp.float32)
         o_c = pc if o_c is None else o_c + pc
         o_m = pm if o_m is None else o_m + pm
     o_c = o_c / l_c
@@ -54,14 +54,12 @@
     for h in range(hp):
         delta_ref[:, h * HD:(h + 1) * HD] = delta[h * tq:(h + 1) * tq]
     row_dot = jnp.sum(g_rows.astype(jnp.float32) * o_c, axis=1, keepdims=True)
-    d_p = jnp.concatenate(
-        [lax.dot_general(g_rows, vr[...], NT_DIMS, preferred_element_type=jnp.float32) for vr in v_refs],
-        axis=1,
-    )
     log_total = m_c + jnp.log(l_c)
-    prob = e_c * (1.0 / l_c)
-    contrib = prob * (d_p + (d_p - row_dot) * (s - log_total))
-    attr_ref[...] += jnp.sum(contrib, axis=0, keepdims=True)
+    inv = 1.0 / l_c
+    for i, vr in enumerate(v_refs):
+        d_p = lax.dot_general(g_rows, vr[...], NT_DIMS, preferred_element_type=jnp.float32)
+        contrib = (ec_l[i] * inv) * (d_p + (d_p - row_dot) * (s_l[i] - log_total))
+        attr_ref[:, spans[i]] += jnp.sum(contrib, axis=0, keepdims=True)
 
 
 def attention_kernel(base_ref, kpos_ref, q_ref, kept_ref, do_ref, *refs, tq, hp, n, split):

time: 103 us -> 102 us (level)
  no operation moved by 1% of the time
where the time goes in v18:
time: 102 us; the launch traced here: 101 us
  starting transfers between devices  36.8 us (36%)
  matrix products  23.5 us (23%)
  Pallas kernels  20.4 us (20%)
  waiting for transfers between devices  8.62 us (8%)
  other arithmetic  8 us (8%)
  local copies, waits for them, and re-layouts  2.94 us (3%)
    pallas_call x1, Pallas kernels, fused_attention(): pl.pallas_call(functools.partial(attention_kernel, tq=tq, hp=hp, n=n, spl...  20.4 us
    ppermute x4, starting transfers between devices, butterfly_sum(): total = total + lax.ppermute(total, axis, [(i, i ^ bit) for i in range(n)])  19.7 us
    dot_general x1, matrix products, local(): jnp.dot(grad_masked, out_weight.T, preferred_element_type=jnp.float32)  12.6 us
    ppermute x2, starting transfers between devices, relay_gather(): forward.append(lax.ppermute(payload, 'ctx', fwd) if fwd else zero)  11.3 us
    dot_general x1, matrix products, local(): send = jnp.dot(delta, send_w, preferred_element_type=jnp.float32)  4.82 us
    dot_general x1, matrix products, local(): jnp.dot(delta, keep_w, preferred_element_type=jnp.float32)  4.82 us
    ppermute x2, waiting for transfers between devices, relay_gather(): backward.append(lax.ppermute(payload, 'ctx', bwd) if bwd else zero)  4.72 us
    ppermute x4, waiting for transfers between devices, butterfly_sum(): total = total + lax.ppermute(total, axis, [(i, i ^ bit) for i in range(n)])  3.4 us
  transfers between devices with their start and end apart: 14, of which 4 were waited for; matrix products, arithmetic and copies ran while one was open for 26% of the time, Pallas kernels for 0%

profile of v18, /device:TPU:0, one launch (start us, length us, event | category | flops | bytes accessed | tf_op | source)
XLA Modules:
  0.0 101.1 jit_solution(4898672218374541715)
XLA Ops:
  0.6 0.0 copy-start.3
  0.6 0.7 convert_element_type.23
  1.4 1.1 %broadcast_select_fusion.3 = bf16[512,512]{1,0:T(8,128)(2,1)S(1)} fusion(bf16[512,512]{1,0:T(8,128)(2,1)} %param.11, bf16[512,512]{1,0:T(8,128)(2,1)} %param.12, pred[]{:T(512)S(6)} %eq.17), kind=kLoop, calls=%fused_computation.19 | loop fusion | flops 262144 | bytes 1572865 | tf_op jit(solution)/shard_map/jit(_where)/select_n | solution.py:176
  2.5 0.8 pad_maximum_fusion.refs_0_
  3.3 6.0 %collective-permute-start.3 = (bf16[528,512]{1,0:T(8,128)(2,1)}, bf16[528,512]{1,0:T(8,128)(2,1)S(1)}, u32[]{:S(2)}, u32[]{:S(2)}) collective-permute-start(bf16[528,512]{1,0:T(8,128)(2,1)} %pad_maximum_fusion.refs_0_), channel_id=1, source_target_pairs={{0,8},{4,12},{1,9},{5,13},{2,10},{6,14},{3,11},{7,15},{16,24},{20,... | collective-permute-start | bytes 1622024 | tf_op jit(solution)/shard_map/ppermute | solution.py:154
  9.3 1.3 %collective-permute-start.4 = (bf16[528,512]{1,0:T(8,128)(2,1)}, bf16[528,512]{1,0:T(8,128)(2,1)S(1)}, u32[]{:S(2)}, u32[]{:S(2)}) collective-permute-start(bf16[528,512]{1,0:T(8,128)(2,1)} %pad_maximum_fusion.refs_0_), channel_id=1, source_target_pairs={{8,0},{9,1},{10,2},{11,3},{24,16},{25,17},{26,18},{27,19}} | collective-permute-start | bytes 1622024 | tf_op jit(solution)/shard_map/ppermute | solution.py:160
  10.6 1.3 %collective-permute-start.7 = (bf16[528,512]{1,0:T(8,128)(2,1)}, bf16[528,512]{1,0:T(8,128)(2,1)S(1)}, u32[]{:S(2)}, u32[]{:S(2)}) collective-permute-start(bf16[528,512]{1,0:T(8,128)(2,1)} %pad_maximum_fusion.refs_0_), channel_id=1, source_target_pairs={{4,0},{8,4},{12,8},{5,1},{9,5},{13,9},{6,2},{10,6},{14,10},{7,3},{... | collective-permute-start | bytes 1622024 | tf_op jit(solution)/shard_map/ppermute | solution.py:160
  11.9 5.4 %collective-permute-start.1 = (bf16[528,512]{1,0:T(8,128)(2,1)}, bf16[528,512]{1,0:T(8,128)(2,1)}, u32[]{:S(2)}, u32[]{:S(2)}) collective-permute-start(bf16[528,512]{1,0:T(8,128)(2,1)} %pad_maximum_fusion.refs_0_), channel_id=1, source_target_pairs={{0,4},{4,8},{8,12},{1,5},{5,9},{9,13},{2,6},{6,10},{10,14},{3,7},{... | collective-permute-start | bytes 1622024 | tf_op jit(solution)/shard_map/ppermute | solution.py:154
  17.2 0.0 collective-permute-start
  17.2 0.7 broadcast_compare_fusion
  17.9 12.6 %convolution_convert_fusion.do_ref = bf16[128,2048]{1,0:T(8,128)(2,1)} fusion(bf16[2048,4096]{1,0:T(8,128)(2,1)} %param.13, bf16[128,4096]{1,0:T(8,128)(2,1)} %param.14, pred[128]{0:T(512)(128)(4,1)S(1)} %broadcast_compare_fusion), kind=kOutput, calls=%fused_computation.6 | convolution fusion | flops 2148270080 | bytes 18350208 | tf_op jit(solution)/shard_map/dot_general | solution.py:239
  30.5 0.1 add_bitcast_fusion
  30.6 0.0 collective-permute-done.3
  30.6 0.9 collective-permute-start.6
  31.5 0.6 copy.11
  32.1 0.0 collective-permute-done.4
  32.1 0.1 broadcast_select_fusion.1.refs_2_
  32.2 0.0 copy-start
  32.2 0.6 collective-permute-start.5
  32.7 0.0 collective-permute-done.1
  32.8 0.0 copy-start.2
  32.8 0.1 collective-permute-start.2
  32.9 4.7 %collective-permute-done.7 = bf16[528,512]{1,0:T(8,128)(2,1)S(1)} collective-permute-done((bf16[528,512]{1,0:T(8,128)(2,1)}, bf16[528,512]{1,0:T(8,128)(2,1)S(1)}, u32[]{:S(2)}, u32[]{:S(2)}) %collective-permute-start.7) | collective-permute-done | bytes 540704 | tf_op jit(solution)/shard_map/ppermute | solution.py:160
  37.6 0.0 collective-permute-done.6
  37.6 0.1 broadcast_select_fusion.refs_3_
  37.7 0.0 copy-start.1
  37.7 0.1 collective-permute-start.8
  37.8 0.6 pad_add_fusion.base_ref
  38.4 0.0 collective-permute-done.refs_4_
  38.4 0.7 fusion.16
  39.1 0.0 collective-permute-done.5.refs_6_
  39.1 0.0 copy-start.4
  39.2 0.0 collective-permute-done.2.refs_5_
  39.2 0.0 copy-start.5
  39.2 0.5 collective-permute-done.8.refs_7_
  39.7 0.0 copy-done.3
  39.7 0.1 compare_reduce_fusion
  39.8 0.6 broadcast_select_fusion.4
  40.5 0.0 copy-done.4
  40.5 0.0 copy-done.5
  40.5 0.0 copy-done
  40.5 0.0 copy-done.2
  40.5 0.0 copy-done.1
  40.5 0.0 copy-done.6
  40.5 20.4 %shard_map.103 = (bf16[128,2048]{1,0:T(8,128)(2,1)}, f32[1,2048]{1,0:T(1,128)}) custom-call(s32[2]{0:T(128)} %pad_add_fusion.base_ref, s32[1,2048]{1,0:T(1,128)} %bitcast.24, bf16[128,2048]{1,0:T(8,128)(2,1)} %q_ref.1, f32[1,2048]{1,0:T(1,128)} %bitcast.23, bf16[128,2048]{1,0:T(8,128)(2,1)} %convolution_convert_fusion.do_ref, ...), custom_call_target="tpu_custom_call" | custom-call | flops 4294967296 | bytes 5775360 | tf_op jit(solution)/shard_map/pallas_call | solution.py:117
  60.9 1.3 %convolution_bitcast_fusion = f32[32]{0:T(128)S(1)} fusion(s32[2048]{0:T(1024)S(1)} %maximum_convert_fusion, f32[1,2048]{1,0:T(1,128)} %get-tuple-element.18), kind=kOutput, calls=%fused_computation.7 | convolution fusion | flops 851968 | bytes 16512 | tf_op jit(solution)/shard_map/dot_general | solution.py:248
  62.1 0.5 broadcast.150
  62.7 1.4 %reduce.13 = f32[2048]{0:T(1024)S(1)} reduce(f32[1,2048]{1,0:T(1,128)} %get-tuple-element.18, f32[]{:T(128)} %broadcast.150), dimensions={0}, to_apply=%get-tuple-element.18.reduce_sub_computation.3 | reduce | bytes 16388 | tf_op jit(solution)/shard_map/pallas_call | solution.py:117
  64.1 0.6 gather_fusion
  64.6 0.3 collective-permute-start.10
  64.9 4.8 %fusion.4 = bf16[128,2048]{1,0:T(8,128)(2,1)S(1)} fusion(bf16[128,2048]{1,0:T(8,128)(2,1)} %get-tuple-element.17, bf16[2048,4096]{1,0:T(8,128)(2,1)} %param.13, s32[]{:T(128)S(6)} %select_n.122), kind=kOutput, calls=%fused_computation.5 | convolution fusion | flops 1074003968 | bytes 9437188 | tf_op jit(solution)/shard_map/dot_general | solution.py:256
  69.8 1.6 %collective-permute-start.9 = (bf16[128,2048]{1,0:T(8,128)(2,1)S(1)}, bf16[128,2048]{1,0:T(8,128)(2,1)S(1)}, u32[]{:S(2)}, u32[]{:S(2)}) collective-permute-start(bf16[128,2048]{1,0:T(8,128)(2,1)S(1)} %fusion.4), channel_id=1, source_target_pairs={{0,2},{2,0},{1,3},{3,1},{4,6},{6,4},{5,7},{7,5},{8,10},{10,8},{9,1... | collective-permute-start | bytes 1572872 | tf_op jit(solution)/shard_map/ppermute | solution.py:257
  71.3 0.0 collective-permute-done.10
  71.3 9.9 %collective-permute-start.11 = (f32[2080]{0:T(1024)S(1)}, f32[2080]{0:T(1024)S(1)}, u32[]{:S(2)}, u32[]{:S(2)}) collective-permute-start(f32[2080]{0:T(1024)S(1)} %fusion.24), channel_id=1, source_target_pairs={{0,4},{4,0},{8,12},{12,8},{1,5},{5,1},{9,13},{13,9},{2,6},{6,2},{1... | collective-permute-start | bytes 24968 | tf_op jit(solution)/shard_map/ppermute | solution.py:202
  81.3 1.7 %collective-permute-done.11 = f32[2080]{0:T(1024)S(1)} collective-permute-done((f32[2080]{0:T(1024)S(1)}, f32[2080]{0:T(1024)S(1)}, u32[]{:S(2)}, u32[]{:S(2)}) %collective-permute-start.11) | collective-permute-done | bytes 8352 | tf_op jit(solution)/shard_map/ppermute | solution.py:202
  83.0 9.0 %collective-permute-start.12 = (f32[2080]{0:T(1024)S(1)}, f32[2080]{0:T(1024)S(1)}, u32[]{:S(2)}, u32[]{:S(2)}) collective-permute-start(f32[2080]{0:T(1024)S(1)} %add.96), channel_id=1, source_target_pairs={{0,8},{4,12},{8,0},{12,4},{1,9},{5,13},{9,1},{13,5},{2,10},{6,14},... | collective-permute-start | bytes 24968 | tf_op jit(solution)/shard_map/ppermute | solution.py:202
  91.9 1.7 %collective-permute-done.12 = f32[2080]{0:T(1024)S(1)} collective-permute-done((f32[2080]{0:T(1024)S(1)}, f32[2080]{0:T(1024)S(1)}, u32[]{:S(2)}, u32[]{:S(2)}) %collective-permute-start.12) | collective-permute-done | bytes 8352 | tf_op jit(solution)/shard_map/ppermute | solution.py:202
  93.7 0.5 collective-permute-start.13
  94.2 4.8 %fusion.2 = f32[128,2048]{1,0:T(8,128)S(1)} fusion(bf16[128,2048]{1,0:T(8,128)(2,1)} %get-tuple-element.17, bf16[2048,4096]{1,0:T(8,128)(2,1)} %param.13, s32[]{:T(128)S(6)} %select_n.121), kind=kOutput, calls=%fused_computation.3 | convolution fusion | flops 1073741824 | bytes 9961476 | tf_op jit(solution)/shard_map/dot_general | solution.py:259
  99.0 0.0 collective-permute-done.13
  99.0 0.5 slice.59
  99.5 0.7 dynamic_slice.11
  100.2 0.0 collective-permute-done.9
  100.2 0.9 add_convert_fusion
  (19 shorter events, 0.2 us)
Async XLA Ops:
  0.6 39.1 %copy-start.3 = (s32[4]{0:T(128)S(1)}, s32[4]{0:T(128)}, u32[]{:S(2)}) copy-start(s32[4]{0:T(128)} %param.17) | copy-start | bytes 52
  3.3 27.3 %collective-permute-start.3 = (bf16[528,512]{1,0:T(8,128)(2,1)}, bf16[528,512]{1,0:T(8,128)(2,1)S(1)}, u32[]{:S(2)}, u32[]{:S(2)}) collective-permute-start(bf16[528,512]{1,0:T(8,128)(2,1)} %pad_maximum_fusion.refs_0_), channel_id=1, source_target_pairs={{0,8},{4,12},{1,9},{5,13},{2,10},{6,14},{3,11},{7,15},{16,24},{20,... | collective-permute-start | bytes 1622024 | tf_op jit(solution)/shard_map/ppermute | solution.py:154
  9.3 22.8 %collective-permute-start.4 = (bf16[528,512]{1,0:T(8,128)(2,1)}, bf16[528,512]{1,0:T(8,128)(2,1)S(1)}, u32[]{:S(2)}, u32[]{:S(2)}) collective-permute-start(bf16[528,512]{1,0:T(8,128)(2,1)} %pad_maximum_fusion.refs_0_), channel_id=1, source_target_pairs={{8,0},{9,1},{10,2},{11,3},{24,16},{25,17},{26,18},{27,19}} | collective-permute-start | bytes 1622024 | tf_op jit(solution)/shard_map/ppermute | solution.py:160
  10.6 27.0 %collective-permute-start.7 = (bf16[528,512]{1,0:T(8,128)(2,1)}, bf16[528,512]{1,0:T(8,128)(2,1)S(1)}, u32[]{:S(2)}, u32[]{:S(2)}) collective-permute-start(bf16[528,512]{1,0:T(8,128)(2,1)} %pad_maximum_fusion.refs_0_), channel_id=1, source_target_pairs={{4,0},{8,4},{12,8},{5,1},{9,5},{13,9},{6,2},{10,6},{14,10},{7,3},{... | collective-permute-start | bytes 1622024 | tf_op jit(solution)/shard_map/ppermute | solution.py:160
  11.9 20.9 %collective-permute-start.1 = (bf16[528,512]{1,0:T(8,128)(2,1)}, bf16[528,512]{1,0:T(8,128)(2,1)}, u32[]{:S(2)}, u32[]{:S(2)}) collective-permute-start(bf16[528,512]{1,0:T(8,128)(2,1)} %pad_maximum_fusion.refs_0_), channel_id=1, source_target_pairs={{0,4},{4,8},{8,12},{1,5},{5,9},{9,13},{2,6},{6,10},{10,14},{3,7},{... | collective-permute-start | bytes 1622024 | tf_op jit(solution)/shard_map/ppermute | solution.py:154
  17.2 21.2 %collective-permute-start = (bf16[528,512]{1,0:T(8,128)(2,1)}, bf16[528,512]{1,0:T(8,128)(2,1)}, u32[]{:S(2)}, u32[]{:S(2)}) collective-permute-start(bf16[528,512]{1,0:T(8,128)(2,1)} %pad_maximum_fusion.refs_0_), channel_id=1, source_target_pairs={{0,1},{1,0},{2,3},{3,2},{4,5},{5,4},{6,7},{7,6},{8,9},{9,8},{10,11... | collective-permute-start | bytes 1622024 | tf_op jit(solution)/shard_map/ppermute | solution.py:181
  30.6 7.0 %collective-permute-start.6 = (bf16[528,512]{1,0:T(8,128)(2,1)S(1)}, bf16[528,512]{1,0:T(8,128)(2,1)S(1)}, u32[]{:S(2)}, u32[]{:S(2)}) collective-permute-start(bf16[528,512]{1,0:T(8,128)(2,1)S(1)} %collective-permute-done.3), channel_id=1, source_target_pairs={{8,12},{9,13},{10,14},{11,15},{24,28},{25,29},{26,30},{27,31}} | collective-permute-start | bytes 1622024 | tf_op jit(solution)/shard_map/ppermute | solution.py:152
  32.2 8.3 %copy-start = (bf16[528,512]{1,0:T(8,128)(2,1)}, bf16[528,512]{1,0:T(8,128)(2,1)S(1)}, u32[]{:S(2)}) copy-start(bf16[528,512]{1,0:T(8,128)(2,1)S(1)} %broadcast_select_fusion.1.refs_2_) | copy-start | bytes 1622020
  32.2 7.0 %collective-permute-start.5 = (bf16[528,512]{1,0:T(8,128)(2,1)S(1)}, bf16[528,512]{1,0:T(8,128)(2,1)S(1)}, u32[]{:S(2)}, u32[]{:S(2)}) collective-permute-start(bf16[528,512]{1,0:T(8,128)(2,1)S(1)} %broadcast_select_fusion.1.refs_2_), channel_id=1, source_target_pairs={{0,1},{1,0},{2,3},{3,2},{4,5},{5,4},{6,7},{7,6},{8,9},{9,8},{10,11... | collective-permute-start | bytes 1622024 | tf_op jit(solution)/shard_map/ppermute | solution.py:181
  32.8 7.7 %copy-start.2 = (bf16[528,512]{1,0:T(8,128)(2,1)}, bf16[528,512]{1,0:T(8,128)(2,1)S(1)}, u32[]{:S(2)}) copy-start(bf16[528,512]{1,0:T(8,128)(2,1)S(1)} %broadcast_select_fusion.2.refs_1_) | copy-start | bytes 1622020
  32.8 6.4 %collective-permute-start.2 = (bf16[528,512]{1,0:T(8,128)(2,1)S(1)}, bf16[528,512]{1,0:T(8,128)(2,1)S(1)}, u32[]{:S(2)}, u32[]{:S(2)}) collective-permute-start(bf16[528,512]{1,0:T(8,128)(2,1)S(1)} %broadcast_select_fusion.2.refs_1_), channel_id=1, source_target_pairs={{0,1},{1,0},{2,3},{3,2},{4,5},{5,4},{6,7},{7,6},{8,9},{9,8},{10,11... | collective-permute-start | bytes 1622024 | tf_op jit(solution)/shard_map/ppermute | solution.py:181
  37.7 2.8 %copy-start.1 = (bf16[528,512]{1,0:T(8,128)(2,1)}, bf16[528,512]{1,0:T(8,128)(2,1)S(1)}, u32[]{:S(2)}) copy-start(bf16[528,512]{1,0:T(8,128)(2,1)S(1)} %broadcast_select_fusion.refs_3_) | copy-start | bytes 1622020
  37.7 2.0 %collective-permute-start.8 = (bf16[528,512]{1,0:T(8,128)(2,1)S(1)}, bf16[528,512]{1,0:T(8,128)(2,1)S(1)}, u32[]{:S(2)}, u32[]{:S(2)}) collective-permute-start(bf16[528,512]{1,0:T(8,128)(2,1)S(1)} %broadcast_select_fusion.refs_3_), channel_id=1, source_target_pairs={{0,1},{1,0},{2,3},{3,2},{4,5},{5,4},{6,7},{7,6},{8,9},{9,8},{10,11... | collective-permute-start | bytes 1622024 | tf_op jit(solution)/shard_map/ppermute | solution.py:181
  39.1 1.3 %copy-start.4 = (bf16[528,512]{1,0:T(8,128)(2,1)}, bf16[528,512]{1,0:T(8,128)(2,1)S(1)}, u32[]{:S(2)}) copy-start(bf16[528,512]{1,0:T(8,128)(2,1)S(1)} %collective-permute-done.5.refs_6_) | copy-start | bytes 1622020
  39.2 1.3 %copy-start.5 = (bf16[528,512]{1,0:T(8,128)(2,1)}, bf16[528,512]{1,0:T(8,128)(2,1)S(1)}, u32[]{:S(2)}) copy-start(bf16[528,512]{1,0:T(8,128)(2,1)S(1)} %collective-permute-done.2.refs_5_) | copy-start | bytes 1622020
  39.7 0.8 copy-start.6
  64.6 6.7 %collective-permute-start.10 = (f32[2080]{0:T(1024)S(1)}, f32[2080]{0:T(1024)S(1)}, u32[]{:S(2)}, u32[]{:S(2)}) collective-permute-start(f32[2080]{0:T(1024)S(1)} %pad_maximum_fusion.1), channel_id=1, source_target_pairs={{0,1},{1,0},{2,3},{3,2},{4,5},{5,4},{6,7},{7,6},{8,9},{9,8},{10,11... | collective-permute-start | bytes 24968 | tf_op jit(solution)/shard_map/ppermute | solution.py:202
  69.8 30.4 %collective-permute-start.9 = (bf16[128,2048]{1,0:T(8,128)(2,1)S(1)}, bf16[128,2048]{1,0:T(8,128)(2,1)S(1)}, u32[]{:S(2)}, u32[]{:S(2)}) collective-permute-start(bf16[128,2048]{1,0:T(8,128)(2,1)S(1)} %fusion.4), channel_id=1, source_target_pairs={{0,2},{2,0},{1,3},{3,1},{4,6},{6,4},{5,7},{7,5},{8,10},{10,8},{9,1... | collective-permute-start | bytes 1572872 | tf_op jit(solution)/shard_map/ppermute | solution.py:257
  71.3 11.6 %collective-permute-start.11 = (f32[2080]{0:T(1024)S(1)}, f32[2080]{0:T(1024)S(1)}, u32[]{:S(2)}, u32[]{:S(2)}) collective-permute-start(f32[2080]{0:T(1024)S(1)} %fusion.24), channel_id=1, source_target_pairs={{0,4},{4,0},{8,12},{12,8},{1,5},{5,1},{9,13},{13,9},{2,6},{6,2},{1... | collective-permute-start | bytes 24968 | tf_op jit(solution)/shard_map/ppermute | solution.py:202
  83.0 10.7 %collective-permute-start.12 = (f32[2080]{0:T(1024)S(1)}, f32[2080]{0:T(1024)S(1)}, u32[]{:S(2)}, u32[]{:S(2)}) collective-permute-start(f32[2080]{0:T(1024)S(1)} %add.96), channel_id=1, source_target_pairs={{0,8},{4,12},{8,0},{12,4},{1,9},{5,13},{9,1},{13,5},{2,10},{6,14},... | collective-permute-start | bytes 24968 | tf_op jit(solution)/shard_map/ppermute | solution.py:202
  93.7 5.3 %collective-permute-start.13 = (f32[2080]{0:T(1024)S(1)}, f32[2080]{0:T(1024)S(1)}, u32[]{:S(2)}, u32[]{:S(2)}) collective-permute-start(f32[2080]{0:T(1024)S(1)} %add.97), channel_id=1, source_target_pairs={{0,2},{2,0},{1,3},{3,1},{4,6},{6,4},{5,7},{7,5},{8,10},{10,8},{9,1... | collective-permute-start | bytes 24968 | tf_op jit(solution)/shard_map/ppermute | solution.py:202

commit v19 on v18

--- a/solution.py
+++ b/solution.py
@@ -59,7 +59,7 @@
     for i, vr in enumerate(v_refs):
         d_p = lax.dot_general(g_rows, vr[...], NT_DIMS, preferred_element_type=jnp.float32)
         contrib = (ec_l[i] * inv) * (d_p + (d_p - row_dot) * (s_l[i] - log_total))
-        attr_ref[:, spans[i]] += jnp.sum(contrib, axis=0, keepdims=True)
+        attr_ref[spans[i]] += jnp.sum(contrib, axis=0)
 
 
 def attention_kernel(base_ref, kpos_ref, q_ref, kept_ref, do_ref, *refs, tq, hp, n, split):
@@ -127,12 +127,12 @@
             ] + [part_spec] * (2 * n),
             out_specs=[
                 pl.BlockSpec((tq, hp * HD), head_map),
-                pl.BlockSpec((1, keys), fixed),
+                pl.BlockSpec((keys,), lambda g, j, r, b: (0,)),
             ],
         ),
         out_shape=[
             jax.ShapeDtypeStruct((qc, width), jnp.bfloat16),
-            jax.ShapeDtypeStruct((1, keys), jnp.float32),
+            jax.ShapeDtypeStruct((keys,), jnp.float32),
         ],
         compiler_params=pltpu.CompilerParams(
             dimension_semantics=("arbitrary", "arbitrary", "arbitrary")
@@ -245,7 +245,7 @@
 
     inverse = (ctx_at - jnp.arange(ctx_count, dtype=jnp.int32)) % ctx_count
     attr_abs = attr.reshape(ctx_count, key_count)[inverse].reshape(-1)
-    seg_part = jnp.dot(attr[0], onehot, precision=lax.Precision.HIGHEST)
+    seg_part = jnp.dot(attr, onehot, precision=lax.Precision.HIGHEST)
     summed = butterfly_sum(jnp.concatenate([attr_abs, seg_part]), ("rep", "ctx", "head"))
     attr_all = summed[:context_len]
     segment_attr = summed[context_len:]

time: 102 us -> 100 us (0.980)
  other arithmetic: 8 us -> 6.58 us
    pallas_call x1 -> x0, other arithmetic: 1.36 us -> none  [fused_attention(): pl.pallas_call(functools.partial(attention_kernel, tq=tq, hp=hp, n=n, spl...]
where the time goes in v19:
time: 100 us; the launch traced here: 99.9 us
  starting transfers between devices  36.8 us (37%)
  matrix products  23.5 us (24%)
  Pallas kernels  20.3 us (20%)
  waiting for transfers between devices  8.64 us (9%)
  other arithmetic  6.58 us (7%)
  local copies, waits for them, and re-layouts  3.13 us (3%)
    pallas_call x1, Pallas kernels, fused_attention(): pl.pallas_call(functools.partial(attention_kernel, tq=tq, hp=hp, n=n, spl...  20.3 us
    ppermute x4, starting transfers between devices, butterfly_sum(): total = total + lax.ppermute(total, axis, [(i, i ^ bit) for i in range(n)])  19.7 us
    dot_general x1, matrix products, local(): jnp.dot(grad_masked, out_weight.T, preferred_element_type=jnp.float32)  12.6 us
    ppermute x2, starting transfers between devices, relay_gather(): forward.append(lax.ppermute(payload, 'ctx', fwd) if fwd else zero)  11.3 us
    dot_general x1, matrix products, local(): send = jnp.dot(delta, send_w, preferred_element_type=jnp.float32)  4.82 us
    dot_general x1, matrix products, local(): jnp.dot(delta, keep_w, preferred_element_type=jnp.float32)  4.82 us
    ppermute x2, waiting for transfers between devices, relay_gather(): backward.append(lax.ppermute(payload, 'ctx', bwd) if bwd else zero)  4.72 us
    ppermute x4, waiting for transfers between devices, butterfly_sum(): total = total + lax.ppermute(total, axis, [(i, i ^ bit) for i in range(n)])  3.39 us
  transfers between devices with their start and end apart: 14, of which 4 were waited for; matrix products, arithmetic and copies ran while one was open for 26% of the time, Pallas kernels for 0%

profile of v19, /device:TPU:0, one launch (start us, length us, event | category | flops | bytes accessed | tf_op | source)
XLA Modules:
  0.0 99.9 jit_solution(11902096259078786329)
XLA Ops:
  0.6 0.0 copy-start.3
  0.6 0.7 convert_element_type.23
  1.4 1.1 %broadcast_select_fusion.3 = bf16[512,512]{1,0:T(8,128)(2,1)S(1)} fusion(bf16[512,512]{1,0:T(8,128)(2,1)} %param.11, bf16[512,512]{1,0:T(8,128)(2,1)} %param.12, pred[]{:T(512)S(6)} %eq.17), kind=kLoop, calls=%fused_computation.19 | loop fusion | flops 262144 | bytes 1572865 | tf_op jit(solution)/shard_map/jit(_where)/select_n | solution.py:176
  2.5 0.8 pad_maximum_fusion.refs_0_
  3.3 6.0 %collective-permute-start.3 = (bf16[528,512]{1,0:T(8,128)(2,1)}, bf16[528,512]{1,0:T(8,128)(2,1)S(1)}, u32[]{:S(2)}, u32[]{:S(2)}) collective-permute-start(bf16[528,512]{1,0:T(8,128)(2,1)} %pad_maximum_fusion.refs_0_), channel_id=1, source_target_pairs={{0,8},{4,12},{1,9},{5,13},{2,10},{6,14},{3,11},{7,15},{16,24},{20,... | collective-permute-start | bytes 1622024 | tf_op jit(solution)/shard_map/ppermute | solution.py:154
  9.3 1.3 %collective-permute-start.4 = (bf16[528,512]{1,0:T(8,128)(2,1)}, bf16[528,512]{1,0:T(8,128)(2,1)S(1)}, u32[]{:S(2)}, u32[]{:S(2)}) collective-permute-start(bf16[528,512]{1,0:T(8,128)(2,1)} %pad_maximum_fusion.refs_0_), channel_id=1, source_target_pairs={{8,0},{9,1},{10,2},{11,3},{24,16},{25,17},{26,18},{27,19}} | collective-permute-start | bytes 1622024 | tf_op jit(solution)/shard_map/ppermute | solution.py:160
  10.6 1.3 %collective-permute-start.7 = (bf16[528,512]{1,0:T(8,128)(2,1)}, bf16[528,512]{1,0:T(8,128)(2,1)S(1)}, u32[]{:S(2)}, u32[]{:S(2)}) collective-permute-start(bf16[528,512]{1,0:T(8,128)(2,1)} %pad_maximum_fusion.refs_0_), channel_id=1, source_target_pairs={{4,0},{8,4},{12,8},{5,1},{9,5},{13,9},{6,2},{10,6},{14,10},{7,3},{... | collective-permute-start | bytes 1622024 | tf_op jit(solution)/shard_map/ppermute | solution.py:160
  11.9 5.4 %collective-permute-start.1 = (bf16[528,512]{1,0:T(8,128)(2,1)}, bf16[528,512]{1,0:T(8,128)(2,1)}, u32[]{:S(2)}, u32[]{:S(2)}) collective-permute-start(bf16[528,512]{1,0:T(8,128)(2,1)} %pad_maximum_fusion.refs_0_), channel_id=1, source_target_pairs={{0,4},{4,8},{8,12},{1,5},{5,9},{9,13},{2,6},{6,10},{10,14},{3,7},{... | collective-permute-start | bytes 1622024 | tf_op jit(solution)/shard_map/ppermute | solution.py:154
  17.3 0.0 collective-permute-start
  17.3 0.7 broadcast_compare_fusion
  17.9 12.6 %convolution_convert_fusion.do_ref = bf16[128,2048]{1,0:T(8,128)(2,1)} fusion(bf16[2048,4096]{1,0:T(8,128)(2,1)} %param.13, bf16[128,4096]{1,0:T(8,128)(2,1)} %param.14, pred[128]{0:T(512)(128)(4,1)S(1)} %broadcast_compare_fusion), kind=kOutput, calls=%fused_computation.6 | convolution fusion | flops 2148270080 | bytes 18350208 | tf_op jit(solution)/shard_map/dot_general | solution.py:239
  30.5 0.1 add_bitcast_fusion
  30.6 0.0 collective-permute-done.3
  30.6 0.9 collective-permute-start.6
  31.5 0.6 copy.11
  32.1 0.0 collective-permute-done.4
  32.1 0.1 broadcast_select_fusion.1.refs_2_
  32.2 0.0 copy-start
  32.2 0.6 collective-permute-start.5
  32.7 0.0 collective-permute-done.1
  32.8 0.0 copy-start.2
  32.8 0.1 collective-permute-start.2
  32.9 4.7 %collective-permute-done.7 = bf16[528,512]{1,0:T(8,128)(2,1)S(1)} collective-permute-done((bf16[528,512]{1,0:T(8,128)(2,1)}, bf16[528,512]{1,0:T(8,128)(2,1)S(1)}, u32[]{:S(2)}, u32[]{:S(2)}) %collective-permute-start.7) | collective-permute-done | bytes 540704 | tf_op jit(solution)/shard_map/ppermute | solution.py:160
  37.6 0.0 collective-permute-done.6
  37.6 0.1 broadcast_select_fusion.refs_3_
  37.7 0.0 copy-start.1
  37.7 0.1 collective-permute-start.8
  37.8 0.6 pad_add_fusion.base_ref
  38.4 0.0 collective-permute-done.refs_4_
  38.4 0.7 fusion.15
  39.1 0.0 collective-permute-done.5.refs_6_
  39.1 0.0 copy-start.4
  39.1 0.0 collective-permute-done.2.refs_5_
  39.2 0.0 copy-start.5
  39.2 0.5 collective-permute-done.8.refs_7_
  39.7 0.0 copy-start.6
  39.7 0.0 copy-done.3
  39.7 0.1 compare_reduce_fusion
  39.9 0.6 broadcast_select_fusion.4
  40.5 0.0 copy-done.4
  40.5 0.0 copy-done.5
  40.5 0.0 copy-done
  40.5 0.0 copy-done.2
  40.5 0.0 copy-done.1
  40.5 0.0 copy-done.6
  40.5 20.3 %shard_map.103 = (bf16[128,2048]{1,0:T(8,128)(2,1)}, f32[2048]{0:T(1024)}) custom-call(s32[2]{0:T(128)} %pad_add_fusion.base_ref, s32[1,2048]{1,0:T(1,128)} %bitcast.22, bf16[128,2048]{1,0:T(8,128)(2,1)} %q_ref.1, f32[1,2048]{1,0:T(1,128)} %bitcast.21, bf16[128,2048]{1,0:T(8,128)(2,1)} %convolution_convert_fusion.do_ref, ...), custom_call_target="tpu_custom_call" | custom-call | flops 4294967296 | bytes 5775360 | tf_op jit(solution)/shard_map/pallas_call | solution.py:117
  60.8 0.7 reshape.168
  61.6 1.3 %convolution_bitcast_fusion = f32[32]{0:T(128)S(1)} fusion(f32[2048,1]{0,1:T(1,128)} %bitcast.23, s32[2048]{0:T(1024)S(1)} %maximum_convert_fusion), kind=kOutput, calls=%fused_computation.7 | convolution fusion | flops 851968 | bytes 16512 | tf_op jit(solution)/shard_map/dot_general | solution.py:248
  62.8 0.6 gather_fusion
  63.4 0.3 collective-permute-start.10
  63.7 4.8 %fusion.4 = bf16[128,2048]{1,0:T(8,128)(2,1)S(1)} fusion(bf16[128,2048]{1,0:T(8,128)(2,1)} %get-tuple-element.17, bf16[2048,4096]{1,0:T(8,128)(2,1)} %param.13, s32[]{:T(128)S(6)} %select_n.122), kind=kOutput, calls=%fused_computation.5 | convolution fusion | flops 1074003968 | bytes 9437188 | tf_op jit(solution)/shard_map/dot_general | solution.py:256
  68.6 1.6 %collective-permute-start.9 = (bf16[128,2048]{1,0:T(8,128)(2,1)S(1)}, bf16[128,2048]{1,0:T(8,128)(2,1)S(1)}, u32[]{:S(2)}, u32[]{:S(2)}) collective-permute-start(bf16[128,2048]{1,0:T(8,128)(2,1)S(1)} %fusion.4), channel_id=1, source_target_pairs={{0,2},{2,0},{1,3},{3,1},{4,6},{6,4},{5,7},{7,5},{8,10},{10,8},{9,1... | collective-permute-start | bytes 1572872 | tf_op jit(solution)/shard_map/ppermute | solution.py:257
  70.1 0.0 collective-permute-done.10
  70.1 9.9 %collective-permute-start.11 = (f32[2080]{0:T(1024)S(1)}, f32[2080]{0:T(1024)S(1)}, u32[]{:S(2)}, u32[]{:S(2)}) collective-permute-start(f32[2080]{0:T(1024)S(1)} %fusion.23), channel_id=1, source_target_pairs={{0,4},{4,0},{8,12},{12,8},{1,5},{5,1},{9,13},{13,9},{2,6},{6,2},{1... | collective-permute-start | bytes 24968 | tf_op jit(solution)/shard_map/ppermute | solution.py:202
  80.1 1.7 %collective-permute-done.11 = f32[2080]{0:T(1024)S(1)} collective-permute-done((f32[2080]{0:T(1024)S(1)}, f32[2080]{0:T(1024)S(1)}, u32[]{:S(2)}, u32[]{:S(2)}) %collective-permute-start.11) | collective-permute-done | bytes 8352 | tf_op jit(solution)/shard_map/ppermute | solution.py:202
  81.7 9.0 %collective-permute-start.12 = (f32[2080]{0:T(1024)S(1)}, f32[2080]{0:T(1024)S(1)}, u32[]{:S(2)}, u32[]{:S(2)}) collective-permute-start(f32[2080]{0:T(1024)S(1)} %add.96), channel_id=1, source_target_pairs={{0,8},{4,12},{8,0},{12,4},{1,9},{5,13},{9,1},{13,5},{2,10},{6,14},... | collective-permute-start | bytes 24968 | tf_op jit(solution)/shard_map/ppermute | solution.py:202
  90.7 1.7 %collective-permute-done.12 = f32[2080]{0:T(1024)S(1)} collective-permute-done((f32[2080]{0:T(1024)S(1)}, f32[2080]{0:T(1024)S(1)}, u32[]{:S(2)}, u32[]{:S(2)}) %collective-permute-start.12) | collective-permute-done | bytes 8352 | tf_op jit(solution)/shard_map/ppermute | solution.py:202
  92.5 0.5 collective-permute-start.13
  93.0 4.8 %fusion.2 = f32[128,2048]{1,0:T(8,128)S(1)} fusion(bf16[128,2048]{1,0:T(8,128)(2,1)} %get-tuple-element.17, bf16[2048,4096]{1,0:T(8,128)(2,1)} %param.13, s32[]{:T(128)S(6)} %select_n.121), kind=kOutput, calls=%fused_computation.3 | convolution fusion | flops 1073741824 | bytes 9961476 | tf_op jit(solution)/shard_map/dot_general | solution.py:259
  97.8 0.0 collective-permute-done.13
  97.8 0.5 slice.59
  98.3 0.7 dynamic_slice.11
  99.0 0.0 collective-permute-done.9
  99.0 0.9 add_convert_fusion
  (17 shorter events, 0.2 us)
Async XLA Ops:
  0.6 39.1 %copy-start.3 = (s32[4]{0:T(128)S(1)}, s32[4]{0:T(128)}, u32[]{:S(2)}) copy-start(s32[4]{0:T(128)} %param.17) | copy-start | bytes 52
  3.3 27.3 %collective-permute-start.3 = (bf16[528,512]{1,0:T(8,128)(2,1)}, bf16[528,512]{1,0:T(8,128)(2,1)S(1)}, u32[]{:S(2)}, u32[]{:S(2)}) collective-permute-start(bf16[528,512]{1,0:T(8,128)(2,1)} %pad_maximum_fusion.refs_0_), channel_id=1, source_target_pairs={{0,8},{4,12},{1,9},{5,13},{2,10},{6,14},{3,11},{7,15},{16,24},{20,... | collective-permute-start | bytes 1622024 | tf_op jit(solution)/shard_map/ppermute | solution.py:154
  9.3 22.8 %collective-permute-start.4 = (bf16[528,512]{1,0:T(8,128)(2,1)}, bf16[528,512]{1,0:T(8,128)(2,1)S(1)}, u32[]{:S(2)}, u32[]{:S(2)}) collective-permute-start(bf16[528,512]{1,0:T(8,128)(2,1)} %pad_maximum_fusion.refs_0_), channel_id=1, source_target_pairs={{8,0},{9,1},{10,2},{11,3},{24,16},{25,17},{26,18},{27,19}} | collective-permute-start | bytes 1622024 | tf_op jit(solution)/shard_map/ppermute | solution.py:160
  10.6 27.0 %collective-permute-start.7 = (bf16[528,512]{1,0:T(8,128)(2,1)}, bf16[528,512]{1,0:T(8,128)(2,1)S(1)}, u32[]{:S(2)}, u32[]{:S(2)}) collective-permute-start(bf16[528,512]{1,0:T(8,128)(2,1)} %pad_maximum_fusion.refs_0_), channel_id=1, source_target_pairs={{4,0},{8,4},{12,8},{5,1},{9,5},{13,9},{6,2},{10,6},{14,10},{7,3},{... | collective-permute-start | bytes 1622024 | tf_op jit(solution)/shard_map/ppermute | solution.py:160
  11.9 20.9 %collective-permute-start.1 = (bf16[528,512]{1,0:T(8,128)(2,1)}, bf16[528,512]{1,0:T(8,128)(2,1)}, u32[]{:S(2)}, u32[]{:S(2)}) collective-permute-start(bf16[528,512]{1,0:T(8,128)(2,1)} %pad_maximum_fusion.refs_0_), channel_id=1, source_target_pairs={{0,4},{4,8},{8,12},{1,5},{5,9},{9,13},{2,6},{6,10},{10,14},{3,7},{... | collective-permute-start | bytes 1622024 | tf_op jit(solution)/shard_map/ppermute | solution.py:154
  17.3 21.1 %collective-permute-start = (bf16[528,512]{1,0:T(8,128)(2,1)}, bf16[528,512]{1,0:T(8,128)(2,1)}, u32[]{:S(2)}, u32[]{:S(2)}) collective-permute-start(bf16[528,512]{1,0:T(8,128)(2,1)} %pad_maximum_fusion.refs_0_), channel_id=1, source_target_pairs={{0,1},{1,0},{2,3},{3,2},{4,5},{5,4},{6,7},{7,6},{8,9},{9,8},{10,11... | collective-permute-start | bytes 1622024 | tf_op jit(solution)/shard_map/ppermute | solution.py:181
  30.6 7.0 %collective-permute-start.6 = (bf16[528,512]{1,0:T(8,128)(2,1)S(1)}, bf16[528,512]{1,0:T(8,128)(2,1)S(1)}, u32[]{:S(2)}, u32[]{:S(2)}) collective-permute-start(bf16[528,512]{1,0:T(8,128)(2,1)S(1)} %collective-permute-done.3), channel_id=1, source_target_pairs={{8,12},{9,13},{10,14},{11,15},{24,28},{25,29},{26,30},{27,31}} | collective-permute-start | bytes 1622024 | tf_op jit(solution)/shard_map/ppermute | solution.py:152
  32.2 8.3 %copy-start = (bf16[528,512]{1,0:T(8,128)(2,1)}, bf16[528,512]{1,0:T(8,128)(2,1)S(1)}, u32[]{:S(2)}) copy-start(bf16[528,512]{1,0:T(8,128)(2,1)S(1)} %broadcast_select_fusion.1.refs_2_) | copy-start | bytes 1622020
  32.2 6.9 %collective-permute-start.5 = (bf16[528,512]{1,0:T(8,128)(2,1)S(1)}, bf16[528,512]{1,0:T(8,128)(2,1)S(1)}, u32[]{:S(2)}, u32[]{:S(2)}) collective-permute-start(bf16[528,512]{1,0:T(8,128)(2,1)S(1)} %broadcast_select_fusion.1.refs_2_), channel_id=1, source_target_pairs={{0,1},{1,0},{2,3},{3,2},{4,5},{5,4},{6,7},{7,6},{8,9},{9,8},{10,11... | collective-permute-start | bytes 1622024 | tf_op jit(solution)/shard_map/ppermute | solution.py:181
  32.8 7.7 %copy-start.2 = (bf16[528,512]{1,0:T(8,128)(2,1)}, bf16[528,512]{1,0:T(8,128)(2,1)S(1)}, u32[]{:S(2)}) copy-start(bf16[528,512]{1,0:T(8,128)(2,1)S(1)} %broadcast_select_fusion.2.refs_1_) | copy-start | bytes 1622020
  32.8 6.3 %collective-permute-start.2 = (bf16[528,512]{1,0:T(8,128)(2,1)S(1)}, bf16[528,512]{1,0:T(8,128)(2,1)S(1)}, u32[]{:S(2)}, u32[]{:S(2)}) collective-permute-start(bf16[528,512]{1,0:T(8,128)(2,1)S(1)} %broadcast_select_fusion.2.refs_1_), channel_id=1, source_target_pairs={{0,1},{1,0},{2,3},{3,2},{4,5},{5,4},{6,7},{7,6},{8,9},{9,8},{10,11... | collective-permute-start | bytes 1622024 | tf_op jit(solution)/shard_map/ppermute | solution.py:181
  37.7 2.8 %copy-start.1 = (bf16[528,512]{1,0:T(8,128)(2,1)}, bf16[528,512]{1,0:T(8,128)(2,1)S(1)}, u32[]{:S(2)}) copy-start(bf16[528,512]{1,0:T(8,128)(2,1)S(1)} %broadcast_select_fusion.refs_3_) | copy-start | bytes 1622020
  37.7 2.0 %collective-permute-start.8 = (bf16[528,512]{1,0:T(8,128)(2,1)S(1)}, bf16[528,512]{1,0:T(8,128)(2,1)S(1)}, u32[]{:S(2)}, u32[]{:S(2)}) collective-permute-start(bf16[528,512]{1,0:T(8,128)(2,1)S(1)} %broadcast_select_fusion.refs_3_), channel_id=1, source_target_pairs={{0,1},{1,0},{2,3},{3,2},{4,5},{5,4},{6,7},{7,6},{8,9},{9,8},{10,11... | collective-permute-start | bytes 1622024 | tf_op jit(solution)/shard_map/ppermute | solution.py:181
  39.1 1.4 %copy-start.4 = (bf16[528,512]{1,0:T(8,128)(2,1)}, bf16[528,512]{1,0:T(8,128)(2,1)S(1)}, u32[]{:S(2)}) copy-start(bf16[528,512]{1,0:T(8,128)(2,1)S(1)} %collective-permute-done.5.refs_6_) | copy-start | bytes 1622020
  39.2 1.3 %copy-start.5 = (bf16[528,512]{1,0:T(8,128)(2,1)}, bf16[528,512]{1,0:T(8,128)(2,1)S(1)}, u32[]{:S(2)}) copy-start(bf16[528,512]{1,0:T(8,128)(2,1)S(1)} %collective-permute-done.2.refs_5_) | copy-start | bytes 1622020
  39.7 0.8 copy-start.6
  63.4 6.7 %collective-permute-start.10 = (f32[2080]{0:T(1024)S(1)}, f32[2080]{0:T(1024)S(1)}, u32[]{:S(2)}, u32[]{:S(2)}) collective-permute-start(f32[2080]{0:T(1024)S(1)} %pad_maximum_fusion.1), channel_id=1, source_target_pairs={{0,1},{1,0},{2,3},{3,2},{4,5},{5,4},{6,7},{7,6},{8,9},{9,8},{10,11... | collective-permute-start | bytes 24968 | tf_op jit(solution)/shard_map/ppermute | solution.py:202
  68.6 30.4 %collective-permute-start.9 = (bf16[128,2048]{1,0:T(8,128)(2,1)S(1)}, bf16[128,2048]{1,0:T(8,128)(2,1)S(1)}, u32[]{:S(2)}, u32[]{:S(2)}) collective-permute-start(bf16[128,2048]{1,0:T(8,128)(2,1)S(1)} %fusion.4), channel_id=1, source_target_pairs={{0,2},{2,0},{1,3},{3,1},{4,6},{6,4},{5,7},{7,5},{8,10},{10,8},{9,1... | collective-permute-start | bytes 1572872 | tf_op jit(solution)/shard_map/ppermute | solution.py:257
  70.1 11.6 %collective-permute-start.11 = (f32[2080]{0:T(1024)S(1)}, f32[2080]{0:T(1024)S(1)}, u32[]{:S(2)}, u32[]{:S(2)}) collective-permute-start(f32[2080]{0:T(1024)S(1)} %fusion.23), channel_id=1, source_target_pairs={{0,4},{4,0},{8,12},{12,8},{1,5},{5,1},{9,13},{13,9},{2,6},{6,2},{1... | collective-permute-start | bytes 24968 | tf_op jit(solution)/shard_map/ppermute | solution.py:202
  81.7 10.7 %collective-permute-start.12 = (f32[2080]{0:T(1024)S(1)}, f32[2080]{0:T(1024)S(1)}, u32[]{:S(2)}, u32[]{:S(2)}) collective-permute-start(f32[2080]{0:T(1024)S(1)} %add.96), channel_id=1, source_target_pairs={{0,8},{4,12},{8,0},{12,4},{1,9},{5,13},{9,1},{13,5},{2,10},{6,14},... | collective-permute-start | bytes 24968 | tf_op jit(solution)/shard_map/ppermute | solution.py:202
  92.5 5.3 %collective-permute-start.13 = (f32[2080]{0:T(1024)S(1)}, f32[2080]{0:T(1024)S(1)}, u32[]{:S(2)}, u32[]{:S(2)}) collective-permute-start(f32[2080]{0:T(1024)S(1)} %add.97), channel_id=1, source_target_pairs={{0,2},{2,0},{1,3},{3,1},{4,6},{6,4},{5,7},{7,5},{8,10},{10,8},{9,1... | collective-permute-start | bytes 24968 | tf_op jit(solution)/shard_map/ppermute | solution.py:202

commit v20 on v19

--- a/solution.py
+++ b/solution.py
@@ -59,7 +59,9 @@
     for i, vr in enumerate(v_refs):
         d_p = lax.dot_general(g_rows, vr[...], NT_DIMS, preferred_element_type=jnp.float32)
         contrib = (ec_l[i] * inv) * (d_p + (d_p - row_dot) * (s_l[i] - log_total))
-        attr_ref[spans[i]] += jnp.sum(contrib, axis=0)
+        src = (base_ref[2] - i + len(v_refs)) % len(v_refs)
+        at = pl.ds(pl.multiple_of(src * kc, kc), kc)
+        attr_ref[at] += jnp.sum(contrib, axis=0)
 
 
 def attention_kernel(base_ref, kpos_ref, q_ref, kept_ref, do_ref, *refs, tq, hp, n, split):
@@ -219,7 +221,7 @@
     context_len = key_count * ctx_count
     query_base = context_len - query_count * ctx_count * rep_count
     base = (query_base + (ctx_at * rep_count + rep_at) * query_count).astype(jnp.int32)
-    base = jnp.stack([base, rep_at.astype(jnp.int32)])
+    base = jnp.stack([base, rep_at.astype(jnp.int32), ctx_at.astype(jnp.int32)])
 
     def needed(receiver, block):
         last_query = query_base + (receiver * rep_count + rep_count) * query_count - 1
@@ -231,8 +233,10 @@
     kept = jnp.where(
         jnp.any(seg_shift[:, None] == masked_segments[None, :], axis=1), 0.0, 1.0
     ).astype(jnp.float32)[None, :]
+    inverse = (ctx_at - jnp.arange(ctx_count, dtype=jnp.int32)) % ctx_count
+    seg_abs = seg_shift.reshape(ctx_count, key_count)[inverse].reshape(-1)
     onehot = (
-        seg_shift[:, None] == jnp.arange(SEG_DEV * ctx_count, dtype=jnp.int32)[None, :]
+        seg_abs[:, None] == jnp.arange(SEG_DEV * ctx_count, dtype=jnp.int32)[None, :]
     ).astype(jnp.float32)
 
     grad_masked = jnp.where(response[:, None] > 0, cotangent, jnp.zeros_like(cotangent))
@@ -244,7 +248,7 @@
     )
 
     inverse = (ctx_at - jnp.arange(ctx_count, dtype=jnp.int32)) % ctx_count
-    attr_abs = attr.reshape(ctx_count, key_count)[inverse].reshape(-1)
+    attr_abs = attr
     seg_part = jnp.dot(attr, onehot, precision=lax.Precision.HIGHEST)
     summed = butterfly_sum(jnp.concatenate([attr_abs, seg_part]), ("rep", "ctx", "head"))
     attr_all = summed[:context_len]

time: 100 us -> 102 us (1.020)
  other arithmetic: 6.58 us -> 7.97 us
  transfers between devices with their start and end apart: 14 -> 14, of which waited for: 4 -> 4; matrix products, arithmetic and copies ran while one was open for 26% -> 27% of each run, Pallas kernels for 0% -> 0%
where the time goes in v20:
time: 102 us; the launch traced here: 101 us
  starting transfers between devices  37 us (36%)
  matrix products  23.5 us (23%)
  Pallas kernels  20.6 us (20%)
  waiting for transfers between devices  8.6 us (8%)
  other arithmetic  7.97 us (8%)
  local copies, waits for them, and re-layouts  2.8 us (3%)
    pallas_call x1, Pallas kernels, fused_attention(): pl.pallas_call(functools.partial(attention_kernel, tq=tq, hp=hp, n=n, spl...  20.6 us
    ppermute x4, starting transfers between devices, butterfly_sum(): total = total + lax.ppermute(total, axis, [(i, i ^ bit) for i in range(n)])  19.9 us
    dot_general x1, matrix products, local(): jnp.dot(grad_masked, out_weight.T, preferred_element_type=jnp.float32)  12.6 us
    ppermute x2, starting transfers between devices, relay_gather(): forward.append(lax.ppermute(payload, 'ctx', fwd) if fwd else zero)  11.3 us
    dot_general x1, matrix products, local(): send = jnp.dot(delta, send_w, preferred_element_type=jnp.float32)  4.82 us
    dot_general x1, matrix products, local(): jnp.dot(delta, keep_w, preferred_element_type=jnp.float32)  4.82 us
    ppermute x2, waiting for transfers between devices, relay_gather(): backward.append(lax.ppermute(payload, 'ctx', bwd) if bwd else zero)  4.72 us
    ppermute x4, waiting for transfers between devices, butterfly_sum(): total = total + lax.ppermute(total, axis, [(i, i ^ bit) for i in range(n)])  3.35 us
  transfers between devices with their start and end apart: 14, of which 4 were waited for; matrix products, arithmetic and copies ran while one was open for 27% of the time, Pallas kernels for 0%

profile of v20, /device:TPU:0, one launch (start us, length us, event | category | flops | bytes accessed | tf_op | source)
XLA Modules:
  0.0 101.3 jit_solution(3704049485788516680)
XLA Ops:
  0.6 0.0 copy-start.3
  0.6 0.7 convert_element_type.29
  1.4 1.1 %broadcast_select_fusion.3 = bf16[512,512]{1,0:T(8,128)(2,1)S(1)} fusion(bf16[512,512]{1,0:T(8,128)(2,1)} %param.11, bf16[512,512]{1,0:T(8,128)(2,1)} %param.12, pred[]{:T(512)S(6)} %eq.19), kind=kLoop, calls=%fused_computation.19 | loop fusion | flops 262144 | bytes 1572865 | tf_op jit(solution)/shard_map/jit(_where)/select_n | solution.py:178
  2.5 0.8 pad_maximum_fusion.refs_0_
  3.3 6.0 %collective-permute-start.3 = (bf16[528,512]{1,0:T(8,128)(2,1)}, bf16[528,512]{1,0:T(8,128)(2,1)S(1)}, u32[]{:S(2)}, u32[]{:S(2)}) collective-permute-start(bf16[528,512]{1,0:T(8,128)(2,1)} %pad_maximum_fusion.refs_0_), channel_id=1, source_target_pairs={{0,8},{4,12},{1,9},{5,13},{2,10},{6,14},{3,11},{7,15},{16,24},{20,... | collective-permute-start | bytes 1622024 | tf_op jit(solution)/shard_map/ppermute | solution.py:156
  9.3 1.3 %collective-permute-start.4 = (bf16[528,512]{1,0:T(8,128)(2,1)}, bf16[528,512]{1,0:T(8,128)(2,1)S(1)}, u32[]{:S(2)}, u32[]{:S(2)}) collective-permute-start(bf16[528,512]{1,0:T(8,128)(2,1)} %pad_maximum_fusion.refs_0_), channel_id=1, source_target_pairs={{8,0},{9,1},{10,2},{11,3},{24,16},{25,17},{26,18},{27,19}} | collective-permute-start | bytes 1622024 | tf_op jit(solution)/shard_map/ppermute | solution.py:162
  10.6 1.3 %collective-permute-start.7 = (bf16[528,512]{1,0:T(8,128)(2,1)}, bf16[528,512]{1,0:T(8,128)(2,1)S(1)}, u32[]{:S(2)}, u32[]{:S(2)}) collective-permute-start(bf16[528,512]{1,0:T(8,128)(2,1)} %pad_maximum_fusion.refs_0_), channel_id=1, source_target_pairs={{4,0},{8,4},{12,8},{5,1},{9,5},{13,9},{6,2},{10,6},{14,10},{7,3},{... | collective-permute-start | bytes 1622024 | tf_op jit(solution)/shard_map/ppermute | solution.py:162
  11.9 5.4 %collective-permute-start.1 = (bf16[528,512]{1,0:T(8,128)(2,1)}, bf16[528,512]{1,0:T(8,128)(2,1)}, u32[]{:S(2)}, u32[]{:S(2)}) collective-permute-start(bf16[528,512]{1,0:T(8,128)(2,1)} %pad_maximum_fusion.refs_0_), channel_id=1, source_target_pairs={{0,4},{4,8},{8,12},{1,5},{5,9},{9,13},{2,6},{6,10},{10,14},{3,7},{... | collective-permute-start | bytes 1622024 | tf_op jit(solution)/shard_map/ppermute | solution.py:156
  17.3 0.0 collective-permute-start
  17.3 0.7 broadcast_compare_fusion
  17.9 12.6 %convolution_convert_fusion.do_ref = bf16[128,2048]{1,0:T(8,128)(2,1)} fusion(bf16[2048,4096]{1,0:T(8,128)(2,1)} %param.13, bf16[128,4096]{1,0:T(8,128)(2,1)} %param.14, pred[128]{0:T(512)(128)(4,1)S(1)} %broadcast_compare_fusion), kind=kOutput, calls=%fused_computation.6 | convolution fusion | flops 2148270080 | bytes 18350208 | tf_op jit(solution)/shard_map/dot_general | solution.py:243
  30.5 0.1 add_bitcast_fusion
  30.6 0.0 collective-permute-done.3
  30.6 0.9 collective-permute-start.6
  31.5 0.6 copy.11
  32.1 0.0 collective-permute-done.4
  32.1 0.1 broadcast_select_fusion.1.refs_2_
  32.2 0.0 copy-start
  32.2 0.6 collective-permute-start.5
  32.7 0.0 collective-permute-done.1
  32.8 0.0 copy-start.2
  32.8 0.1 collective-permute-start.2
  32.9 4.7 %collective-permute-done.7 = bf16[528,512]{1,0:T(8,128)(2,1)S(1)} collective-permute-done((bf16[528,512]{1,0:T(8,128)(2,1)}, bf16[528,512]{1,0:T(8,128)(2,1)S(1)}, u32[]{:S(2)}, u32[]{:S(2)}) %collective-permute-start.7) | collective-permute-done | bytes 540704 | tf_op jit(solution)/shard_map/ppermute | solution.py:162
  37.6 0.0 collective-permute-done.6
  37.6 0.1 broadcast_select_fusion.refs_3_
  37.7 0.0 copy-start.1
  37.7 0.1 collective-permute-start.8
  37.8 0.6 pad_add_fusion.base_ref
  38.4 0.0 collective-permute-done.refs_4_
  38.4 0.7 fusion.15
  39.1 0.0 collective-permute-done.5.refs_6_
  39.1 0.0 copy-start.4
  39.1 0.0 collective-permute-done.2.refs_5_
  39.2 0.0 copy-start.5
  39.2 0.5 collective-permute-done.8.refs_7_
  39.7 0.2 copy-done.4
  39.9 0.2 copy-done.5
  40.1 0.0 copy-done.3
  40.2 0.1 compare_reduce_fusion
  40.3 0.6 broadcast_select_fusion.4
  40.9 0.6 gather_fusion
  41.4 0.0 copy-done
  41.4 0.0 copy-done.2
  41.5 0.0 copy-done.1
  41.5 0.0 copy-done.6
  41.5 20.6 %shard_map.103 = (bf16[128,2048]{1,0:T(8,128)(2,1)}, f32[2048]{0:T(1024)}) custom-call(s32[3]{0:T(128)} %pad_add_fusion.base_ref, s32[1,2048]{1,0:T(1,128)} %bitcast.22, bf16[128,2048]{1,0:T(8,128)(2,1)} %q_ref.1, f32[1,2048]{1,0:T(1,128)} %bitcast.21, bf16[128,2048]{1,0:T(8,128)(2,1)} %convolution_convert_fusion.do_ref, ...), custom_call_target="tpu_custom_call" | custom-call | flops 4294967296 | bytes 5775360 | tf_op jit(solution)/shard_map/pallas_call | solution.py:119
  62.0 1.3 %convolution_bitcast_fusion = f32[32]{0:T(128)S(1)} fusion(f32[2048,1]{0,1:T(1,128)} %bitcast.20, s32[2048]{0:T(1024)S(1)} %bitcast.23), kind=kOutput, calls=%fused_computation.7 | convolution fusion | flops 851968 | bytes 16512 | tf_op jit(solution)/shard_map/dot_general | solution.py:252
  63.3 0.7 pad_maximum_fusion.1
  64.0 0.5 collective-permute-start.10
  64.5 4.8 %fusion.4 = bf16[128,2048]{1,0:T(8,128)(2,1)S(1)} fusion(bf16[128,2048]{1,0:T(8,128)(2,1)} %get-tuple-element.17, bf16[2048,4096]{1,0:T(8,128)(2,1)} %param.13, s32[]{:T(128)S(6)} %select_n.122), kind=kOutput, calls=%fused_computation.5 | convolution fusion | flops 1074003968 | bytes 9437188 | tf_op jit(solution)/shard_map/dot_general | solution.py:260
  69.3 1.5 %collective-permute-start.9 = (bf16[128,2048]{1,0:T(8,128)(2,1)S(1)}, bf16[128,2048]{1,0:T(8,128)(2,1)S(1)}, u32[]{:S(2)}, u32[]{:S(2)}) collective-permute-start(bf16[128,2048]{1,0:T(8,128)(2,1)S(1)} %fusion.4), channel_id=1, source_target_pairs={{0,2},{2,0},{1,3},{3,1},{4,6},{6,4},{5,7},{7,5},{8,10},{10,8},{9,1... | collective-permute-start | bytes 1572872 | tf_op jit(solution)/shard_map/ppermute | solution.py:261
  70.9 0.0 collective-permute-done.10
  70.9 0.7 fusion.23
  71.6 9.4 %collective-permute-start.11 = (f32[2080]{0:T(1024)S(1)}, f32[2080]{0:T(1024)S(1)}, u32[]{:S(2)}, u32[]{:S(2)}) collective-permute-start(f32[2080]{0:T(1024)S(1)} %fusion.23), channel_id=1, source_target_pairs={{0,4},{4,0},{8,12},{12,8},{1,5},{5,1},{9,13},{13,9},{2,6},{6,2},{1... | collective-permute-start | bytes 24968 | tf_op jit(solution)/shard_map/ppermute | solution.py:204
  81.0 1.7 %collective-permute-done.11 = f32[2080]{0:T(1024)S(1)} collective-permute-done((f32[2080]{0:T(1024)S(1)}, f32[2080]{0:T(1024)S(1)}, u32[]{:S(2)}, u32[]{:S(2)}) %collective-permute-start.11) | collective-permute-done | bytes 8352 | tf_op jit(solution)/shard_map/ppermute | solution.py:204
  82.6 9.5 %collective-permute-start.12 = (f32[2080]{0:T(1024)S(1)}, f32[2080]{0:T(1024)S(1)}, u32[]{:S(2)}, u32[]{:S(2)}) collective-permute-start(f32[2080]{0:T(1024)S(1)} %add.96), channel_id=1, source_target_pairs={{0,8},{4,12},{8,0},{12,4},{1,9},{5,13},{9,1},{13,5},{2,10},{6,14},... | collective-permute-start | bytes 24968 | tf_op jit(solution)/shard_map/ppermute | solution.py:204
  92.2 1.7 %collective-permute-done.12 = f32[2080]{0:T(1024)S(1)} collective-permute-done((f32[2080]{0:T(1024)S(1)}, f32[2080]{0:T(1024)S(1)}, u32[]{:S(2)}, u32[]{:S(2)}) %collective-permute-start.12) | collective-permute-done | bytes 8352 | tf_op jit(solution)/shard_map/ppermute | solution.py:204
  93.8 0.5 collective-permute-start.13
  94.4 4.8 %fusion.2 = f32[128,2048]{1,0:T(8,128)S(1)} fusion(bf16[128,2048]{1,0:T(8,128)(2,1)} %get-tuple-element.17, bf16[2048,4096]{1,0:T(8,128)(2,1)} %param.13, s32[]{:T(128)S(6)} %select_n.121), kind=kOutput, calls=%fused_computation.3 | convolution fusion | flops 1073741824 | bytes 9961476 | tf_op jit(solution)/shard_map/dot_general | solution.py:263
  99.2 0.0 collective-permute-done.13
  99.2 0.5 slice.59
  99.7 0.7 dynamic_slice.11
  100.4 0.0 collective-permute-done.9
  100.4 0.9 add_convert_fusion
  (17 shorter events, 0.2 us)
Async XLA Ops:
  0.6 39.5 %copy-start.3 = (s32[4]{0:T(128)S(1)}, s32[4]{0:T(128)}, u32[]{:S(2)}) copy-start(s32[4]{0:T(128)} %param.17) | copy-start | bytes 52
  3.3 27.3 %collective-permute-start.3 = (bf16[528,512]{1,0:T(8,128)(2,1)}, bf16[528,512]{1,0:T(8,128)(2,1)S(1)}, u32[]{:S(2)}, u32[]{:S(2)}) collective-permute-start(bf16[528,512]{1,0:T(8,128)(2,1)} %pad_maximum_fusion.refs_0_), channel_id=1, source_target_pairs={{0,8},{4,12},{1,9},{5,13},{2,10},{6,14},{3,11},{7,15},{16,24},{20,... | collective-permute-start | bytes 1622024 | tf_op jit(solution)/shard_map/ppermute | solution.py:156
  9.3 22.8 %collective-permute-start.4 = (bf16[528,512]{1,0:T(8,128)(2,1)}, bf16[528,512]{1,0:T(8,128)(2,1)S(1)}, u32[]{:S(2)}, u32[]{:S(2)}) collective-permute-start(bf16[528,512]{1,0:T(8,128)(2,1)} %pad_maximum_fusion.refs_0_), channel_id=1, source_target_pairs={{8,0},{9,1},{10,2},{11,3},{24,16},{25,17},{26,18},{27,19}} | collective-permute-start | bytes 1622024 | tf_op jit(solution)/shard_map/ppermute | solution.py:162
  10.6 27.0 %collective-permute-start.7 = (bf16[528,512]{1,0:T(8,128)(2,1)}, bf16[528,512]{1,0:T(8,128)(2,1)S(1)}, u32[]{:S(2)}, u32[]{:S(2)}) collective-permute-start(bf16[528,512]{1,0:T(8,128)(2,1)} %pad_maximum_fusion.refs_0_), channel_id=1, source_target_pairs={{4,0},{8,4},{12,8},{5,1},{9,5},{13,9},{6,2},{10,6},{14,10},{7,3},{... | collective-permute-start | bytes 1622024 | tf_op jit(solution)/shard_map/ppermute | solution.py:162
  11.9 20.9 %collective-permute-start.1 = (bf16[528,512]{1,0:T(8,128)(2,1)}, bf16[528,512]{1,0:T(8,128)(2,1)}, u32[]{:S(2)}, u32[]{:S(2)}) collective-permute-start(bf16[528,512]{1,0:T(8,128)(2,1)} %pad_maximum_fusion.refs_0_), channel_id=1, source_target_pairs={{0,4},{4,8},{8,12},{1,5},{5,9},{9,13},{2,6},{6,10},{10,14},{3,7},{... | collective-permute-start | bytes 1622024 | tf_op jit(solution)/shard_map/ppermute | solution.py:156
  17.3 21.1 %collective-permute-start = (bf16[528,512]{1,0:T(8,128)(2,1)}, bf16[528,512]{1,0:T(8,128)(2,1)}, u32[]{:S(2)}, u32[]{:S(2)}) collective-permute-start(bf16[528,512]{1,0:T(8,128)(2,1)} %pad_maximum_fusion.refs_0_), channel_id=1, source_target_pairs={{0,1},{1,0},{2,3},{3,2},{4,5},{5,4},{6,7},{7,6},{8,9},{9,8},{10,11... | collective-permute-start | bytes 1622024 | tf_op jit(solution)/shard_map/ppermute | solution.py:183
  30.6 7.0 %collective-permute-start.6 = (bf16[528,512]{1,0:T(8,128)(2,1)S(1)}, bf16[528,512]{1,0:T(8,128)(2,1)S(1)}, u32[]{:S(2)}, u32[]{:S(2)}) collective-permute-start(bf16[528,512]{1,0:T(8,128)(2,1)S(1)} %collective-permute-done.3), channel_id=1, source_target_pairs={{8,12},{9,13},{10,14},{11,15},{24,28},{25,29},{26,30},{27,31}} | collective-permute-start | bytes 1622024 | tf_op jit(solution)/shard_map/ppermute | solution.py:154
  32.2 9.3 %copy-start = (bf16[528,512]{1,0:T(8,128)(2,1)}, bf16[528,512]{1,0:T(8,128)(2,1)S(1)}, u32[]{:S(2)}) copy-start(bf16[528,512]{1,0:T(8,128)(2,1)S(1)} %broadcast_select_fusion.1.refs_2_) | copy-start | bytes 1622020
  32.2 6.9 %collective-permute-start.5 = (bf16[528,512]{1,0:T(8,128)(2,1)S(1)}, bf16[528,512]{1,0:T(8,128)(2,1)S(1)}, u32[]{:S(2)}, u32[]{:S(2)}) collective-permute-start(bf16[528,512]{1,0:T(8,128)(2,1)S(1)} %broadcast_select_fusion.1.refs_2_), channel_id=1, source_target_pairs={{0,1},{1,0},{2,3},{3,2},{4,5},{5,4},{6,7},{7,6},{8,9},{9,8},{10,11... | collective-permute-start | bytes 1622024 | tf_op jit(solution)/shard_map/ppermute | solution.py:183
  32.8 8.6 %copy-start.2 = (bf16[528,512]{1,0:T(8,128)(2,1)}, bf16[528,512]{1,0:T(8,128)(2,1)S(1)}, u32[]{:S(2)}) copy-start(bf16[528,512]{1,0:T(8,128)(2,1)S(1)} %broadcast_select_fusion.2.refs_1_) | copy-start | bytes 1622020
  32.8 6.3 %collective-permute-start.2 = (bf16[528,512]{1,0:T(8,128)(2,1)S(1)}, bf16[528,512]{1,0:T(8,128)(2,1)S(1)}, u32[]{:S(2)}, u32[]{:S(2)}) collective-permute-start(bf16[528,512]{1,0:T(8,128)(2,1)S(1)} %broadcast_select_fusion.2.refs_1_), channel_id=1, source_target_pairs={{0,1},{1,0},{2,3},{3,2},{4,5},{5,4},{6,7},{7,6},{8,9},{9,8},{10,11... | collective-permute-start | bytes 1622024 | tf_op jit(solution)/shard_map/ppermute | solution.py:183
  37.7 3.8 %copy-start.1 = (bf16[528,512]{1,0:T(8,128)(2,1)}, bf16[528,512]{1,0:T(8,128)(2,1)S(1)}, u32[]{:S(2)}) copy-start(bf16[528,512]{1,0:T(8,128)(2,1)S(1)} %broadcast_select_fusion.refs_3_) | copy-start | bytes 1622020
  37.7 2.0 %collective-permute-start.8 = (bf16[528,512]{1,0:T(8,128)(2,1)S(1)}, bf16[528,512]{1,0:T(8,128)(2,1)S(1)}, u32[]{:S(2)}, u32[]{:S(2)}) collective-permute-start(bf16[528,512]{1,0:T(8,128)(2,1)S(1)} %broadcast_select_fusion.refs_3_), channel_id=1, source_target_pairs={{0,1},{1,0},{2,3},{3,2},{4,5},{5,4},{6,7},{7,6},{8,9},{9,8},{10,11... | collective-permute-start | bytes 1622024 | tf_op jit(solution)/shard_map/ppermute | solution.py:183
  39.1 0.8 copy-start.4
  39.2 1.0 copy-start.5
  39.7 1.8 %copy-start.6 = (bf16[528,512]{1,0:T(8,128)(2,1)}, bf16[528,512]{1,0:T(8,128)(2,1)S(1)}, u32[]{:S(2)}) copy-start(bf16[528,512]{1,0:T(8,128)(2,1)S(1)} %collective-permute-done.8.refs_7_) | copy-start | bytes 1622020
  64.0 6.9 %collective-permute-start.10 = (f32[2080]{0:T(1024)S(1)}, f32[2080]{0:T(1024)S(1)}, u32[]{:S(2)}, u32[]{:S(2)}) collective-permute-start(f32[2080]{0:T(1024)S(1)} %pad_maximum_fusion.1), channel_id=1, source_target_pairs={{0,1},{1,0},{2,3},{3,2},{4,5},{5,4},{6,7},{7,6},{8,9},{9,8},{10,11... | collective-permute-start | bytes 24968 | tf_op jit(solution)/shard_map/ppermute | solution.py:204
  69.3 31.0 %collective-permute-start.9 = (bf16[128,2048]{1,0:T(8,128)(2,1)S(1)}, bf16[128,2048]{1,0:T(8,128)(2,1)S(1)}, u32[]{:S(2)}, u32[]{:S(2)}) collective-permute-start(bf16[128,2048]{1,0:T(8,128)(2,1)S(1)} %fusion.4), channel_id=1, source_target_pairs={{0,2},{2,0},{1,3},{3,1},{4,6},{6,4},{5,7},{7,5},{8,10},{10,8},{9,1... | collective-permute-start | bytes 1572872 | tf_op jit(solution)/shard_map/ppermute | solution.py:261
  71.6 11.0 %collective-permute-start.11 = (f32[2080]{0:T(1024)S(1)}, f32[2080]{0:T(1024)S(1)}, u32[]{:S(2)}, u32[]{:S(2)}) collective-permute-start(f32[2080]{0:T(1024)S(1)} %fusion.23), channel_id=1, source_target_pairs={{0,4},{4,0},{8,12},{12,8},{1,5},{5,1},{9,13},{13,9},{2,6},{6,2},{1... | collective-permute-start | bytes 24968 | tf_op jit(solution)/shard_map/ppermute | solution.py:204
  82.6 11.2 %collective-permute-start.12 = (f32[2080]{0:T(1024)S(1)}, f32[2080]{0:T(1024)S(1)}, u32[]{:S(2)}, u32[]{:S(2)}) collective-permute-start(f32[2080]{0:T(1024)S(1)} %add.96), channel_id=1, source_target_pairs={{0,8},{4,12},{8,0},{12,4},{1,9},{5,13},{9,1},{13,5},{2,10},{6,14},... | collective-permute-start | bytes 24968 | tf_op jit(solution)/shard_map/ppermute | solution.py:204
  93.8 5.4 %collective-permute-start.13 = (f32[2080]{0:T(1024)S(1)}, f32[2080]{0:T(1024)S(1)}, u32[]{:S(2)}, u32[]{:S(2)}) collective-permute-start(f32[2080]{0:T(1024)S(1)} %add.97), channel_id=1, source_target_pairs={{0,2},{2,0},{1,3},{3,1},{4,6},{6,4},{5,7},{7,5},{8,10},{10,8},{9,1... | collective-permute-start | bytes 24968 | tf_op jit(solution)/shard_map/ppermute | solution.py:204

commit v21 on v19

--- a/solution.py
+++ b/solution.py
@@ -245,7 +245,7 @@
 
     inverse = (ctx_at - jnp.arange(ctx_count, dtype=jnp.int32)) % ctx_count
     attr_abs = attr.reshape(ctx_count, key_count)[inverse].reshape(-1)
-    seg_part = jnp.dot(attr, onehot, precision=lax.Precision.HIGHEST)
+    seg_part = jnp.sum(jnp.where(onehot > 0.0, attr[:, None], 0.0), axis=0)
     summed = butterfly_sum(jnp.concatenate([attr_abs, seg_part]), ("rep", "ctx", "head"))
     attr_all = summed[:context_len]
     segment_attr = summed[context_len:]

time: 100 us -> 100 us (level)
  matrix products: 23.5 us -> 22.2 us
    dot_general x1 -> x0, matrix products: 1.27 us -> none  [local(): seg_part = jnp.dot(attr, onehot, precision=lax.Precision.HIGHEST)]
  transfers between devices with their start and end apart: 14 -> 14, of which waited for: 4 -> 5; matrix products, arithmetic and copies ran while one was open for 26% -> 26% of each run, Pallas kernels for 0% -> 0%
where the time goes in v21:
time: 100 us; the launch traced here: 99.6 us
  starting transfers between devices  36.6 us (37%)
  matrix products  22.2 us (22%)
  Pallas kernels  20.5 us (20%)
  waiting for transfers between devices  8.81 us (9%)
  other arithmetic  7.48 us (7%)
  local copies, waits for them, and re-layouts  3.11 us (3%)
    pallas_call x1, Pallas kernels, fused_attention(): pl.pallas_call(functools.partial(attention_kernel, tq=tq, hp=hp, n=n, spl...  20.5 us
    ppermute x4, starting transfers between devices, butterfly_sum(): total = total + lax.ppermute(total, axis, [(i, i ^ bit) for i in range(n)])  19.7 us
    dot_general x1, matrix products, local(): jnp.dot(grad_masked, out_weight.T, preferred_element_type=jnp.float32)  12.6 us
    ppermute x2, starting transfers between devices, relay_gather(): forward.append(lax.ppermute(payload, 'ctx', fwd) if fwd else zero)  11.3 us
    dot_general x1, matrix products, local(): send = jnp.dot(delta, send_w, preferred_element_type=jnp.float32)  4.82 us
    dot_general x1, matrix products, local(): jnp.dot(delta, keep_w, preferred_element_type=jnp.float32)  4.82 us
    ppermute x2, waiting for transfers between devices, relay_gather(): backward.append(lax.ppermute(payload, 'ctx', bwd) if bwd else zero)  4.76 us
    ppermute x4, waiting for transfers between devices, butterfly_sum(): total = total + lax.ppermute(total, axis, [(i, i ^ bit) for i in range(n)])  3.4 us
  transfers between devices with their start and end apart: 14, of which 5 were waited for; matrix products, arithmetic and copies ran while one was open for 26% of the time, Pallas kernels for 0%

profile of v21, /device:TPU:0, one launch (start us, length us, event | category | flops | bytes accessed | tf_op | source)
XLA Modules:
  0.0 99.6 jit_solution(15450583843263617170)
XLA Ops:
  0.6 0.0 copy-start.3
  0.6 0.7 convert_element_type.25
  1.4 1.1 %broadcast_select_fusion.3 = bf16[512,512]{1,0:T(8,128)(2,1)S(1)} fusion(bf16[512,512]{1,0:T(8,128)(2,1)} %param.11, bf16[512,512]{1,0:T(8,128)(2,1)} %param.12, pred[]{:T(512)S(6)} %eq.17), kind=kLoop, calls=%fused_computation.16 | loop fusion | flops 262144 | bytes 1572865 | tf_op jit(solution)/shard_map/jit(_where)/select_n | solution.py:176
  2.5 0.8 pad_maximum_fusion.refs_0_
  3.3 6.0 %collective-permute-start.3 = (bf16[528,512]{1,0:T(8,128)(2,1)}, bf16[528,512]{1,0:T(8,128)(2,1)S(1)}, u32[]{:S(2)}, u32[]{:S(2)}) collective-permute-start(bf16[528,512]{1,0:T(8,128)(2,1)} %pad_maximum_fusion.refs_0_), channel_id=1, source_target_pairs={{0,8},{4,12},{1,9},{5,13},{2,10},{6,14},{3,11},{7,15},{16,24},{20,... | collective-permute-start | bytes 1622024 | tf_op jit(solution)/shard_map/ppermute | solution.py:154
  9.3 1.3 %collective-permute-start.4 = (bf16[528,512]{1,0:T(8,128)(2,1)}, bf16[528,512]{1,0:T(8,128)(2,1)S(1)}, u32[]{:S(2)}, u32[]{:S(2)}) collective-permute-start(bf16[528,512]{1,0:T(8,128)(2,1)} %pad_maximum_fusion.refs_0_), channel_id=1, source_target_pairs={{8,0},{9,1},{10,2},{11,3},{24,16},{25,17},{26,18},{27,19}} | collective-permute-start | bytes 1622024 | tf_op jit(solution)/shard_map/ppermute | solution.py:160
  10.6 1.3 %collective-permute-start.7 = (bf16[528,512]{1,0:T(8,128)(2,1)}, bf16[528,512]{1,0:T(8,128)(2,1)S(1)}, u32[]{:S(2)}, u32[]{:S(2)}) collective-permute-start(bf16[528,512]{1,0:T(8,128)(2,1)} %pad_maximum_fusion.refs_0_), channel_id=1, source_target_pairs={{4,0},{8,4},{12,8},{5,1},{9,5},{13,9},{6,2},{10,6},{14,10},{7,3},{... | collective-permute-start | bytes 1622024 | tf_op jit(solution)/shard_map/ppermute | solution.py:160
  11.9 5.4 %collective-permute-start.1 = (bf16[528,512]{1,0:T(8,128)(2,1)}, bf16[528,512]{1,0:T(8,128)(2,1)}, u32[]{:S(2)}, u32[]{:S(2)}) collective-permute-start(bf16[528,512]{1,0:T(8,128)(2,1)} %pad_maximum_fusion.refs_0_), channel_id=1, source_target_pairs={{0,4},{4,8},{8,12},{1,5},{5,9},{9,13},{2,6},{6,10},{10,14},{3,7},{... | collective-permute-start | bytes 1622024 | tf_op jit(solution)/shard_map/ppermute | solution.py:154
  17.2 0.0 collective-permute-start
  17.2 0.7 broadcast_compare_fusion
  17.9 12.6 %convolution_convert_fusion.do_ref = bf16[128,2048]{1,0:T(8,128)(2,1)} fusion(bf16[2048,4096]{1,0:T(8,128)(2,1)} %param.13, bf16[128,4096]{1,0:T(8,128)(2,1)} %param.14, pred[128]{0:T(512)(128)(4,1)S(1)} %broadcast_compare_fusion), kind=kOutput, calls=%fused_computation.6 | convolution fusion | flops 2148270080 | bytes 18350208 | tf_op jit(solution)/shard_map/dot_general | solution.py:239
  30.5 0.1 add_bitcast_fusion
  30.6 0.0 collective-permute-done.3
  30.6 0.7 collective-permute-start.6
  31.3 0.6 copy.11
  31.9 0.0 collective-permute-done.4
  31.9 0.1 broadcast_select_fusion.1.refs_2_
  32.0 0.0 copy-start
  32.0 0.6 collective-permute-start.5
  32.6 0.2 collective-permute-done.1
  32.8 0.0 copy-start.2
  32.8 0.1 collective-permute-start.2
  32.9 4.8 %collective-permute-done.7 = bf16[528,512]{1,0:T(8,128)(2,1)S(1)} collective-permute-done((bf16[528,512]{1,0:T(8,128)(2,1)}, bf16[528,512]{1,0:T(8,128)(2,1)S(1)}, u32[]{:S(2)}, u32[]{:S(2)}) %collective-permute-start.7) | collective-permute-done | bytes 540704 | tf_op jit(solution)/shard_map/ppermute | solution.py:160
  37.6 0.0 collective-permute-done.6
  37.6 0.1 broadcast_select_fusion.refs_3_
  37.7 0.0 copy-start.1
  37.7 0.1 collective-permute-start.8
  37.8 0.6 pad_add_fusion.base_ref
  38.4 0.0 collective-permute-done.refs_4_
  38.4 0.7 fusion.14
  39.1 0.0 collective-permute-done.5.refs_6_
  39.1 0.0 copy-start.4
  39.2 0.0 collective-permute-done.2.refs_5_
  39.2 0.0 copy-start.5
  39.2 0.5 collective-permute-done.8.refs_7_
  39.7 0.0 copy-start.6
  39.7 0.0 copy-done.3
  39.7 0.1 compare_reduce_fusion
  39.8 0.6 broadcast_select_fusion.4
  40.5 0.0 copy-done.4
  40.5 0.0 copy-done.5
  40.5 0.0 copy-done
  40.5 0.0 copy-done.2
  40.5 0.0 copy-done.1
  40.5 0.0 copy-done.6
  40.5 20.5 %shard_map.103 = (bf16[128,2048]{1,0:T(8,128)(2,1)}, f32[2048]{0:T(1024)}) custom-call(s32[2]{0:T(128)} %pad_add_fusion.base_ref, s32[1,2048]{1,0:T(1,128)} %bitcast.18, bf16[128,2048]{1,0:T(8,128)(2,1)} %q_ref.1, f32[1,2048]{1,0:T(1,128)} %bitcast.17, bf16[128,2048]{1,0:T(8,128)(2,1)} %convolution_convert_fusion.do_ref, ...), custom_call_target="tpu_custom_call" | custom-call | flops 4294967296 | bytes 5775360 | tf_op jit(solution)/shard_map/pallas_call | solution.py:117
  61.0 0.8 select_reduce_fusion
  61.9 0.7 reshape.169
  62.6 0.6 gather_fusion
  63.2 0.3 collective-permute-start.10
  63.5 4.8 %fusion.4 = bf16[128,2048]{1,0:T(8,128)(2,1)S(1)} fusion(bf16[128,2048]{1,0:T(8,128)(2,1)} %get-tuple-element.17, bf16[2048,4096]{1,0:T(8,128)(2,1)} %param.13, s32[]{:T(128)S(6)} %select_n.126), kind=kOutput, calls=%fused_computation.5 | convolution fusion | flops 1074003968 | bytes 9437188 | tf_op jit(solution)/shard_map/dot_general | solution.py:256
  68.3 1.6 %collective-permute-start.9 = (bf16[128,2048]{1,0:T(8,128)(2,1)S(1)}, bf16[128,2048]{1,0:T(8,128)(2,1)S(1)}, u32[]{:S(2)}, u32[]{:S(2)}) collective-permute-start(bf16[128,2048]{1,0:T(8,128)(2,1)S(1)} %fusion.4), channel_id=1, source_target_pairs={{0,2},{2,0},{1,3},{3,1},{4,6},{6,4},{5,7},{7,5},{8,10},{10,8},{9,1... | collective-permute-start | bytes 1572872 | tf_op jit(solution)/shard_map/ppermute | solution.py:257
  69.9 0.0 collective-permute-done.10
  69.9 9.9 %collective-permute-start.11 = (f32[2080]{0:T(1024)S(1)}, f32[2080]{0:T(1024)S(1)}, u32[]{:S(2)}, u32[]{:S(2)}) collective-permute-start(f32[2080]{0:T(1024)S(1)} %fusion.22), channel_id=1, source_target_pairs={{0,4},{4,0},{8,12},{12,8},{1,5},{5,1},{9,13},{13,9},{2,6},{6,2},{1... | collective-permute-start | bytes 24968 | tf_op jit(solution)/shard_map/ppermute | solution.py:202
  79.8 1.7 %collective-permute-done.11 = f32[2080]{0:T(1024)S(1)} collective-permute-done((f32[2080]{0:T(1024)S(1)}, f32[2080]{0:T(1024)S(1)}, u32[]{:S(2)}, u32[]{:S(2)}) %collective-permute-start.11) | collective-permute-done | bytes 8352 | tf_op jit(solution)/shard_map/ppermute | solution.py:202
  81.5 9.0 %collective-permute-start.12 = (f32[2080]{0:T(1024)S(1)}, f32[2080]{0:T(1024)S(1)}, u32[]{:S(2)}, u32[]{:S(2)}) collective-permute-start(f32[2080]{0:T(1024)S(1)} %add.96), channel_id=1, source_target_pairs={{0,8},{4,12},{8,0},{12,4},{1,9},{5,13},{9,1},{13,5},{2,10},{6,14},... | collective-permute-start | bytes 24968 | tf_op jit(solution)/shard_map/ppermute | solution.py:202
  90.5 1.7 %collective-permute-done.12 = f32[2080]{0:T(1024)S(1)} collective-permute-done((f32[2080]{0:T(1024)S(1)}, f32[2080]{0:T(1024)S(1)}, u32[]{:S(2)}, u32[]{:S(2)}) %collective-permute-start.12) | collective-permute-done | bytes 8352 | tf_op jit(solution)/shard_map/ppermute | solution.py:202
  92.2 0.5 collective-permute-start.13
  92.7 4.8 %fusion.2 = f32[128,2048]{1,0:T(8,128)S(1)} fusion(bf16[128,2048]{1,0:T(8,128)(2,1)} %get-tuple-element.17, bf16[2048,4096]{1,0:T(8,128)(2,1)} %param.13, s32[]{:T(128)S(6)} %select_n.125), kind=kOutput, calls=%fused_computation.3 | convolution fusion | flops 1073741824 | bytes 9961476 | tf_op jit(solution)/shard_map/dot_general | solution.py:259
  97.5 0.0 collective-permute-done.13
  97.6 0.5 slice.59
  98.1 0.7 dynamic_slice.11
  98.7 0.0 collective-permute-done.9
  98.7 0.9 add_convert_fusion
  (17 shorter events, 0.2 us)
Async XLA Ops:
  0.6 39.1 %copy-start.3 = (s32[4]{0:T(128)S(1)}, s32[4]{0:T(128)}, u32[]{:S(2)}) copy-start(s32[4]{0:T(128)} %param.17) | copy-start | bytes 52
  3.3 27.3 %collective-permute-start.3 = (bf16[528,512]{1,0:T(8,128)(2,1)}, bf16[528,512]{1,0:T(8,128)(2,1)S(1)}, u32[]{:S(2)}, u32[]{:S(2)}) collective-permute-start(bf16[528,512]{1,0:T(8,128)(2,1)} %pad_maximum_fusion.refs_0_), channel_id=1, source_target_pairs={{0,8},{4,12},{1,9},{5,13},{2,10},{6,14},{3,11},{7,15},{16,24},{20,... | collective-permute-start | bytes 1622024 | tf_op jit(solution)/shard_map/ppermute | solution.py:154
  9.3 22.6 %collective-permute-start.4 = (bf16[528,512]{1,0:T(8,128)(2,1)}, bf16[528,512]{1,0:T(8,128)(2,1)S(1)}, u32[]{:S(2)}, u32[]{:S(2)}) collective-permute-start(bf16[528,512]{1,0:T(8,128)(2,1)} %pad_maximum_fusion.refs_0_), channel_id=1, source_target_pairs={{8,0},{9,1},{10,2},{11,3},{24,16},{25,17},{26,18},{27,19}} | collective-permute-start | bytes 1622024 | tf_op jit(solution)/shard_map/ppermute | solution.py:160
  10.6 27.0 %collective-permute-start.7 = (bf16[528,512]{1,0:T(8,128)(2,1)}, bf16[528,512]{1,0:T(8,128)(2,1)S(1)}, u32[]{:S(2)}, u32[]{:S(2)}) collective-permute-start(bf16[528,512]{1,0:T(8,128)(2,1)} %pad_maximum_fusion.refs_0_), channel_id=1, source_target_pairs={{4,0},{8,4},{12,8},{5,1},{9,5},{13,9},{6,2},{10,6},{14,10},{7,3},{... | collective-permute-start | bytes 1622024 | tf_op jit(solution)/shard_map/ppermute | solution.py:160
  11.9 20.8 %collective-permute-start.1 = (bf16[528,512]{1,0:T(8,128)(2,1)}, bf16[528,512]{1,0:T(8,128)(2,1)}, u32[]{:S(2)}, u32[]{:S(2)}) collective-permute-start(bf16[528,512]{1,0:T(8,128)(2,1)} %pad_maximum_fusion.refs_0_), channel_id=1, source_target_pairs={{0,4},{4,8},{8,12},{1,5},{5,9},{9,13},{2,6},{6,10},{10,14},{3,7},{... | collective-permute-start | bytes 1622024 | tf_op jit(solution)/shard_map/ppermute | solution.py:154
  17.2 21.2 %collective-permute-start = (bf16[528,512]{1,0:T(8,128)(2,1)}, bf16[528,512]{1,0:T(8,128)(2,1)}, u32[]{:S(2)}, u32[]{:S(2)}) collective-permute-start(bf16[528,512]{1,0:T(8,128)(2,1)} %pad_maximum_fusion.refs_0_), channel_id=1, source_target_pairs={{0,1},{1,0},{2,3},{3,2},{4,5},{5,4},{6,7},{7,6},{8,9},{9,8},{10,11... | collective-permute-start | bytes 1622024 | tf_op jit(solution)/shard_map/ppermute | solution.py:181
  30.6 7.0 %collective-permute-start.6 = (bf16[528,512]{1,0:T(8,128)(2,1)S(1)}, bf16[528,512]{1,0:T(8,128)(2,1)S(1)}, u32[]{:S(2)}, u32[]{:S(2)}) collective-permute-start(bf16[528,512]{1,0:T(8,128)(2,1)S(1)} %collective-permute-done.3), channel_id=1, source_target_pairs={{8,12},{9,13},{10,14},{11,15},{24,28},{25,29},{26,30},{27,31}} | collective-permute-start | bytes 1622024 | tf_op jit(solution)/shard_map/ppermute | solution.py:152
  32.0 8.5 %copy-start = (bf16[528,512]{1,0:T(8,128)(2,1)}, bf16[528,512]{1,0:T(8,128)(2,1)S(1)}, u32[]{:S(2)}) copy-start(bf16[528,512]{1,0:T(8,128)(2,1)S(1)} %broadcast_select_fusion.1.refs_2_) | copy-start | bytes 1622020
  32.0 7.2 %collective-permute-start.5 = (bf16[528,512]{1,0:T(8,128)(2,1)S(1)}, bf16[528,512]{1,0:T(8,128)(2,1)S(1)}, u32[]{:S(2)}, u32[]{:S(2)}) collective-permute-start(bf16[528,512]{1,0:T(8,128)(2,1)S(1)} %broadcast_select_fusion.1.refs_2_), channel_id=1, source_target_pairs={{0,1},{1,0},{2,3},{3,2},{4,5},{5,4},{6,7},{7,6},{8,9},{9,8},{10,11... | collective-permute-start | bytes 1622024 | tf_op jit(solution)/shard_map/ppermute | solution.py:181
  32.8 7.7 %copy-start.2 = (bf16[528,512]{1,0:T(8,128)(2,1)}, bf16[528,512]{1,0:T(8,128)(2,1)S(1)}, u32[]{:S(2)}) copy-start(bf16[528,512]{1,0:T(8,128)(2,1)S(1)} %broadcast_select_fusion.2.refs_1_) | copy-start | bytes 1622020
  32.8 6.4 %collective-permute-start.2 = (bf16[528,512]{1,0:T(8,128)(2,1)S(1)}, bf16[528,512]{1,0:T(8,128)(2,1)S(1)}, u32[]{:S(2)}, u32[]{:S(2)}) collective-permute-start(bf16[528,512]{1,0:T(8,128)(2,1)S(1)} %broadcast_select_fusion.2.refs_1_), channel_id=1, source_target_pairs={{0,1},{1,0},{2,3},{3,2},{4,5},{5,4},{6,7},{7,6},{8,9},{9,8},{10,11... | collective-permute-start | bytes 1622024 | tf_op jit(solution)/shard_map/ppermute | solution.py:181
  37.7 2.8 %copy-start.1 = (bf16[528,512]{1,0:T(8,128)(2,1)}, bf16[528,512]{1,0:T(8,128)(2,1)S(1)}, u32[]{:S(2)}) copy-start(bf16[528,512]{1,0:T(8,128)(2,1)S(1)} %broadcast_select_fusion.refs_3_) | copy-start | bytes 1622020
  37.7 2.0 %collective-permute-start.8 = (bf16[528,512]{1,0:T(8,128)(2,1)S(1)}, bf16[528,512]{1,0:T(8,128)(2,1)S(1)}, u32[]{:S(2)}, u32[]{:S(2)}) collective-permute-start(bf16[528,512]{1,0:T(8,128)(2,1)S(1)} %broadcast_select_fusion.refs_3_), channel_id=1, source_target_pairs={{0,1},{1,0},{2,3},{3,2},{4,5},{5,4},{6,7},{7,6},{8,9},{9,8},{10,11... | collective-permute-start | bytes 1622024 | tf_op jit(solution)/shard_map/ppermute | solution.py:181
  39.1 1.3 %copy-start.4 = (bf16[528,512]{1,0:T(8,128)(2,1)}, bf16[528,512]{1,0:T(8,128)(2,1)S(1)}, u32[]{:S(2)}) copy-start(bf16[528,512]{1,0:T(8,128)(2,1)S(1)} %collective-permute-done.5.refs_6_) | copy-start | bytes 1622020
  39.2 1.3 %copy-start.5 = (bf16[528,512]{1,0:T(8,128)(2,1)}, bf16[528,512]{1,0:T(8,128)(2,1)S(1)}, u32[]{:S(2)}) copy-start(bf16[528,512]{1,0:T(8,128)(2,1)S(1)} %collective-permute-done.2.refs_5_) | copy-start | bytes 1622020
  39.7 0.8 copy-start.6
  63.2 6.7 %collective-permute-start.10 = (f32[2080]{0:T(1024)S(1)}, f32[2080]{0:T(1024)S(1)}, u32[]{:S(2)}, u32[]{:S(2)}) collective-permute-start(f32[2080]{0:T(1024)S(1)} %pad_maximum_fusion.1), channel_id=1, source_target_pairs={{0,1},{1,0},{2,3},{3,2},{4,5},{5,4},{6,7},{7,6},{8,9},{9,8},{10,11... | collective-permute-start | bytes 24968 | tf_op jit(solution)/shard_map/ppermute | solution.py:202
  68.3 30.4 %collective-permute-start.9 = (bf16[128,2048]{1,0:T(8,128)(2,1)S(1)}, bf16[128,2048]{1,0:T(8,128)(2,1)S(1)}, u32[]{:S(2)}, u32[]{:S(2)}) collective-permute-start(bf16[128,2048]{1,0:T(8,128)(2,1)S(1)} %fusion.4), channel_id=1, source_target_pairs={{0,2},{2,0},{1,3},{3,1},{4,6},{6,4},{5,7},{7,5},{8,10},{10,8},{9,1... | collective-permute-start | bytes 1572872 | tf_op jit(solution)/shard_map/ppermute | solution.py:257
  69.9 11.6 %collective-permute-start.11 = (f32[2080]{0:T(1024)S(1)}, f32[2080]{0:T(1024)S(1)}, u32[]{:S(2)}, u32[]{:S(2)}) collective-permute-start(f32[2080]{0:T(1024)S(1)} %fusion.22), channel_id=1, source_target_pairs={{0,4},{4,0},{8,12},{12,8},{1,5},{5,1},{9,13},{13,9},{2,6},{6,2},{1... | collective-permute-start | bytes 24968 | tf_op jit(solution)/shard_map/ppermute | solution.py:202
  81.5 10.7 %collective-permute-start.12 = (f32[2080]{0:T(1024)S(1)}, f32[2080]{0:T(1024)S(1)}, u32[]{:S(2)}, u32[]{:S(2)}) collective-permute-start(f32[2080]{0:T(1024)S(1)} %add.96), channel_id=1, source_target_pairs={{0,8},{4,12},{8,0},{12,4},{1,9},{5,13},{9,1},{13,5},{2,10},{6,14},... | collective-permute-start | bytes 24968 | tf_op jit(solution)/shard_map/ppermute | solution.py:202
  92.2 5.3 %collective-permute-start.13 = (f32[2080]{0:T(1024)S(1)}, f32[2080]{0:T(1024)S(1)}, u32[]{:S(2)}, u32[]{:S(2)}) collective-permute-start(f32[2080]{0:T(1024)S(1)} %add.97), channel_id=1, source_target_pairs={{0,2},{2,0},{1,3},{3,1},{4,6},{6,4},{5,7},{7,5},{8,10},{10,8},{9,1... | collective-permute-start | bytes 24968 | tf_op jit(solution)/shard_map/ppermute | solution.py:202
